TPU v7x, 128 devices: a whole 4x4x4 slice. The times are simulated.
128 devices in a mesh: tm: 4 (over x), space: 16 (over z, y), ens: 2 (over core).
Axes of the slice: x: 4, y: 4, z: 4, core: 2. Of those that a mesh axis runs over, the one named last changes fastest.
Arguments:
- start_states: float32 [4, 16, 1024, 1024], P('tm', 'ens', 'space'), may hold values from -6 to 6
- velocity_x: float32 [1024, 1024], P('space'), may hold values from -0.15 to 0.15
- velocity_y: float32 [1024, 1024], P('space'), may hold values from -0.15 to 0.15
- diffusivity: float32 [1024, 1024], P('space'), may hold values from 0.06 to 0.2
- source_shape: float32 [1024, 1024], P('space'), may hold values from -6 to 6
- params: float32 [16, 128], P('ens'), may hold values from -6 to 6
- obs_cell: int32 [4, 1024], P('tm', 'space'), may hold values from 0 to 1048575, as said below
- obs_data: float32 [4, 1024], P('tm', 'space'), may hold values from -6 to 6
- obs_noise: float32 [4, 1024, 16], P('tm', 'space'), may hold values from -6 to 6
- obs_var: float32 [4, 1024], P('tm', 'space'), may hold values from 0.05 to 0.5
Outputs:
- new_states: float32 [4, 16, 1024, 1024], P('tm', 'ens', 'space')
- new_params: float32 [16, 128], P('ens')
Inputs may be any that keep to these rules, and one draw needn't show every extreme that they name: `obs_cell`: entry (n, o) lies in the rows of slab o // 64, that is row (o // 64) * 64 up to 63 rows further.
All inputs are finite; a program needn't handle non-finite values.
Results may differ from a plain program's by a relative error of at most 0.0003.
Values sent between devices are 32-bit elements; how exact they have to be, the bound alone decides.
No kernel may reach another device: no remote copies, remote signals or barrier semaphores. Data moves between devices by JAX's collectives and lax.ppermute only.
A program may use at most 128 MiB of HBM per device.

v0:
```python
import math

import jax
import jax.numpy as jnp
from jax import lax
from jax.sharding import PartitionSpec as P

FINE = 4


FINE_DT = 0.25


def with_halo(cells, sides, width):
    for axis, dim in sides:
        count = lax.axis_size(axis)
        ends = count - 1
        head = lax.slice_in_dim(cells, 0, width, axis=dim)
        tail = lax.slice_in_dim(cells, cells.shape[dim] - width, cells.shape[dim], axis=dim)
        cells = jnp.concatenate(
            [
                lax.ppermute(tail, axis, [(i, (i + 1) % count) for i in range(ends)]),
                cells,
                lax.ppermute(head, axis, [((i + 1) % count, i) for i in range(ends)]),
            ],
            axis=dim,
        )
    return cells


def shifted(value, axis, steps):
    count = lax.axis_size(axis)
    first, last = (max(0, -steps), min(count, count - steps))
    return lax.ppermute(value, axis, [(source, source + steps) for source in range(first, last)])


def advance(values_in, coeffs, inside, step_size, forcing):
    middle = values_in[:, 1:-1, :]
    above_row = values_in[:, :-2, :]
    below_row = values_in[:, 2:, :]
    west_cell = jnp.pad(middle[:, :, :-1], ((0, 0), (0, 0), (1, 0)))
    east_cell = jnp.pad(middle[:, :, 1:], ((0, 0), (0, 0), (0, 1)))
    spread_term = coeffs[0] * (above_row + below_row + west_cell + east_cell - 4.0 * middle)
    tendency = (
        spread_term
        - coeffs[1] * (east_cell - west_cell) * 0.5
        - coeffs[2] * (below_row - above_row) * 0.5
    )
    if forcing is not None:
        tendency = tendency + forcing
    return (middle + step_size * tendency) * inside


def row_inside(first_row, count, total_rows):
    global_rows = first_row + jnp.arange(count, dtype=jnp.int32)
    return ((global_rows >= 0) & (global_rows < total_rows)).astype(jnp.float32)[:, None]


def per_device(
    start_states,
    velocity_x,
    velocity_y,
    diffusivity,
    source_shape,
    params,
    obs_cell,
    obs_data,
    obs_noise,
    obs_var,
):
    coarse_dt = FINE_DT * FINE
    state = start_states[0]
    members_here, row_count, col_count = state.shape
    slabs = row_count * lax.axis_size("space")
    first_row = lax.axis_index("space") * row_count
    slice_index = lax.axis_index("tm")
    band_width = col_count // params.shape[1]
    spread_params = jnp.repeat(params, band_width, axis=1)
    coeffs = jnp.stack([diffusivity, velocity_x, velocity_y])
    own_rows = row_inside(first_row, row_count, slabs)
    forcing = source_shape[None] * spread_params[:, None, :]
    current = state
    coarse_part = state
    for section in range(FINE):
        padded = with_halo(current, (("space", 1),), 1)
        if section == 0:
            coarse_part = advance(padded, coeffs, own_rows, coarse_dt, None)
        current = advance(padded, coeffs, own_rows, FINE_DT, forcing)
    correction = jnp.where(slice_index > 0, current - coarse_part, current)
    running = correction
    for link in range(lax.axis_size("tm") - 1):
        earlier = shifted(running, "tm", 1)
        padded = with_halo(earlier, (("space", 1),), 1)
        running = correction + advance(padded, coeffs, own_rows, coarse_dt, None)
    new_states = running[None]
    flat = running.reshape(members_here, row_count * col_count)
    local_cell = obs_cell[0] - first_row * col_count
    predicted = jnp.take(flat, local_cell, axis=1)
    every_pred, every_param = (
        lax.all_gather(predicted, "ens", axis=0, tiled=True),
        lax.all_gather(params, "ens", axis=0, tiled=True),
    )
    total = every_pred.shape[0]
    norm_factor = 1.0 / math.sqrt(total - 1)
    inv_spread = lax.rsqrt(obs_var[0])[None, :]
    pred_mean = jnp.mean(every_pred, axis=0, keepdims=True)
    anomaly = (every_pred - pred_mean) * (inv_spread * norm_factor)
    misfit = (obs_data[0][None, :] + obs_noise[0].T - every_pred) * inv_spread
    gram = jnp.dot(anomaly, anomaly.T, precision=lax.Precision.HIGHEST)
    cross = jnp.dot(anomaly, misfit.T, precision=lax.Precision.HIGHEST)
    gram, cross = lax.psum((gram, cross), ("tm", "space"))
    system = jnp.eye(total, dtype=jnp.float32) + gram
    factor = jnp.linalg.cholesky(system)
    weights = jax.scipy.linalg.cho_solve((factor, True), cross)
    param_anom = every_param - jnp.mean(every_param, axis=0)
    own_weights = lax.dynamic_slice_in_dim(
        weights, lax.axis_index("ens") * members_here, members_here, 1
    )
    new_params = (
        params + jnp.dot(own_weights.T, param_anom, precision=lax.Precision.HIGHEST) * norm_factor
    )
    return (new_states, new_params)


def solution(mesh):
    in_specs = (
        P("tm", "ens", "space", None),
        P("space", None),
        P("space", None),
        P("space", None),
        P("space", None),
        P("ens", None),
        P("tm", "space"),
        P("tm", "space"),
        P("tm", "space", None),
        P("tm", "space"),
    )
    out_specs = (P("tm", "ens", "space", None), P("ens", None))
    return jax.shard_map(
        per_device, mesh=mesh, in_specs=in_specs, out_specs=out_specs, check_vma=False
    )
```

profile of v0, /device:TPU:0, one launch (start us, length us, event | category | flops | bytes accessed | tf_op | source)
XLA Modules:
  0.0 608.6 jit_solution(10801937823309952952)
XLA Ops:
  0.6 1.1 fusion.53
  1.7 3.6 collective-permute-start
  5.3 1.3 collective-permute-start.1
  6.7 5.1 fusion.52
  11.8 1.0 broadcast_in_dim.22
  12.8 1.3 mul.162
  14.2 3.4 fusion.2
  17.7 4.5 collective-permute-start.2
  22.3 1.3 collective-permute-start.3
  23.6 0.8 fusion.51
  24.4 3.7 collective-permute-done.3
  28.1 2.1 fusion.5
  30.2 3.5 collective-permute-start.4
  33.7 1.3 collective-permute-start.5
  35.0 0.8 fusion.49
  35.8 4.6 collective-permute-done.5
  40.4 2.1 fusion.8
  42.6 6.0 collective-permute-start.6
  48.6 1.6 collective-permute-start.7
  50.2 0.8 fusion.47
  51.0 3.7 collective-permute-done.7
  54.7 4.7 subtract_select_fusion
  59.4 3.5 collective-permute-start.8
  63.0 40.2 %collective-permute-done.8 = f32[8,64,1024]{2,1,0:T(8,128)S(1)} collective-permute-done((f32[8,64,1024]{2,1,0:T(8,128)S(1)}, f32[8,64,1024]{2,1,0:T(8,128)S(1)}, u32[]{:S(2)}, u32[]{:S(2)}) %collective-permute-start.8) | collective-permute-done | bytes 2097184 | tf_op jit(solution)/shard_map/ppermute | solution.py:34
  103.2 1.3 collective-permute-start.10
  104.5 5.2 collective-permute-start.9
  109.7 0.8 fusion.45
  111.2 2.0 multiply_add_fusion.6
  113.2 4.7 collective-permute-start.11
  117.9 38.7 %collective-permute-done.11 = f32[8,64,1024]{2,1,0:T(8,128)S(1)} collective-permute-done((f32[8,64,1024]{2,1,0:T(8,128)S(1)}, f32[8,64,1024]{2,1,0:T(8,128)S(1)}, u32[]{:S(2)}, u32[]{:S(2)}) %collective-permute-start.11) | collective-permute-done | bytes 2097184 | tf_op jit(solution)/shard_map/ppermute | solution.py:34
  156.7 3.9 collective-permute-start.12
  160.7 1.3 collective-permute-start.13
  162.0 0.8 fusion.43
  162.8 3.7 collective-permute-done.13
  166.5 3.0 multiply_add_fusion.5
  169.5 4.5 collective-permute-start.14
  174.0 1.8 all_gather.7
  175.9 34.7 %collective-permute-done.14 = f32[8,64,1024]{2,1,0:T(8,128)S(1)} collective-permute-done((f32[8,64,1024]{2,1,0:T(8,128)}, f32[8,64,1024]{2,1,0:T(8,128)S(1)}, u32[]{:S(2)}, u32[]{:S(2)}) %collective-permute-start.14) | collective-permute-done | bytes 2097184 | tf_op jit(solution)/shard_map/ppermute | solution.py:34
  210.6 5.4 collective-permute-start.15
  216.1 1.4 collective-permute-start.16
  218.2 5.6 collective-permute-done.16
  223.8 2.9 multiply_add_fusion.4
  226.7 17.9 %copy.18 = f32[8,64,1024]{0,2,1:T(8,128)} copy(f32[8,64,1024]{2,1,0:T(8,128)} %multiply_add_fusion.4) | data formatting | bytes 4194304 | tf_op jit(solution)/shard_map/add | solution.py:94
  244.6 11.1 %gather_fusion = f32[64,8]{1,0:T(8,128)S(1)} fusion(f32[8,65536]{0,1:T(8,128)} %bitcast.43, s32[1024]{0:T(1024)S(1)} %pad_clamp_fusion), kind=kCustom, calls=%fused_computation | custom fusion | bytes 4352 | tf_op jit(solution)/shard_map/jit(_take)/gather | solution.py:98
  255.9 1.8 all_gather.6
  258.0 345.3 %all-reduce.14 = (f32[16,16]{1,0:T(8,128)S(1)}, f32[16,16]{1,0:T(8,128)S(1)}) all-reduce(f32[16,16]{1,0:T(8,128)S(1)} %fusion.21, f32[16,16]{1,0:T(8,128)S(1)} %fusion.29), channel_id=1, replica_groups=mesh['tm'=4,'space'=16,'ens'=2] {'tm','space'}, use_global_device_ids=true, to_apply=%region_4.5 | all-reduce | flops 512 | bytes 4096 | tf_op jit(solution)/shard_map/psum | solution.py:111
  603.4 1.5 cholesky.17
  606.2 1.2 custom-call.10
  (66 shorter events, 4.9 us)
Async XLA Ops:
  1.7 12.4 %collective-permute-start = (f32[8,1,1024]{2,1,0:T(1,128)S(1)}, f32[8,1,1024]{2,1,0:T(1,128)S(1)}, u32[]{:S(2)}, u32[]{:S(2)}) collective-permute-start(f32[8,1,1024]{2,1,0:T(1,128)S(1)} %get-tuple-element.31), channel_id=1, source_target_pairs={{0,2},{2,4},{4,6},{6,8},{8,10},{10,12},{12,14},{14,16},{16,18},{18... | collective-permute-start | bytes 98312 | tf_op jit(solution)/shard_map/ppermute | solution.py:22
  5.3 8.9 %collective-permute-start.1 = (f32[8,1,1024]{2,1,0:T(1,128)S(1)}, f32[8,1,1024]{2,1,0:T(1,128)S(1)}, u32[]{:S(2)}, u32[]{:S(2)}) collective-permute-start(f32[8,1,1024]{2,1,0:T(1,128)S(1)} %get-tuple-element.30), channel_id=1, source_target_pairs={{2,0},{4,2},{6,4},{8,6},{10,8},{12,10},{14,12},{16,14},{18,16},{20... | collective-permute-start | bytes 98312 | tf_op jit(solution)/shard_map/ppermute | solution.py:24
  6.6 5.2 copy-start.9
  6.6 7.6 %copy-start = (f32[1,8,64,1024]{3,2,1,0:T(8,128)S(1)}, f32[1,8,64,1024]{3,2,1,0:T(8,128)}, u32[]{:S(2)}) copy-start(f32[1,8,64,1024]{3,2,1,0:T(8,128)} %param.10) | copy-start | bytes 6291460
  6.6 7.6 %copy-start.5 = (f32[64,1024]{1,0:T(8,128)S(1)}, f32[64,1024]{1,0:T(8,128)}, u32[]{:S(2)}) copy-start(f32[64,1024]{1,0:T(8,128)} %param.12) | copy-start | bytes 786436
  6.6 7.6 %copy-start.6 = (f32[64,1024]{1,0:T(8,128)S(1)}, f32[64,1024]{1,0:T(8,128)}, u32[]{:S(2)}) copy-start(f32[64,1024]{1,0:T(8,128)} %param.11) | copy-start | bytes 786436
  6.6 7.6 %copy-start.7 = (f32[64,1024]{1,0:T(8,128)S(1)}, f32[64,1024]{1,0:T(8,128)}, u32[]{:S(2)}) copy-start(f32[64,1024]{1,0:T(8,128)} %param.13) | copy-start | bytes 786436
  6.6 7.5 %copy-start.8 = (f32[64,1024]{1,0:T(8,128)S(1)}, f32[64,1024]{1,0:T(8,128)}, u32[]{:S(2)}) copy-start(f32[64,1024]{1,0:T(8,128)} %param.14) | copy-start | bytes 786436
  17.7 6.7 %collective-permute-start.2 = (f32[8,1,1024]{2,1,0:T(1,128)S(1)}, f32[8,1,1024]{2,1,0:T(1,128)S(1)}, u32[]{:S(2)}, u32[]{:S(2)}) collective-permute-start(f32[8,1,1024]{2,1,0:T(1,128)S(1)} %get-tuple-element.25), channel_id=1, source_target_pairs={{0,2},{2,4},{4,6},{6,8},{8,10},{10,12},{12,14},{14,16},{16,18},{18... | collective-permute-start | bytes 98312 | tf_op jit(solution)/shard_map/ppermute | solution.py:22
  22.3 5.8 collective-permute-start.3
  30.2 5.6 collective-permute-start.4
  33.7 6.8 %collective-permute-start.5 = (f32[8,1,1024]{2,1,0:T(1,128)S(1)}, f32[8,1,1024]{2,1,0:T(1,128)S(1)}, u32[]{:S(2)}, u32[]{:S(2)}) collective-permute-start(f32[8,1,1024]{2,1,0:T(1,128)S(1)} %get-tuple-element.20), channel_id=1, source_target_pairs={{2,0},{4,2},{6,4},{8,6},{10,8},{12,10},{14,12},{16,14},{18,16},{20... | collective-permute-start | bytes 98312 | tf_op jit(solution)/shard_map/ppermute | solution.py:24
  42.6 8.5 %collective-permute-start.6 = (f32[8,1,1024]{2,1,0:T(1,128)S(1)}, f32[8,1,1024]{2,1,0:T(1,128)S(1)}, u32[]{:S(2)}, u32[]{:S(2)}) collective-permute-start(f32[8,1,1024]{2,1,0:T(1,128)S(1)} %get-tuple-element.17), channel_id=1, source_target_pairs={{0,2},{2,4},{4,6},{6,8},{8,10},{10,12},{12,14},{14,16},{16,18},{18... | collective-permute-start | bytes 98312 | tf_op jit(solution)/shard_map/ppermute | solution.py:22
  48.6 6.1 %copy-start.3 = (f32[8,64,1023]{2,1,0:T(8,128)S(1)}, f32[8,64,1023]{2,1,0:T(8,128)}, u32[]{:S(2)}) copy-start(f32[8,64,1023]{2,1,0:T(8,128)} %get-tuple-element.28) | copy-start | bytes 6285316
  48.6 6.1 %copy-start.4 = (f32[8,64,1023]{2,1,0:T(8,128)S(1)}, f32[8,64,1023]{2,1,0:T(8,128)}, u32[]{:S(2)}) copy-start(f32[8,64,1023]{2,1,0:T(8,128)} %get-tuple-element.29) | copy-start | bytes 6285316
  48.6 6.1 collective-permute-start.7
  59.4 107.1 %copy-start.1 = (f32[8,64,1024]{2,1,0:T(8,128)}, f32[8,64,1024]{2,1,0:T(8,128)S(1)}, u32[]{:S(2)}) copy-start(f32[8,64,1024]{2,1,0:T(8,128)S(1)} %subtract_select_fusion) | copy-start | bytes 6291460
  59.4 43.7 %collective-permute-start.8 = (f32[8,64,1024]{2,1,0:T(8,128)S(1)}, f32[8,64,1024]{2,1,0:T(8,128)S(1)}, u32[]{:S(2)}, u32[]{:S(2)}) collective-permute-start(f32[8,64,1024]{2,1,0:T(8,128)S(1)} %subtract_select_fusion), channel_id=1, source_target_pairs={{0,32},{32,64},{64,96},{1,33},{33,65},{65,97},{2,34},{34,66},{66,9... | collective-permute-start | bytes 6291464 | tf_op jit(solution)/shard_map/ppermute | solution.py:34
  103.2 7.3 %collective-permute-start.10 = (f32[8,1,1024]{2,1,0:T(1,128)S(1)}, f32[8,1,1024]{2,1,0:T(1,128)S(1)}, u32[]{:S(2)}, u32[]{:S(2)}) collective-permute-start(f32[8,1,1024]{2,1,0:T(1,128)S(1)} %get-tuple-element.12), channel_id=1, source_target_pairs={{2,0},{4,2},{6,4},{8,6},{10,8},{12,10},{14,12},{16,14},{18,16},{20... | collective-permute-start | bytes 98312 | tf_op jit(solution)/shard_map/ppermute | solution.py:24
  104.5 6.8 %collective-permute-start.9 = (f32[8,1,1024]{2,1,0:T(1,128)S(1)}, f32[8,1,1024]{2,1,0:T(1,128)S(1)}, u32[]{:S(2)}, u32[]{:S(2)}) collective-permute-start(f32[8,1,1024]{2,1,0:T(1,128)S(1)} %get-tuple-element.13), channel_id=1, source_target_pairs={{0,2},{2,4},{4,6},{6,8},{8,10},{10,12},{12,14},{14,16},{16,18},{18... | collective-permute-start | bytes 98312 | tf_op jit(solution)/shard_map/ppermute | solution.py:22
  113.2 43.4 %collective-permute-start.11 = (f32[8,64,1024]{2,1,0:T(8,128)S(1)}, f32[8,64,1024]{2,1,0:T(8,128)S(1)}, u32[]{:S(2)}, u32[]{:S(2)}) collective-permute-start(f32[8,64,1024]{2,1,0:T(8,128)S(1)} %multiply_add_fusion.6), channel_id=1, source_target_pairs={{0,32},{32,64},{64,96},{1,33},{33,65},{65,97},{2,34},{34,66},{66,9... | collective-permute-start | bytes 6291464 | tf_op jit(solution)/shard_map/ppermute | solution.py:34
  156.7 6.1 collective-permute-start.12
  160.7 5.8 collective-permute-start.13
  166.5 9.3 %copy-start.12 = (s32[1,64]{1,0:T(1,128)S(1)}, s32[1,64]{1,0:T(1,128)}, u32[]{:S(2)}) copy-start(s32[1,64]{1,0:T(1,128)} %param.16) | copy-start | bytes 772
  166.5 9.4 %copy-start.13 = (f32[1,64]{1,0:T(1,128)S(1)}, f32[1,64]{1,0:T(1,128)}, u32[]{:S(2)}) copy-start(f32[1,64]{1,0:T(1,128)} %param.19) | copy-start | bytes 772
  169.5 41.1 %collective-permute-start.14 = (f32[8,64,1024]{2,1,0:T(8,128)}, f32[8,64,1024]{2,1,0:T(8,128)S(1)}, u32[]{:S(2)}, u32[]{:S(2)}) collective-permute-start(f32[8,64,1024]{2,1,0:T(8,128)} %multiply_add_fusion.5), channel_id=1, source_target_pairs={{0,32},{32,64},{64,96},{1,33},{33,65},{65,97},{2,34},{34,66},{66,9... | collective-permute-start | bytes 6291464 | tf_op jit(solution)/shard_map/ppermute | solution.py:34
  210.6 7.6 %collective-permute-start.15 = (f32[8,1,1024]{2,1,0:T(1,128)S(1)}, f32[8,1,1024]{2,1,0:T(1,128)S(1)}, u32[]{:S(2)}, u32[]{:S(2)}) collective-permute-start(f32[8,1,1024]{2,1,0:T(1,128)S(1)} %get-tuple-element.5), channel_id=1, source_target_pairs={{0,2},{2,4},{4,6},{6,8},{8,10},{10,12},{12,14},{14,16},{16,18},{18... | collective-permute-start | bytes 98312 | tf_op jit(solution)/shard_map/ppermute | solution.py:22
  216.0 7.8 %copy-start.2 = (f32[8,64,1024]{2,1,0:T(8,128)S(1)}, f32[8,64,1024]{2,1,0:T(8,128)}, u32[]{:S(2)}) copy-start(f32[8,64,1024]{2,1,0:T(8,128)} %copy-done.1) | copy-start | bytes 6291460
  216.1 7.8 %collective-permute-start.16 = (f32[8,1,1024]{2,1,0:T(1,128)S(1)}, f32[8,1,1024]{2,1,0:T(1,128)S(1)}, u32[]{:S(2)}, u32[]{:S(2)}) collective-permute-start(f32[8,1,1024]{2,1,0:T(1,128)S(1)} %get-tuple-element.4), channel_id=1, source_target_pairs={{2,0},{4,2},{6,4},{8,6},{10,8},{12,10},{14,12},{16,14},{18,16},{20... | collective-permute-start | bytes 98312 | tf_op jit(solution)/shard_map/ppermute | solution.py:24
  226.7 31.1 %copy-start.10 = (f32[1,64,16]{1,2,0:T(8,128)S(1)}, f32[1,64,16]{1,2,0:T(8,128)}, u32[]{:S(2)}) copy-start(f32[1,64,16]{1,2,0:T(8,128)} %param.18) | copy-start | bytes 12292
  226.7 31.1 %copy-start.11 = (f32[1,64]{1,0:T(1,128)S(1)}, f32[1,64]{1,0:T(1,128)}, u32[]{:S(2)}) copy-start(f32[1,64]{1,0:T(1,128)} %param.17) | copy-start | bytes 772
where the time goes:
time: 610 us; the launch traced here: 609 us
  blocking collectives  349 us (57%)
  waiting for transfers between devices  135 us (22%)
  starting transfers between devices  54.3 us (9%)
  local copies, waits for them, and re-layouts  43 us (7%)
  other arithmetic  24.3 us (4%)
    psum x1, blocking collectives, per_device(): gram, cross = lax.psum((gram, cross), ('tm', 'space'))  345 us
    ppermute x3, waiting for transfers between devices, shifted(): lax.ppermute(value, axis, [(source, source + steps) for source in range(f...  114 us
    ppermute x7, starting transfers between devices, with_halo(): lax.ppermute(tail, axis, [(i, (i + 1) % count) for i in range(ends)])  32.1 us
    ppermute x7, waiting for transfers between devices, with_halo(): lax.ppermute(head, axis, [((i + 1) % count, i) for i in range(ends)])  21.2 us
    add x1, local copies, waits for them, and re-layouts, per_device(): running = correction + advance(padded, coeffs, own_rows, coarse_dt, None)  17.9 us
    ppermute x3, starting transfers between devices, shifted(): lax.ppermute(value, axis, [(source, source + steps) for source in range(f...  12.7 us
  transfers between devices with their start and end apart: 17, of which 9 were waited for; matrix products, arithmetic and copies ran while one was open for 2% of the time, Pallas kernels for 0%

commit v1 on v0

v1 whole, which is shorter than its diff:
```python
import math

import jax
import jax.numpy as jnp
from jax import lax
from jax.sharding import PartitionSpec as P

FINE = 4


FINE_DT = 0.25


def with_halo(cells, axis, width):
    count = lax.axis_size(axis)
    ends = count - 1
    head = cells[:, :width]
    tail = cells[:, cells.shape[1] - width :]
    return jnp.concatenate(
        [
            lax.ppermute(tail, axis, [(i, i + 1) for i in range(ends)]),
            cells,
            lax.ppermute(head, axis, [(i + 1, i) for i in range(ends)]),
        ],
        axis=1,
    )


def butterfly_sum(value, axis):
    count = lax.axis_size(axis)
    if count & (count - 1):
        return lax.psum(value, axis)
    bit = 1
    while bit < count:
        value = value + lax.ppermute(value, axis, [(i, i ^ bit) for i in range(count)])
        bit *= 2
    return value


def both_halves(value, axis):
    other = lax.ppermute(value, axis, [(0, 1), (1, 0)])
    first = lax.axis_index(axis) == 0
    return jnp.where(first, jnp.concatenate([value, other]), jnp.concatenate([other, value]))


def advance(values_in, coeffs, inside, step_size, forcing):
    middle = values_in[:, 1:-1, :]
    above_row = values_in[:, :-2, :]
    below_row = values_in[:, 2:, :]
    west_cell = jnp.pad(middle[:, :, :-1], ((0, 0), (0, 0), (1, 0)))
    east_cell = jnp.pad(middle[:, :, 1:], ((0, 0), (0, 0), (0, 1)))
    spread_term = coeffs[0] * (above_row + below_row + west_cell + east_cell - 4.0 * middle)
    tendency = (
        spread_term
        - coeffs[1] * (east_cell - west_cell) * 0.5
        - coeffs[2] * (below_row - above_row) * 0.5
    )
    if forcing is not None:
        tendency = tendency + forcing
    return (middle + step_size * tendency) * inside


def per_device(
    start_states,
    velocity_x,
    velocity_y,
    diffusivity,
    source_shape,
    params,
    obs_cell,
    obs_data,
    obs_noise,
    obs_var,
):
    coarse_dt = FINE_DT * FINE
    state = start_states[0]
    members_here, row_count, col_count = state.shape
    slabs = row_count * lax.axis_size("space")
    first_row = lax.axis_index("space") * row_count
    slice_index = lax.axis_index("tm")
    links = lax.axis_size("tm") - 1
    depth = FINE + links
    band_width = col_count // params.shape[1]
    spread_params = jnp.repeat(params, band_width, axis=1)

    fields = jnp.stack([diffusivity, velocity_x, velocity_y, source_shape])
    wide = with_halo(jnp.concatenate([state, fields]), "space", depth)
    wide_state = wide[:members_here]
    wide_coeffs = wide[members_here : members_here + 3]
    wide_forcing = wide[members_here + 3][None] * spread_params[:, None, :]
    global_rows = first_row - depth + jnp.arange(row_count + 2 * depth, dtype=jnp.int32)
    wide_inside = ((global_rows >= 0) & (global_rows < slabs)).astype(jnp.float32)[:, None]

    def step(values, low, step_size, forcing):
        n = values.shape[1]
        lo, hi = low + 1, low + n - 1
        q = None if forcing is None else forcing[:, lo:hi]
        return advance(values, wide_coeffs[:, lo:hi], wide_inside[lo:hi], step_size, q)

    current = wide_state
    coarse_part = step(wide_state, 0, coarse_dt, None)
    for section in range(FINE):
        current = step(current, section, FINE_DT, wide_forcing)
    coarse_part = coarse_part[:, FINE - 1 : FINE - 1 + current.shape[1]]
    correction = jnp.where(slice_index > 0, current - coarse_part, current)
    running = correction
    for link in range(1, links + 1):
        earlier = lax.ppermute(running, "tm", [(i, i + 1) for i in range(links)])
        stepped = step(earlier, FINE + link - 1, coarse_dt, None)
        running = correction[:, link : correction.shape[1] - link] + stepped
    new_states = running[None]

    local_cell = obs_cell[0] - first_row * col_count
    rows = local_cell // col_count
    cols = local_cell % col_count
    predicted = running[:, rows, cols]
    every_pred = both_halves(predicted, "ens")
    every_param = both_halves(params, "ens")
    total = every_pred.shape[0]
    norm_factor = 1.0 / math.sqrt(total - 1)
    inv_spread = lax.rsqrt(obs_var[0])[None, :]
    pred_mean = jnp.mean(every_pred, axis=0, keepdims=True)
    anomaly = (every_pred - pred_mean) * (inv_spread * norm_factor)
    misfit = (obs_data[0][None, :] + obs_noise[0].T - every_pred) * inv_spread
    gram = jnp.dot(anomaly, anomaly.T, precision=lax.Precision.HIGHEST)
    cross = jnp.dot(anomaly, misfit.T, precision=lax.Precision.HIGHEST)
    sums = jnp.stack([gram, cross])
    sums = butterfly_sum(sums, "tm")
    sums = butterfly_sum(sums, "space")
    gram, cross = sums[0], sums[1]
    system = jnp.eye(total, dtype=jnp.float32) + gram
    factor = jnp.linalg.cholesky(system)
    weights = jax.scipy.linalg.cho_solve((factor, True), cross)
    param_anom = every_param - jnp.mean(every_param, axis=0)
    own_weights = lax.dynamic_slice_in_dim(
        weights, lax.axis_index("ens") * members_here, members_here, 1
    )
    new_params = (
        params + jnp.dot(own_weights.T, param_anom, precision=lax.Precision.HIGHEST) * norm_factor
    )
    return (new_states, new_params)


def solution(mesh):
    in_specs = (
        P("tm", "ens", "space", None),
        P("space", None),
        P("space", None),
        P("space", None),
        P("space", None),
        P("ens", None),
        P("tm", "space"),
        P("tm", "space"),
        P("tm", "space", None),
        P("tm", "space"),
    )
    out_specs = (P("tm", "ens", "space", None), P("ens", None))
    return jax.shard_map(
        per_device, mesh=mesh, in_specs=in_specs, out_specs=out_specs, check_vma=False
    )
```

time: 610 us -> 278 us (0.46)
  blocking collectives: 349 us -> 0 us
  starting transfers between devices: 54.3 us -> 35 us
  waiting for transfers between devices: 135 us -> 154 us
  other arithmetic: 24.3 us -> 41.3 us
    psum x1 -> x0, blocking collectives: 345 us -> none  [per_device(): gram, cross = lax.psum((gram, cross), ('tm', 'space'))]
    ppermute x17 -> x13, starting transfers between devices: 54.3 us -> 35 us  [the longest x6 16.5 us: butterfly_sum(): lax.ppermute(value, axis, [(i, i ^ bit) for i in range(count)])]
    ppermute x17 -> x13, waiting for transfers between devices: 135 us -> 154 us  [the longest x3 136 us: per_device(): earlier = lax.ppermute(running, 'tm', [(i, i + 1) for i in range(links)])]
    gather x1 -> x2, local copies, waits for them, and re-layouts: 11.1 us -> 1.54 us  [per_device(): predicted = running[:, rows, cols]]
    unnamed x28 -> x59, local copies, waits for them, and re-layouts: 0.08 us -> 8.84 us
    mul x3, other arithmetic: 7.55 us -> 16.3 us  [advance(): return (middle + step_size * tendency) * inside]
    add x3 -> x10, other arithmetic: 7.89 us -> 15.7 us  [the longest x3 13.3 us: per_device(): running = correction[:, link:correction.shape[1] - link] + stepped]
  transfers between devices with their start and end apart: 17 -> 13, of which waited for: 9 -> 11; matrix products, arithmetic and copies ran while one was open for 2% -> 2% of each run, Pallas kernels for 0% -> 0%
where the time goes in v1:
time: 278 us; the launch traced here: 276 us
  waiting for transfers between devices  154 us (55%)
  local copies, waits for them, and re-layouts  42.9 us (15%)
  other arithmetic  41.3 us (15%)
  starting transfers between devices  35 us (13%)
    ppermute x3, waiting for transfers between devices, per_device(): earlier = lax.ppermute(running, 'tm', [(i, i + 1) for i in range(links)])  136 us
    add x1, local copies, waits for them, and re-layouts, per_device(): running = correction[:, link:correction.shape[1] - link] + stepped  16.5 us
    ppermute x6, starting transfers between devices, butterfly_sum(): lax.ppermute(value, axis, [(i, i ^ bit) for i in range(count)])  16.5 us
    mul x3, other arithmetic, advance(): return (middle + step_size * tendency) * inside  16.3 us
    add x3, other arithmetic, per_device(): running = correction[:, link:correction.shape[1] - link] + stepped  13.3 us
    ppermute x3, starting transfers between devices, per_device(): earlier = lax.ppermute(running, 'tm', [(i, i + 1) for i in range(links)])  12.8 us
    ppermute x6, waiting for transfers between devices, butterfly_sum(): lax.ppermute(value, axis, [(i, i ^ bit) for i in range(count)])  9.82 us
    unnamed x59, local copies, waits for them, and re-layouts  8.84 us
  transfers between devices with their start and end apart: 13, of which 11 were waited for; matrix products, arithmetic and copies ran while one was open for 2% of the time, Pallas kernels for 0%

profile of v1, /device:TPU:0, one launch (start us, length us, event | category | flops | bytes accessed | tf_op | source)
XLA Modules:
  0.0 276.2 jit_solution(11528866141110942654)
XLA Ops:
  0.7 1.8 bitcast_dynamic-update-slice_fusion
  3.5 4.3 %collective-permute-start = (f32[12,7,1024]{2,1,0:T(8,128)}, f32[12,7,1024]{2,1,0:T(8,128)}, u32[]{:S(2)}, u32[]{:S(2)}) collective-permute-start(f32[12,7,1024]{2,1,0:T(8,128)} %get-tuple-element.40), channel_id=1, source_target_pairs={{0,2},{2,4},{4,6},{6,8},{8,10},{10,12},{12,14},{14,16},{16,18},{18... | collective-permute-start | bytes 1032200 | tf_op jit(solution)/shard_map/ppermute | solution.py:21
  7.8 1.3 collective-permute-start.1
  9.9 1.0 broadcast_in_dim.5
  10.9 1.9 mul.460
  12.8 2.9 %collective-permute-done = f32[12,7,1024]{2,1,0:T(8,128)} collective-permute-done((f32[12,7,1024]{2,1,0:T(8,128)}, f32[12,7,1024]{2,1,0:T(8,128)}, u32[]{:S(2)}, u32[]{:S(2)}) %collective-permute-start) | collective-permute-done | bytes 344096 | tf_op jit(solution)/shard_map/ppermute | solution.py:21
  15.7 4.6 %collective-permute-done.1 = f32[12,7,1024]{2,1,0:T(8,128)} collective-permute-done((f32[12,7,1024]{2,1,0:T(8,128)S(1)}, f32[12,7,1024]{2,1,0:T(8,128)}, u32[]{:S(2)}, u32[]{:S(2)}) %collective-permute-start.1) | collective-permute-done | bytes 344096 | tf_op jit(solution)/shard_map/ppermute | solution.py:23
  20.3 2.0 pad_maximum_fusion
  22.4 1.0 fusion.54
  23.5 1.2 fusion.55
  25.6 1.0 slice_bitcast_fusion.18
  26.5 0.9 slice_bitcast_fusion.15
  27.5 1.4 copy.119
  28.9 1.4 copy.120
  30.7 10.1 %fusion.2 = (f32[8,76,1024]{2,0,1:T(8,128)S(1)}, f32[8,76,1024]{2,0,1:T(8,128)S(1)}, f32[8,76,1024]{2,0,1:T(8,128)S(1)}) fusion(f32[8,78,1024]{2,0,1:T(8,128)S(1)} %broadcast_multiply_fusion, f32[76]{0:T(128)S(1)} %slice.326, f32[76,1024]{1,0:T(8,128)S(1)} %get-tuple-element.36, f32[76,1024]{1,0:T(8,128)S(1)} %get-tuple-element.37, ...), kind=kLoop, calls=%fused_computation.6 | loop fusion | flops 11206656 | bytes 23342640 | tf_op jit(solution)/shard_map/mul | solution.py:60
  40.9 1.0 fusion.57
  41.9 3.1 %fusion.5 = f32[8,74,1024]{2,0,1:T(8,128)S(1)} fusion(f32[8,78,1024]{2,0,1:T(8,128)S(1)} %broadcast_multiply_fusion, f32[8,76,1024]{2,0,1:T(8,128)S(1)} %get-tuple-element.12, f32[8,74,1023]{2,0,1:T(8,128)S(1)} %get-tuple-element.43, f32[8,74,1023]{2,0,1:T(8,128)S(1)} %get-tuple-element.42, f32[74]{0:T(128)S(1)} %copy-done.19, ...), kind=kLoop, calls=%fused_computation.11 | loop fusion | flops 10911744 | bytes 17878696 | tf_op jit(solution)/shard_map/mul | solution.py:60
  46.1 3.1 %fusion.8 = f32[8,72,1024]{2,0,1:T(8,128)S(1)} fusion(f32[8,78,1024]{2,0,1:T(8,128)S(1)} %broadcast_multiply_fusion, f32[8,74,1024]{2,0,1:T(8,128)S(1)} %fusion.5, f32[8,72,1023]{2,0,1:T(8,128)S(1)} %get-tuple-element.45, f32[8,72,1023]{2,0,1:T(8,128)S(1)} %get-tuple-element.44, f32[72]{0:T(128)S(1)} %slice.346, f32[72,1024]{1,0:T(8,128)S(1)} %copy-done.8, ...), kind=kLoop, calls=%fused_computation.15 | loop fusion | flops 10616832 | bytes 17395488 | tf_op jit(solution)/shard_map/mul | solution.py:60
  49.2 0.9 fusion.59
  50.3 3.0 %subtract_select_fusion = f32[8,70,1024]{2,0,1:T(8,128)S(1)} fusion(f32[8,76,1024]{2,0,1:T(8,128)S(1)} %get-tuple-element.13, f32[8,76,1024]{2,0,1:T(8,128)S(1)} %get-tuple-element.14, f32[8,78,1024]{2,0,1:T(8,128)S(1)} %broadcast_multiply_fusion, f32[8,72,1024]{2,0,1:T(8,128)S(1)} %fusion.8, f32[8,70,1023]{2,0,1:T(8,128)S(1)} %get-tuple-element.47, ...), kind=kLoop, calls=%fused_computation.2 | loop fusion | flops 12615680 | bytes 21499800 | tf_op jit(solution)/shard_map/jit(_where)/select_n | solution.py:105
  53.3 3.8 %collective-permute-start.2 = (f32[8,70,1024]{2,0,1:T(8,128)S(1)}, f32[8,70,1024]{2,0,1:T(8,128)S(1)}, u32[]{:S(2)}, u32[]{:S(2)}) collective-permute-start(f32[8,70,1024]{2,0,1:T(8,128)S(1)} %subtract_select_fusion), channel_id=1, source_target_pairs={{0,32},{32,64},{64,96},{1,33},{33,65},{65,97},{2,34},{34,66},{66,9... | collective-permute-start | bytes 6881288 | tf_op jit(solution)/shard_map/ppermute | solution.py:108
  57.3 47.4 %collective-permute-done.2 = f32[8,70,1024]{2,0,1:T(8,128)S(1)} collective-permute-done((f32[8,70,1024]{2,0,1:T(8,128)S(1)}, f32[8,70,1024]{2,0,1:T(8,128)S(1)}, u32[]{:S(2)}, u32[]{:S(2)}) %collective-permute-start.2) | collective-permute-done | bytes 2293792 | tf_op jit(solution)/shard_map/ppermute | solution.py:108
  104.6 0.9 fusion.60
  105.5 2.8 slice_add_fusion.5
  108.3 4.5 %collective-permute-start.3 = (f32[8,68,1024]{2,0,1:T(8,128)S(1)}, f32[8,68,1024]{2,0,1:T(8,128)S(1)}, u32[]{:S(2)}, u32[]{:S(2)}) collective-permute-start(f32[8,68,1024]{2,0,1:T(8,128)S(1)} %slice_add_fusion.5), channel_id=1, source_target_pairs={{0,32},{32,64},{64,96},{1,33},{33,65},{65,97},{2,34},{34,66},{66,9... | collective-permute-start | bytes 6684680 | tf_op jit(solution)/shard_map/ppermute | solution.py:108
  113.0 45.3 %collective-permute-done.3 = f32[8,68,1024]{2,0,1:T(8,128)S(1)} collective-permute-done((f32[8,68,1024]{2,0,1:T(8,128)S(1)}, f32[8,68,1024]{2,0,1:T(8,128)S(1)}, u32[]{:S(2)}, u32[]{:S(2)}) %collective-permute-start.3) | collective-permute-done | bytes 2228256 | tf_op jit(solution)/shard_map/ppermute | solution.py:108
  158.3 0.9 fusion.61
  159.1 3.7 %slice_add_fusion.6 = f32[8,66,1024]{2,0,1:T(8,128)} fusion(f32[8,70,1024]{2,0,1:T(8,128)S(1)} %subtract_select_fusion, f32[8,68,1024]{2,0,1:T(8,128)S(1)} %collective-permute-done.3, f32[8,66,1023]{2,0,1:T(8,128)S(1)} %get-tuple-element.51, f32[8,66,1023]{2,0,1:T(8,128)S(1)} %get-tuple-element.50, f32[66]{0:T(128)S(1)} %slice.378, ...), kind=kLoop, calls=%fused_computation.23 | loop fusion | flops 9191424 | bytes 15945864 | tf_op jit(solution)/shard_map/add | solution.py:110
  162.8 4.5 %collective-permute-start.4 = (f32[8,66,1024]{2,0,1:T(8,128)}, f32[8,66,1024]{2,0,1:T(8,128)S(1)}, u32[]{:S(2)}, u32[]{:S(2)}) collective-permute-start(f32[8,66,1024]{2,0,1:T(8,128)} %slice_add_fusion.6), channel_id=1, source_target_pairs={{0,32},{32,64},{64,96},{1,33},{33,65},{65,97},{2,34},{34,66},{66,9... | collective-permute-start | bytes 6488072 | tf_op jit(solution)/shard_map/ppermute | solution.py:108
  167.4 43.3 %collective-permute-done.4 = f32[8,66,1024]{2,0,1:T(8,128)S(1)} collective-permute-done((f32[8,66,1024]{2,0,1:T(8,128)}, f32[8,66,1024]{2,0,1:T(8,128)S(1)}, u32[]{:S(2)}, u32[]{:S(2)}) %collective-permute-start.4) | collective-permute-done | bytes 2162720 | tf_op jit(solution)/shard_map/ppermute | solution.py:108
  211.3 2.3 copy_add_fusion.1
  215.4 6.9 %slice_add_fusion.7 = f32[8,64,1024]{2,0,1:T(8,128)} fusion(f32[8,70,1024]{2,0,1:T(8,128)S(1)} %copy-done.1, f32[8,64,1024]{2,1,0:T(8,128)S(1)} %get-tuple-element.16, f32[8,64,1024]{2,1,0:T(8,128)S(1)} %get-tuple-element.15, f32[8,66,1024]{2,0,1:T(8,128)S(1)} %collective-permute-done.4, f32[8,64,1023]{2,0,1:T(8,128)S(1)} %get-tuple-element.53, ...), kind=kLoop, calls=%fused_computation.24 | loop fusion | flops 7864320 | bytes 15462656 | tf_op jit(solution)/shard_map/add | solution.py:110
  222.3 16.5 %copy.109 = f32[8,64,1024]{0,2,1:T(8,128)} copy(f32[8,64,1024]{2,0,1:T(8,128)} %slice_add_fusion.7) | data formatting | bytes 4194304 | tf_op jit(solution)/shard_map/add | solution.py:110
  238.8 1.5 gather_fusion
  240.5 1.1 collective-permute-done.5
  242.0 2.4 collective-permute-start.6
  244.5 1.7 collective-permute-done.6
  246.2 3.6 %collective-permute-start.7 = (f32[2,16,16]{2,1,0:T(8,128)S(1)}, f32[2,16,16]{2,1,0:T(8,128)S(1)}, u32[]{:S(2)}, u32[]{:S(2)}) collective-permute-start(f32[2,16,16]{2,1,0:T(8,128)S(1)} %fusion.53), channel_id=1, source_target_pairs={{0,64},{32,96},{64,0},{96,32},{1,65},{33,97},{65,1},{97,33},{2,66}... | collective-permute-start | bytes 6152 | tf_op jit(solution)/shard_map/ppermute | solution.py:35
  249.8 1.7 collective-permute-done.7
  252.3 2.9 %collective-permute-done.8 = f32[2,16,16]{2,1,0:T(8,128)S(1)} collective-permute-done((f32[2,16,16]{2,1,0:T(8,128)S(1)}, f32[2,16,16]{2,1,0:T(8,128)S(1)}, u32[]{:S(2)}, u32[]{:S(2)}) %collective-permute-start.8) | collective-permute-done | bytes 2080 | tf_op jit(solution)/shard_map/ppermute | solution.py:35
  255.2 4.0 %collective-permute-start.9 = (f32[2,16,16]{2,1,0:T(8,128)S(1)}, f32[2,16,16]{2,1,0:T(8,128)S(1)}, u32[]{:S(2)}, u32[]{:S(2)}) collective-permute-start(f32[2,16,16]{2,1,0:T(8,128)S(1)} %add.294), channel_id=1, source_target_pairs={{0,4},{2,6},{4,0},{6,2},{8,12},{10,14},{12,8},{14,10},{16,20},{18,... | collective-permute-start | bytes 6152 | tf_op jit(solution)/shard_map/ppermute | solution.py:35
  259.2 1.7 collective-permute-done.9
  260.9 1.9 collective-permute-start.10
  262.9 1.8 collective-permute-done.10
  264.7 3.8 %collective-permute-start.11 = (f32[2,16,16]{2,1,0:T(8,128)S(1)}, f32[2,16,16]{2,1,0:T(8,128)S(1)}, u32[]{:S(2)}, u32[]{:S(2)}) collective-permute-start(f32[2,16,16]{2,1,0:T(8,128)S(1)} %add.296), channel_id=1, source_target_pairs={{0,16},{2,18},{4,20},{6,22},{8,24},{10,26},{12,28},{14,30},{16,0},... | collective-permute-start | bytes 6152 | tf_op jit(solution)/shard_map/ppermute | solution.py:35
  268.4 2.5 copy.115
  271.1 1.5 cholesky.17
  273.9 1.2 custom-call.10
  (105 shorter events, 11.0 us)
Async XLA Ops:
  0.6 1.9 copy-start.10
  0.6 1.9 copy-start.12
  0.7 1.9 copy-start.14
  0.7 1.9 copy-start.16
  2.5 7.4 %copy-start.18 = (f32[8,128]{1,0:T(8,128)S(1)}, f32[8,128]{1,0:T(8,128)}, u32[]{:S(2)}) copy-start(f32[8,128]{1,0:T(8,128)} %param.15) | copy-start | bytes 12292
  3.5 12.2 %collective-permute-start = (f32[12,7,1024]{2,1,0:T(8,128)}, f32[12,7,1024]{2,1,0:T(8,128)}, u32[]{:S(2)}, u32[]{:S(2)}) collective-permute-start(f32[12,7,1024]{2,1,0:T(8,128)} %get-tuple-element.40), channel_id=1, source_target_pairs={{0,2},{2,4},{4,6},{6,8},{8,10},{10,12},{12,14},{14,16},{16,18},{18... | collective-permute-start | bytes 1032200 | tf_op jit(solution)/shard_map/ppermute | solution.py:21
  7.8 12.6 %collective-permute-start.1 = (f32[12,7,1024]{2,1,0:T(8,128)S(1)}, f32[12,7,1024]{2,1,0:T(8,128)}, u32[]{:S(2)}, u32[]{:S(2)}) collective-permute-start(f32[12,7,1024]{2,1,0:T(8,128)S(1)} %get-tuple-element.41), channel_id=1, source_target_pairs={{2,0},{4,2},{6,4},{8,6},{10,8},{12,10},{14,12},{16,14},{18,16},{20... | collective-permute-start | bytes 1032200 | tf_op jit(solution)/shard_map/ppermute | solution.py:23
  9.1 0.7 copy-start.24
  28.9 1.5 copy-start.17
  40.8 1.0 copy-start.3
  40.9 1.0 copy-start.19
  45.0 1.0 copy-start.7
  45.0 1.0 copy-start.8
  45.0 1.1 copy-start.9
  49.2 1.0 copy-start.4
  49.2 1.0 copy-start.5
  49.2 1.1 copy-start.6
  50.3 6.8 %copy-start.25 = (f32[78]{0:T(128)S(1)}, f32[78]{0:T(128)}, u32[]{:S(2)}) copy-start(f32[78]{0:T(128)} %copy-done.24) | copy-start | bytes 940
  53.3 105.8 %copy-start = (f32[8,70,1024]{2,0,1:T(8,128)}, f32[8,70,1024]{2,0,1:T(8,128)S(1)}, u32[]{:S(2)}) copy-start(f32[8,70,1024]{2,0,1:T(8,128)S(1)} %subtract_select_fusion) | copy-start | bytes 6881284
  53.3 51.3 %collective-permute-start.2 = (f32[8,70,1024]{2,0,1:T(8,128)S(1)}, f32[8,70,1024]{2,0,1:T(8,128)S(1)}, u32[]{:S(2)}, u32[]{:S(2)}) collective-permute-start(f32[8,70,1024]{2,0,1:T(8,128)S(1)} %subtract_select_fusion), channel_id=1, source_target_pairs={{0,32},{32,64},{64,96},{1,33},{33,65},{65,97},{2,34},{34,66},{66,9... | collective-permute-start | bytes 6881288 | tf_op jit(solution)/shard_map/ppermute | solution.py:108
  108.3 50.0 %collective-permute-start.3 = (f32[8,68,1024]{2,0,1:T(8,128)S(1)}, f32[8,68,1024]{2,0,1:T(8,128)S(1)}, u32[]{:S(2)}, u32[]{:S(2)}) collective-permute-start(f32[8,68,1024]{2,0,1:T(8,128)S(1)} %slice_add_fusion.5), channel_id=1, source_target_pairs={{0,32},{32,64},{64,96},{1,33},{33,65},{65,97},{2,34},{34,66},{66,9... | collective-permute-start | bytes 6684680 | tf_op jit(solution)/shard_map/ppermute | solution.py:108
  159.1 8.3 %copy-start.21 = (s32[1,64]{1,0:T(1,128)S(1)}, s32[1,64]{1,0:T(1,128)}, u32[]{:S(2)}) copy-start(s32[1,64]{1,0:T(1,128)} %param.16) | copy-start | bytes 772
  162.8 47.9 %collective-permute-start.4 = (f32[8,66,1024]{2,0,1:T(8,128)}, f32[8,66,1024]{2,0,1:T(8,128)S(1)}, u32[]{:S(2)}, u32[]{:S(2)}) collective-permute-start(f32[8,66,1024]{2,0,1:T(8,128)} %slice_add_fusion.6), channel_id=1, source_target_pairs={{0,32},{32,64},{64,96},{1,33},{33,65},{65,97},{2,34},{34,66},{66,9... | collective-permute-start | bytes 6488072 | tf_op jit(solution)/shard_map/ppermute | solution.py:108
  213.6 1.6 copy-start.1
  213.6 1.6 copy-start.11
  213.6 1.7 copy-start.13
  213.6 1.8 copy-start.15
  222.3 18.1 %copy-start.22 = (f32[1,64]{1,0:T(1,128)S(1)}, f32[1,64]{1,0:T(1,128)}, u32[]{:S(2)}) copy-start(f32[1,64]{1,0:T(1,128)} %param.19) | copy-start | bytes 772
  222.3 19.5 %copy-start.20 = (f32[1,64,16]{1,2,0:T(8,128)S(1)}, f32[1,64,16]{1,2,0:T(8,128)}, u32[]{:S(2)}) copy-start(f32[1,64,16]{1,2,0:T(8,128)} %param.18) | copy-start | bytes 12292
  222.3 19.6 %copy-start.23 = (f32[1,64]{1,0:T(1,128)S(1)}, f32[1,64]{1,0:T(1,128)}, u32[]{:S(2)}) copy-start(f32[1,64]{1,0:T(1,128)} %param.17) | copy-start | bytes 772
  222.3 46.1 %copy-start.2 = (f32[8,64,1024]{2,0,1:T(8,128)S(1)}, f32[8,64,1024]{2,0,1:T(8,128)}, u32[]{:S(2)}) copy-start(f32[8,64,1024]{2,0,1:T(8,128)} %slice_add_fusion.7) | copy-start | bytes 6291460
  240.3 1.3 collective-permute-start.5
  242.0 4.2 %collective-permute-start.6 = (f32[2,16,16]{2,1,0:T(8,128)S(1)}, f32[2,16,16]{2,1,0:T(8,128)S(1)}, u32[]{:S(2)}, u32[]{:S(2)}) collective-permute-start(f32[2,16,16]{2,1,0:T(8,128)S(1)} %pad_maximum_fusion.1), channel_id=1, source_target_pairs={{0,32},{32,0},{64,96},{96,64},{1,33},{33,1},{65,97},{97,65},{2,34}... | collective-permute-start | bytes 6152 | tf_op jit(solution)/shard_map/ppermute | solution.py:35
  246.2 5.3 %collective-permute-start.7 = (f32[2,16,16]{2,1,0:T(8,128)S(1)}, f32[2,16,16]{2,1,0:T(8,128)S(1)}, u32[]{:S(2)}, u32[]{:S(2)}) collective-permute-start(f32[2,16,16]{2,1,0:T(8,128)S(1)} %fusion.53), channel_id=1, source_target_pairs={{0,64},{32,96},{64,0},{96,32},{1,65},{33,97},{65,1},{97,33},{2,66}... | collective-permute-start | bytes 6152 | tf_op jit(solution)/shard_map/ppermute | solution.py:35
  251.5 3.7 %collective-permute-start.8 = (f32[2,16,16]{2,1,0:T(8,128)S(1)}, f32[2,16,16]{2,1,0:T(8,128)S(1)}, u32[]{:S(2)}, u32[]{:S(2)}) collective-permute-start(f32[2,16,16]{2,1,0:T(8,128)S(1)} %fusion.65), channel_id=1, source_target_pairs={{0,2},{2,0},{4,6},{6,4},{8,10},{10,8},{12,14},{14,12},{16,18},{18,... | collective-permute-start | bytes 6152 | tf_op jit(solution)/shard_map/ppermute | solution.py:35
  252.3 10.5 %collective-permute-start.12 = (f32[8,128]{1,0:T(8,128)S(1)}, f32[8,128]{1,0:T(8,128)S(1)}, u32[]{:S(2)}, u32[]{:S(2)}) collective-permute-start(f32[8,128]{1,0:T(8,128)S(1)} %copy-done.18), channel_id=1, source_target_pairs={{0,1},{1,0},{2,3},{3,2},{4,5},{5,4},{6,7},{7,6},{8,9},{9,8},{10,11... | collective-permute-start | bytes 12296 | tf_op jit(solution)/shard_map/ppermute | solution.py:41
  255.2 5.7 %collective-permute-start.9 = (f32[2,16,16]{2,1,0:T(8,128)S(1)}, f32[2,16,16]{2,1,0:T(8,128)S(1)}, u32[]{:S(2)}, u32[]{:S(2)}) collective-permute-start(f32[2,16,16]{2,1,0:T(8,128)S(1)} %add.294), channel_id=1, source_target_pairs={{0,4},{2,6},{4,0},{6,2},{8,12},{10,14},{12,8},{14,10},{16,20},{18,... | collective-permute-start | bytes 6152 | tf_op jit(solution)/shard_map/ppermute | solution.py:35
  260.9 3.7 %collective-permute-start.10 = (f32[2,16,16]{2,1,0:T(8,128)S(1)}, f32[2,16,16]{2,1,0:T(8,128)S(1)}, u32[]{:S(2)}, u32[]{:S(2)}) collective-permute-start(f32[2,16,16]{2,1,0:T(8,128)S(1)} %add.295), channel_id=1, source_target_pairs={{0,8},{2,10},{4,12},{6,14},{8,0},{10,2},{12,4},{14,6},{16,24},{18,... | collective-permute-start | bytes 6152 | tf_op jit(solution)/shard_map/ppermute | solution.py:35
  264.7 6.3 %collective-permute-start.11 = (f32[2,16,16]{2,1,0:T(8,128)S(1)}, f32[2,16,16]{2,1,0:T(8,128)S(1)}, u32[]{:S(2)}, u32[]{:S(2)}) collective-permute-start(f32[2,16,16]{2,1,0:T(8,128)S(1)} %add.296), channel_id=1, source_target_pairs={{0,16},{2,18},{4,20},{6,22},{8,24},{10,26},{12,28},{14,30},{16,0},... | collective-permute-start | bytes 6152 | tf_op jit(solution)/shard_map/ppermute | solution.py:35

commit v2 on v1

--- a/solution.py
+++ b/solution.py
@@ -78,16 +78,24 @@
     slabs = row_count * lax.axis_size("space")
     first_row = lax.axis_index("space") * row_count
     slice_index = lax.axis_index("tm")
-    links = lax.axis_size("tm") - 1
+    slices = lax.axis_size("tm")
+    links = slices - 1
     depth = FINE + links
+    group = members_here // slices
     band_width = col_count // params.shape[1]
-    spread_params = jnp.repeat(params, band_width, axis=1)
+
+    mine = lax.all_to_all(
+        state.reshape(slices, group, row_count, col_count), "tm", 0, 0, tiled=True
+    ).reshape(slices * group, row_count, col_count)
+    my_params = lax.dynamic_slice_in_dim(params, slice_index * group, group, 0)
+    spread_params = jnp.repeat(my_params, band_width, axis=1)
 
     fields = jnp.stack([diffusivity, velocity_x, velocity_y, source_shape])
-    wide = with_halo(jnp.concatenate([state, fields]), "space", depth)
-    wide_state = wide[:members_here]
-    wide_coeffs = wide[members_here : members_here + 3]
-    wide_forcing = wide[members_here + 3][None] * spread_params[:, None, :]
+    wide = with_halo(jnp.concatenate([mine, fields]), "space", depth)
+    count = slices * group
+    wide_state = wide[:count]
+    wide_coeffs = wide[count : count + 3]
+    wide_forcing = jnp.tile(wide[count + 3][None] * spread_params[:, None, :], (slices, 1, 1))
     global_rows = first_row - depth + jnp.arange(row_count + 2 * depth, dtype=jnp.int32)
     wide_inside = ((global_rows >= 0) & (global_rows < slabs)).astype(jnp.float32)[:, None]
 
@@ -102,18 +110,27 @@
     for section in range(FINE):
         current = step(current, section, FINE_DT, wide_forcing)
     coarse_part = coarse_part[:, FINE - 1 : FINE - 1 + current.shape[1]]
-    correction = jnp.where(slice_index > 0, current - coarse_part, current)
-    running = correction
-    for link in range(1, links + 1):
-        earlier = lax.ppermute(running, "tm", [(i, i + 1) for i in range(links)])
-        stepped = step(earlier, FINE + link - 1, coarse_dt, None)
+    fine = current.reshape(slices, group, -1, col_count)
+    coarse_part = coarse_part.reshape(slices, group, -1, col_count)
+    running = fine[0]
+    results = [running[:, links : links + row_count]]
+    for link in range(1, slices):
+        correction = fine[link] - coarse_part[link]
+        stepped = step(running, FINE + link - 1, coarse_dt, None)
         running = correction[:, link : correction.shape[1] - link] + stepped
+        results.append(running[:, links - link : links - link + row_count])
+    done = jnp.stack(results)
+    running = lax.all_to_all(done, "tm", 0, 0, tiled=True).reshape(
+        members_here, row_count, col_count
+    )
     new_states = running[None]
 
     local_cell = obs_cell[0] - first_row * col_count
     rows = local_cell // col_count
     cols = local_cell % col_count
-    predicted = running[:, rows, cols]
+    picked_rows = jnp.take(running, rows, axis=1)
+    at_col = lax.broadcasted_iota(jnp.int32, picked_rows.shape, 2) == cols[None, :, None]
+    predicted = jnp.sum(jnp.where(at_col, picked_rows, 0.0), axis=2)
     every_pred = both_halves(predicted, "ens")
     every_param = both_halves(params, "ens")
     total = every_pred.shape[0]

time: 278 us -> 156 us (0.56)
  waiting for transfers between devices: 154 us -> 40.6 us
  blocking collectives: 0 us -> 30.5 us
  other arithmetic: 41.3 us -> 21 us
  local copies, waits for them, and re-layouts: 42.9 us -> 32.8 us
  starting transfers between devices: 35 us -> 28.3 us
    ppermute x3 -> x0, waiting for transfers between devices: 136 us -> none  [per_device(): earlier = lax.ppermute(running, 'tm', [(i, i + 1) for i in range(links)])]
    all_to_all x0 -> x1, blocking collectives: none -> 30.5 us  [per_device(): lax.all_to_all(state.reshape(slices, group, row_count, col_count), 'tm',...]
    all_to_all x0 -> x1, waiting for transfers between devices: none -> 24.1 us  [per_device(): lax.all_to_all(done, 'tm', 0, 0, tiled=True)]
    add x1 -> x0, local copies, waits for them, and re-layouts: 16.5 us -> none  [per_device(): running = correction[:, link:correction.shape[1] - link] + stepped]
    ppermute x3 -> x0, starting transfers between devices: 12.8 us -> none  [per_device(): earlier = lax.ppermute(running, 'tm', [(i, i + 1) for i in range(links)])]
    add x3 -> x2, other arithmetic: 13.3 us -> 1.18 us  [per_device(): running = correction[:, link:correction.shape[1] - link] + stepped]
    unnamed x59 -> x38, local copies, waits for them, and re-layouts: 8.84 us -> 1.82 us
    another operation x0 -> x5, local copies, waits for them, and re-layouts: none -> 6.56 us  [the longest x1 3.21 us: per_device(): state.reshape(slices, group, row_count, col_count)]
  transfers between devices with their start and end apart: 13 -> 11, of which waited for: 11 -> 9; matrix products, arithmetic and copies ran while one was open for 2% -> 4% of each run, Pallas kernels for 0% -> 0%
where the time goes in v2:
time: 156 us
  waiting for transfers between devices  40.6 us (26%)
  local copies, waits for them, and re-layouts  32.8 us (21%)
  blocking collectives  30.5 us (20%)
  starting transfers between devices  28.3 us (18%)
  other arithmetic  21 us (13%)
    all_to_all x1, blocking collectives, per_device(): lax.all_to_all(state.reshape(slices, group, row_count, col_count), 'tm',...  30.5 us
    all_to_all x1, waiting for transfers between devices, per_device(): lax.all_to_all(done, 'tm', 0, 0, tiled=True)  24.1 us
    ppermute x6, starting transfers between devices, butterfly_sum(): lax.ppermute(value, axis, [(i, i ^ bit) for i in range(count)])  17.9 us
    ppermute x6, waiting for transfers between devices, butterfly_sum(): lax.ppermute(value, axis, [(i, i ^ bit) for i in range(count)])  12.9 us
    mul x5, other arithmetic, advance(): return (middle + step_size * tendency) * inside  11.1 us
    slice x7, local copies, waits for them, and re-layouts, advance(): west_cell = jnp.pad(middle[:, :, :-1], ((0, 0), (0, 0), (1, 0)))  5.62 us
    ppermute x1, starting transfers between devices, with_halo(): lax.ppermute(tail, axis, [(i, i + 1) for i in range(ends)])  5.32 us
    all_to_all x2, local copies, waits for them, and re-layouts, per_device(): lax.all_to_all(done, 'tm', 0, 0, tiled=True)  4.59 us
  transfers between devices with their start and end apart: 11, of which 9 were waited for; matrix products, arithmetic and copies ran while one was open for 4% of the time, Pallas kernels for 0%

profile of v2, /device:TPU:0, one launch (start us, length us, event | category | flops | bytes accessed | tf_op | source)
XLA Modules:
  0.0 155.8 jit_solution(2244062004232465099)
XLA Ops:
  0.6 3.2 %copy.39 = f32[4,2,64,1024]{3,1,2,0:T(2,128)S(1)} copy(f32[4,2,64,1024]{3,2,1,0:T(8,128)} %bitcast.135) | data formatting | bytes 4194304 | tf_op jit(solution)/shard_map/reshape;squeeze | solution.py:88
  3.8 30.5 %all_to_all.10 = f32[4,2,64,1024]{3,1,2,0:T(2,128)S(1)} all-to-all(f32[4,2,64,1024]{3,1,2,0:T(2,128)S(1)} %copy.39), channel_id=1, replica_groups=mesh['tm'=4,'space'=16,'ens'=2] {'tm'}, dimensions={0} | all-to-all | bytes 4194304 | tf_op jit(solution)/shard_map/all_to_all | solution.py:87
  34.3 0.6 copy.40
  35.3 0.7 copy-done
  36.2 0.9 fusion.46
  37.2 1.3 collective-permute-start.1
  38.4 5.3 %collective-permute-start = (f32[12,7,1024]{2,1,0:T(8,128)}, f32[12,7,1024]{2,1,0:T(8,128)}, u32[]{:S(2)}, u32[]{:S(2)}) collective-permute-start(f32[12,7,1024]{2,1,0:T(8,128)} %get-tuple-element.26), channel_id=1, source_target_pairs={{0,2},{2,4},{4,6},{6,8},{8,10},{10,12},{12,14},{14,16},{16,18},{18... | collective-permute-start | bytes 1032200 | tf_op jit(solution)/shard_map/ppermute | solution.py:21
  44.4 0.6 slice.384
  45.6 0.6 slice.407
  46.2 0.6 slice.420
  46.8 0.7 slice.429
  47.7 1.3 collective-permute-done.1
  49.0 1.2 collective-permute-done
  50.2 1.7 %pad_maximum_fusion = f32[12,78,1024]{2,1,0:T(8,128)S(1)} fusion(f32[12,7,1024]{2,1,0:T(8,128)} %collective-permute-done.1, f32[12,64,1024]{2,1,0:T(8,128)S(1)} %bitcast_dynamic-update-slice_fusion, f32[12,7,1024]{2,1,0:T(8,128)} %collective-permute-done), kind=kLoop, calls=%fused_computation.1 | loop fusion | flops 1916928 | bytes 7667712 | tf_op jit(solution)/shard_map/concatenate | solution.py:19
  52.0 1.4 fusion.45
  54.4 2.6 %fusion.5 = (f32[8,76,1024]{2,1,0:T(8,128)S(1)}, f32[8,76,1024]{2,1,0:T(8,128)S(1)}) fusion(f32[8,78,1024]{2,1,0:T(8,128)S(1)} %bitcast.130, f32[12,78,1024]{2,1,0:T(8,128)S(1)} %pad_maximum_fusion, f32[76]{0:T(128)S(1)} %slice.364, f32[76,1024]{1,0:T(8,128)S(1)} %get-tuple-element.22, f32[76,1024]{1,0:T(8,128)S(1)} %get-tuple-element.23, ...), kind=kLoop, calls=%fused_computation.9 | loop fusion | flops 11206656 | bytes 20852272 | tf_op jit(solution)/shard_map/mul | solution.py:60
  57.1 0.9 add_multiply_fusion
  58.0 1.4 fusion.49
  59.4 2.6 %fusion.2 = f32[8,74,1024]{2,1,0:T(8,128)S(1)} fusion(f32[8,78,1024]{2,1,0:T(8,128)S(1)} %bitcast.131, f32[8,76,1024]{2,1,0:T(8,128)S(1)} %get-tuple-element.4, f32[8,74,1023]{2,1,0:T(8,128)S(1)} %get-tuple-element.34, f32[8,74,1023]{2,1,0:T(8,128)S(1)} %get-tuple-element.33, f32[74]{0:T(128)S(1)} %copy-done.12, f32[74,1024]{1,0:T(8,128)S(1)} %get-tuple-element.19, ...), kind=kLoop, calls=%fused_computation.5 | loop fusion | flops 10911744 | bytes 17878696 | tf_op jit(solution)/shard_map/mul | solution.py:60
  62.1 1.1 fusion.48
  63.2 2.4 %fusion.11 = f32[8,72,1024]{2,1,0:T(8,128)S(1)} fusion(f32[8,78,1024]{2,1,0:T(8,128)S(1)} %bitcast.132, f32[8,74,1024]{2,1,0:T(8,128)S(1)} %fusion.2, f32[8,72,1023]{2,1,0:T(8,128)S(1)} %get-tuple-element.32, f32[8,72,1023]{2,1,0:T(8,128)S(1)} %get-tuple-element.31, f32[72]{0:T(128)S(1)} %copy-done.8, f32[72,1024]{1,0:T(8,128)S(1)} %get-tuple-element.16, ...), kind=kLoop, calls=%fused_computation.19 | loop fusion | flops 10616832 | bytes 17395488 | tf_op jit(solution)/shard_map/mul | solution.py:60
  65.6 1.1 fusion.52
  66.7 2.6 %fusion.8 = f32[8,70,1024]{2,1,0:T(8,128)S(1)} fusion(f32[8,78,1024]{2,1,0:T(8,128)S(1)} %bitcast.133, f32[8,72,1024]{2,1,0:T(8,128)S(1)} %fusion.11, f32[8,70,1023]{2,1,0:T(8,128)S(1)} %get-tuple-element.41, f32[8,70,1023]{2,1,0:T(8,128)S(1)} %get-tuple-element.40, f32[70]{0:T(128)S(1)} %copy-done.7, f32[70,1024]{1,0:T(8,128)S(1)} %get-tuple-element.13, ...), kind=kLoop, calls=%fused_computation.15 | loop fusion | flops 10321920 | bytes 16912280 | tf_op jit(solution)/shard_map/mul | solution.py:60
  73.1 2.9 %copy.41 = f32[4,2,64,1024]{3,1,2,0:T(2,128)} copy(f32[4,2,64,1024]{3,2,1,0:T(8,128)S(1)} %pad_maximum_fusion.1) | data formatting | bytes 4194304 | tf_op jit(solution)/shard_map/stack | solution.py:122
  76.0 3.7 %all-to-all-start.1 = ((f32[4,2,64,1024]{3,1,2,0:T(2,128)}), f32[4,2,64,1024]{3,1,2,0:T(2,128)S(1)}, u32[]{:S(2)}, u32[]{:S(2)}) async-start(f32[4,2,64,1024]{3,1,2,0:T(2,128)} %copy.41), calls=%async_computation.1 | async-start | bytes 4194304 | tf_op jit(solution)/shard_map/all_to_all | solution.py:123
  79.8 24.1 %all-to-all-done.1 = f32[4,2,64,1024]{3,1,2,0:T(2,128)S(1)} async-done(((f32[4,2,64,1024]{3,1,2,0:T(2,128)}), f32[4,2,64,1024]{3,1,2,0:T(2,128)S(1)}, u32[]{:S(2)}, u32[]{:S(2)}) %all-to-all-start.1) | async-done | bytes 2097184 | tf_op jit(solution)/shard_map/all_to_all | solution.py:123
  104.0 2.6 %copy.43 = f32[4,2,64,1024]{3,1,0,2:T(2,128)} copy(f32[4,2,64,1024]{3,1,2,0:T(2,128)S(1)} %all-to-all-done.1) | data formatting | bytes 4194304 | tf_op jit(solution)/shard_map/all_to_all | solution.py:123
  106.6 3.6 %reshape.167 = f32[8,64,1024]{2,0,1:T(8,128)} reshape(f32[4,2,64,1024]{3,1,0,2:T(2,128)} %copy.43) | data formatting | bytes 4194304 | tf_op jit(solution)/shard_map/reshape | solution.py:123
  110.2 3.6 %gather_fusion = f32[64,8,1024]{2,1,0:T(8,128)} fusion(f32[8,64,1024]{2,0,1:T(8,128)} %reshape.167, s32[1024]{0:T(1024)S(1)} %pad_clamp_fusion), kind=kCustom, calls=%fused_computation | custom fusion | bytes 4194560 | tf_op jit(solution)/shard_map/jit(_take)/gather | solution.py:131
  113.9 2.1 %fusion.12 = f32[8,64]{0,1:T(8,128)S(1)} fusion(f32[64,8,1024]{2,1,0:T(8,128)} %gather_fusion, s32[64]{0:T(128)S(1)} %and_select_fusion.2, pred[64]{0:T(512)(128)(4,1)S(1)} %get-tuple-element.2), kind=kLoop, calls=%fused_computation.22 | loop fusion | flops 2096640 | bytes 2099520 | tf_op jit(solution)/shard_map/reduce_sum | solution.py:133
  116.1 1.1 collective-permute-done.2
  117.6 0.6 collective-permute-start.3
  118.3 3.2 %collective-permute-done.3 = f32[2,16,16]{2,1,0:T(8,128)S(1)} collective-permute-done((f32[2,16,16]{2,1,0:T(8,128)S(1)}, f32[2,16,16]{2,1,0:T(8,128)S(1)}, u32[]{:S(2)}, u32[]{:S(2)}) %collective-permute-start.3) | collective-permute-done | bytes 2080 | tf_op jit(solution)/shard_map/ppermute | solution.py:35
  121.5 0.6 collective-permute-start.4
  122.1 4.6 %collective-permute-done.4 = f32[2,16,16]{2,1,0:T(8,128)S(1)} collective-permute-done((f32[2,16,16]{2,1,0:T(8,128)S(1)}, f32[2,16,16]{2,1,0:T(8,128)S(1)}, u32[]{:S(2)}, u32[]{:S(2)}) %collective-permute-start.4) | collective-permute-done | bytes 2080 | tf_op jit(solution)/shard_map/ppermute | solution.py:35
  126.7 2.5 %collective-permute-start.5 = (f32[2,16,16]{2,1,0:T(8,128)S(1)}, f32[2,16,16]{2,1,0:T(8,128)S(1)}, u32[]{:S(2)}, u32[]{:S(2)}) collective-permute-start(f32[2,16,16]{2,1,0:T(8,128)S(1)} %fusion.56), channel_id=1, source_target_pairs={{0,2},{2,0},{4,6},{6,4},{8,10},{10,8},{12,14},{14,12},{16,18},{18,... | collective-permute-start | bytes 6152 | tf_op jit(solution)/shard_map/ppermute | solution.py:35
  129.2 1.7 %collective-permute-done.5 = f32[2,16,16]{2,1,0:T(8,128)S(1)} collective-permute-done((f32[2,16,16]{2,1,0:T(8,128)S(1)}, f32[2,16,16]{2,1,0:T(8,128)S(1)}, u32[]{:S(2)}, u32[]{:S(2)}) %collective-permute-start.5) | collective-permute-done | bytes 2080 | tf_op jit(solution)/shard_map/ppermute | solution.py:35
  130.9 4.3 %collective-permute-start.6 = (f32[2,16,16]{2,1,0:T(8,128)S(1)}, f32[2,16,16]{2,1,0:T(8,128)S(1)}, u32[]{:S(2)}, u32[]{:S(2)}) collective-permute-start(f32[2,16,16]{2,1,0:T(8,128)S(1)} %add.295), channel_id=1, source_target_pairs={{0,4},{2,6},{4,0},{6,2},{8,12},{10,14},{12,8},{14,10},{16,20},{18,... | collective-permute-start | bytes 6152 | tf_op jit(solution)/shard_map/ppermute | solution.py:35
  135.2 1.7 %collective-permute-done.6 = f32[2,16,16]{2,1,0:T(8,128)S(1)} collective-permute-done((f32[2,16,16]{2,1,0:T(8,128)S(1)}, f32[2,16,16]{2,1,0:T(8,128)S(1)}, u32[]{:S(2)}, u32[]{:S(2)}) %collective-permute-start.6) | collective-permute-done | bytes 2080 | tf_op jit(solution)/shard_map/ppermute | solution.py:35
  136.9 5.9 %collective-permute-start.7 = (f32[2,16,16]{2,1,0:T(8,128)S(1)}, f32[2,16,16]{2,1,0:T(8,128)S(1)}, u32[]{:S(2)}, u32[]{:S(2)}) collective-permute-start(f32[2,16,16]{2,1,0:T(8,128)S(1)} %add.296), channel_id=1, source_target_pairs={{0,8},{2,10},{4,12},{6,14},{8,0},{10,2},{12,4},{14,6},{16,24},{18,... | collective-permute-start | bytes 6152 | tf_op jit(solution)/shard_map/ppermute | solution.py:35
  142.9 1.7 %collective-permute-done.7 = f32[2,16,16]{2,1,0:T(8,128)S(1)} collective-permute-done((f32[2,16,16]{2,1,0:T(8,128)S(1)}, f32[2,16,16]{2,1,0:T(8,128)S(1)}, u32[]{:S(2)}, u32[]{:S(2)}) %collective-permute-start.7) | collective-permute-done | bytes 2080 | tf_op jit(solution)/shard_map/ppermute | solution.py:35
  144.6 4.0 %collective-permute-start.8 = (f32[2,16,16]{2,1,0:T(8,128)S(1)}, f32[2,16,16]{2,1,0:T(8,128)S(1)}, u32[]{:S(2)}, u32[]{:S(2)}) collective-permute-start(f32[2,16,16]{2,1,0:T(8,128)S(1)} %add.297), channel_id=1, source_target_pairs={{0,16},{2,18},{4,20},{6,22},{8,24},{10,26},{12,28},{14,30},{16,0},... | collective-permute-start | bytes 6152 | tf_op jit(solution)/shard_map/ppermute | solution.py:35
  148.5 2.0 %copy.42 = f32[4,2,64,1024]{3,2,1,0:T(8,128)} copy(f32[4,2,64,1024]{3,1,2,0:T(2,128)S(1)} %all-to-all-done.1) | data formatting | bytes 4194304 | tf_op jit(solution)/shard_map/all_to_all | solution.py:123
  150.6 1.5 cholesky.17
  152.1 0.6 compare_reduce_fusion
  152.7 0.6 fusion.18
  153.4 1.2 custom-call.10
  155.0 0.7 fusion.13
  (94 shorter events, 8.0 us)
Async XLA Ops:
  35.0 1.0 copy-start
  35.0 1.0 copy-start.1
  35.0 1.1 copy-start.3
  35.0 1.2 copy-start.5
  35.9 11.6 %copy-start.6 = (f32[8,128]{1,0:T(8,128)S(1)}, f32[8,128]{1,0:T(8,128)}, u32[]{:S(2)}) copy-start(f32[8,128]{1,0:T(8,128)} %param.15) | copy-start | bytes 12292
  37.2 11.9 %collective-permute-start.1 = (f32[12,7,1024]{2,1,0:T(8,128)}, f32[12,7,1024]{2,1,0:T(8,128)}, u32[]{:S(2)}, u32[]{:S(2)}) collective-permute-start(f32[12,7,1024]{2,1,0:T(8,128)} %get-tuple-element.27), channel_id=1, source_target_pairs={{2,0},{4,2},{6,4},{8,6},{10,8},{12,10},{14,12},{16,14},{18,16},{20... | collective-permute-start | bytes 1032200 | tf_op jit(solution)/shard_map/ppermute | solution.py:23
  38.4 11.8 %collective-permute-start = (f32[12,7,1024]{2,1,0:T(8,128)}, f32[12,7,1024]{2,1,0:T(8,128)}, u32[]{:S(2)}, u32[]{:S(2)}) collective-permute-start(f32[12,7,1024]{2,1,0:T(8,128)} %get-tuple-element.26), channel_id=1, source_target_pairs={{0,2},{2,4},{4,6},{6,8},{8,10},{10,12},{12,14},{14,16},{16,18},{18... | collective-permute-start | bytes 1032200 | tf_op jit(solution)/shard_map/ppermute | solution.py:21
  58.0 1.4 copy-start.12
  62.1 1.1 copy-start.8
  65.5 1.1 copy-start.7
  69.5 0.6 copy-start.11
  70.7 0.6 copy-start.10
  71.3 0.9 copy-start.2
  71.3 1.0 copy-start.4
  71.3 1.0 copy-start.9
  76.0 3.8 %copy-start.13 = (s32[1,64]{1,0:T(1,128)S(1)}, s32[1,64]{1,0:T(1,128)}, u32[]{:S(2)}) copy-start(s32[1,64]{1,0:T(1,128)} %param.16) | copy-start | bytes 772
  76.0 27.9 %all-to-all-start.1 = ((f32[4,2,64,1024]{3,1,2,0:T(2,128)}), f32[4,2,64,1024]{3,1,2,0:T(2,128)S(1)}, u32[]{:S(2)}, u32[]{:S(2)}) async-start(f32[4,2,64,1024]{3,1,2,0:T(2,128)} %copy.41), calls=%async_computation.1 | async-start | bytes 4194304 | tf_op jit(solution)/shard_map/all_to_all | solution.py:123
  110.2 5.8 %copy-start.15 = (f32[1,64]{1,0:T(1,128)S(1)}, f32[1,64]{1,0:T(1,128)}, u32[]{:S(2)}) copy-start(f32[1,64]{1,0:T(1,128)} %param.19) | copy-start | bytes 772
  110.2 7.2 %copy-start.14 = (f32[1,64,16]{1,2,0:T(8,128)S(1)}, f32[1,64,16]{1,2,0:T(8,128)}, u32[]{:S(2)}) copy-start(f32[1,64,16]{1,2,0:T(8,128)} %param.18) | copy-start | bytes 12292
  110.2 7.2 %copy-start.16 = (f32[1,64]{1,0:T(1,128)S(1)}, f32[1,64]{1,0:T(1,128)}, u32[]{:S(2)}) copy-start(f32[1,64]{1,0:T(1,128)} %param.17) | copy-start | bytes 772
  116.0 1.3 collective-permute-start.2
  117.6 3.8 %collective-permute-start.3 = (f32[2,16,16]{2,1,0:T(8,128)S(1)}, f32[2,16,16]{2,1,0:T(8,128)S(1)}, u32[]{:S(2)}, u32[]{:S(2)}) collective-permute-start(f32[2,16,16]{2,1,0:T(8,128)S(1)} %pad_maximum_fusion.2), channel_id=1, source_target_pairs={{0,32},{32,0},{64,96},{96,64},{1,33},{33,1},{65,97},{97,65},{2,34}... | collective-permute-start | bytes 6152 | tf_op jit(solution)/shard_map/ppermute | solution.py:35
  121.5 5.2 %collective-permute-start.4 = (f32[2,16,16]{2,1,0:T(8,128)S(1)}, f32[2,16,16]{2,1,0:T(8,128)S(1)}, u32[]{:S(2)}, u32[]{:S(2)}) collective-permute-start(f32[2,16,16]{2,1,0:T(8,128)S(1)} %fusion.44), channel_id=1, source_target_pairs={{0,64},{32,96},{64,0},{96,32},{1,65},{33,97},{65,1},{97,33},{2,66}... | collective-permute-start | bytes 6152 | tf_op jit(solution)/shard_map/ppermute | solution.py:35
  126.7 4.2 %collective-permute-start.5 = (f32[2,16,16]{2,1,0:T(8,128)S(1)}, f32[2,16,16]{2,1,0:T(8,128)S(1)}, u32[]{:S(2)}, u32[]{:S(2)}) collective-permute-start(f32[2,16,16]{2,1,0:T(8,128)S(1)} %fusion.56), channel_id=1, source_target_pairs={{0,2},{2,0},{4,6},{6,4},{8,10},{10,8},{12,14},{14,12},{16,18},{18,... | collective-permute-start | bytes 6152 | tf_op jit(solution)/shard_map/ppermute | solution.py:35
  129.2 13.6 %collective-permute-start.9 = (f32[8,128]{1,0:T(8,128)S(1)}, f32[8,128]{1,0:T(8,128)S(1)}, u32[]{:S(2)}, u32[]{:S(2)}) collective-permute-start(f32[8,128]{1,0:T(8,128)S(1)} %copy-done.6), channel_id=1, source_target_pairs={{0,1},{1,0},{2,3},{3,2},{4,5},{5,4},{6,7},{7,6},{8,9},{9,8},{10,11... | collective-permute-start | bytes 12296 | tf_op jit(solution)/shard_map/ppermute | solution.py:41
  130.9 6.0 %collective-permute-start.6 = (f32[2,16,16]{2,1,0:T(8,128)S(1)}, f32[2,16,16]{2,1,0:T(8,128)S(1)}, u32[]{:S(2)}, u32[]{:S(2)}) collective-permute-start(f32[2,16,16]{2,1,0:T(8,128)S(1)} %add.295), channel_id=1, source_target_pairs={{0,4},{2,6},{4,0},{6,2},{8,12},{10,14},{12,8},{14,10},{16,20},{18,... | collective-permute-start | bytes 6152 | tf_op jit(solution)/shard_map/ppermute | solution.py:35
  136.9 7.6 %collective-permute-start.7 = (f32[2,16,16]{2,1,0:T(8,128)S(1)}, f32[2,16,16]{2,1,0:T(8,128)S(1)}, u32[]{:S(2)}, u32[]{:S(2)}) collective-permute-start(f32[2,16,16]{2,1,0:T(8,128)S(1)} %add.296), channel_id=1, source_target_pairs={{0,8},{2,10},{4,12},{6,14},{8,0},{10,2},{12,4},{14,6},{16,24},{18,... | collective-permute-start | bytes 6152 | tf_op jit(solution)/shard_map/ppermute | solution.py:35
  144.6 6.0 %collective-permute-start.8 = (f32[2,16,16]{2,1,0:T(8,128)S(1)}, f32[2,16,16]{2,1,0:T(8,128)S(1)}, u32[]{:S(2)}, u32[]{:S(2)}) collective-permute-start(f32[2,16,16]{2,1,0:T(8,128)S(1)} %add.297), channel_id=1, source_target_pairs={{0,16},{2,18},{4,20},{6,22},{8,24},{10,26},{12,28},{14,30},{16,0},... | collective-permute-start | bytes 6152 | tf_op jit(solution)/shard_map/ppermute | solution.py:35

commit v3 on v2

--- a/solution.py
+++ b/solution.py
@@ -26,15 +26,53 @@
     )
 
 
-def butterfly_sum(value, axis):
+def quad_sum(value, axis):
     count = lax.axis_size(axis)
     if count & (count - 1):
         return lax.psum(value, axis)
     bit = 1
     while bit < count:
-        value = value + lax.ppermute(value, axis, [(i, i ^ bit) for i in range(count)])
-        bit *= 2
+        if bit * 4 <= count:
+            near, far, both = (
+                lax.ppermute(value, axis, [(i, i ^ (k * bit)) for i in range(count)])
+                for k in (1, 2, 3)
+            )
+            value = (value + near) + (far + both)
+            bit *= 4
+        else:
+            value = value + lax.ppermute(value, axis, [(i, i ^ bit) for i in range(count)])
+            bit *= 2
     return value
+
+
+def by_source(pieces, axis):
+    count = lax.axis_size(axis)
+    stacked = jnp.stack(pieces)
+    order = (lax.axis_index(axis) - jnp.arange(count)) % count
+    return jnp.take(stacked, order, axis=0)
+
+
+def gather_axis(value, axis):
+    count = lax.axis_size(axis)
+    pieces = [value] + [
+        lax.ppermute(value, axis, [(i, (i + d) % count) for i in range(count)])
+        for d in range(1, count)
+    ]
+    return by_source(pieces, axis)
+
+
+def exchange_axis(values, axis):
+    count = lax.axis_size(axis)
+    own = lax.axis_index(axis)
+    pieces = [jnp.take(values, own, axis=0)] + [
+        lax.ppermute(
+            jnp.take(values, (own + d) % count, axis=0),
+            axis,
+            [(i, (i + d) % count) for i in range(count)],
+        )
+        for d in range(1, count)
+    ]
+    return by_source(pieces, axis)
 
 
 def both_halves(value, axis):
@@ -84,18 +122,20 @@
     group = members_here // slices
     band_width = col_count // params.shape[1]
 
+    fields = jnp.stack([diffusivity, velocity_x, velocity_y, source_shape])
+    wide_fields = with_halo(fields, "space", depth)
+    every_cell = gather_axis(obs_cell[0], "tm")
+    every_param = both_halves(params, "ens")
+
     mine = lax.all_to_all(
         state.reshape(slices, group, row_count, col_count), "tm", 0, 0, tiled=True
     ).reshape(slices * group, row_count, col_count)
     my_params = lax.dynamic_slice_in_dim(params, slice_index * group, group, 0)
     spread_params = jnp.repeat(my_params, band_width, axis=1)
 
-    fields = jnp.stack([diffusivity, velocity_x, velocity_y, source_shape])
-    wide = with_halo(jnp.concatenate([mine, fields]), "space", depth)
-    count = slices * group
-    wide_state = wide[:count]
-    wide_coeffs = wide[count : count + 3]
-    wide_forcing = jnp.tile(wide[count + 3][None] * spread_params[:, None, :], (slices, 1, 1))
+    wide_state = with_halo(mine, "space", depth)
+    wide_coeffs = wide_fields[:3]
+    wide_forcing = jnp.tile(wide_fields[3][None] * spread_params[:, None, :], (slices, 1, 1))
     global_rows = first_row - depth + jnp.arange(row_count + 2 * depth, dtype=jnp.int32)
     wide_inside = ((global_rows >= 0) & (global_rows < slabs)).astype(jnp.float32)[:, None]
 
@@ -125,14 +165,14 @@
     )
     new_states = running[None]
 
-    local_cell = obs_cell[0] - first_row * col_count
+    local_cell = every_cell - first_row * col_count
     rows = local_cell // col_count
     cols = local_cell % col_count
-    picked_rows = jnp.take(running, rows, axis=1)
-    at_col = lax.broadcasted_iota(jnp.int32, picked_rows.shape, 2) == cols[None, :, None]
-    predicted = jnp.sum(jnp.where(at_col, picked_rows, 0.0), axis=2)
+    picked_rows = jnp.take_along_axis(done, rows[:, None, :, None], axis=2)
+    at_col = lax.broadcasted_iota(jnp.int32, picked_rows.shape, 3) == cols[:, None, :, None]
+    local_pred = jnp.sum(jnp.where(at_col, picked_rows, 0.0), axis=3)
+    predicted = exchange_axis(local_pred, "tm").reshape(members_here, -1)
     every_pred = both_halves(predicted, "ens")
-    every_param = both_halves(params, "ens")
     total = every_pred.shape[0]
     norm_factor = 1.0 / math.sqrt(total - 1)
     inv_spread = lax.rsqrt(obs_var[0])[None, :]
@@ -142,8 +182,8 @@
     gram = jnp.dot(anomaly, anomaly.T, precision=lax.Precision.HIGHEST)
     cross = jnp.dot(anomaly, misfit.T, precision=lax.Precision.HIGHEST)
     sums = jnp.stack([gram, cross])
-    sums = butterfly_sum(sums, "tm")
-    sums = butterfly_sum(sums, "space")
+    sums = quad_sum(sums, "tm")
+    sums = quad_sum(sums, "space")
     gram, cross = sums[0], sums[1]
     system = jnp.eye(total, dtype=jnp.float32) + gram
     factor = jnp.linalg.cholesky(system)

time: 156 us -> 168 us (1.077)
  blocking collectives: 30.5 us -> 0 us
  starting transfers between devices: 28.3 us -> 41.4 us
  local copies, waits for them, and re-layouts: 32.8 us -> 45.2 us
  other arithmetic: 21 us -> 31.5 us
  waiting for transfers between devices: 40.6 us -> 46 us
    all_to_all x1 -> x0, blocking collectives: 30.5 us -> none  [per_device(): lax.all_to_all(state.reshape(slices, group, row_count, col_count), 'tm',...]
    all_to_all x0 -> x1, waiting for transfers between devices: none -> 10 us  [per_device(): lax.all_to_all(state.reshape(slices, group, row_count, col_count), 'tm',...]
    mul x6, local copies, waits for them, and re-layouts: 0.69 us -> 7.47 us  [advance(): coeffs[0] * (above_row + below_row + west_cell + east_cell - 4.0 * middle)]
    all_to_all x1, waiting for transfers between devices: 24.1 us -> 17.8 us  [per_device(): lax.all_to_all(done, 'tm', 0, 0, tiled=True)]
    another operation x1 -> x2, local copies, waits for them, and re-layouts: 0.31 us -> 5.59 us  [per_device(): jnp.tile(wide_fields[3][None] * spread_params[:, None, :], (slices, 1, 1))]
    all_to_all x0 -> x1, starting transfers between devices: none -> 4.59 us  [per_device(): lax.all_to_all(state.reshape(slices, group, row_count, col_count), 'tm',...]
    ppermute x6 -> x15, starting transfers between devices: 17.9 us -> 22.4 us  [the longest x9 15.1 us: quad_sum(): lax.ppermute(value, axis, [(i, i ^ k * bit) for i in range(count)])]
    ppermute x1 -> x2, waiting for transfers between devices: 1.28 us -> 5.5 us  [with_halo(): lax.ppermute(head, axis, [(i + 1, i) for i in range(ends)])]
  transfers between devices with their start and end apart: 11 -> 23, of which waited for: 9 -> 13; matrix products, arithmetic and copies ran while one was open for 4% -> 16% of each run, Pallas kernels for 0% -> 0%
where the time goes in v3:
time: 168 us; the launch traced here: 167 us
  waiting for transfers between devices  46 us (27%)
  local copies, waits for them, and re-layouts  45.2 us (27%)
  starting transfers between devices  41.4 us (25%)
  other arithmetic  31.5 us (19%)
    all_to_all x1, waiting for transfers between devices, per_device(): lax.all_to_all(done, 'tm', 0, 0, tiled=True)  17.8 us
    ppermute x9, starting transfers between devices, quad_sum(): lax.ppermute(value, axis, [(i, i ^ k * bit) for i in range(count)])  15.1 us
    mul x5, other arithmetic, advance(): return (middle + step_size * tendency) * inside  12.4 us
    all_to_all x1, waiting for transfers between devices, per_device(): lax.all_to_all(state.reshape(slices, group, row_count, col_count), 'tm',...  10 us
    ppermute x2, starting transfers between devices, with_halo(): lax.ppermute(tail, axis, [(i, i + 1) for i in range(ends)])  8.04 us
    mul x6, local copies, waits for them, and re-layouts, advance(): coeffs[0] * (above_row + below_row + west_cell + east_cell - 4.0 * middle)  7.47 us
    ppermute x9, waiting for transfers between devices, quad_sum(): lax.ppermute(value, axis, [(i, i ^ k * bit) for i in range(count)])  6.27 us
    slice x7, local copies, waits for them, and re-layouts, advance(): west_cell = jnp.pad(middle[:, :, :-1], ((0, 0), (0, 0), (1, 0)))  5.72 us
  transfers between devices with their start and end apart: 23, of which 13 were waited for; matrix products, arithmetic and copies ran while one was open for 16% of the time, Pallas kernels for 0%

profile of v3, /device:TPU:0, one launch (start us, length us, event | category | flops | bytes accessed | tf_op | source)
XLA Modules:
  0.0 167.0 jit_solution(9664121322502322952)
XLA Ops:
  0.6 2.9 %collective-permute-start.6 = (s32[64]{0:T(128)}, s32[64]{0:T(128)S(1)}, u32[]{:S(2)}, u32[]{:S(2)}) collective-permute-start(s32[64]{0:T(128)} %bitcast.139), channel_id=1, source_target_pairs={{0,96},{32,0},{64,32},{96,64},{1,97},{33,1},{65,33},{97,65},{2,98}... | collective-permute-start | bytes 776 | tf_op jit(solution)/shard_map/ppermute | solution.py:58
  6.1 1.3 collective-permute-start.3
  7.4 4.6 %collective-permute-start.2 = (f32[4,7,1024]{2,1,0:T(8,128)S(1)}, f32[4,7,1024]{2,1,0:T(8,128)S(1)}, u32[]{:S(2)}, u32[]{:S(2)}) collective-permute-start(f32[4,7,1024]{2,1,0:T(8,128)S(1)} %get-tuple-element.52), channel_id=1, source_target_pairs={{0,2},{2,4},{4,6},{6,8},{8,10},{10,12},{12,14},{14,16},{16,18},{18... | collective-permute-start | bytes 344072 | tf_op jit(solution)/shard_map/ppermute | solution.py:21
  12.0 4.5 %copy.25 = f32[4,2,64,1024]{3,1,2,0:T(2,128)} copy(f32[4,2,64,1024]{3,2,1,0:T(8,128)} %bitcast.128) | data formatting | bytes 4194304 | tf_op jit(solution)/shard_map/reshape;squeeze | solution.py:131
  16.6 4.6 %all-to-all-start = ((f32[4,2,64,1024]{3,1,2,0:T(2,128)}), f32[4,2,64,1024]{3,1,2,0:T(2,128)}, u32[]{:S(2)}, u32[]{:S(2)}) async-start(f32[4,2,64,1024]{3,1,2,0:T(2,128)} %copy.25), calls=%async_computation | async-start | bytes 4194304 | tf_op jit(solution)/shard_map/all_to_all | solution.py:130
  23.3 1.1 copy-done
  24.6 2.3 %tile.4 = f32[4,2,78,1024]{3,1,0,2:T(2,128)} broadcast(f32[2,78,1024]{2,0,1:T(2,128)S(1)} %broadcast_multiply_fusion), dimensions={1,2,3} | broadcast | bytes 3194880 | tf_op jit(solution)/shard_map/tile | solution.py:138
  26.8 3.3 %tile.10 = f32[8,78,1024]{2,0,1:T(8,128)S(1)} reshape(f32[4,2,78,1024]{3,1,0,2:T(2,128)} %tile.4) | data formatting | bytes 5111808 | tf_op jit(solution)/shard_map/tile | solution.py:138
  30.2 2.2 %slice_bitcast_fusion.21 = (f32[72,1024]{1,0:T(8,128)}, f32[72,1024]{1,0:T(8,128)}, f32[72,1024]{1,0:T(8,128)}) fusion(f32[4,78,1024]{2,1,0:T(8,128)} %copy-done), kind=kLoop, calls=%fused_computation.58 | loop fusion | bytes 1769472 | tf_op jit(solution)/shard_map/mul | solution.py:90
  35.3 1.1 slice_bitcast_fusion.5
  36.4 10.0 %all-to-all-done = f32[4,2,64,1024]{3,1,2,0:T(2,128)} async-done(((f32[4,2,64,1024]{3,1,2,0:T(2,128)}), f32[4,2,64,1024]{3,1,2,0:T(2,128)}, u32[]{:S(2)}, u32[]{:S(2)}) %all-to-all-start) | async-done | bytes 2097184 | tf_op jit(solution)/shard_map/all_to_all | solution.py:130
  46.4 4.2 %copy.26 = f32[4,2,64,1024]{3,1,0,2:T(2,128)} copy(f32[4,2,64,1024]{3,1,2,0:T(2,128)} %all-to-all-done) | data formatting | bytes 4194304 | tf_op jit(solution)/shard_map/all_to_all | solution.py:130
  50.6 3.7 %reshape.267 = f32[8,64,1024]{2,0,1:T(8,128)} reshape(f32[4,2,64,1024]{3,1,0,2:T(2,128)} %copy.26) | data formatting | bytes 4194304 | tf_op jit(solution)/shard_map/reshape | solution.py:132
  54.3 1.2 fusion.60
  55.5 3.5 %collective-permute-start = (f32[8,7,1024]{2,0,1:T(8,128)S(1)}, f32[8,7,1024]{2,0,1:T(8,128)S(1)}, u32[]{:S(2)}, u32[]{:S(2)}) collective-permute-start(f32[8,7,1024]{2,0,1:T(8,128)S(1)} %get-tuple-element.33), channel_id=1, source_target_pairs={{0,2},{2,4},{4,6},{6,8},{8,10},{10,12},{12,14},{14,16},{16,18},{18... | collective-permute-start | bytes 688136 | tf_op jit(solution)/shard_map/ppermute | solution.py:21
  59.0 1.3 slice_bitcast_fusion.12
  60.3 1.5 collective-permute-start.1
  62.7 5.5 %collective-permute-done.1 = f32[8,7,1024]{2,0,1:T(8,128)S(1)} collective-permute-done((f32[8,7,1024]{2,0,1:T(8,128)S(1)}, f32[8,7,1024]{2,0,1:T(8,128)S(1)}, u32[]{:S(2)}, u32[]{:S(2)}) %collective-permute-start.1) | collective-permute-done | bytes 229408 | tf_op jit(solution)/shard_map/ppermute | solution.py:23
  68.3 1.0 fusion.53
  69.4 3.1 %fusion.2 = (f32[8,76,1024]{2,0,1:T(8,128)S(1)}, f32[8,76,1024]{2,0,1:T(8,128)S(1)}) fusion(f32[8,78,1024]{2,0,1:T(8,128)S(1)} %tile.10, f32[8,78,1024]{2,0,1:T(8,128)S(1)} %constant_dynamic-update-slice_fusion, f32[76]{0:T(128)S(1)} %slice.368, f32[76,1024]{1,0:T(8,128)S(1)} %copy-done.7, f32[76,1024]{1,0:T(8,128)S(1)} %copy-done.8, ...), kind=kLoop, calls=%fused_computation.7 | loop fusion | flops 11206656 | bytes 20852272 | tf_op jit(solution)/shard_map/mul | solution.py:98
  74.1 3.0 %fusion.5 = f32[8,74,1024]{2,0,1:T(8,128)S(1)} fusion(f32[8,78,1024]{2,0,1:T(8,128)S(1)} %tile.10, f32[8,76,1024]{2,0,1:T(8,128)S(1)} %get-tuple-element.14, f32[8,74,1023]{2,0,1:T(8,128)S(1)} %get-tuple-element.22, f32[8,74,1023]{2,0,1:T(8,128)S(1)} %get-tuple-element.21, f32[74]{0:T(128)S(1)} %slice.378, f32[74,1024]{1,0:T(8,128)S(1)} %copy-done.10, ...), kind=kLoop, calls=%fused_computation.13 | loop fusion | flops 10911744 | bytes 17878696 | tf_op jit(solution)/shard_map/mul | solution.py:98
  78.2 3.0 %fusion.8 = f32[8,72,1024]{2,0,1:T(8,128)S(1)} fusion(f32[8,78,1024]{2,0,1:T(8,128)S(1)} %tile.10, f32[8,74,1024]{2,0,1:T(8,128)S(1)} %fusion.5, f32[8,72,1023]{2,0,1:T(8,128)S(1)} %get-tuple-element.24, f32[8,72,1023]{2,0,1:T(8,128)S(1)} %get-tuple-element.23, f32[72]{0:T(128)S(1)} %slice.388, f32[72,1024]{1,0:T(8,128)S(1)} %copy-done.19, ...), kind=kLoop, calls=%fused_computation.17 | loop fusion | flops 10616832 | bytes 17395488 | tf_op jit(solution)/shard_map/mul | solution.py:98
  82.4 2.9 %fusion.11 = f32[8,70,1024]{2,0,1:T(8,128)S(1)} fusion(f32[8,78,1024]{2,0,1:T(8,128)S(1)} %tile.10, f32[8,72,1024]{2,0,1:T(8,128)S(1)} %fusion.8, f32[8,70,1023]{2,0,1:T(8,128)S(1)} %get-tuple-element.26, f32[8,70,1023]{2,0,1:T(8,128)S(1)} %get-tuple-element.25, f32[70]{0:T(128)S(1)} %slice.398, f32[70,1024]{1,0:T(8,128)S(1)} %copy-done.16, ...), kind=kLoop, calls=%fused_computation.21 | loop fusion | flops 10321920 | bytes 16912280 | tf_op jit(solution)/shard_map/mul | solution.py:98
  86.1 1.3 fusion.54
  87.5 2.9 %fusion.14 = f32[2,68,1024]{2,0,1:T(2,128)S(1)} fusion(f32[2,70,1024]{2,0,1:T(2,128)S(1)} %get-tuple-element.18, f32[2,70,1024]{2,0,1:T(2,128)S(1)} %get-tuple-element.68, f32[8,70,1024]{2,0,1:T(8,128)S(1)} %fusion.11, f32[2,68,1023]{2,0,1:T(2,128)S(1)} %get-tuple-element.28, f32[2,68,1023]{2,0,1:T(2,128)S(1)} %get-tuple-element.27, f32[68]{0:T(128)S(1)} %slice.411, ...), kind=kLoop, calls=%fused_computation.30 | loop fusion | flops 2506752 | bytes 5291216 | tf_op jit(solution)/shard_map/add | solution.py:160
  91.2 2.3 %fusion.15 = f32[2,66,1024]{2,0,1:T(2,128)S(1)} fusion(f32[2,70,1024]{2,0,1:T(2,128)S(1)} %get-tuple-element.20, f32[2,70,1024]{2,0,1:T(2,128)S(1)} %get-tuple-element.66, f32[2,68,1024]{2,0,1:T(2,128)S(1)} %fusion.14, f32[2,66,1023]{2,0,1:T(2,128)S(1)} %get-tuple-element.55, f32[2,66,1023]{2,0,1:T(2,128)S(1)} %get-tuple-element.54, f32[66]{0:T(128)S(1)} %slice.424, ...), kind=kLoop, calls=%fused_computation.32 | loop fusion | flops 2433024 | bytes 5135592 | tf_op jit(solution)/shard_map/add | solution.py:160
  94.1 2.0 %slice_bitcast_fusion.2 = (f32[1,2,64,1024]{3,1,2,0:T(2,128)S(1)}, f32[1,2,64,1024]{3,1,2,0:T(2,128)S(1)}) fusion(f32[2,66,1024]{2,0,1:T(2,128)S(1)} %fusion.15, f32[64]{0:T(128)S(1)} %slice.433, f32[64,1024]{1,0:T(8,128)S(1)} %copy-done.3, f32[64,1024]{1,0:T(8,128)S(1)} %copy-done.4, f32[2,64,1023]{2,0,1:T(2,128)S(1)} %get-tuple-element.59, ...), kind=kLoop, calls=%fused_computation.38 | loop fusion | flops 2359296 | bytes 5504256 | tf_op jit(solution)/shard_map/stack | solution.py:162
  96.1 2.0 %pad_maximum_fusion = f32[4,2,64,1024]{3,1,2,0:T(2,128)} fusion(f32[1,2,64,1024]{3,1,2,0:T(2,128)S(1)} %get-tuple-element.57, f32[1,2,64,1024]{3,1,2,0:T(2,128)S(1)} %get-tuple-element.56, f32[1,2,64,1024]{3,1,2,0:T(2,128)S(1)} %slice_bitcast_fusion, f32[1,2,64,1024]{3,1,2,0:T(2,128)S(1)} %slice_bitcast_fusion.1), kind=kLoop, calls=%fused_computation.23 | loop fusion | flops 1572864 | bytes 4194304 | tf_op jit(solution)/shard_map/stack | solution.py:162
  98.1 4.8 %gather_fusion.2 = f32[256,2,1024]{2,1,0:T(2,128)S(1)} fusion(f32[4,2,64,1024]{3,1,2,0:T(2,128)} %pad_maximum_fusion, s32[256]{0:T(256)S(1)} %reshape.355), kind=kCustom, calls=%fused_computation.2 | custom fusion | bytes 4196352 | tf_op jit(solution)/shard_map/jit(take_along_axis)/gather | solution.py:171
  102.9 4.2 %fusion.12 = f32[4,2,64]{1,2,0:T(8,128)S(1)} fusion(f32[4,64,2,1024]{3,2,1,0:T(2,128)S(1)} %bitcast.121, pred[4,64]{1,0:T(4,128)(4,1)S(1)} %compare_and_fusion, s32[4,64]{1,0:T(4,128)S(1)} %add_select_fusion.2), kind=kLoop, calls=%fused_computation.22 | loop fusion | flops 2096640 | bytes 2100480 | tf_op jit(solution)/shard_map/reduce_sum | solution.py:173
  107.2 1.3 collective-permute-start.9
  108.5 1.4 collective-permute-start.8
  110.7 2.9 %collective-permute-done.8 = f32[2,64]{1,0:T(2,128)S(1)} collective-permute-done((f32[2,64]{1,0:T(2,128)S(1)}, f32[2,64]{1,0:T(2,128)S(1)}, u32[]{:S(2)}, u32[]{:S(2)}) %collective-permute-start.8) | collective-permute-done | bytes 544 | tf_op jit(solution)/shard_map/ppermute | solution.py:68
  113.6 1.1 collective-permute-done.7
  115.5 1.1 collective-permute-done.10
  116.9 1.0 collective-permute-start.12
  118.0 1.3 collective-permute-start.13
  119.3 1.2 collective-permute-start.11
  120.5 1.8 %collective-permute-done.12 = f32[2,16,16]{2,1,0:T(8,128)S(1)} collective-permute-done((f32[2,16,16]{2,1,0:T(8,128)S(1)}, f32[2,16,16]{2,1,0:T(8,128)S(1)}, u32[]{:S(2)}, u32[]{:S(2)}) %collective-permute-start.12) | collective-permute-done | bytes 2080 | tf_op jit(solution)/shard_map/ppermute | solution.py:37
  123.0 5.1 %collective-permute-start.15 = (f32[2,16,16]{2,1,0:T(8,128)S(1)}, f32[2,16,16]{2,1,0:T(8,128)S(1)}, u32[]{:S(2)}, u32[]{:S(2)}) collective-permute-start(f32[2,16,16]{2,1,0:T(8,128)S(1)} %add_add_fusion.2), channel_id=1, source_target_pairs={{0,4},{2,6},{4,0},{6,2},{8,12},{10,14},{12,8},{14,10},{16,20},{18,... | collective-permute-start | bytes 6152 | tf_op jit(solution)/shard_map/ppermute | solution.py:37
  128.1 1.0 collective-permute-start.16
  129.9 3.1 %collective-permute-done.16 = f32[2,16,16]{2,1,0:T(8,128)S(1)} collective-permute-done((f32[2,16,16]{2,1,0:T(8,128)S(1)}, f32[2,16,16]{2,1,0:T(8,128)S(1)}, u32[]{:S(2)}, u32[]{:S(2)}) %collective-permute-start.16) | collective-permute-done | bytes 2080 | tf_op jit(solution)/shard_map/ppermute | solution.py:37
  133.1 4.0 %collective-permute-start.18 = (f32[2,16,16]{2,1,0:T(8,128)S(1)}, f32[2,16,16]{2,1,0:T(8,128)S(1)}, u32[]{:S(2)}, u32[]{:S(2)}) collective-permute-start(f32[2,16,16]{2,1,0:T(8,128)S(1)} %add_add_fusion.1), channel_id=1, source_target_pairs={{0,16},{2,18},{4,20},{6,22},{8,24},{10,26},{12,28},{14,30},{16,0},... | collective-permute-start | bytes 6152 | tf_op jit(solution)/shard_map/ppermute | solution.py:37
  137.8 3.6 %all-to-all-start.1 = ((f32[4,2,64,1024]{3,1,2,0:T(2,128)}), f32[4,2,64,1024]{3,1,2,0:T(2,128)S(1)}, u32[]{:S(2)}, u32[]{:S(2)}) async-start(f32[4,2,64,1024]{3,1,2,0:T(2,128)} %pad_maximum_fusion), calls=%async_computation.1 | async-start | bytes 4194304 | tf_op jit(solution)/shard_map/all_to_all | solution.py:163
  142.1 1.5 cholesky.17
  144.9 1.2 custom-call.10
  147.3 17.8 %all-to-all-done.1 = f32[4,2,64,1024]{3,1,2,0:T(2,128)S(1)} async-done(((f32[4,2,64,1024]{3,1,2,0:T(2,128)}), f32[4,2,64,1024]{3,1,2,0:T(2,128)S(1)}, u32[]{:S(2)}, u32[]{:S(2)}) %all-to-all-start.1) | async-done | bytes 2097184 | tf_op jit(solution)/shard_map/all_to_all | solution.py:163
  165.1 2.0 %copy.27 = f32[4,2,64,1024]{3,2,1,0:T(8,128)} copy(f32[4,2,64,1024]{3,1,2,0:T(2,128)S(1)} %all-to-all-done.1) | data formatting | bytes 4194304 | tf_op jit(solution)/shard_map/all_to_all | solution.py:163
  (145 shorter events, 22.0 us)
Async XLA Ops:
  0.6 21.4 %collective-permute-start.6 = (s32[64]{0:T(128)}, s32[64]{0:T(128)S(1)}, u32[]{:S(2)}, u32[]{:S(2)}) collective-permute-start(s32[64]{0:T(128)} %bitcast.139), channel_id=1, source_target_pairs={{0,96},{32,0},{64,32},{96,64},{1,97},{33,1},{65,33},{97,65},{2,98}... | collective-permute-start | bytes 776 | tf_op jit(solution)/shard_map/ppermute | solution.py:58
  3.5 18.5 %collective-permute-start.5 = (s32[64]{0:T(128)}, s32[64]{0:T(128)S(1)}, u32[]{:S(2)}, u32[]{:S(2)}) collective-permute-start(s32[64]{0:T(128)} %bitcast.140), channel_id=1, source_target_pairs={{0,64},{32,96},{64,0},{96,32},{1,65},{33,97},{65,1},{97,33},{2,66}... | collective-permute-start | bytes 776 | tf_op jit(solution)/shard_map/ppermute | solution.py:58
  4.3 17.7 %collective-permute-start.4 = (s32[64]{0:T(128)}, s32[64]{0:T(128)S(1)}, u32[]{:S(2)}, u32[]{:S(2)}) collective-permute-start(s32[64]{0:T(128)} %bitcast.141), channel_id=1, source_target_pairs={{0,32},{32,64},{64,96},{96,0},{1,33},{33,65},{65,97},{97,1},{2,34}... | collective-permute-start | bytes 776 | tf_op jit(solution)/shard_map/ppermute | solution.py:58
  6.1 16.9 %collective-permute-start.3 = (f32[4,7,1024]{2,1,0:T(8,128)S(1)}, f32[4,7,1024]{2,1,0:T(8,128)S(1)}, u32[]{:S(2)}, u32[]{:S(2)}) collective-permute-start(f32[4,7,1024]{2,1,0:T(8,128)S(1)} %get-tuple-element.53), channel_id=1, source_target_pairs={{2,0},{4,2},{6,4},{8,6},{10,8},{12,10},{14,12},{16,14},{18,16},{20... | collective-permute-start | bytes 344072 | tf_op jit(solution)/shard_map/ppermute | solution.py:23
  7.4 15.6 %collective-permute-start.2 = (f32[4,7,1024]{2,1,0:T(8,128)S(1)}, f32[4,7,1024]{2,1,0:T(8,128)S(1)}, u32[]{:S(2)}, u32[]{:S(2)}) collective-permute-start(f32[4,7,1024]{2,1,0:T(8,128)S(1)} %get-tuple-element.52), channel_id=1, source_target_pairs={{0,2},{2,4},{4,6},{6,8},{8,10},{10,12},{12,14},{14,16},{16,18},{18... | collective-permute-start | bytes 344072 | tf_op jit(solution)/shard_map/ppermute | solution.py:21
  16.5 5.3 %copy-start.22 = (f32[8,128]{1,0:T(8,128)S(1)}, f32[8,128]{1,0:T(8,128)}, u32[]{:S(2)}) copy-start(f32[8,128]{1,0:T(8,128)} %param.17) | copy-start | bytes 12292
  16.5 5.6 %copy-start.23 = (s32[1,64]{1,0:T(1,128)S(1)}, s32[1,64]{1,0:T(1,128)}, u32[]{:S(2)}) copy-start(s32[1,64]{1,0:T(1,128)} %param.18) | copy-start | bytes 772
  16.5 6.5 %copy-start.3 = (f32[64,1024]{1,0:T(8,128)S(1)}, f32[64,1024]{1,0:T(8,128)}, u32[]{:S(2)}) copy-start(f32[64,1024]{1,0:T(8,128)} %param.14) | copy-start | bytes 786436
  16.5 6.5 %copy-start.4 = (f32[64,1024]{1,0:T(8,128)S(1)}, f32[64,1024]{1,0:T(8,128)}, u32[]{:S(2)}) copy-start(f32[64,1024]{1,0:T(8,128)} %param.13) | copy-start | bytes 786436
  16.5 6.5 %copy-start.5 = (f32[64,1024]{1,0:T(8,128)S(1)}, f32[64,1024]{1,0:T(8,128)}, u32[]{:S(2)}) copy-start(f32[64,1024]{1,0:T(8,128)} %param.15) | copy-start | bytes 786436
  16.5 6.5 %copy-start.21 = (f32[64,1024]{1,0:T(8,128)S(1)}, f32[64,1024]{1,0:T(8,128)}, u32[]{:S(2)}) copy-start(f32[64,1024]{1,0:T(8,128)} %param.16) | copy-start | bytes 786436
  16.6 29.9 %all-to-all-start = ((f32[4,2,64,1024]{3,1,2,0:T(2,128)}), f32[4,2,64,1024]{3,1,2,0:T(2,128)}, u32[]{:S(2)}, u32[]{:S(2)}) async-start(f32[4,2,64,1024]{3,1,2,0:T(2,128)} %copy.25), calls=%async_computation | async-start | bytes 4194304 | tf_op jit(solution)/shard_map/all_to_all | solution.py:130
  23.2 1.1 copy-start
  30.2 2.3 %copy-start.1 = (f32[4,78,1024]{2,1,0:T(8,128)S(1)}, f32[4,78,1024]{2,1,0:T(8,128)}, u32[]{:S(2)}) copy-start(f32[4,78,1024]{2,1,0:T(8,128)} %copy-done) | copy-start | bytes 3833860
  54.3 8.3 %copy-start.2 = (f32[8,64,1024]{2,0,1:T(8,128)S(1)}, f32[8,64,1024]{2,0,1:T(8,128)}, u32[]{:S(2)}) copy-start(f32[8,64,1024]{2,0,1:T(8,128)} %reshape.267) | copy-start | bytes 6291460
  55.5 7.0 %collective-permute-start = (f32[8,7,1024]{2,0,1:T(8,128)S(1)}, f32[8,7,1024]{2,0,1:T(8,128)S(1)}, u32[]{:S(2)}, u32[]{:S(2)}) collective-permute-start(f32[8,7,1024]{2,0,1:T(8,128)S(1)} %get-tuple-element.33), channel_id=1, source_target_pairs={{0,2},{2,4},{4,6},{6,8},{8,10},{10,12},{12,14},{14,16},{16,18},{18... | collective-permute-start | bytes 688136 | tf_op jit(solution)/shard_map/ppermute | solution.py:21
  60.3 7.9 %collective-permute-start.1 = (f32[8,7,1024]{2,0,1:T(8,128)S(1)}, f32[8,7,1024]{2,0,1:T(8,128)S(1)}, u32[]{:S(2)}, u32[]{:S(2)}) collective-permute-start(f32[8,7,1024]{2,0,1:T(8,128)S(1)} %get-tuple-element.32), channel_id=1, source_target_pairs={{2,0},{4,2},{6,4},{8,6},{10,8},{12,10},{14,12},{16,14},{18,16},{20... | collective-permute-start | bytes 688136 | tf_op jit(solution)/shard_map/ppermute | solution.py:23
  68.2 1.0 copy-start.6
  68.3 1.1 copy-start.7
  68.3 1.2 copy-start.8
  72.9 1.0 copy-start.9
  72.9 1.1 copy-start.10
  72.9 1.2 copy-start.11
  77.1 1.0 copy-start.19
  77.1 1.1 copy-start.20
  81.3 1.0 copy-start.16
  81.3 1.1 copy-start.17
  86.1 1.4 copy-start.12
  86.1 1.4 copy-start.13
  86.1 1.4 copy-start.14
  102.9 12.6 %copy-start.25 = (f32[1,64]{1,0:T(1,128)S(1)}, f32[1,64]{1,0:T(1,128)}, u32[]{:S(2)}) copy-start(f32[1,64]{1,0:T(1,128)} %param.21) | copy-start | bytes 772
  102.9 13.9 %copy-start.24 = (f32[1,64,16]{1,2,0:T(8,128)S(1)}, f32[1,64,16]{1,2,0:T(8,128)}, u32[]{:S(2)}) copy-start(f32[1,64,16]{1,2,0:T(8,128)} %param.20) | copy-start | bytes 12292
  102.9 13.9 %copy-start.26 = (f32[1,64]{1,0:T(1,128)S(1)}, f32[1,64]{1,0:T(1,128)}, u32[]{:S(2)}) copy-start(f32[1,64]{1,0:T(1,128)} %param.19) | copy-start | bytes 772
  107.2 3.6 %collective-permute-start.9 = (f32[2,64]{1,0:T(2,128)S(1)}, f32[2,64]{1,0:T(2,128)S(1)}, u32[]{:S(2)}, u32[]{:S(2)}) collective-permute-start(f32[2,64]{1,0:T(2,128)S(1)} %bitcast.133), channel_id=1, source_target_pairs={{0,96},{32,0},{64,32},{96,64},{1,97},{33,1},{65,33},{97,65},{2,98}... | collective-permute-start | bytes 1544 | tf_op jit(solution)/shard_map/ppermute | solution.py:68
  108.5 5.1 %collective-permute-start.8 = (f32[2,64]{1,0:T(2,128)S(1)}, f32[2,64]{1,0:T(2,128)S(1)}, u32[]{:S(2)}, u32[]{:S(2)}) collective-permute-start(f32[2,64]{1,0:T(2,128)S(1)} %bitcast.134), channel_id=1, source_target_pairs={{0,64},{32,96},{64,0},{96,32},{1,65},{33,97},{65,1},{97,33},{2,66}... | collective-permute-start | bytes 1544 | tf_op jit(solution)/shard_map/ppermute | solution.py:68
  110.0 4.8 %collective-permute-start.7 = (f32[2,64]{1,0:T(2,128)S(1)}, f32[2,64]{1,0:T(2,128)S(1)}, u32[]{:S(2)}, u32[]{:S(2)}) collective-permute-start(f32[2,64]{1,0:T(2,128)S(1)} %bitcast.135), channel_id=1, source_target_pairs={{0,32},{32,64},{64,96},{96,0},{1,33},{33,65},{65,97},{97,1},{2,34}... | collective-permute-start | bytes 1544 | tf_op jit(solution)/shard_map/ppermute | solution.py:68
  115.4 1.2 collective-permute-start.10
  116.9 5.3 %collective-permute-start.12 = (f32[2,16,16]{2,1,0:T(8,128)S(1)}, f32[2,16,16]{2,1,0:T(8,128)S(1)}, u32[]{:S(2)}, u32[]{:S(2)}) collective-permute-start(f32[2,16,16]{2,1,0:T(8,128)S(1)} %pad_maximum_fusion.6), channel_id=1, source_target_pairs={{0,64},{32,96},{64,0},{96,32},{1,65},{33,97},{65,1},{97,33},{2,66}... | collective-permute-start | bytes 6152 | tf_op jit(solution)/shard_map/ppermute | solution.py:37
  118.0 4.9 %collective-permute-start.13 = (f32[2,16,16]{2,1,0:T(8,128)S(1)}, f32[2,16,16]{2,1,0:T(8,128)S(1)}, u32[]{:S(2)}, u32[]{:S(2)}) collective-permute-start(f32[2,16,16]{2,1,0:T(8,128)S(1)} %pad_maximum_fusion.6), channel_id=1, source_target_pairs={{0,96},{32,64},{64,32},{96,0},{1,97},{33,65},{65,33},{97,1},{2,98}... | collective-permute-start | bytes 6152 | tf_op jit(solution)/shard_map/ppermute | solution.py:37
  119.3 3.7 %collective-permute-start.11 = (f32[2,16,16]{2,1,0:T(8,128)S(1)}, f32[2,16,16]{2,1,0:T(8,128)S(1)}, u32[]{:S(2)}, u32[]{:S(2)}) collective-permute-start(f32[2,16,16]{2,1,0:T(8,128)S(1)} %pad_maximum_fusion.6), channel_id=1, source_target_pairs={{0,32},{32,0},{64,96},{96,64},{1,33},{33,1},{65,97},{97,65},{2,34}... | collective-permute-start | bytes 6152 | tf_op jit(solution)/shard_map/ppermute | solution.py:37
  120.5 9.4 %collective-permute-start.20 = (f32[8,128]{1,0:T(8,128)S(1)}, f32[8,128]{1,0:T(8,128)S(1)}, u32[]{:S(2)}, u32[]{:S(2)}) collective-permute-start(f32[8,128]{1,0:T(8,128)S(1)} %copy-done.22), channel_id=1, source_target_pairs={{0,1},{1,0},{2,3},{3,2},{4,5},{5,4},{6,7},{7,6},{8,9},{9,8},{10,11... | collective-permute-start | bytes 12296 | tf_op jit(solution)/shard_map/ppermute | solution.py:79
  123.0 6.9 %collective-permute-start.15 = (f32[2,16,16]{2,1,0:T(8,128)S(1)}, f32[2,16,16]{2,1,0:T(8,128)S(1)}, u32[]{:S(2)}, u32[]{:S(2)}) collective-permute-start(f32[2,16,16]{2,1,0:T(8,128)S(1)} %add_add_fusion.2), channel_id=1, source_target_pairs={{0,4},{2,6},{4,0},{6,2},{8,12},{10,14},{12,8},{14,10},{16,20},{18,... | collective-permute-start | bytes 6152 | tf_op jit(solution)/shard_map/ppermute | solution.py:37
  128.1 4.9 %collective-permute-start.16 = (f32[2,16,16]{2,1,0:T(8,128)S(1)}, f32[2,16,16]{2,1,0:T(8,128)S(1)}, u32[]{:S(2)}, u32[]{:S(2)}) collective-permute-start(f32[2,16,16]{2,1,0:T(8,128)S(1)} %add_add_fusion.2), channel_id=1, source_target_pairs={{0,6},{2,4},{4,2},{6,0},{8,14},{10,12},{12,10},{14,8},{16,22},{18,... | collective-permute-start | bytes 6152 | tf_op jit(solution)/shard_map/ppermute | solution.py:37
  129.2 3.9 %collective-permute-start.14 = (f32[2,16,16]{2,1,0:T(8,128)S(1)}, f32[2,16,16]{2,1,0:T(8,128)S(1)}, u32[]{:S(2)}, u32[]{:S(2)}) collective-permute-start(f32[2,16,16]{2,1,0:T(8,128)S(1)} %add_add_fusion.2), channel_id=1, source_target_pairs={{0,2},{2,0},{4,6},{6,4},{8,10},{10,8},{12,14},{14,12},{16,18},{18,... | collective-permute-start | bytes 6152 | tf_op jit(solution)/shard_map/ppermute | solution.py:37
  133.1 8.3 %collective-permute-start.18 = (f32[2,16,16]{2,1,0:T(8,128)S(1)}, f32[2,16,16]{2,1,0:T(8,128)S(1)}, u32[]{:S(2)}, u32[]{:S(2)}) collective-permute-start(f32[2,16,16]{2,1,0:T(8,128)S(1)} %add_add_fusion.1), channel_id=1, source_target_pairs={{0,16},{2,18},{4,20},{6,22},{8,24},{10,26},{12,28},{14,30},{16,0},... | collective-permute-start | bytes 6152 | tf_op jit(solution)/shard_map/ppermute | solution.py:37
  137.0 4.9 %collective-permute-start.19 = (f32[2,16,16]{2,1,0:T(8,128)S(1)}, f32[2,16,16]{2,1,0:T(8,128)S(1)}, u32[]{:S(2)}, u32[]{:S(2)}) collective-permute-start(f32[2,16,16]{2,1,0:T(8,128)S(1)} %add_add_fusion.1), channel_id=1, source_target_pairs={{0,24},{2,26},{4,28},{6,30},{8,16},{10,18},{12,20},{14,22},{16,8},... | collective-permute-start | bytes 6152 | tf_op jit(solution)/shard_map/ppermute | solution.py:37
  137.8 4.2 %collective-permute-start.17 = (f32[2,16,16]{2,1,0:T(8,128)S(1)}, f32[2,16,16]{2,1,0:T(8,128)S(1)}, u32[]{:S(2)}, u32[]{:S(2)}) collective-permute-start(f32[2,16,16]{2,1,0:T(8,128)S(1)} %add_add_fusion.1), channel_id=1, source_target_pairs={{0,8},{2,10},{4,12},{6,14},{8,0},{10,2},{12,4},{14,6},{16,24},{18,... | collective-permute-start | bytes 6152 | tf_op jit(solution)/shard_map/ppermute | solution.py:37
  137.8 27.3 %all-to-all-start.1 = ((f32[4,2,64,1024]{3,1,2,0:T(2,128)}), f32[4,2,64,1024]{3,1,2,0:T(2,128)S(1)}, u32[]{:S(2)}, u32[]{:S(2)}) async-start(f32[4,2,64,1024]{3,1,2,0:T(2,128)} %pad_maximum_fusion), calls=%async_computation.1 | async-start | bytes 4194304 | tf_op jit(solution)/shard_map/all_to_all | solution.py:163
  (2 other events, 2.0 us)

commit v4 on v3

--- a/solution.py
+++ b/solution.py
@@ -56,20 +56,6 @@
     count = lax.axis_size(axis)
     pieces = [value] + [
         lax.ppermute(value, axis, [(i, (i + d) % count) for i in range(count)])
-        for d in range(1, count)
-    ]
-    return by_source(pieces, axis)
-
-
-def exchange_axis(values, axis):
-    count = lax.axis_size(axis)
-    own = lax.axis_index(axis)
-    pieces = [jnp.take(values, own, axis=0)] + [
-        lax.ppermute(
-            jnp.take(values, (own + d) % count, axis=0),
-            axis,
-            [(i, (i + d) % count) for i in range(count)],
-        )
         for d in range(1, count)
     ]
     return by_source(pieces, axis)
@@ -124,7 +110,21 @@
 
     fields = jnp.stack([diffusivity, velocity_x, velocity_y, source_shape])
     wide_fields = with_halo(fields, "space", depth)
-    every_cell = gather_axis(obs_cell[0], "tm")
+    obs_pack = jnp.concatenate(
+        [
+            obs_cell[0].astype(jnp.float32)[:, None],
+            obs_data[0][:, None],
+            obs_var[0][:, None],
+            obs_noise[0],
+        ],
+        axis=1,
+    )
+    every_obs = gather_axis(obs_pack, "tm")
+    every_cell = every_obs[:, :, 0].astype(jnp.int32)
+    every_obs = every_obs[:, :, 1:]
+    every_data = every_obs[:, :, 0]
+    every_var = every_obs[:, :, 1]
+    every_noise = every_obs[:, :, 2:]
     every_param = both_halves(params, "ens")
 
     mine = lax.all_to_all(
@@ -171,18 +171,19 @@
     picked_rows = jnp.take_along_axis(done, rows[:, None, :, None], axis=2)
     at_col = lax.broadcasted_iota(jnp.int32, picked_rows.shape, 3) == cols[:, None, :, None]
     local_pred = jnp.sum(jnp.where(at_col, picked_rows, 0.0), axis=3)
-    predicted = exchange_axis(local_pred, "tm").reshape(members_here, -1)
-    every_pred = both_halves(predicted, "ens")
+    pred = gather_axis(local_pred, "tm")
+    pred = jnp.transpose(pred, (0, 2, 1, 3)).reshape(members_here, -1)
+    every_pred = both_halves(pred, "ens")
     total = every_pred.shape[0]
     norm_factor = 1.0 / math.sqrt(total - 1)
-    inv_spread = lax.rsqrt(obs_var[0])[None, :]
+    inv_spread = lax.rsqrt(every_var).reshape(1, -1)
     pred_mean = jnp.mean(every_pred, axis=0, keepdims=True)
     anomaly = (every_pred - pred_mean) * (inv_spread * norm_factor)
-    misfit = (obs_data[0][None, :] + obs_noise[0].T - every_pred) * inv_spread
+    noise = jnp.transpose(every_noise, (2, 0, 1)).reshape(total, -1)
+    misfit = (every_data.reshape(1, -1) + noise - every_pred) * inv_spread
     gram = jnp.dot(anomaly, anomaly.T, precision=lax.Precision.HIGHEST)
     cross = jnp.dot(anomaly, misfit.T, precision=lax.Precision.HIGHEST)
     sums = jnp.stack([gram, cross])
-    sums = quad_sum(sums, "tm")
     sums = quad_sum(sums, "space")
     gram, cross = sums[0], sums[1]
     system = jnp.eye(total, dtype=jnp.float32) + gram

time: 168 us -> 163 us (0.970)
  waiting for transfers between devices: 46 us -> 40.8 us
    all_to_all x1, waiting for transfers between devices: 10 us -> 3.63 us  [per_device(): lax.all_to_all(state.reshape(slices, group, row_count, col_count), 'tm',...]
    ppermute x3 -> x6, waiting for transfers between devices: 0.01 us -> 4.71 us  [gather_axis(): lax.ppermute(value, axis, [(i, (i + d) % count) for i in range(count)])]
    ppermute x3 -> x0, waiting for transfers between devices: 4.53 us -> none  [exchange_axis(): lax.ppermute(jnp.take(values, (own + d) % count, axis=0), axis, [(i, (i +...]
    ppermute x9 -> x6, waiting for transfers between devices: 6.27 us -> 3.56 us  [quad_sum(): lax.ppermute(value, axis, [(i, i ^ k * bit) for i in range(count)])]
    ppermute x3 -> x0, starting transfers between devices: 2.69 us -> none  [exchange_axis(): lax.ppermute(jnp.take(values, (own + d) % count, axis=0), axis, [(i, (i +...]
    ppermute x3 -> x6, starting transfers between devices: 4.6 us -> 7.25 us  [gather_axis(): lax.ppermute(value, axis, [(i, (i + d) % count) for i in range(count)])]
    ppermute x2, waiting for transfers between devices: 0.77 us -> 3.29 us  [with_halo(): lax.ppermute(tail, axis, [(i, i + 1) for i in range(ends)])]
    ppermute x9 -> x6, starting transfers between devices: 15.1 us -> 13.7 us  [quad_sum(): lax.ppermute(value, axis, [(i, i ^ k * bit) for i in range(count)])]
  transfers between devices with their start and end apart: 23 -> 20, of which waited for: 13 -> 12; matrix products, arithmetic and copies ran while one was open for 16% -> 46% of each run, Pallas kernels for 0% -> 0%
where the time goes in v4:
time: 163 us; the launch traced here: 162 us
  local copies, waits for them, and re-layouts  45.2 us (28%)
  starting transfers between devices  40.9 us (25%)
  waiting for transfers between devices  40.8 us (25%)
  other arithmetic  32.8 us (20%)
    all_to_all x1, waiting for transfers between devices, per_device(): lax.all_to_all(done, 'tm', 0, 0, tiled=True)  19.1 us
    ppermute x6, starting transfers between devices, quad_sum(): lax.ppermute(value, axis, [(i, i ^ k * bit) for i in range(count)])  13.7 us
    mul x5, other arithmetic, advance(): return (middle + step_size * tendency) * inside  12.4 us
    ppermute x2, starting transfers between devices, with_halo(): lax.ppermute(tail, axis, [(i, i + 1) for i in range(ends)])  8.83 us
    mul x6, local copies, waits for them, and re-layouts, advance(): coeffs[0] * (above_row + below_row + west_cell + east_cell - 4.0 * middle)  7.44 us
    ppermute x6, starting transfers between devices, gather_axis(): lax.ppermute(value, axis, [(i, (i + d) % count) for i in range(count)])  7.25 us
    slice x7, local copies, waits for them, and re-layouts, advance(): west_cell = jnp.pad(middle[:, :, :-1], ((0, 0), (0, 0), (1, 0)))  5.72 us
    another operation x2, local copies, waits for them, and re-layouts, per_device(): jnp.tile(wide_fields[3][None] * spread_params[:, None, :], (slices, 1, 1))  5.59 us
  transfers between devices with their start and end apart: 20, of which 12 were waited for; matrix products, arithmetic and copies ran while one was open for 46% of the time, Pallas kernels for 0%

profile of v4, /device:TPU:0, one launch (start us, length us, event | category | flops | bytes accessed | tf_op | source)
XLA Modules:
  0.0 162.3 jit_solution(17661734413465608975)
XLA Ops:
  2.0 2.9 %collective-permute-start.6 = (f32[64,19]{0,1:T(8,128)S(1)}, f32[64,19]{0,1:T(8,128)S(1)}, u32[]{:S(2)}, u32[]{:S(2)}) collective-permute-start(f32[64,19]{0,1:T(8,128)S(1)} %get-tuple-element.54), channel_id=1, source_target_pairs={{0,96},{32,0},{64,32},{96,64},{1,97},{33,1},{65,33},{97,65},{2,98}... | collective-permute-start | bytes 14600 | tf_op jit(solution)/shard_map/ppermute | solution.py:58
  7.5 1.3 collective-permute-start.3
  8.8 4.5 %copy.28 = f32[4,2,64,1024]{3,1,2,0:T(2,128)} copy(f32[4,2,64,1024]{3,2,1,0:T(8,128)} %bitcast.115) | data formatting | bytes 4194304 | tf_op jit(solution)/shard_map/reshape;squeeze | solution.py:131
  13.4 4.6 %all-to-all-start = ((f32[4,2,64,1024]{3,1,2,0:T(2,128)}), f32[4,2,64,1024]{3,1,2,0:T(2,128)}, u32[]{:S(2)}, u32[]{:S(2)}) async-start(f32[4,2,64,1024]{3,1,2,0:T(2,128)} %copy.28), calls=%async_computation | async-start | bytes 4194304 | tf_op jit(solution)/shard_map/all_to_all | solution.py:130
  18.9 4.6 %collective-permute-start.2 = (f32[4,7,1024]{2,1,0:T(8,128)S(1)}, f32[4,7,1024]{2,1,0:T(8,128)S(1)}, u32[]{:S(2)}, u32[]{:S(2)}) collective-permute-start(f32[4,7,1024]{2,1,0:T(8,128)S(1)} %get-tuple-element.45), channel_id=1, source_target_pairs={{0,2},{2,4},{4,6},{6,8},{8,10},{10,12},{12,14},{14,16},{16,18},{18... | collective-permute-start | bytes 344072 | tf_op jit(solution)/shard_map/ppermute | solution.py:21
  24.3 2.5 %collective-permute-done.2 = f32[4,7,1024]{2,1,0:T(8,128)S(1)} collective-permute-done((f32[4,7,1024]{2,1,0:T(8,128)S(1)}, f32[4,7,1024]{2,1,0:T(8,128)S(1)}, u32[]{:S(2)}, u32[]{:S(2)}) %collective-permute-start.2) | collective-permute-done | bytes 114720 | tf_op jit(solution)/shard_map/ppermute | solution.py:21
  27.1 1.1 copy-done
  28.4 2.3 %tile.4 = f32[4,2,78,1024]{3,1,0,2:T(2,128)} broadcast(f32[2,78,1024]{2,0,1:T(2,128)S(1)} %broadcast_multiply_fusion), dimensions={1,2,3} | broadcast | bytes 3194880 | tf_op jit(solution)/shard_map/tile | solution.py:138
  30.7 3.3 %tile.10 = f32[8,78,1024]{2,0,1:T(8,128)S(1)} reshape(f32[4,2,78,1024]{3,1,0,2:T(2,128)} %tile.4) | data formatting | bytes 5111808 | tf_op jit(solution)/shard_map/tile | solution.py:138
  34.0 2.2 %slice_bitcast_fusion.21 = (f32[72,1024]{1,0:T(8,128)}, f32[72,1024]{1,0:T(8,128)}, f32[72,1024]{1,0:T(8,128)}) fusion(f32[4,78,1024]{2,1,0:T(8,128)} %copy-done), kind=kLoop, calls=%fused_computation.58 | loop fusion | bytes 1769472 | tf_op jit(solution)/shard_map/mul | solution.py:76
  37.2 1.0 slice_bitcast_fusion.15
  38.2 1.0 slice_bitcast_fusion.9
  39.1 1.1 slice_bitcast_fusion.5
  40.2 3.6 %all-to-all-done = f32[4,2,64,1024]{3,1,2,0:T(2,128)} async-done(((f32[4,2,64,1024]{3,1,2,0:T(2,128)}), f32[4,2,64,1024]{3,1,2,0:T(2,128)}, u32[]{:S(2)}, u32[]{:S(2)}) %all-to-all-start) | async-done | bytes 2097184 | tf_op jit(solution)/shard_map/all_to_all | solution.py:130
  43.8 4.2 %copy.29 = f32[4,2,64,1024]{3,1,0,2:T(2,128)} copy(f32[4,2,64,1024]{3,1,2,0:T(2,128)} %all-to-all-done) | data formatting | bytes 4194304 | tf_op jit(solution)/shard_map/all_to_all | solution.py:130
  48.0 3.6 %reshape.192 = f32[8,64,1024]{2,0,1:T(8,128)} reshape(f32[4,2,64,1024]{3,1,0,2:T(2,128)} %copy.29) | data formatting | bytes 4194304 | tf_op jit(solution)/shard_map/reshape | solution.py:132
  51.7 1.2 fusion.59
  52.9 4.3 %collective-permute-start = (f32[8,7,1024]{2,0,1:T(8,128)S(1)}, f32[8,7,1024]{2,0,1:T(8,128)S(1)}, u32[]{:S(2)}, u32[]{:S(2)}) collective-permute-start(f32[8,7,1024]{2,0,1:T(8,128)S(1)} %get-tuple-element.26), channel_id=1, source_target_pairs={{0,2},{2,4},{4,6},{6,8},{8,10},{10,12},{12,14},{14,16},{16,18},{18... | collective-permute-start | bytes 688136 | tf_op jit(solution)/shard_map/ppermute | solution.py:21
  57.2 1.3 slice_bitcast_fusion.12
  58.5 1.5 collective-permute-start.1
  60.9 5.5 %collective-permute-done.1 = f32[8,7,1024]{2,0,1:T(8,128)S(1)} collective-permute-done((f32[8,7,1024]{2,0,1:T(8,128)S(1)}, f32[8,7,1024]{2,0,1:T(8,128)S(1)}, u32[]{:S(2)}, u32[]{:S(2)}) %collective-permute-start.1) | collective-permute-done | bytes 229408 | tf_op jit(solution)/shard_map/ppermute | solution.py:23
  66.4 1.0 fusion.52
  67.6 3.1 %fusion.2 = (f32[8,76,1024]{2,0,1:T(8,128)S(1)}, f32[8,76,1024]{2,0,1:T(8,128)S(1)}) fusion(f32[8,78,1024]{2,0,1:T(8,128)S(1)} %tile.10, f32[8,78,1024]{2,0,1:T(8,128)S(1)} %constant_dynamic-update-slice_fusion, f32[76]{0:T(128)S(1)} %slice.384, f32[76,1024]{1,0:T(8,128)S(1)} %copy-done.7, f32[76,1024]{1,0:T(8,128)S(1)} %copy-done.8, ...), kind=kLoop, calls=%fused_computation.7 | loop fusion | flops 11206656 | bytes 20852272 | tf_op jit(solution)/shard_map/mul | solution.py:84
  71.1 1.0 fusion.54
  72.2 3.0 %fusion.5 = f32[8,74,1024]{2,0,1:T(8,128)S(1)} fusion(f32[8,78,1024]{2,0,1:T(8,128)S(1)} %tile.10, f32[8,76,1024]{2,0,1:T(8,128)S(1)} %get-tuple-element.7, f32[8,74,1023]{2,0,1:T(8,128)S(1)} %get-tuple-element.15, f32[8,74,1023]{2,0,1:T(8,128)S(1)} %get-tuple-element.14, f32[74]{0:T(128)S(1)} %slice.394, f32[74,1024]{1,0:T(8,128)S(1)} %copy-done.10, ...), kind=kLoop, calls=%fused_computation.13 | loop fusion | flops 10911744 | bytes 17878696 | tf_op jit(solution)/shard_map/mul | solution.py:84
  76.4 3.0 %fusion.8 = f32[8,72,1024]{2,0,1:T(8,128)S(1)} fusion(f32[8,78,1024]{2,0,1:T(8,128)S(1)} %tile.10, f32[8,74,1024]{2,0,1:T(8,128)S(1)} %fusion.5, f32[8,72,1023]{2,0,1:T(8,128)S(1)} %get-tuple-element.17, f32[8,72,1023]{2,0,1:T(8,128)S(1)} %get-tuple-element.16, f32[72]{0:T(128)S(1)} %slice.404, f32[72,1024]{1,0:T(8,128)S(1)} %copy-done.19, ...), kind=kLoop, calls=%fused_computation.17 | loop fusion | flops 10616832 | bytes 17395488 | tf_op jit(solution)/shard_map/mul | solution.py:84
  80.6 2.9 %fusion.11 = f32[8,70,1024]{2,0,1:T(8,128)S(1)} fusion(f32[8,78,1024]{2,0,1:T(8,128)S(1)} %tile.10, f32[8,72,1024]{2,0,1:T(8,128)S(1)} %fusion.8, f32[8,70,1023]{2,0,1:T(8,128)S(1)} %get-tuple-element.19, f32[8,70,1023]{2,0,1:T(8,128)S(1)} %get-tuple-element.18, f32[70]{0:T(128)S(1)} %slice.414, f32[70,1024]{1,0:T(8,128)S(1)} %copy-done.16, ...), kind=kLoop, calls=%fused_computation.21 | loop fusion | flops 10321920 | bytes 16912280 | tf_op jit(solution)/shard_map/mul | solution.py:84
  84.3 1.3 fusion.53
  85.6 2.9 %fusion.14 = f32[2,68,1024]{2,0,1:T(2,128)S(1)} fusion(f32[2,70,1024]{2,0,1:T(2,128)S(1)} %get-tuple-element.11, f32[2,70,1024]{2,0,1:T(2,128)S(1)} %get-tuple-element.57, f32[8,70,1024]{2,0,1:T(8,128)S(1)} %fusion.11, f32[2,68,1023]{2,0,1:T(2,128)S(1)} %get-tuple-element.21, f32[2,68,1023]{2,0,1:T(2,128)S(1)} %get-tuple-element.20, f32[68]{0:T(128)S(1)} %slice.427, ...), kind=kLoop, calls=%fused_computation.30 | loop fusion | flops 2506752 | bytes 5291216 | tf_op jit(solution)/shard_map/add | solution.py:160
  89.3 2.3 %fusion.15 = f32[2,66,1024]{2,0,1:T(2,128)S(1)} fusion(f32[2,70,1024]{2,0,1:T(2,128)S(1)} %get-tuple-element.13, f32[2,70,1024]{2,0,1:T(2,128)S(1)} %get-tuple-element.55, f32[2,68,1024]{2,0,1:T(2,128)S(1)} %fusion.14, f32[2,66,1023]{2,0,1:T(2,128)S(1)} %get-tuple-element.48, f32[2,66,1023]{2,0,1:T(2,128)S(1)} %get-tuple-element.47, f32[66]{0:T(128)S(1)} %slice.440, ...), kind=kLoop, calls=%fused_computation.32 | loop fusion | flops 2433024 | bytes 5135592 | tf_op jit(solution)/shard_map/add | solution.py:160
  92.3 2.0 %slice_bitcast_fusion.2 = (f32[1,2,64,1024]{3,1,2,0:T(2,128)S(1)}, f32[1,2,64,1024]{3,1,2,0:T(2,128)S(1)}) fusion(f32[2,66,1024]{2,0,1:T(2,128)S(1)} %fusion.15, f32[64]{0:T(128)S(1)} %slice.449, f32[64,1024]{1,0:T(8,128)S(1)} %copy-done.3, f32[64,1024]{1,0:T(8,128)S(1)} %copy-done.4, f32[2,64,1023]{2,0,1:T(2,128)S(1)} %get-tuple-element.52, ...), kind=kLoop, calls=%fused_computation.38 | loop fusion | flops 2359296 | bytes 5504256 | tf_op jit(solution)/shard_map/stack | solution.py:162
  94.3 2.0 %pad_maximum_fusion = f32[4,2,64,1024]{3,1,2,0:T(2,128)} fusion(f32[1,2,64,1024]{3,1,2,0:T(2,128)S(1)} %get-tuple-element.50, f32[1,2,64,1024]{3,1,2,0:T(2,128)S(1)} %get-tuple-element.49, f32[1,2,64,1024]{3,1,2,0:T(2,128)S(1)} %slice_bitcast_fusion, f32[1,2,64,1024]{3,1,2,0:T(2,128)S(1)} %slice_bitcast_fusion.1), kind=kLoop, calls=%fused_computation.23 | loop fusion | flops 1572864 | bytes 4194304 | tf_op jit(solution)/shard_map/stack | solution.py:162
  96.2 4.8 %gather_fusion.2 = f32[256,2,1024]{2,1,0:T(2,128)S(1)} fusion(f32[4,2,64,1024]{3,1,2,0:T(2,128)} %pad_maximum_fusion, s32[256]{0:T(256)S(1)} %reshape.211), kind=kCustom, calls=%fused_computation.2 | custom fusion | bytes 4196352 | tf_op jit(solution)/shard_map/jit(take_along_axis)/gather | solution.py:171
  101.0 4.2 %fusion.12 = f32[4,2,64]{1,2,0:T(8,128)S(1)} fusion(f32[4,64,2,1024]{3,2,1,0:T(2,128)S(1)} %bitcast.108, pred[4,64]{1,0:T(4,128)(4,1)S(1)} %bitcast.128, s32[4,64]{1,0:T(4,128)S(1)} %add_select_fusion), kind=kLoop, calls=%fused_computation.22 | loop fusion | flops 2096640 | bytes 2100480 | tf_op jit(solution)/shard_map/reduce_sum | solution.py:173
  105.3 1.3 collective-permute-start.9
  106.5 1.4 collective-permute-start.8
  108.9 2.7 %collective-permute-done.8 = f32[4,2,64]{2,0,1:T(4,128)S(1)} collective-permute-done((f32[4,2,64]{2,0,1:T(4,128)S(1)}, f32[4,2,64]{2,0,1:T(4,128)S(1)}, u32[]{:S(2)}, u32[]{:S(2)}) %collective-permute-start.8) | collective-permute-done | bytes 2080 | tf_op jit(solution)/shard_map/ppermute | solution.py:58
  111.6 1.1 collective-permute-done.7
  115.0 5.8 %collective-permute-start.12 = (f32[2,16,16]{2,1,0:T(8,128)S(1)}, f32[2,16,16]{2,1,0:T(8,128)S(1)}, u32[]{:S(2)}, u32[]{:S(2)}) collective-permute-start(f32[2,16,16]{2,1,0:T(8,128)S(1)} %pad_maximum_fusion.8), channel_id=1, source_target_pairs={{0,4},{2,6},{4,0},{6,2},{8,12},{10,14},{12,8},{14,10},{16,20},{18,... | collective-permute-start | bytes 6152 | tf_op jit(solution)/shard_map/ppermute | solution.py:37
  120.8 2.5 %collective-permute-start.13 = (f32[2,16,16]{2,1,0:T(8,128)S(1)}, f32[2,16,16]{2,1,0:T(8,128)S(1)}, u32[]{:S(2)}, u32[]{:S(2)}) collective-permute-start(f32[2,16,16]{2,1,0:T(8,128)S(1)} %pad_maximum_fusion.8), channel_id=1, source_target_pairs={{0,6},{2,4},{4,2},{6,0},{8,14},{10,12},{12,10},{14,8},{16,22},{18,... | collective-permute-start | bytes 6152 | tf_op jit(solution)/shard_map/ppermute | solution.py:37
  124.1 1.7 %collective-permute-done.13 = f32[2,16,16]{2,1,0:T(8,128)S(1)} collective-permute-done((f32[2,16,16]{2,1,0:T(8,128)S(1)}, f32[2,16,16]{2,1,0:T(8,128)S(1)}, u32[]{:S(2)}, u32[]{:S(2)}) %collective-permute-start.13) | collective-permute-done | bytes 2080 | tf_op jit(solution)/shard_map/ppermute | solution.py:37
  125.7 1.3 collective-permute-done.11
  127.0 4.0 %collective-permute-start.15 = (f32[2,16,16]{2,1,0:T(8,128)S(1)}, f32[2,16,16]{2,1,0:T(8,128)S(1)}, u32[]{:S(2)}, u32[]{:S(2)}) collective-permute-start(f32[2,16,16]{2,1,0:T(8,128)S(1)} %add_add_fusion.1), channel_id=1, source_target_pairs={{0,16},{2,18},{4,20},{6,22},{8,24},{10,26},{12,28},{14,30},{16,0},... | collective-permute-start | bytes 6152 | tf_op jit(solution)/shard_map/ppermute | solution.py:37
  131.7 3.6 %all-to-all-start.1 = ((f32[4,2,64,1024]{3,1,2,0:T(2,128)}), f32[4,2,64,1024]{3,1,2,0:T(2,128)S(1)}, u32[]{:S(2)}, u32[]{:S(2)}) async-start(f32[4,2,64,1024]{3,1,2,0:T(2,128)} %pad_maximum_fusion), calls=%async_computation.1 | async-start | bytes 4194304 | tf_op jit(solution)/shard_map/all_to_all | solution.py:163
  136.0 1.5 cholesky.17
  138.8 1.2 custom-call.10
  141.2 19.1 %all-to-all-done.1 = f32[4,2,64,1024]{3,1,2,0:T(2,128)S(1)} async-done(((f32[4,2,64,1024]{3,1,2,0:T(2,128)}), f32[4,2,64,1024]{3,1,2,0:T(2,128)S(1)}, u32[]{:S(2)}, u32[]{:S(2)}) %all-to-all-start.1) | async-done | bytes 2097184 | tf_op jit(solution)/shard_map/all_to_all | solution.py:163
  160.3 2.0 %copy.30 = f32[4,2,64,1024]{3,2,1,0:T(8,128)} copy(f32[4,2,64,1024]{3,1,2,0:T(2,128)S(1)} %all-to-all-done.1) | data formatting | bytes 4194304 | tf_op jit(solution)/shard_map/all_to_all | solution.py:163
  (135 shorter events, 20.9 us)
Async XLA Ops:
  2.0 16.9 %collective-permute-start.6 = (f32[64,19]{0,1:T(8,128)S(1)}, f32[64,19]{0,1:T(8,128)S(1)}, u32[]{:S(2)}, u32[]{:S(2)}) collective-permute-start(f32[64,19]{0,1:T(8,128)S(1)} %get-tuple-element.54), channel_id=1, source_target_pairs={{0,96},{32,0},{64,32},{96,64},{1,97},{33,1},{65,33},{97,65},{2,98}... | collective-permute-start | bytes 14600 | tf_op jit(solution)/shard_map/ppermute | solution.py:58
  4.9 18.6 %collective-permute-start.5 = (f32[64,19]{0,1:T(8,128)S(1)}, f32[64,19]{0,1:T(8,128)S(1)}, u32[]{:S(2)}, u32[]{:S(2)}) collective-permute-start(f32[64,19]{0,1:T(8,128)S(1)} %get-tuple-element.54), channel_id=1, source_target_pairs={{0,64},{32,96},{64,0},{96,32},{1,65},{33,97},{65,1},{97,33},{2,66}... | collective-permute-start | bytes 14600 | tf_op jit(solution)/shard_map/ppermute | solution.py:58
  5.7 17.8 %collective-permute-start.4 = (f32[64,19]{0,1:T(8,128)S(1)}, f32[64,19]{0,1:T(8,128)S(1)}, u32[]{:S(2)}, u32[]{:S(2)}) collective-permute-start(f32[64,19]{0,1:T(8,128)S(1)} %get-tuple-element.54), channel_id=1, source_target_pairs={{0,32},{32,64},{64,96},{96,0},{1,33},{33,65},{65,97},{97,1},{2,34}... | collective-permute-start | bytes 14600 | tf_op jit(solution)/shard_map/ppermute | solution.py:58
  7.5 16.8 %collective-permute-start.3 = (f32[4,7,1024]{2,1,0:T(8,128)S(1)}, f32[4,7,1024]{2,1,0:T(8,128)S(1)}, u32[]{:S(2)}, u32[]{:S(2)}) collective-permute-start(f32[4,7,1024]{2,1,0:T(8,128)S(1)} %get-tuple-element.46), channel_id=1, source_target_pairs={{2,0},{4,2},{6,4},{8,6},{10,8},{12,10},{14,12},{16,14},{18,16},{20... | collective-permute-start | bytes 344072 | tf_op jit(solution)/shard_map/ppermute | solution.py:23
  13.3 4.6 %copy-start.22 = (f32[8,128]{1,0:T(8,128)S(1)}, f32[8,128]{1,0:T(8,128)}, u32[]{:S(2)}) copy-start(f32[8,128]{1,0:T(8,128)} %param.15) | copy-start | bytes 12292
  13.3 13.5 %copy-start.3 = (f32[64,1024]{1,0:T(8,128)S(1)}, f32[64,1024]{1,0:T(8,128)}, u32[]{:S(2)}) copy-start(f32[64,1024]{1,0:T(8,128)} %param.12) | copy-start | bytes 786436
  13.3 13.5 %copy-start.4 = (f32[64,1024]{1,0:T(8,128)S(1)}, f32[64,1024]{1,0:T(8,128)}, u32[]{:S(2)}) copy-start(f32[64,1024]{1,0:T(8,128)} %param.11) | copy-start | bytes 786436
  13.3 13.5 %copy-start.5 = (f32[64,1024]{1,0:T(8,128)S(1)}, f32[64,1024]{1,0:T(8,128)}, u32[]{:S(2)}) copy-start(f32[64,1024]{1,0:T(8,128)} %param.13) | copy-start | bytes 786436
  13.3 13.5 %copy-start.21 = (f32[64,1024]{1,0:T(8,128)S(1)}, f32[64,1024]{1,0:T(8,128)}, u32[]{:S(2)}) copy-start(f32[64,1024]{1,0:T(8,128)} %param.14) | copy-start | bytes 786436
  13.4 30.4 %all-to-all-start = ((f32[4,2,64,1024]{3,1,2,0:T(2,128)}), f32[4,2,64,1024]{3,1,2,0:T(2,128)}, u32[]{:S(2)}, u32[]{:S(2)}) async-start(f32[4,2,64,1024]{3,1,2,0:T(2,128)} %copy.28), calls=%async_computation | async-start | bytes 4194304 | tf_op jit(solution)/shard_map/all_to_all | solution.py:130
  18.0 106.0 %collective-permute-start.17 = (f32[8,128]{1,0:T(8,128)S(1)}, f32[8,128]{1,0:T(8,128)S(1)}, u32[]{:S(2)}, u32[]{:S(2)}) collective-permute-start(f32[8,128]{1,0:T(8,128)S(1)} %copy-done.22), channel_id=1, source_target_pairs={{0,1},{1,0},{2,3},{3,2},{4,5},{5,4},{6,7},{7,6},{8,9},{9,8},{10,11... | collective-permute-start | bytes 12296 | tf_op jit(solution)/shard_map/ppermute | solution.py:65
  18.9 7.9 %collective-permute-start.2 = (f32[4,7,1024]{2,1,0:T(8,128)S(1)}, f32[4,7,1024]{2,1,0:T(8,128)S(1)}, u32[]{:S(2)}, u32[]{:S(2)}) collective-permute-start(f32[4,7,1024]{2,1,0:T(8,128)S(1)} %get-tuple-element.45), channel_id=1, source_target_pairs={{0,2},{2,4},{4,6},{6,8},{8,10},{10,12},{12,14},{14,16},{16,18},{18... | collective-permute-start | bytes 344072 | tf_op jit(solution)/shard_map/ppermute | solution.py:21
  27.1 1.1 copy-start
  34.0 2.2 %copy-start.1 = (f32[4,78,1024]{2,1,0:T(8,128)S(1)}, f32[4,78,1024]{2,1,0:T(8,128)}, u32[]{:S(2)}) copy-start(f32[4,78,1024]{2,1,0:T(8,128)} %copy-done) | copy-start | bytes 3833860
  51.7 9.1 %copy-start.2 = (f32[8,64,1024]{2,0,1:T(8,128)S(1)}, f32[8,64,1024]{2,0,1:T(8,128)}, u32[]{:S(2)}) copy-start(f32[8,64,1024]{2,0,1:T(8,128)} %reshape.192) | copy-start | bytes 6291460
  52.9 7.8 %collective-permute-start = (f32[8,7,1024]{2,0,1:T(8,128)S(1)}, f32[8,7,1024]{2,0,1:T(8,128)S(1)}, u32[]{:S(2)}, u32[]{:S(2)}) collective-permute-start(f32[8,7,1024]{2,0,1:T(8,128)S(1)} %get-tuple-element.26), channel_id=1, source_target_pairs={{0,2},{2,4},{4,6},{6,8},{8,10},{10,12},{12,14},{14,16},{16,18},{18... | collective-permute-start | bytes 688136 | tf_op jit(solution)/shard_map/ppermute | solution.py:21
  58.5 7.9 %collective-permute-start.1 = (f32[8,7,1024]{2,0,1:T(8,128)S(1)}, f32[8,7,1024]{2,0,1:T(8,128)S(1)}, u32[]{:S(2)}, u32[]{:S(2)}) collective-permute-start(f32[8,7,1024]{2,0,1:T(8,128)S(1)} %get-tuple-element.25), channel_id=1, source_target_pairs={{2,0},{4,2},{6,4},{8,6},{10,8},{12,10},{14,12},{16,14},{18,16},{20... | collective-permute-start | bytes 688136 | tf_op jit(solution)/shard_map/ppermute | solution.py:23
  66.4 1.0 copy-start.6
  66.4 1.1 copy-start.7
  66.4 1.2 copy-start.8
  71.0 1.0 copy-start.9
  71.0 1.1 copy-start.10
  71.1 1.2 copy-start.11
  75.2 1.0 copy-start.18
  75.2 1.0 copy-start.19
  75.2 1.1 copy-start.20
  79.4 1.0 copy-start.15
  79.4 1.0 copy-start.16
  79.4 1.1 copy-start.17
  84.2 1.4 copy-start.12
  84.2 1.4 copy-start.13
  84.2 1.4 copy-start.14
  105.3 3.6 %collective-permute-start.9 = (f32[4,2,64]{2,0,1:T(4,128)S(1)}, f32[4,2,64]{2,0,1:T(4,128)S(1)}, u32[]{:S(2)}, u32[]{:S(2)}) collective-permute-start(f32[4,2,64]{2,0,1:T(4,128)S(1)} %copy.31), channel_id=1, source_target_pairs={{0,96},{32,0},{64,32},{96,64},{1,97},{33,1},{65,33},{97,65},{2,98}... | collective-permute-start | bytes 6152 | tf_op jit(solution)/shard_map/ppermute | solution.py:58
  106.5 5.1 %collective-permute-start.8 = (f32[4,2,64]{2,0,1:T(4,128)S(1)}, f32[4,2,64]{2,0,1:T(4,128)S(1)}, u32[]{:S(2)}, u32[]{:S(2)}) collective-permute-start(f32[4,2,64]{2,0,1:T(4,128)S(1)} %copy.31), channel_id=1, source_target_pairs={{0,64},{32,96},{64,0},{96,32},{1,65},{33,97},{65,1},{97,33},{2,66}... | collective-permute-start | bytes 6152 | tf_op jit(solution)/shard_map/ppermute | solution.py:58
  107.9 4.8 %collective-permute-start.7 = (f32[4,2,64]{2,0,1:T(4,128)S(1)}, f32[4,2,64]{2,0,1:T(4,128)S(1)}, u32[]{:S(2)}, u32[]{:S(2)}) collective-permute-start(f32[4,2,64]{2,0,1:T(4,128)S(1)} %copy.31), channel_id=1, source_target_pairs={{0,32},{32,64},{64,96},{96,0},{1,33},{33,65},{65,97},{97,1},{2,34}... | collective-permute-start | bytes 6152 | tf_op jit(solution)/shard_map/ppermute | solution.py:58
  113.5 1.2 collective-permute-start.10
  115.0 9.1 %collective-permute-start.12 = (f32[2,16,16]{2,1,0:T(8,128)S(1)}, f32[2,16,16]{2,1,0:T(8,128)S(1)}, u32[]{:S(2)}, u32[]{:S(2)}) collective-permute-start(f32[2,16,16]{2,1,0:T(8,128)S(1)} %pad_maximum_fusion.8), channel_id=1, source_target_pairs={{0,4},{2,6},{4,0},{6,2},{8,12},{10,14},{12,8},{14,10},{16,20},{18,... | collective-permute-start | bytes 6152 | tf_op jit(solution)/shard_map/ppermute | solution.py:37
  120.8 4.9 %collective-permute-start.13 = (f32[2,16,16]{2,1,0:T(8,128)S(1)}, f32[2,16,16]{2,1,0:T(8,128)S(1)}, u32[]{:S(2)}, u32[]{:S(2)}) collective-permute-start(f32[2,16,16]{2,1,0:T(8,128)S(1)} %pad_maximum_fusion.8), channel_id=1, source_target_pairs={{0,6},{2,4},{4,2},{6,0},{8,14},{10,12},{12,10},{14,8},{16,22},{18,... | collective-permute-start | bytes 6152 | tf_op jit(solution)/shard_map/ppermute | solution.py:37
  123.3 3.7 %collective-permute-start.11 = (f32[2,16,16]{2,1,0:T(8,128)S(1)}, f32[2,16,16]{2,1,0:T(8,128)S(1)}, u32[]{:S(2)}, u32[]{:S(2)}) collective-permute-start(f32[2,16,16]{2,1,0:T(8,128)S(1)} %pad_maximum_fusion.8), channel_id=1, source_target_pairs={{0,2},{2,0},{4,6},{6,4},{8,10},{10,8},{12,14},{14,12},{16,18},{18,... | collective-permute-start | bytes 6152 | tf_op jit(solution)/shard_map/ppermute | solution.py:37
  127.0 8.3 %collective-permute-start.15 = (f32[2,16,16]{2,1,0:T(8,128)S(1)}, f32[2,16,16]{2,1,0:T(8,128)S(1)}, u32[]{:S(2)}, u32[]{:S(2)}) collective-permute-start(f32[2,16,16]{2,1,0:T(8,128)S(1)} %add_add_fusion.1), channel_id=1, source_target_pairs={{0,16},{2,18},{4,20},{6,22},{8,24},{10,26},{12,28},{14,30},{16,0},... | collective-permute-start | bytes 6152 | tf_op jit(solution)/shard_map/ppermute | solution.py:37
  131.0 4.9 %collective-permute-start.16 = (f32[2,16,16]{2,1,0:T(8,128)S(1)}, f32[2,16,16]{2,1,0:T(8,128)S(1)}, u32[]{:S(2)}, u32[]{:S(2)}) collective-permute-start(f32[2,16,16]{2,1,0:T(8,128)S(1)} %add_add_fusion.1), channel_id=1, source_target_pairs={{0,24},{2,26},{4,28},{6,30},{8,16},{10,18},{12,20},{14,22},{16,8},... | collective-permute-start | bytes 6152 | tf_op jit(solution)/shard_map/ppermute | solution.py:37
  131.7 4.2 %collective-permute-start.14 = (f32[2,16,16]{2,1,0:T(8,128)S(1)}, f32[2,16,16]{2,1,0:T(8,128)S(1)}, u32[]{:S(2)}, u32[]{:S(2)}) collective-permute-start(f32[2,16,16]{2,1,0:T(8,128)S(1)} %add_add_fusion.1), channel_id=1, source_target_pairs={{0,8},{2,10},{4,12},{6,14},{8,0},{10,2},{12,4},{14,6},{16,24},{18,... | collective-permute-start | bytes 6152 | tf_op jit(solution)/shard_map/ppermute | solution.py:37
  131.7 28.6 %all-to-all-start.1 = ((f32[4,2,64,1024]{3,1,2,0:T(2,128)}), f32[4,2,64,1024]{3,1,2,0:T(2,128)S(1)}, u32[]{:S(2)}, u32[]{:S(2)}) async-start(f32[4,2,64,1024]{3,1,2,0:T(2,128)} %pad_maximum_fusion), calls=%async_computation.1 | async-start | bytes 4194304 | tf_op jit(solution)/shard_map/all_to_all | solution.py:163

commit v5 on v4

--- a/solution.py
+++ b/solution.py
@@ -68,11 +68,12 @@
 
 
 def advance(values_in, coeffs, inside, step_size, forcing):
-    middle = values_in[:, 1:-1, :]
-    above_row = values_in[:, :-2, :]
-    below_row = values_in[:, 2:, :]
-    west_cell = jnp.pad(middle[:, :, :-1], ((0, 0), (0, 0), (1, 0)))
-    east_cell = jnp.pad(middle[:, :, 1:], ((0, 0), (0, 0), (0, 1)))
+    middle = values_in[..., 1:-1, :]
+    above_row = values_in[..., :-2, :]
+    below_row = values_in[..., 2:, :]
+    edge = [(0, 0)] * (values_in.ndim - 1)
+    west_cell = jnp.pad(middle[..., :-1], edge + [(1, 0)])
+    east_cell = jnp.pad(middle[..., 1:], edge + [(0, 1)])
     spread_term = coeffs[0] * (above_row + below_row + west_cell + east_cell - 4.0 * middle)
     tendency = (
         spread_term
@@ -108,8 +109,7 @@
     group = members_here // slices
     band_width = col_count // params.shape[1]
 
-    fields = jnp.stack([diffusivity, velocity_x, velocity_y, source_shape])
-    wide_fields = with_halo(fields, "space", depth)
+    every_param = both_halves(params, "ens")
     obs_pack = jnp.concatenate(
         [
             obs_cell[0].astype(jnp.float32)[:, None],
@@ -125,22 +125,25 @@
     every_data = every_obs[:, :, 0]
     every_var = every_obs[:, :, 1]
     every_noise = every_obs[:, :, 2:]
-    every_param = both_halves(params, "ens")
-
-    mine = lax.all_to_all(
-        state.reshape(slices, group, row_count, col_count), "tm", 0, 0, tiled=True
-    ).reshape(slices * group, row_count, col_count)
+
+    fields = jnp.stack([diffusivity, velocity_x, velocity_y, source_shape])
+    wide = with_halo(jnp.concatenate([state, fields]), "space", depth)
+    wide_coeffs = wide[members_here : members_here + 3]
+    wide_state = lax.all_to_all(
+        wide[:members_here].reshape(slices, group, row_count + 2 * depth, col_count),
+        "tm",
+        0,
+        0,
+        tiled=True,
+    )
     my_params = lax.dynamic_slice_in_dim(params, slice_index * group, group, 0)
     spread_params = jnp.repeat(my_params, band_width, axis=1)
-
-    wide_state = with_halo(mine, "space", depth)
-    wide_coeffs = wide_fields[:3]
-    wide_forcing = jnp.tile(wide_fields[3][None] * spread_params[:, None, :], (slices, 1, 1))
+    wide_forcing = wide[members_here + 3][None] * spread_params[:, None, :]
     global_rows = first_row - depth + jnp.arange(row_count + 2 * depth, dtype=jnp.int32)
     wide_inside = ((global_rows >= 0) & (global_rows < slabs)).astype(jnp.float32)[:, None]
 
     def step(values, low, step_size, forcing):
-        n = values.shape[1]
+        n = values.shape[-2]
         lo, hi = low + 1, low + n - 1
         q = None if forcing is None else forcing[:, lo:hi]
         return advance(values, wide_coeffs[:, lo:hi], wide_inside[lo:hi], step_size, q)
@@ -149,9 +152,8 @@
     coarse_part = step(wide_state, 0, coarse_dt, None)
     for section in range(FINE):
         current = step(current, section, FINE_DT, wide_forcing)
-    coarse_part = coarse_part[:, FINE - 1 : FINE - 1 + current.shape[1]]
-    fine = current.reshape(slices, group, -1, col_count)
-    coarse_part = coarse_part.reshape(slices, group, -1, col_count)
+    fine = current
+    coarse_part = coarse_part[:, :, FINE - 1 : FINE - 1 + current.shape[2]]
     running = fine[0]
     results = [running[:, links : links + row_count]]
     for link in range(1, slices):
@@ -168,9 +170,9 @@
     local_cell = every_cell - first_row * col_count
     rows = local_cell // col_count
     cols = local_cell % col_count
-    picked_rows = jnp.take_along_axis(done, rows[:, None, :, None], axis=2)
-    at_col = lax.broadcasted_iota(jnp.int32, picked_rows.shape, 3) == cols[:, None, :, None]
-    local_pred = jnp.sum(jnp.where(at_col, picked_rows, 0.0), axis=3)
+    at_slice = lax.broadcasted_iota(jnp.int32, (slices, group, rows.shape[1]), 0)
+    at_member = lax.broadcasted_iota(jnp.int32, (slices, group, rows.shape[1]), 1)
+    local_pred = done[at_slice, at_member, rows[:, None, :], cols[:, None, :]]
     pred = gather_axis(local_pred, "tm")
     pred = jnp.transpose(pred, (0, 2, 1, 3)).reshape(members_here, -1)
     every_pred = both_halves(pred, "ens")

time: 163 us -> 169 us (1.037)
  waiting for transfers between devices: 40.8 us -> 58.2 us
  other arithmetic: 32.8 us -> 23.9 us
  starting transfers between devices: 40.9 us -> 32.3 us
  local copies, waits for them, and re-layouts: 45.2 us -> 51.1 us
    all_to_all x1, waiting for transfers between devices: 3.63 us -> 21.5 us  [per_device(): lax.all_to_all(wide[:members_here].reshape(slices, group, row_count + 2 *...]
    another operation x3 -> x2, local copies, waits for them, and re-layouts: 10.1 us -> 0.09 us  [by_source(): stacked = jnp.stack(pieces)]
    slice x9 -> x14, local copies, waits for them, and re-layouts: 8.27 us -> 16.3 us  [the longest x7 7.89 us: advance(): west_cell = jnp.pad(middle[..., :-1], edge + [(1, 0)])]
    unnamed x49 -> x89, local copies, waits for them, and re-layouts: 2 us -> 8.65 us
    all_to_all x2 -> x0, local copies, waits for them, and re-layouts: 6.18 us -> none  [the longest x1 4.21 us: per_device(): lax.all_to_all(state.reshape(slices, group, row_count, col_count), 'tm',...]
    ppermute x2 -> x1, waiting for transfers between devices: 5.5 us -> 11 us  [with_halo(): lax.ppermute(head, axis, [(i + 1, i) for i in range(ends)])]
    ppermute x2 -> x1, starting transfers between devices: 8.83 us -> 4.23 us  [with_halo(): lax.ppermute(tail, axis, [(i, i + 1) for i in range(ends)])]
    reduce_sum x1 -> x0, other arithmetic: 4.17 us -> none  [per_device(): local_pred = jnp.sum(jnp.where(at_col, picked_rows, 0.0), axis=3)]
  transfers between devices with their start and end apart: 20 -> 18, of which waited for: 12 -> 10; matrix products, arithmetic and copies ran while one was open for 46% -> 41% of each run, Pallas kernels for 0% -> 0%
where the time goes in v5:
time: 169 us; the launch traced here: 168 us
  waiting for transfers between devices  58.2 us (34%)
  local copies, waits for them, and re-layouts  51.1 us (30%)
  starting transfers between devices  32.3 us (19%)
  other arithmetic  23.9 us (14%)
    all_to_all x1, waiting for transfers between devices, per_device(): lax.all_to_all(wide[:members_here].reshape(slices, group, row_count + 2 *...  21.5 us
    all_to_all x1, waiting for transfers between devices, per_device(): lax.all_to_all(done, 'tm', 0, 0, tiled=True)  18.7 us
    mul x5, other arithmetic, advance(): return (middle + step_size * tendency) * inside  12.8 us
    ppermute x1, waiting for transfers between devices, with_halo(): lax.ppermute(head, axis, [(i + 1, i) for i in range(ends)])  11 us
    ppermute x6, starting transfers between devices, quad_sum(): lax.ppermute(value, axis, [(i, i ^ k * bit) for i in range(count)])  10.2 us
    ppermute x6, starting transfers between devices, gather_axis(): lax.ppermute(value, axis, [(i, (i + d) % count) for i in range(count)])  9.14 us
    unnamed x89, local copies, waits for them, and re-layouts  8.65 us
    gather x3, local copies, waits for them, and re-layouts, per_device(): local_pred = done[at_slice, at_member, rows[:, None, :], cols[:, None, :]]  8.29 us
  transfers between devices with their start and end apart: 18, of which 10 were waited for; matrix products, arithmetic and copies ran while one was open for 41% of the time, Pallas kernels for 0%

profile of v5, /device:TPU:0, one launch (start us, length us, event | category | flops | bytes accessed | tf_op | source)
XLA Modules:
  0.0 168.5 jit_solution(12087079249723782802)
XLA Ops:
  2.1 1.6 collective-permute-start.2
  3.8 2.7 %collective-permute-start.3 = (f32[64,19]{0,1:T(8,128)S(1)}, f32[64,19]{0,1:T(8,128)S(1)}, u32[]{:S(2)}, u32[]{:S(2)}) collective-permute-start(f32[64,19]{0,1:T(8,128)S(1)} %get-tuple-element.52), channel_id=1, source_target_pairs={{0,64},{32,96},{64,0},{96,32},{1,65},{33,97},{65,1},{97,33},{2,66}... | collective-permute-start | bytes 14600 | tf_op jit(solution)/shard_map/ppermute | solution.py:58
  6.5 1.4 collective-permute-start.4
  7.9 1.7 %bitcast_dynamic-update-slice_fusion = f32[12,64,1024]{2,1,0:T(8,128)S(1)} fusion(f32[1,8,64,1024]{3,2,1,0:T(8,128)} %param.10), kind=kLoop, calls=%fused_computation.11 | loop fusion | bytes 4194304
  9.8 0.9 fusion.41
  10.8 4.2 %collective-permute-start = (f32[12,7,1024]{2,1,0:T(8,128)}, f32[12,7,1024]{2,1,0:T(8,128)}, u32[]{:S(2)}, u32[]{:S(2)}) collective-permute-start(f32[12,7,1024]{2,1,0:T(8,128)} %get-tuple-element.29), channel_id=1, source_target_pairs={{0,2},{2,4},{4,6},{6,8},{8,10},{10,12},{12,14},{14,16},{16,18},{18... | collective-permute-start | bytes 1032200 | tf_op jit(solution)/shard_map/ppermute | solution.py:21
  19.5 1.3 collective-permute-start.1
  22.2 11.0 %collective-permute-done.1 = f32[12,7,1024]{2,1,0:T(8,128)} collective-permute-done((f32[12,7,1024]{2,1,0:T(8,128)}, f32[12,7,1024]{2,1,0:T(8,128)}, u32[]{:S(2)}, u32[]{:S(2)}) %collective-permute-start.1) | collective-permute-done | bytes 344096 | tf_op jit(solution)/shard_map/ppermute | solution.py:23
  33.2 1.7 pad_maximum_fusion
  34.9 1.9 %copy-done = f32[12,78,1024]{2,1,0:T(8,128)} copy-done((f32[12,78,1024]{2,1,0:T(8,128)}, f32[12,78,1024]{2,1,0:T(8,128)S(1)}, u32[]{:S(2)}) %copy-start) | copy-done | bytes 3833880
  37.1 3.5 %copy.32 = f32[4,2,78,1024]{3,1,2,0:T(2,128)} copy(f32[4,2,78,1024]{3,2,1,0:T(8,128)S(1)} %bitcast.114) | data formatting | bytes 5111808 | tf_op jit(solution)/shard_map/reshape | solution.py:133
  40.6 3.8 %all-to-all-start = ((f32[4,2,78,1024]{3,1,2,0:T(2,128)}), f32[4,2,78,1024]{3,1,2,0:T(2,128)S(1)}, u32[]{:S(2)}, u32[]{:S(2)}) async-start(f32[4,2,78,1024]{3,1,2,0:T(2,128)} %copy.32), calls=%async_computation | async-start | bytes 5111808 | tf_op jit(solution)/shard_map/all_to_all | solution.py:132
  44.4 1.0 slice_bitcast_fusion.7
  45.5 0.9 slice.464
  47.4 0.9 slice.491
  48.3 1.0 slice_bitcast_fusion.22
  49.2 1.0 slice_bitcast_fusion.19
  50.2 1.0 slice_bitcast_fusion.16
  51.1 1.0 slice_bitcast_fusion.13
  52.1 1.0 slice_bitcast_fusion.10
  53.1 1.0 slice_bitcast_fusion.6
  54.1 21.5 %all-to-all-done = f32[4,2,78,1024]{3,1,2,0:T(2,128)S(1)} async-done(((f32[4,2,78,1024]{3,1,2,0:T(2,128)}), f32[4,2,78,1024]{3,1,2,0:T(2,128)S(1)}, u32[]{:S(2)}, u32[]{:S(2)}) %all-to-all-start) | async-done | bytes 2555936 | tf_op jit(solution)/shard_map/all_to_all | solution.py:132
  75.6 3.5 %fusion.45 = (f32[4,2,76,1023]{3,1,2,0:T(2,128)S(1)}, f32[4,2,76,1023]{3,1,2,0:T(2,128)S(1)}) fusion(f32[4,2,78,1024]{3,1,2,0:T(2,128)S(1)} %all-to-all-done), kind=kLoop, calls=%fused_computation.141 | loop fusion | bytes 9951744 | tf_op jit(solution)/shard_map/slice | solution.py:75
  80.7 4.4 %fusion.44 = (f32[4,2,76,1024]{3,1,2,0:T(2,128)}, f32[4,2,76,1024]{3,1,2,0:T(2,128)}, f32[4,2,76,1024]{3,1,2,0:T(2,128)S(1)}) fusion(f32[4,2,78,1024]{3,1,2,0:T(2,128)S(1)} %all-to-all-done), kind=kLoop, calls=%fused_computation.140 | loop fusion | bytes 14942208 | tf_op jit(solution)/shard_map/slice | solution.py:72
  85.2 4.9 %add_multiply_fusion.2 = (f32[4,2,76,1024]{3,2,1,0:T(8,128)S(1)}, f32[4,2,76,1024]{3,2,1,0:T(8,128)S(1)}) fusion(f32[4,2,76,1024]{3,1,2,0:T(2,128)S(1)} %get-tuple-element.37, f32[76]{0:T(128)S(1)} %copy-done.34, f32[2,76,1024]{2,1,0:T(8,128)S(1)} %copy-done.2, f32[76,1024]{1,0:T(8,128)S(1)} %copy-done.8, f32[76,1024]{1,0:T(8,128)S(1)} %copy-done.9, ...), kind=kLoop, calls=%fused_computation.6 | loop fusion | flops 11206656 | bytes 18984496 | tf_op jit(solution)/shard_map/mul | solution.py:85
  90.1 1.4 fusion.43
  91.6 2.6 %add_multiply_fusion.1 = f32[4,2,74,1024]{3,2,1,0:T(8,128)S(1)} fusion(f32[4,2,76,1024]{3,2,1,0:T(8,128)S(1)} %get-tuple-element.6, f32[4,2,74,1023]{3,2,1,0:T(8,128)S(1)} %get-tuple-element.34, f32[4,2,74,1023]{3,2,1,0:T(8,128)S(1)} %get-tuple-element.33, f32[74]{0:T(128)S(1)} %copy-done.37, f32[2,74,1024]{2,1,0:T(8,128)S(1)} %slice.473, ...), kind=kLoop, calls=%fused_computation.5 | loop fusion | flops 10911744 | bytes 16060072 | tf_op jit(solution)/shard_map/mul | solution.py:85
  94.3 1.1 fusion.42
  95.5 2.1 %add_multiply_fusion.4 = f32[4,2,72,1024]{3,2,1,0:T(8,128)S(1)} fusion(f32[4,2,74,1024]{3,2,1,0:T(8,128)S(1)} %add_multiply_fusion.1, f32[4,2,72,1023]{3,2,1,0:T(8,128)S(1)} %get-tuple-element.32, f32[4,2,72,1023]{3,2,1,0:T(8,128)S(1)} %get-tuple-element.31, f32[72]{0:T(128)S(1)} %copy-done.36, f32[2,72,1024]{2,1,0:T(8,128)S(1)} %copy-done.4, ...), kind=kLoop, calls=%fused_computation.9 | loop fusion | flops 10616832 | bytes 15626016 | tf_op jit(solution)/shard_map/mul | solution.py:85
  97.7 1.2 fusion.46
  99.0 1.0 add_multiply_fusion
  100.3 2.2 %add_multiply_fusion.3 = f32[4,2,70,1024]{3,2,1,0:T(8,128)S(1)} fusion(f32[4,2,72,1024]{3,2,1,0:T(8,128)S(1)} %add_multiply_fusion.4, f32[4,2,70,1023]{3,2,1,0:T(8,128)S(1)} %get-tuple-element.42, f32[4,2,70,1023]{3,2,1,0:T(8,128)S(1)} %get-tuple-element.41, f32[70]{0:T(128)S(1)} %copy-done.35, f32[2,70,1024]{2,1,0:T(8,128)S(1)} %copy-done.3, ...), kind=kLoop, calls=%fused_computation.8 | loop fusion | flops 10321920 | bytes 15191960 | tf_op jit(solution)/shard_map/mul | solution.py:85
  106.9 1.5 pad_maximum_fusion.1
  108.4 8.2 %gather_fusion.1 = f32[512]{0:T(512)S(1)} fusion(f32[4,2,64,1024]{3,2,1,0:T(8,128)} %pad_maximum_fusion.1, s32[512]{0:T(512)S(1)} %reshape.182), kind=kCustom, calls=%fused_computation.1 | custom fusion | bytes 12288 | tf_op jit(solution)/shard_map/gather | solution.py:175
  117.3 2.1 %collective-permute-start.6 = (f32[4,2,64]{2,0,1:T(4,128)S(1)}, f32[4,2,64]{2,0,1:T(4,128)S(1)}, u32[]{:S(2)}, u32[]{:S(2)}) collective-permute-start(f32[4,2,64]{2,0,1:T(4,128)S(1)} %copy.38), channel_id=1, source_target_pairs={{0,64},{32,96},{64,0},{96,32},{1,65},{33,97},{65,1},{97,33},{2,66}... | collective-permute-start | bytes 6152 | tf_op jit(solution)/shard_map/ppermute | solution.py:58
  123.9 1.0 collective-permute-done.8
  125.2 2.3 %collective-permute-start.10 = (f32[2,16,16]{2,1,0:T(8,128)S(1)}, f32[2,16,16]{2,1,0:T(8,128)S(1)}, u32[]{:S(2)}, u32[]{:S(2)}) collective-permute-start(f32[2,16,16]{2,1,0:T(8,128)S(1)} %pad_maximum_fusion.4), channel_id=1, source_target_pairs={{0,4},{2,6},{4,0},{6,2},{8,12},{10,14},{12,8},{14,10},{16,20},{18,... | collective-permute-start | bytes 6152 | tf_op jit(solution)/shard_map/ppermute | solution.py:37
  127.5 2.3 %collective-permute-start.11 = (f32[2,16,16]{2,1,0:T(8,128)S(1)}, f32[2,16,16]{2,1,0:T(8,128)S(1)}, u32[]{:S(2)}, u32[]{:S(2)}) collective-permute-start(f32[2,16,16]{2,1,0:T(8,128)S(1)} %pad_maximum_fusion.4), channel_id=1, source_target_pairs={{0,6},{2,4},{4,2},{6,0},{8,14},{10,12},{12,10},{14,8},{16,22},{18,... | collective-permute-start | bytes 6152 | tf_op jit(solution)/shard_map/ppermute | solution.py:37
  130.6 1.8 %collective-permute-done.11 = f32[2,16,16]{2,1,0:T(8,128)S(1)} collective-permute-done((f32[2,16,16]{2,1,0:T(8,128)S(1)}, f32[2,16,16]{2,1,0:T(8,128)S(1)}, u32[]{:S(2)}, u32[]{:S(2)}) %collective-permute-start.11) | collective-permute-done | bytes 2080 | tf_op jit(solution)/shard_map/ppermute | solution.py:37
  132.4 1.1 collective-permute-done.9
  133.6 2.0 %collective-permute-start.12 = (f32[2,16,16]{2,1,0:T(8,128)S(1)}, f32[2,16,16]{2,1,0:T(8,128)S(1)}, u32[]{:S(2)}, u32[]{:S(2)}) collective-permute-start(f32[2,16,16]{2,1,0:T(8,128)S(1)} %add_add_fusion.1), channel_id=1, source_target_pairs={{0,8},{2,10},{4,12},{6,14},{8,0},{10,2},{12,4},{14,6},{16,24},{18,... | collective-permute-start | bytes 6152 | tf_op jit(solution)/shard_map/ppermute | solution.py:37
  135.6 2.6 %collective-permute-start.13 = (f32[2,16,16]{2,1,0:T(8,128)S(1)}, f32[2,16,16]{2,1,0:T(8,128)S(1)}, u32[]{:S(2)}, u32[]{:S(2)}) collective-permute-start(f32[2,16,16]{2,1,0:T(8,128)S(1)} %add_add_fusion.1), channel_id=1, source_target_pairs={{0,16},{2,18},{4,20},{6,22},{8,24},{10,26},{12,28},{14,30},{16,0},... | collective-permute-start | bytes 6152 | tf_op jit(solution)/shard_map/ppermute | solution.py:37
  138.3 3.6 %all-to-all-start.1 = ((f32[4,2,64,1024]{3,2,1,0:T(8,128)}), f32[4,2,64,1024]{3,2,1,0:T(8,128)S(1)}, u32[]{:S(2)}, u32[]{:S(2)}) async-start(f32[4,2,64,1024]{3,2,1,0:T(8,128)} %pad_maximum_fusion.1), calls=%async_computation.1 | async-start | bytes 4194304 | tf_op jit(solution)/shard_map/all_to_all | solution.py:165
  142.0 1.1 collective-permute-done.14
  143.2 1.5 cholesky.17
  146.0 1.2 custom-call.10
  148.4 18.7 %all-to-all-done.1 = f32[4,2,64,1024]{3,2,1,0:T(8,128)S(1)} async-done(((f32[4,2,64,1024]{3,2,1,0:T(8,128)}), f32[4,2,64,1024]{3,2,1,0:T(8,128)S(1)}, u32[]{:S(2)}, u32[]{:S(2)}) %all-to-all-start.1) | async-done | bytes 2097184 | tf_op jit(solution)/shard_map/all_to_all | solution.py:165
  167.1 1.3 copy.62
  (172 shorter events, 24.3 us)
Async XLA Ops:
  0.6 9.0 %copy-start.22 = (f32[64,1024]{1,0:T(8,128)S(1)}, f32[64,1024]{1,0:T(8,128)}, u32[]{:S(2)}) copy-start(f32[64,1024]{1,0:T(8,128)} %param.13) | copy-start | bytes 786436
  0.6 9.1 %copy-start.24 = (f32[64,1024]{1,0:T(8,128)S(1)}, f32[64,1024]{1,0:T(8,128)}, u32[]{:S(2)}) copy-start(f32[64,1024]{1,0:T(8,128)} %param.11) | copy-start | bytes 786436
  2.1 7.7 %copy-start.26 = (f32[64,1024]{1,0:T(8,128)S(1)}, f32[64,1024]{1,0:T(8,128)}, u32[]{:S(2)}) copy-start(f32[64,1024]{1,0:T(8,128)} %param.12) | copy-start | bytes 786436
  2.1 7.7 %copy-start.28 = (f32[64,1024]{1,0:T(8,128)S(1)}, f32[64,1024]{1,0:T(8,128)}, u32[]{:S(2)}) copy-start(f32[64,1024]{1,0:T(8,128)} %param.14) | copy-start | bytes 786436
  2.1 17.4 %collective-permute-start.2 = (f32[64,19]{0,1:T(8,128)S(1)}, f32[64,19]{0,1:T(8,128)S(1)}, u32[]{:S(2)}, u32[]{:S(2)}) collective-permute-start(f32[64,19]{0,1:T(8,128)S(1)} %get-tuple-element.52), channel_id=1, source_target_pairs={{0,32},{32,64},{64,96},{96,0},{1,33},{33,65},{65,97},{97,1},{2,34}... | collective-permute-start | bytes 14600 | tf_op jit(solution)/shard_map/ppermute | solution.py:58
  3.8 17.0 %collective-permute-start.3 = (f32[64,19]{0,1:T(8,128)S(1)}, f32[64,19]{0,1:T(8,128)S(1)}, u32[]{:S(2)}, u32[]{:S(2)}) collective-permute-start(f32[64,19]{0,1:T(8,128)S(1)} %get-tuple-element.52), channel_id=1, source_target_pairs={{0,64},{32,96},{64,0},{96,32},{1,65},{33,97},{65,1},{97,33},{2,66}... | collective-permute-start | bytes 14600 | tf_op jit(solution)/shard_map/ppermute | solution.py:58
  6.5 14.3 %collective-permute-start.4 = (f32[64,19]{0,1:T(8,128)S(1)}, f32[64,19]{0,1:T(8,128)S(1)}, u32[]{:S(2)}, u32[]{:S(2)}) collective-permute-start(f32[64,19]{0,1:T(8,128)S(1)} %get-tuple-element.52), channel_id=1, source_target_pairs={{0,96},{32,0},{64,32},{96,64},{1,97},{33,1},{65,33},{97,65},{2,98}... | collective-permute-start | bytes 14600 | tf_op jit(solution)/shard_map/ppermute | solution.py:58
  9.7 5.3 %copy-start.31 = (f32[8,128]{1,0:T(8,128)S(1)}, f32[8,128]{1,0:T(8,128)}, u32[]{:S(2)}) copy-start(f32[8,128]{1,0:T(8,128)} %param.15) | copy-start | bytes 12292
  10.8 11.5 %collective-permute-start = (f32[12,7,1024]{2,1,0:T(8,128)}, f32[12,7,1024]{2,1,0:T(8,128)}, u32[]{:S(2)}, u32[]{:S(2)}) collective-permute-start(f32[12,7,1024]{2,1,0:T(8,128)} %get-tuple-element.29), channel_id=1, source_target_pairs={{0,2},{2,4},{4,6},{6,8},{8,10},{10,12},{12,14},{14,16},{16,18},{18... | collective-permute-start | bytes 1032200 | tf_op jit(solution)/shard_map/ppermute | solution.py:21
  15.0 115.6 %collective-permute-start.15 = (f32[8,128]{1,0:T(8,128)S(1)}, f32[8,128]{1,0:T(8,128)S(1)}, u32[]{:S(2)}, u32[]{:S(2)}) collective-permute-start(f32[8,128]{1,0:T(8,128)S(1)} %copy-done.31), channel_id=1, source_target_pairs={{0,1},{1,0},{2,3},{3,2},{4,5},{5,4},{6,7},{7,6},{8,9},{9,8},{10,11... | collective-permute-start | bytes 12296 | tf_op jit(solution)/shard_map/ppermute | solution.py:65
  15.0 19.9 %copy-start.32 = (pred[4]{0:T(512)(128)(4,1)}, pred[4]{0:T(512)(128)(4,1)S(1)}, u32[]{:S(2)}) copy-start(pred[4]{0:T(512)(128)(4,1)S(1)} %compare_and_fusion) | copy-start | bytes 16
  19.5 13.7 %collective-permute-start.1 = (f32[12,7,1024]{2,1,0:T(8,128)}, f32[12,7,1024]{2,1,0:T(8,128)}, u32[]{:S(2)}, u32[]{:S(2)}) collective-permute-start(f32[12,7,1024]{2,1,0:T(8,128)} %get-tuple-element.30), channel_id=1, source_target_pairs={{2,0},{4,2},{6,4},{8,6},{10,8},{12,10},{14,12},{16,14},{18,16},{20... | collective-permute-start | bytes 1032200 | tf_op jit(solution)/shard_map/ppermute | solution.py:23
  21.5 13.4 %copy-start.29 = (f32[4,64,19]{1,2,0:T(8,128)}, f32[4,64,19]{1,2,0:T(8,128)S(1)}, u32[]{:S(2)}) copy-start(f32[4,64,19]{1,2,0:T(8,128)S(1)} %broadcast_select_fusion) | copy-start | bytes 58372
  34.9 1.9 %copy-start = (f32[12,78,1024]{2,1,0:T(8,128)}, f32[12,78,1024]{2,1,0:T(8,128)S(1)}, u32[]{:S(2)}) copy-start(f32[12,78,1024]{2,1,0:T(8,128)S(1)} %pad_maximum_fusion) | copy-start | bytes 11501572
  40.6 35.0 %all-to-all-start = ((f32[4,2,78,1024]{3,1,2,0:T(2,128)}), f32[4,2,78,1024]{3,1,2,0:T(2,128)S(1)}, u32[]{:S(2)}, u32[]{:S(2)}) async-start(f32[4,2,78,1024]{3,1,2,0:T(2,128)} %copy.32), calls=%async_computation | async-start | bytes 5111808 | tf_op jit(solution)/shard_map/all_to_all | solution.py:132
  45.5 2.8 %copy-start.1 = (f32[12,78,1024]{2,1,0:T(8,128)S(1)}, f32[12,78,1024]{2,1,0:T(8,128)}, u32[]{:S(2)}) copy-start(f32[12,78,1024]{2,1,0:T(8,128)} %copy-done) | copy-start | bytes 11501572
  80.7 4.5 %copy-start.2 = (f32[2,76,1024]{2,1,0:T(8,128)S(1)}, f32[2,76,1024]{2,1,0:T(8,128)}, u32[]{:S(2)}) copy-start(f32[2,76,1024]{2,1,0:T(8,128)} %slice.464) | copy-start | bytes 1867780
  80.7 4.4 %copy-start.7 = (f32[76,1024]{1,0:T(8,128)S(1)}, f32[76,1024]{1,0:T(8,128)}, u32[]{:S(2)}) copy-start(f32[76,1024]{1,0:T(8,128)} %get-tuple-element.26) | copy-start | bytes 933892
  80.7 4.4 %copy-start.8 = (f32[76,1024]{1,0:T(8,128)S(1)}, f32[76,1024]{1,0:T(8,128)}, u32[]{:S(2)}) copy-start(f32[76,1024]{1,0:T(8,128)} %get-tuple-element.27) | copy-start | bytes 933892
  80.7 4.4 %copy-start.9 = (f32[76,1024]{1,0:T(8,128)S(1)}, f32[76,1024]{1,0:T(8,128)}, u32[]{:S(2)}) copy-start(f32[76,1024]{1,0:T(8,128)} %get-tuple-element.28) | copy-start | bytes 933892
  80.7 4.4 %copy-start.34 = (f32[76]{0:T(128)S(1)}, f32[76]{0:T(128)}, u32[]{:S(2)}) copy-start(f32[76]{0:T(128)} %slice.371) | copy-start | bytes 916
  90.1 1.4 copy-start.5
  90.1 1.4 copy-start.6
  90.1 1.4 copy-start.37
  94.2 1.1 copy-start.4
  94.2 1.1 copy-start.19
  94.2 1.2 copy-start.20
  94.3 1.3 copy-start.21
  94.3 1.3 copy-start.36
  98.9 1.1 copy-start.16
  99.0 1.2 copy-start.17
  99.0 1.3 copy-start.18
  99.0 1.3 copy-start.35
  102.5 1.1 copy-start.15
  104.2 1.1 copy-start.12
  108.4 15.1 %copy-start.33 = (pred[4]{0:T(512)(128)(4,1)S(1)}, pred[4]{0:T(512)(128)(4,1)}, u32[]{:S(2)}) copy-start(pred[4]{0:T(512)(128)(4,1)} %copy-done.32) | copy-start | bytes 16
  108.4 15.4 %copy-start.30 = (f32[16,4,64]{2,0,1:T(8,128)S(1)}, f32[16,4,64]{2,0,1:T(8,128)}, u32[]{:S(2)}) copy-start(f32[16,4,64]{2,0,1:T(8,128)} %slice_bitcast_fusion.23) | copy-start | bytes 49156
  116.7 4.8 %collective-permute-start.5 = (f32[4,2,64]{2,0,1:T(4,128)S(1)}, f32[4,2,64]{2,0,1:T(4,128)S(1)}, u32[]{:S(2)}, u32[]{:S(2)}) collective-permute-start(f32[4,2,64]{2,0,1:T(4,128)S(1)} %copy.38), channel_id=1, source_target_pairs={{0,32},{32,64},{64,96},{96,0},{1,33},{33,65},{65,97},{97,1},{2,34}... | collective-permute-start | bytes 6152 | tf_op jit(solution)/shard_map/ppermute | solution.py:58
  117.3 5.1 %collective-permute-start.6 = (f32[4,2,64]{2,0,1:T(4,128)S(1)}, f32[4,2,64]{2,0,1:T(4,128)S(1)}, u32[]{:S(2)}, u32[]{:S(2)}) collective-permute-start(f32[4,2,64]{2,0,1:T(4,128)S(1)} %copy.38), channel_id=1, source_target_pairs={{0,64},{32,96},{64,0},{96,32},{1,65},{33,97},{65,1},{97,33},{2,66}... | collective-permute-start | bytes 6152 | tf_op jit(solution)/shard_map/ppermute | solution.py:58
  119.3 3.6 %collective-permute-start.7 = (f32[4,2,64]{2,0,1:T(4,128)S(1)}, f32[4,2,64]{2,0,1:T(4,128)S(1)}, u32[]{:S(2)}, u32[]{:S(2)}) collective-permute-start(f32[4,2,64]{2,0,1:T(4,128)S(1)} %copy.38), channel_id=1, source_target_pairs={{0,96},{32,0},{64,32},{96,64},{1,97},{33,1},{65,33},{97,65},{2,98}... | collective-permute-start | bytes 6152 | tf_op jit(solution)/shard_map/ppermute | solution.py:58
  123.7 1.2 collective-permute-start.8
  125.2 5.4 %collective-permute-start.10 = (f32[2,16,16]{2,1,0:T(8,128)S(1)}, f32[2,16,16]{2,1,0:T(8,128)S(1)}, u32[]{:S(2)}, u32[]{:S(2)}) collective-permute-start(f32[2,16,16]{2,1,0:T(8,128)S(1)} %pad_maximum_fusion.4), channel_id=1, source_target_pairs={{0,4},{2,6},{4,0},{6,2},{8,12},{10,14},{12,8},{14,10},{16,20},{18,... | collective-permute-start | bytes 6152 | tf_op jit(solution)/shard_map/ppermute | solution.py:37
  127.5 4.9 %collective-permute-start.11 = (f32[2,16,16]{2,1,0:T(8,128)S(1)}, f32[2,16,16]{2,1,0:T(8,128)S(1)}, u32[]{:S(2)}, u32[]{:S(2)}) collective-permute-start(f32[2,16,16]{2,1,0:T(8,128)S(1)} %pad_maximum_fusion.4), channel_id=1, source_target_pairs={{0,6},{2,4},{4,2},{6,0},{8,14},{10,12},{12,10},{14,8},{16,22},{18,... | collective-permute-start | bytes 6152 | tf_op jit(solution)/shard_map/ppermute | solution.py:37
  129.8 3.7 %collective-permute-start.9 = (f32[2,16,16]{2,1,0:T(8,128)S(1)}, f32[2,16,16]{2,1,0:T(8,128)S(1)}, u32[]{:S(2)}, u32[]{:S(2)}) collective-permute-start(f32[2,16,16]{2,1,0:T(8,128)S(1)} %pad_maximum_fusion.4), channel_id=1, source_target_pairs={{0,2},{2,0},{4,6},{6,4},{8,10},{10,8},{12,14},{14,12},{16,18},{18,... | collective-permute-start | bytes 6152 | tf_op jit(solution)/shard_map/ppermute | solution.py:37
  133.6 8.4 %collective-permute-start.12 = (f32[2,16,16]{2,1,0:T(8,128)S(1)}, f32[2,16,16]{2,1,0:T(8,128)S(1)}, u32[]{:S(2)}, u32[]{:S(2)}) collective-permute-start(f32[2,16,16]{2,1,0:T(8,128)S(1)} %add_add_fusion.1), channel_id=1, source_target_pairs={{0,8},{2,10},{4,12},{6,14},{8,0},{10,2},{12,4},{14,6},{16,24},{18,... | collective-permute-start | bytes 6152 | tf_op jit(solution)/shard_map/ppermute | solution.py:37
  135.6 6.4 %collective-permute-start.13 = (f32[2,16,16]{2,1,0:T(8,128)S(1)}, f32[2,16,16]{2,1,0:T(8,128)S(1)}, u32[]{:S(2)}, u32[]{:S(2)}) collective-permute-start(f32[2,16,16]{2,1,0:T(8,128)S(1)} %add_add_fusion.1), channel_id=1, source_target_pairs={{0,16},{2,18},{4,20},{6,22},{8,24},{10,26},{12,28},{14,30},{16,0},... | collective-permute-start | bytes 6152 | tf_op jit(solution)/shard_map/ppermute | solution.py:37
  138.2 4.9 %collective-permute-start.14 = (f32[2,16,16]{2,1,0:T(8,128)S(1)}, f32[2,16,16]{2,1,0:T(8,128)S(1)}, u32[]{:S(2)}, u32[]{:S(2)}) collective-permute-start(f32[2,16,16]{2,1,0:T(8,128)S(1)} %add_add_fusion.1), channel_id=1, source_target_pairs={{0,24},{2,26},{4,28},{6,30},{8,16},{10,18},{12,20},{14,22},{16,8},... | collective-permute-start | bytes 6152 | tf_op jit(solution)/shard_map/ppermute | solution.py:37
  138.3 28.8 %all-to-all-start.1 = ((f32[4,2,64,1024]{3,2,1,0:T(8,128)}), f32[4,2,64,1024]{3,2,1,0:T(8,128)S(1)}, u32[]{:S(2)}, u32[]{:S(2)}) async-start(f32[4,2,64,1024]{3,2,1,0:T(8,128)} %pad_maximum_fusion.1), calls=%async_computation.1 | async-start | bytes 4194304 | tf_op jit(solution)/shard_map/all_to_all | solution.py:165
  (11 other events, 11.5 us)

commit v6 on v2

--- a/solution.py
+++ b/solution.py
@@ -24,17 +24,6 @@
         ],
         axis=1,
     )
-
-
-def butterfly_sum(value, axis):
-    count = lax.axis_size(axis)
-    if count & (count - 1):
-        return lax.psum(value, axis)
-    bit = 1
-    while bit < count:
-        value = value + lax.ppermute(value, axis, [(i, i ^ bit) for i in range(count)])
-        bit *= 2
-    return value
 
 
 def both_halves(value, axis):
@@ -139,11 +128,13 @@
     pred_mean = jnp.mean(every_pred, axis=0, keepdims=True)
     anomaly = (every_pred - pred_mean) * (inv_spread * norm_factor)
     misfit = (obs_data[0][None, :] + obs_noise[0].T - every_pred) * inv_spread
-    gram = jnp.dot(anomaly, anomaly.T, precision=lax.Precision.HIGHEST)
-    cross = jnp.dot(anomaly, misfit.T, precision=lax.Precision.HIGHEST)
-    sums = jnp.stack([gram, cross])
-    sums = butterfly_sum(sums, "tm")
-    sums = butterfly_sum(sums, "space")
+    half = anomaly.shape[1] // 2
+    own_half = lax.axis_index("ens") * half
+    part_anom = lax.dynamic_slice_in_dim(anomaly, own_half, half, 1)
+    part_misfit = lax.dynamic_slice_in_dim(misfit, own_half, half, 1)
+    gram = jnp.dot(part_anom, part_anom.T, precision=lax.Precision.HIGHEST)
+    cross = jnp.dot(part_anom, part_misfit.T, precision=lax.Precision.HIGHEST)
+    sums = lax.psum(jnp.stack([gram, cross]), ("tm", "space", "ens"))
     gram, cross = sums[0], sums[1]
     system = jnp.eye(total, dtype=jnp.float32) + gram
     factor = jnp.linalg.cholesky(system)

time: 156 us -> 197 us (1.26)
  blocking collectives: 30.5 us -> 102 us
  starting transfers between devices: 28.3 us -> 10.5 us
  waiting for transfers between devices: 40.6 us -> 26.3 us
    psum x0 -> x1, blocking collectives: none -> 71.7 us  [per_device(): sums = lax.psum(jnp.stack([gram, cross]), ('tm', 'space', 'ens'))]
    ppermute x6 -> x0, starting transfers between devices: 17.9 us -> none  [butterfly_sum(): lax.ppermute(value, axis, [(i, i ^ bit) for i in range(count)])]
    ppermute x6 -> x0, waiting for transfers between devices: 12.9 us -> none  [butterfly_sum(): lax.ppermute(value, axis, [(i, i ^ bit) for i in range(count)])]
  transfers between devices with their start and end apart: 11 -> 5, of which waited for: 9 -> 4; matrix products, arithmetic and copies ran while one was open for 4% -> 3% of each run, Pallas kernels for 0% -> 0%
where the time goes in v6:
time: 197 us; the launch traced here: 196 us
  blocking collectives  102 us (52%)
  local copies, waits for them, and re-layouts  33 us (17%)
  waiting for transfers between devices  26.3 us (13%)
  other arithmetic  21 us (11%)
  starting transfers between devices  10.5 us (5%)
    psum x1, blocking collectives, per_device(): sums = lax.psum(jnp.stack([gram, cross]), ('tm', 'space', 'ens'))  71.7 us
    all_to_all x1, blocking collectives, per_device(): lax.all_to_all(state.reshape(slices, group, row_count, col_count), 'tm',...  30.5 us
    all_to_all x1, waiting for transfers between devices, per_device(): lax.all_to_all(done, 'tm', 0, 0, tiled=True)  22.9 us
    mul x5, other arithmetic, advance(): return (middle + step_size * tendency) * inside  11.1 us
    slice x7, local copies, waits for them, and re-layouts, advance(): west_cell = jnp.pad(middle[:, :, :-1], ((0, 0), (0, 0), (1, 0)))  5.62 us
    ppermute x1, starting transfers between devices, with_halo(): lax.ppermute(tail, axis, [(i, i + 1) for i in range(ends)])  5.32 us
    all_to_all x2, local copies, waits for them, and re-layouts, per_device(): lax.all_to_all(done, 'tm', 0, 0, tiled=True)  4.6 us
  transfers between devices with their start and end apart: 5, of which 4 were waited for; matrix products, arithmetic and copies ran while one was open for 3% of the time, Pallas kernels for 0%

profile of v6, /device:TPU:0, one launch (start us, length us, event | category | flops | bytes accessed | tf_op | source)
XLA Modules:
  0.0 195.6 jit_solution(2950559301572762960)
XLA Ops:
  0.6 3.2 %copy.39 = f32[4,2,64,1024]{3,1,2,0:T(2,128)S(1)} copy(f32[4,2,64,1024]{3,2,1,0:T(8,128)} %bitcast.131) | data formatting | bytes 4194304 | tf_op jit(solution)/shard_map/reshape;squeeze | solution.py:77
  3.8 30.5 %all_to_all.10 = f32[4,2,64,1024]{3,1,2,0:T(2,128)S(1)} all-to-all(f32[4,2,64,1024]{3,1,2,0:T(2,128)S(1)} %copy.39), channel_id=1, replica_groups=mesh['tm'=4,'space'=16,'ens'=2] {'tm'}, dimensions={0} | all-to-all | bytes 4194304 | tf_op jit(solution)/shard_map/all_to_all | solution.py:76
  34.3 0.6 copy.40
  35.0 0.2 constant_dynamic-update-slice_fusion
  35.3 0.7 copy-done
  36.2 0.9 fusion.47
  37.2 1.3 collective-permute-start.1
  38.4 5.3 %collective-permute-start = (f32[12,7,1024]{2,1,0:T(8,128)}, f32[12,7,1024]{2,1,0:T(8,128)}, u32[]{:S(2)}, u32[]{:S(2)}) collective-permute-start(f32[12,7,1024]{2,1,0:T(8,128)} %get-tuple-element.28), channel_id=1, source_target_pairs={{0,2},{2,4},{4,6},{6,8},{8,10},{10,12},{12,14},{14,16},{16,18},{18... | collective-permute-start | bytes 1032200 | tf_op jit(solution)/shard_map/ppermute | solution.py:21
  43.8 0.6 slice.374
  44.4 0.6 slice.384
  45.0 0.6 slice.394
  45.7 0.6 slice.407
  46.2 0.7 slice.420
  46.9 0.6 slice.429
  47.7 1.3 collective-permute-done.1
  49.0 1.2 collective-permute-done
  50.2 1.7 pad_maximum_fusion
  52.0 1.4 fusion.46
  54.1 0.3 tile.4
  54.4 2.6 %fusion.5 = (f32[8,76,1024]{2,1,0:T(8,128)S(1)}, f32[8,76,1024]{2,1,0:T(8,128)S(1)}) fusion(f32[8,78,1024]{2,1,0:T(8,128)S(1)} %bitcast.126, f32[12,78,1024]{2,1,0:T(8,128)S(1)} %pad_maximum_fusion, f32[76]{0:T(128)S(1)} %slice.364, f32[76,1024]{1,0:T(8,128)S(1)} %get-tuple-element.24, f32[76,1024]{1,0:T(8,128)S(1)} %get-tuple-element.25, ...), kind=kLoop, calls=%fused_computation.9 | loop fusion | flops 11206656 | bytes 20852272 | tf_op jit(solution)/shard_map/mul | solution.py:49
  57.1 0.9 add_multiply_fusion
  58.0 1.4 fusion.50
  59.4 2.6 %fusion.2 = f32[8,74,1024]{2,1,0:T(8,128)S(1)} fusion(f32[8,78,1024]{2,1,0:T(8,128)S(1)} %bitcast.127, f32[8,76,1024]{2,1,0:T(8,128)S(1)} %get-tuple-element.6, f32[8,74,1023]{2,1,0:T(8,128)S(1)} %get-tuple-element.36, f32[8,74,1023]{2,1,0:T(8,128)S(1)} %get-tuple-element.35, f32[74]{0:T(128)S(1)} %copy-done.13, f32[74,1024]{1,0:T(8,128)S(1)} %get-tuple-element.21, ...), kind=kLoop, calls=%fused_computation.5 | loop fusion | flops 10911744 | bytes 17878696 | tf_op jit(solution)/shard_map/mul | solution.py:49
  62.1 1.1 fusion.49
  63.2 2.4 %fusion.11 = f32[8,72,1024]{2,1,0:T(8,128)S(1)} fusion(f32[8,78,1024]{2,1,0:T(8,128)S(1)} %bitcast.128, f32[8,74,1024]{2,1,0:T(8,128)S(1)} %fusion.2, f32[8,72,1023]{2,1,0:T(8,128)S(1)} %get-tuple-element.34, f32[8,72,1023]{2,1,0:T(8,128)S(1)} %get-tuple-element.33, f32[72]{0:T(128)S(1)} %copy-done.9, f32[72,1024]{1,0:T(8,128)S(1)} %get-tuple-element.18, ...), kind=kLoop, calls=%fused_computation.19 | loop fusion | flops 10616832 | bytes 17395488 | tf_op jit(solution)/shard_map/mul | solution.py:49
  65.6 1.1 fusion.53
  66.7 2.6 %fusion.8 = f32[8,70,1024]{2,1,0:T(8,128)S(1)} fusion(f32[8,78,1024]{2,1,0:T(8,128)S(1)} %bitcast.129, f32[8,72,1024]{2,1,0:T(8,128)S(1)} %fusion.11, f32[8,70,1023]{2,1,0:T(8,128)S(1)} %get-tuple-element.43, f32[8,70,1023]{2,1,0:T(8,128)S(1)} %get-tuple-element.42, f32[70]{0:T(128)S(1)} %copy-done.8, f32[70,1024]{1,0:T(8,128)S(1)} %get-tuple-element.15, ...), kind=kLoop, calls=%fused_computation.15 | loop fusion | flops 10321920 | bytes 16912280 | tf_op jit(solution)/shard_map/mul | solution.py:49
  69.5 0.5 fusion.48
  70.1 0.6 fusion.15
  70.7 0.2 fusion.55
  71.0 0.3 copy-done.11
  71.3 0.6 fusion.14
  72.4 0.5 slice_bitcast_fusion.2
  73.1 2.9 %copy.41 = f32[4,2,64,1024]{3,1,2,0:T(2,128)} copy(f32[4,2,64,1024]{3,2,1,0:T(8,128)S(1)} %pad_maximum_fusion.1) | data formatting | bytes 4194304 | tf_op jit(solution)/shard_map/stack | solution.py:111
  76.0 3.8 %all-to-all-start.1 = ((f32[4,2,64,1024]{3,1,2,0:T(2,128)}), f32[4,2,64,1024]{3,1,2,0:T(2,128)S(1)}, u32[]{:S(2)}, u32[]{:S(2)}) async-start(f32[4,2,64,1024]{3,1,2,0:T(2,128)} %copy.41), calls=%async_computation.1 | async-start | bytes 4194304 | tf_op jit(solution)/shard_map/all_to_all | solution.py:112
  80.2 0.9 collective-permute-done.3
  81.0 22.9 %all-to-all-done.1 = f32[4,2,64,1024]{3,1,2,0:T(2,128)S(1)} async-done(((f32[4,2,64,1024]{3,1,2,0:T(2,128)}), f32[4,2,64,1024]{3,1,2,0:T(2,128)S(1)}, u32[]{:S(2)}, u32[]{:S(2)}) %all-to-all-start.1) | async-done | bytes 2097184 | tf_op jit(solution)/shard_map/all_to_all | solution.py:112
  104.0 2.6 %copy.43 = f32[4,2,64,1024]{3,1,0,2:T(2,128)} copy(f32[4,2,64,1024]{3,1,2,0:T(2,128)S(1)} %all-to-all-done.1) | data formatting | bytes 4194304 | tf_op jit(solution)/shard_map/all_to_all | solution.py:112
  106.6 3.6 %reshape.167 = f32[8,64,1024]{2,0,1:T(8,128)} reshape(f32[4,2,64,1024]{3,1,0,2:T(2,128)} %copy.43) | data formatting | bytes 4194304 | tf_op jit(solution)/shard_map/reshape | solution.py:112
  110.2 3.6 %gather_fusion = f32[64,8,1024]{2,1,0:T(8,128)} fusion(f32[8,64,1024]{2,0,1:T(8,128)} %reshape.167, s32[1024]{0:T(1024)S(1)} %pad_clamp_fusion), kind=kCustom, calls=%fused_computation | custom fusion | bytes 4194560 | tf_op jit(solution)/shard_map/jit(_take)/gather | solution.py:120
  113.8 2.1 %fusion.12 = f32[8,64]{0,1:T(8,128)S(1)} fusion(f32[64,8,1024]{2,1,0:T(8,128)} %gather_fusion, s32[64]{0:T(128)S(1)} %and_select_fusion.2, pred[64]{0:T(512)(128)(4,1)S(1)} %get-tuple-element.4), kind=kLoop, calls=%fused_computation.22 | loop fusion | flops 2096640 | bytes 2099520 | tf_op jit(solution)/shard_map/reduce_sum | solution.py:122
  116.1 2.0 %copy.42 = f32[4,2,64,1024]{3,2,1,0:T(8,128)} copy(f32[4,2,64,1024]{3,1,2,0:T(2,128)S(1)} %all-to-all-done.1) | data formatting | bytes 4194304 | tf_op jit(solution)/shard_map/all_to_all | solution.py:112
  118.7 71.7 %psum.7 = f32[2,16,16]{2,1,0:T(8,128)S(1)} all-reduce(f32[2,16,16]{2,1,0:T(8,128)S(1)} %pad_maximum_fusion.2), channel_id=1, replica_groups=mesh['tm'=4,'space'=16,'ens'=2] {'tm','space','ens'}, use_global_device_ids=true, to_apply=%region_2.3 | all-reduce | flops 512 | bytes 4096 | tf_op jit(solution)/shard_map/psum | solution.py:137
  190.4 1.5 cholesky.17
  191.9 0.6 compare_reduce_fusion
  192.6 0.6 fusion.18
  193.2 1.2 custom-call.10
  194.9 0.7 fusion.13
  (81 shorter events, 4.0 us)
Async XLA Ops:
  35.0 1.0 copy-start
  35.0 1.0 copy-start.1
  35.0 1.1 copy-start.3
  35.0 1.2 copy-start.5
  35.9 11.5 %copy-start.6 = (f32[8,128]{1,0:T(8,128)S(1)}, f32[8,128]{1,0:T(8,128)}, u32[]{:S(2)}) copy-start(f32[8,128]{1,0:T(8,128)} %param.15) | copy-start | bytes 12292
  37.2 11.9 %collective-permute-start.1 = (f32[12,7,1024]{2,1,0:T(8,128)}, f32[12,7,1024]{2,1,0:T(8,128)}, u32[]{:S(2)}, u32[]{:S(2)}) collective-permute-start(f32[12,7,1024]{2,1,0:T(8,128)} %get-tuple-element.29), channel_id=1, source_target_pairs={{2,0},{4,2},{6,4},{8,6},{10,8},{12,10},{14,12},{16,14},{18,16},{20... | collective-permute-start | bytes 1032200 | tf_op jit(solution)/shard_map/ppermute | solution.py:23
  38.4 11.8 %collective-permute-start = (f32[12,7,1024]{2,1,0:T(8,128)}, f32[12,7,1024]{2,1,0:T(8,128)}, u32[]{:S(2)}, u32[]{:S(2)}) collective-permute-start(f32[12,7,1024]{2,1,0:T(8,128)} %get-tuple-element.28), channel_id=1, source_target_pairs={{0,2},{2,4},{4,6},{6,8},{8,10},{10,12},{12,14},{14,16},{16,18},{18... | collective-permute-start | bytes 1032200 | tf_op jit(solution)/shard_map/ppermute | solution.py:21
  58.0 1.4 copy-start.13
  62.1 1.1 copy-start.9
  65.5 1.1 copy-start.8
  69.5 0.6 copy-start.12
  70.6 0.7 copy-start.11
  71.3 0.9 copy-start.2
  71.3 1.0 copy-start.4
  71.3 1.0 copy-start.10
  76.0 3.9 %copy-start.15 = (s32[1,64]{1,0:T(1,128)S(1)}, s32[1,64]{1,0:T(1,128)}, u32[]{:S(2)}) copy-start(s32[1,64]{1,0:T(1,128)} %param.16) | copy-start | bytes 772
  76.0 3.9 %copy-start.16 = (f32[1,64]{1,0:T(1,128)S(1)}, f32[1,64]{1,0:T(1,128)}, u32[]{:S(2)}) copy-start(f32[1,64]{1,0:T(1,128)} %param.19) | copy-start | bytes 772
  76.0 3.9 %copy-start.7 = (f32[1,64,16]{1,2,0:T(8,128)S(1)}, f32[1,64,16]{1,2,0:T(8,128)}, u32[]{:S(2)}) copy-start(f32[1,64,16]{1,2,0:T(8,128)} %param.18) | copy-start | bytes 12292
  76.0 4.0 %copy-start.14 = (f32[1,64]{1,0:T(1,128)S(1)}, f32[1,64]{1,0:T(1,128)}, u32[]{:S(2)}) copy-start(f32[1,64]{1,0:T(1,128)} %param.17) | copy-start | bytes 772
  76.0 27.9 %all-to-all-start.1 = ((f32[4,2,64,1024]{3,1,2,0:T(2,128)}), f32[4,2,64,1024]{3,1,2,0:T(2,128)S(1)}, u32[]{:S(2)}, u32[]{:S(2)}) async-start(f32[4,2,64,1024]{3,1,2,0:T(2,128)} %copy.41), calls=%async_computation.1 | async-start | bytes 4194304 | tf_op jit(solution)/shard_map/all_to_all | solution.py:112
  79.8 1.2 collective-permute-start.3
  115.9 2.1 %collective-permute-start.2 = (f32[8,64]{0,1:T(8,128)S(1)}, f32[8,64]{0,1:T(8,128)S(1)}, u32[]{:S(2)}, u32[]{:S(2)}) collective-permute-start(f32[8,64]{0,1:T(8,128)S(1)} %fusion.12), channel_id=1, source_target_pairs={{0,1},{1,0},{2,3},{3,2},{4,5},{5,4},{6,7},{7,6},{8,9},{9,8},{10,11... | collective-permute-start | bytes 6152 | tf_op jit(solution)/shard_map/ppermute | solution.py:30

commit v7 on v2

--- a/solution.py
+++ b/solution.py
@@ -128,7 +128,8 @@
     local_cell = obs_cell[0] - first_row * col_count
     rows = local_cell // col_count
     cols = local_cell % col_count
-    picked_rows = jnp.take(running, rows, axis=1)
+    row_pick = (rows[:, None] == jnp.arange(row_count, dtype=jnp.int32)[None, :]).astype(jnp.float32)
+    picked_rows = jnp.einsum("or,mrc->moc", row_pick, running, precision=lax.Precision.HIGHEST)
     at_col = lax.broadcasted_iota(jnp.int32, picked_rows.shape, 2) == cols[None, :, None]
     predicted = jnp.sum(jnp.where(at_col, picked_rows, 0.0), axis=2)
     every_pred = both_halves(predicted, "ens")

time: 156 us -> 141 us (0.904)
  local copies, waits for them, and re-layouts: 32.8 us -> 15.4 us
  waiting for transfers between devices: 40.6 us -> 42.4 us
    all_to_all x3 -> x0, local copies, waits for them, and re-layouts: 5.23 us -> none  [the longest x2 4.59 us: per_device(): lax.all_to_all(done, 'tm', 0, 0, tiled=True)]
    reshape x1 -> x0, local copies, waits for them, and re-layouts: 3.65 us -> none  [per_device(): lax.all_to_all(done, 'tm', 0, 0, tiled=True)]
    gather x1 -> x0, local copies, waits for them, and re-layouts: 3.63 us -> none  [per_device(): picked_rows = jnp.take(running, rows, axis=1)]
    another operation x1 -> x0, local copies, waits for them, and re-layouts: 3.21 us -> none  [per_device(): state.reshape(slices, group, row_count, col_count)]
    another operation x3 -> x2, local copies, waits for them, and re-layouts: 3.03 us -> 0.09 us  [per_device(): done = jnp.stack(results)]
    reduce_sum x1 -> x0, other arithmetic: 2.09 us -> none  [per_device(): predicted = jnp.sum(jnp.where(at_col, picked_rows, 0.0), axis=2)]
    ppermute x6, waiting for transfers between devices: 12.9 us -> 14.6 us  [butterfly_sum(): lax.ppermute(value, axis, [(i, i ^ bit) for i in range(count)])]
    unnamed x38 -> x39, local copies, waits for them, and re-layouts: 1.82 us -> 3.16 us
  transfers between devices with their start and end apart: 11 -> 11, of which waited for: 9 -> 10; matrix products, arithmetic and copies ran while one was open for 4% -> 3% of each run, Pallas kernels for 0% -> 0%
where the time goes in v7:
time: 141 us
  waiting for transfers between devices  42.4 us (30%)
  blocking collectives  30.7 us (22%)
  starting transfers between devices  28.4 us (20%)
  other arithmetic  20.2 us (14%)
  local copies, waits for them, and re-layouts  15.4 us (11%)
  matrix products  2.95 us (2%)
    all_to_all x1, blocking collectives, per_device(): lax.all_to_all(state.reshape(slices, group, row_count, col_count), 'tm',...  30.7 us
    all_to_all x1, waiting for transfers between devices, per_device(): lax.all_to_all(done, 'tm', 0, 0, tiled=True)  24.1 us
    ppermute x6, starting transfers between devices, butterfly_sum(): lax.ppermute(value, axis, [(i, i ^ bit) for i in range(count)])  17.9 us
    ppermute x6, waiting for transfers between devices, butterfly_sum(): lax.ppermute(value, axis, [(i, i ^ bit) for i in range(count)])  14.6 us
    mul x5, other arithmetic, advance(): return (middle + step_size * tendency) * inside  11.1 us
    slice x7, local copies, waits for them, and re-layouts, advance(): west_cell = jnp.pad(middle[:, :, :-1], ((0, 0), (0, 0), (1, 0)))  5.62 us
    ppermute x1, starting transfers between devices, with_halo(): lax.ppermute(tail, axis, [(i, i + 1) for i in range(ends)])  5.32 us
    all_to_all x1, starting transfers between devices, per_device(): lax.all_to_all(done, 'tm', 0, 0, tiled=True)  3.75 us
  transfers between devices with their start and end apart: 11, of which 10 were waited for; matrix products, arithmetic and copies ran while one was open for 3% of the time, Pallas kernels for 0%

profile of v7, /device:TPU:0, one launch (start us, length us, event | category | flops | bytes accessed | tf_op | source)
XLA Modules:
  0.0 141.0 jit_solution(8300833497402084103)
XLA Ops:
  0.6 30.7 %all_to_all.10 = f32[4,2,64,1024]{3,2,1,0:T(8,128)S(1)} all-to-all(f32[4,2,64,1024]{3,2,1,0:T(8,128)} %bitcast.126), channel_id=1, replica_groups=mesh['tm'=4,'space'=16,'ens'=2] {'tm'}, dimensions={0} | all-to-all | bytes 4194304 | tf_op jit(solution)/shard_map/all_to_all | solution.py:87
  31.6 0.7 copy-done
  32.6 0.9 fusion.48
  33.5 1.3 collective-permute-start.1
  34.8 5.3 %collective-permute-start = (f32[12,7,1024]{2,1,0:T(8,128)}, f32[12,7,1024]{2,1,0:T(8,128)}, u32[]{:S(2)}, u32[]{:S(2)}) collective-permute-start(f32[12,7,1024]{2,1,0:T(8,128)} %get-tuple-element.26), channel_id=1, source_target_pairs={{0,2},{2,4},{4,6},{6,8},{8,10},{10,12},{12,14},{14,16},{16,18},{18... | collective-permute-start | bytes 1032200 | tf_op jit(solution)/shard_map/ppermute | solution.py:21
  40.2 0.6 slice.374
  40.8 0.6 slice.384
  41.4 0.6 slice.394
  42.0 0.6 slice.407
  42.6 0.6 slice.420
  43.2 0.7 slice.429
  44.1 1.3 collective-permute-done.1
  45.4 1.2 collective-permute-done
  46.5 1.7 %pad_maximum_fusion = f32[12,78,1024]{2,1,0:T(8,128)S(1)} fusion(f32[12,7,1024]{2,1,0:T(8,128)} %collective-permute-done.1, f32[12,64,1024]{2,1,0:T(8,128)S(1)} %bitcast_dynamic-update-slice_fusion, f32[12,7,1024]{2,1,0:T(8,128)} %collective-permute-done), kind=kLoop, calls=%fused_computation | loop fusion | flops 1916928 | bytes 7667712 | tf_op jit(solution)/shard_map/concatenate | solution.py:19
  48.4 1.4 fusion.47
  50.8 2.6 %fusion.5 = (f32[8,76,1024]{2,1,0:T(8,128)S(1)}, f32[8,76,1024]{2,1,0:T(8,128)S(1)}) fusion(f32[8,78,1024]{2,1,0:T(8,128)S(1)} %bitcast.119, f32[12,78,1024]{2,1,0:T(8,128)S(1)} %pad_maximum_fusion, f32[76]{0:T(128)S(1)} %slice.364, f32[76,1024]{1,0:T(8,128)S(1)} %get-tuple-element.22, f32[76,1024]{1,0:T(8,128)S(1)} %get-tuple-element.23, ...), kind=kLoop, calls=%fused_computation.8 | loop fusion | flops 11206656 | bytes 20852272 | tf_op jit(solution)/shard_map/mul | solution.py:60
  53.4 0.9 add_multiply_fusion
  54.3 1.4 fusion.51
  55.8 2.6 %fusion.2 = f32[8,74,1024]{2,1,0:T(8,128)S(1)} fusion(f32[8,78,1024]{2,1,0:T(8,128)S(1)} %bitcast.120, f32[8,76,1024]{2,1,0:T(8,128)S(1)} %get-tuple-element.4, f32[8,74,1023]{2,1,0:T(8,128)S(1)} %get-tuple-element.34, f32[8,74,1023]{2,1,0:T(8,128)S(1)} %get-tuple-element.33, f32[74]{0:T(128)S(1)} %copy-done.12, f32[74,1024]{1,0:T(8,128)S(1)} %get-tuple-element.19, ...), kind=kLoop, calls=%fused_computation.4 | loop fusion | flops 10911744 | bytes 17878696 | tf_op jit(solution)/shard_map/mul | solution.py:60
  58.4 1.1 fusion.50
  59.5 2.4 %fusion.11 = f32[8,72,1024]{2,1,0:T(8,128)S(1)} fusion(f32[8,78,1024]{2,1,0:T(8,128)S(1)} %bitcast.121, f32[8,74,1024]{2,1,0:T(8,128)S(1)} %fusion.2, f32[8,72,1023]{2,1,0:T(8,128)S(1)} %get-tuple-element.32, f32[8,72,1023]{2,1,0:T(8,128)S(1)} %get-tuple-element.31, f32[72]{0:T(128)S(1)} %copy-done.8, f32[72,1024]{1,0:T(8,128)S(1)} %get-tuple-element.16, ...), kind=kLoop, calls=%fused_computation.18 | loop fusion | flops 10616832 | bytes 17395488 | tf_op jit(solution)/shard_map/mul | solution.py:60
  61.9 1.1 fusion.54
  63.0 2.5 %fusion.8 = f32[8,70,1024]{2,1,0:T(8,128)S(1)} fusion(f32[8,78,1024]{2,1,0:T(8,128)S(1)} %bitcast.122, f32[8,72,1024]{2,1,0:T(8,128)S(1)} %fusion.11, f32[8,70,1023]{2,1,0:T(8,128)S(1)} %get-tuple-element.41, f32[8,70,1023]{2,1,0:T(8,128)S(1)} %get-tuple-element.40, f32[70]{0:T(128)S(1)} %copy-done.7, f32[70,1024]{1,0:T(8,128)S(1)} %get-tuple-element.13, ...), kind=kLoop, calls=%fused_computation.14 | loop fusion | flops 10321920 | bytes 16912280 | tf_op jit(solution)/shard_map/mul | solution.py:60
  66.4 0.6 fusion.15
  67.6 0.6 fusion.14
  69.2 1.5 %pad_maximum_fusion.1 = f32[4,2,64,1024]{3,2,1,0:T(8,128)} fusion(f32[1,2,64,1024]{3,2,1,0:T(8,128)S(1)} %get-tuple-element.43, f32[1,2,64,1024]{3,2,1,0:T(8,128)S(1)} %get-tuple-element.42, f32[1,2,64,1024]{3,2,1,0:T(8,128)S(1)} %slice_bitcast_fusion, f32[1,2,64,1024]{3,2,1,0:T(8,128)S(1)} %slice_bitcast_fusion.1), kind=kLoop, calls=%fused_computation.19 | loop fusion | flops 1572864 | bytes 4194304 | tf_op jit(solution)/shard_map/stack | solution.py:122
  70.7 3.8 %all-to-all-start.1 = ((f32[4,2,64,1024]{3,2,1,0:T(8,128)}), f32[4,2,64,1024]{3,2,1,0:T(8,128)S(1)}, u32[]{:S(2)}, u32[]{:S(2)}) async-start(f32[4,2,64,1024]{3,2,1,0:T(8,128)} %pad_maximum_fusion.1), calls=%async_computation.1 | async-start | bytes 4194304 | tf_op jit(solution)/shard_map/all_to_all | solution.py:123
  74.5 24.1 %all-to-all-done.1 = f32[4,2,64,1024]{3,2,1,0:T(8,128)S(1)} async-done(((f32[4,2,64,1024]{3,2,1,0:T(8,128)}), f32[4,2,64,1024]{3,2,1,0:T(8,128)S(1)}, u32[]{:S(2)}, u32[]{:S(2)}) %all-to-all-start.1) | async-done | bytes 2097184 | tf_op jit(solution)/shard_map/all_to_all | solution.py:123
  98.7 1.5 %fusion.12 = f32[8,64]{1,0:T(8,128)S(1)} fusion(f32[8,64,1024]{2,1,0:T(8,128)S(1)} %bitcast.123, s32[64]{0:T(128)S(1)} %and_select_fusion.1, s32[64]{0:T(128)S(1)} %get-tuple-element.2), kind=kOutput, calls=%fused_computation.21 | convolution fusion | flops 404229632 | bytes 2099712 | tf_op jit(solution)/shard_map/or,mrc->moc/dot_general | solution.py:132
  100.3 1.1 collective-permute-done.2
  101.7 0.7 collective-permute-start.3
  102.4 3.2 %collective-permute-done.3 = f32[2,16,16]{2,1,0:T(8,128)S(1)} collective-permute-done((f32[2,16,16]{2,1,0:T(8,128)S(1)}, f32[2,16,16]{2,1,0:T(8,128)S(1)}, u32[]{:S(2)}, u32[]{:S(2)}) %collective-permute-start.3) | collective-permute-done | bytes 2080 | tf_op jit(solution)/shard_map/ppermute | solution.py:35
  105.5 0.6 collective-permute-start.4
  106.2 4.6 %collective-permute-done.4 = f32[2,16,16]{2,1,0:T(8,128)S(1)} collective-permute-done((f32[2,16,16]{2,1,0:T(8,128)S(1)}, f32[2,16,16]{2,1,0:T(8,128)S(1)}, u32[]{:S(2)}, u32[]{:S(2)}) %collective-permute-start.4) | collective-permute-done | bytes 2080 | tf_op jit(solution)/shard_map/ppermute | solution.py:35
  110.8 2.5 %collective-permute-start.5 = (f32[2,16,16]{2,1,0:T(8,128)S(1)}, f32[2,16,16]{2,1,0:T(8,128)S(1)}, u32[]{:S(2)}, u32[]{:S(2)}) collective-permute-start(f32[2,16,16]{2,1,0:T(8,128)S(1)} %fusion.59), channel_id=1, source_target_pairs={{0,2},{2,0},{4,6},{6,4},{8,10},{10,8},{12,14},{14,12},{16,18},{18,... | collective-permute-start | bytes 6152 | tf_op jit(solution)/shard_map/ppermute | solution.py:35
  113.3 1.7 %collective-permute-done.5 = f32[2,16,16]{2,1,0:T(8,128)S(1)} collective-permute-done((f32[2,16,16]{2,1,0:T(8,128)S(1)}, f32[2,16,16]{2,1,0:T(8,128)S(1)}, u32[]{:S(2)}, u32[]{:S(2)}) %collective-permute-start.5) | collective-permute-done | bytes 2080 | tf_op jit(solution)/shard_map/ppermute | solution.py:35
  115.0 4.3 %collective-permute-start.6 = (f32[2,16,16]{2,1,0:T(8,128)S(1)}, f32[2,16,16]{2,1,0:T(8,128)S(1)}, u32[]{:S(2)}, u32[]{:S(2)}) collective-permute-start(f32[2,16,16]{2,1,0:T(8,128)S(1)} %add.265), channel_id=1, source_target_pairs={{0,4},{2,6},{4,0},{6,2},{8,12},{10,14},{12,8},{14,10},{16,20},{18,... | collective-permute-start | bytes 6152 | tf_op jit(solution)/shard_map/ppermute | solution.py:35
  119.3 1.7 %collective-permute-done.6 = f32[2,16,16]{2,1,0:T(8,128)S(1)} collective-permute-done((f32[2,16,16]{2,1,0:T(8,128)S(1)}, f32[2,16,16]{2,1,0:T(8,128)S(1)}, u32[]{:S(2)}, u32[]{:S(2)}) %collective-permute-start.6) | collective-permute-done | bytes 2080 | tf_op jit(solution)/shard_map/ppermute | solution.py:35
  121.0 5.9 %collective-permute-start.7 = (f32[2,16,16]{2,1,0:T(8,128)S(1)}, f32[2,16,16]{2,1,0:T(8,128)S(1)}, u32[]{:S(2)}, u32[]{:S(2)}) collective-permute-start(f32[2,16,16]{2,1,0:T(8,128)S(1)} %add.266), channel_id=1, source_target_pairs={{0,8},{2,10},{4,12},{6,14},{8,0},{10,2},{12,4},{14,6},{16,24},{18,... | collective-permute-start | bytes 6152 | tf_op jit(solution)/shard_map/ppermute | solution.py:35
  126.9 1.7 %collective-permute-done.7 = f32[2,16,16]{2,1,0:T(8,128)S(1)} collective-permute-done((f32[2,16,16]{2,1,0:T(8,128)S(1)}, f32[2,16,16]{2,1,0:T(8,128)S(1)}, u32[]{:S(2)}, u32[]{:S(2)}) %collective-permute-start.7) | collective-permute-done | bytes 2080 | tf_op jit(solution)/shard_map/ppermute | solution.py:35
  128.6 4.0 %collective-permute-start.8 = (f32[2,16,16]{2,1,0:T(8,128)S(1)}, f32[2,16,16]{2,1,0:T(8,128)S(1)}, u32[]{:S(2)}, u32[]{:S(2)}) collective-permute-start(f32[2,16,16]{2,1,0:T(8,128)S(1)} %add.267), channel_id=1, source_target_pairs={{0,16},{2,18},{4,20},{6,22},{8,24},{10,26},{12,28},{14,30},{16,0},... | collective-permute-start | bytes 6152 | tf_op jit(solution)/shard_map/ppermute | solution.py:35
  132.6 1.7 %collective-permute-done.8 = f32[2,16,16]{2,1,0:T(8,128)S(1)} collective-permute-done((f32[2,16,16]{2,1,0:T(8,128)S(1)}, f32[2,16,16]{2,1,0:T(8,128)S(1)}, u32[]{:S(2)}, u32[]{:S(2)}) %collective-permute-start.8) | collective-permute-done | bytes 2080 | tf_op jit(solution)/shard_map/ppermute | solution.py:35
  134.4 1.5 %cholesky.17 = f32[16,16]{1,0:T(8,128)S(1)} custom-call(f32[16,16]{1,0:T(8,128)S(1)} %fusion.27), custom_call_target="Cholesky" | custom-call | tf_op jit(solution)/shard_map/jit(cholesky)/cholesky | solution.py:150
  135.9 0.6 compare_reduce_fusion
  136.6 0.6 fusion.21
  137.2 1.2 custom-call.10
  138.8 0.9 fusion.13
  139.7 1.3 copy.19
  (84 shorter events, 5.3 us)
Async XLA Ops:
  31.3 1.0 copy-start
  31.3 1.0 copy-start.1
  31.4 1.1 copy-start.3
  31.4 1.2 copy-start.5
  32.3 11.6 %copy-start.6 = (f32[8,128]{1,0:T(8,128)S(1)}, f32[8,128]{1,0:T(8,128)}, u32[]{:S(2)}) copy-start(f32[8,128]{1,0:T(8,128)} %param.15) | copy-start | bytes 12292
  33.5 11.9 %collective-permute-start.1 = (f32[12,7,1024]{2,1,0:T(8,128)}, f32[12,7,1024]{2,1,0:T(8,128)}, u32[]{:S(2)}, u32[]{:S(2)}) collective-permute-start(f32[12,7,1024]{2,1,0:T(8,128)} %get-tuple-element.27), channel_id=1, source_target_pairs={{2,0},{4,2},{6,4},{8,6},{10,8},{12,10},{14,12},{16,14},{18,16},{20... | collective-permute-start | bytes 1032200 | tf_op jit(solution)/shard_map/ppermute | solution.py:23
  34.8 11.8 %collective-permute-start = (f32[12,7,1024]{2,1,0:T(8,128)}, f32[12,7,1024]{2,1,0:T(8,128)}, u32[]{:S(2)}, u32[]{:S(2)}) collective-permute-start(f32[12,7,1024]{2,1,0:T(8,128)} %get-tuple-element.26), channel_id=1, source_target_pairs={{0,2},{2,4},{4,6},{6,8},{8,10},{10,12},{12,14},{14,16},{16,18},{18... | collective-permute-start | bytes 1032200 | tf_op jit(solution)/shard_map/ppermute | solution.py:21
  54.3 1.4 %copy-start.12 = (f32[74]{0:T(128)S(1)}, f32[74]{0:T(128)}, u32[]{:S(2)}) copy-start(f32[74]{0:T(128)} %slice.374) | copy-start | bytes 892
  58.4 1.1 copy-start.8
  61.9 1.1 copy-start.7
  65.8 0.6 copy-start.11
  67.0 0.6 copy-start.10
  67.6 0.9 copy-start.2
  67.6 1.0 copy-start.4
  67.6 1.0 copy-start.9
  70.7 3.8 %copy-start.13 = (s32[1,64]{1,0:T(1,128)S(1)}, s32[1,64]{1,0:T(1,128)}, u32[]{:S(2)}) copy-start(s32[1,64]{1,0:T(1,128)} %param.16) | copy-start | bytes 772
  70.7 29.5 %copy-start.15 = (f32[1,64]{1,0:T(1,128)S(1)}, f32[1,64]{1,0:T(1,128)}, u32[]{:S(2)}) copy-start(f32[1,64]{1,0:T(1,128)} %param.19) | copy-start | bytes 772
  70.7 30.8 %copy-start.14 = (f32[1,64,16]{1,2,0:T(8,128)S(1)}, f32[1,64,16]{1,2,0:T(8,128)}, u32[]{:S(2)}) copy-start(f32[1,64,16]{1,2,0:T(8,128)} %param.18) | copy-start | bytes 12292
  70.7 30.8 %copy-start.16 = (f32[1,64]{1,0:T(1,128)S(1)}, f32[1,64]{1,0:T(1,128)}, u32[]{:S(2)}) copy-start(f32[1,64]{1,0:T(1,128)} %param.17) | copy-start | bytes 772
  70.7 27.9 %all-to-all-start.1 = ((f32[4,2,64,1024]{3,2,1,0:T(8,128)}), f32[4,2,64,1024]{3,2,1,0:T(8,128)S(1)}, u32[]{:S(2)}, u32[]{:S(2)}) async-start(f32[4,2,64,1024]{3,2,1,0:T(8,128)} %pad_maximum_fusion.1), calls=%async_computation.1 | async-start | bytes 4194304 | tf_op jit(solution)/shard_map/all_to_all | solution.py:123
  100.1 1.2 collective-permute-start.2
  101.7 3.8 %collective-permute-start.3 = (f32[2,16,16]{2,1,0:T(8,128)S(1)}, f32[2,16,16]{2,1,0:T(8,128)S(1)}, u32[]{:S(2)}, u32[]{:S(2)}) collective-permute-start(f32[2,16,16]{2,1,0:T(8,128)S(1)} %pad_maximum_fusion.2), channel_id=1, source_target_pairs={{0,32},{32,0},{64,96},{96,64},{1,33},{33,1},{65,97},{97,65},{2,34}... | collective-permute-start | bytes 6152 | tf_op jit(solution)/shard_map/ppermute | solution.py:35
  105.5 5.2 %collective-permute-start.4 = (f32[2,16,16]{2,1,0:T(8,128)S(1)}, f32[2,16,16]{2,1,0:T(8,128)S(1)}, u32[]{:S(2)}, u32[]{:S(2)}) collective-permute-start(f32[2,16,16]{2,1,0:T(8,128)S(1)} %fusion.46), channel_id=1, source_target_pairs={{0,64},{32,96},{64,0},{96,32},{1,65},{33,97},{65,1},{97,33},{2,66}... | collective-permute-start | bytes 6152 | tf_op jit(solution)/shard_map/ppermute | solution.py:35
  110.8 4.2 %collective-permute-start.5 = (f32[2,16,16]{2,1,0:T(8,128)S(1)}, f32[2,16,16]{2,1,0:T(8,128)S(1)}, u32[]{:S(2)}, u32[]{:S(2)}) collective-permute-start(f32[2,16,16]{2,1,0:T(8,128)S(1)} %fusion.59), channel_id=1, source_target_pairs={{0,2},{2,0},{4,6},{6,4},{8,10},{10,8},{12,14},{14,12},{16,18},{18,... | collective-permute-start | bytes 6152 | tf_op jit(solution)/shard_map/ppermute | solution.py:35
  113.3 13.6 %collective-permute-start.9 = (f32[8,128]{1,0:T(8,128)S(1)}, f32[8,128]{1,0:T(8,128)S(1)}, u32[]{:S(2)}, u32[]{:S(2)}) collective-permute-start(f32[8,128]{1,0:T(8,128)S(1)} %copy-done.6), channel_id=1, source_target_pairs={{0,1},{1,0},{2,3},{3,2},{4,5},{5,4},{6,7},{7,6},{8,9},{9,8},{10,11... | collective-permute-start | bytes 12296 | tf_op jit(solution)/shard_map/ppermute | solution.py:41
  115.0 6.0 %collective-permute-start.6 = (f32[2,16,16]{2,1,0:T(8,128)S(1)}, f32[2,16,16]{2,1,0:T(8,128)S(1)}, u32[]{:S(2)}, u32[]{:S(2)}) collective-permute-start(f32[2,16,16]{2,1,0:T(8,128)S(1)} %add.265), channel_id=1, source_target_pairs={{0,4},{2,6},{4,0},{6,2},{8,12},{10,14},{12,8},{14,10},{16,20},{18,... | collective-permute-start | bytes 6152 | tf_op jit(solution)/shard_map/ppermute | solution.py:35
  121.0 7.6 %collective-permute-start.7 = (f32[2,16,16]{2,1,0:T(8,128)S(1)}, f32[2,16,16]{2,1,0:T(8,128)S(1)}, u32[]{:S(2)}, u32[]{:S(2)}) collective-permute-start(f32[2,16,16]{2,1,0:T(8,128)S(1)} %add.266), channel_id=1, source_target_pairs={{0,8},{2,10},{4,12},{6,14},{8,0},{10,2},{12,4},{14,6},{16,24},{18,... | collective-permute-start | bytes 6152 | tf_op jit(solution)/shard_map/ppermute | solution.py:35
  128.6 5.7 %collective-permute-start.8 = (f32[2,16,16]{2,1,0:T(8,128)S(1)}, f32[2,16,16]{2,1,0:T(8,128)S(1)}, u32[]{:S(2)}, u32[]{:S(2)}) collective-permute-start(f32[2,16,16]{2,1,0:T(8,128)S(1)} %add.267), channel_id=1, source_target_pairs={{0,16},{2,18},{4,20},{6,22},{8,24},{10,26},{12,28},{14,30},{16,0},... | collective-permute-start | bytes 6152 | tf_op jit(solution)/shard_map/ppermute | solution.py:35

commit v8 on v7

--- a/solution.py
+++ b/solution.py
@@ -26,14 +26,22 @@
     )
 
 
-def butterfly_sum(value, axis):
+def quad_sum(value, axis):
     count = lax.axis_size(axis)
     if count & (count - 1):
         return lax.psum(value, axis)
     bit = 1
     while bit < count:
-        value = value + lax.ppermute(value, axis, [(i, i ^ bit) for i in range(count)])
-        bit *= 2
+        if bit * 4 <= count:
+            near, far, both = (
+                lax.ppermute(value, axis, [(i, i ^ (k * bit)) for i in range(count)])
+                for k in (1, 2, 3)
+            )
+            value = (value + near) + (far + both)
+            bit *= 4
+        else:
+            value = value + lax.ppermute(value, axis, [(i, i ^ bit) for i in range(count)])
+            bit *= 2
     return value
 
 
@@ -143,8 +151,8 @@
     gram = jnp.dot(anomaly, anomaly.T, precision=lax.Precision.HIGHEST)
     cross = jnp.dot(anomaly, misfit.T, precision=lax.Precision.HIGHEST)
     sums = jnp.stack([gram, cross])
-    sums = butterfly_sum(sums, "tm")
-    sums = butterfly_sum(sums, "space")
+    sums = quad_sum(sums, "tm")
+    sums = quad_sum(sums, "space")
     gram, cross = sums[0], sums[1]
     system = jnp.eye(total, dtype=jnp.float32) + gram
     factor = jnp.linalg.cholesky(system)

time: 141 us -> 136 us (0.965)
  waiting for transfers between devices: 42.4 us -> 37.9 us
  starting transfers between devices: 28.4 us -> 26.7 us
    ppermute x6 -> x9, waiting for transfers between devices: 14.6 us -> 10.2 us  [quad_sum(): lax.ppermute(value, axis, [(i, i ^ k * bit) for i in range(count)])]
    ppermute x6 -> x9, starting transfers between devices: 17.9 us -> 16.2 us  [quad_sum(): lax.ppermute(value, axis, [(i, i ^ k * bit) for i in range(count)])]
  transfers between devices with their start and end apart: 11 -> 14, of which waited for: 10 -> 10; matrix products, arithmetic and copies ran while one was open for 3% -> 3% of each run, Pallas kernels for 0% -> 0%
where the time goes in v8:
time: 136 us; the launch traced here: 135 us
  waiting for transfers between devices  37.9 us (28%)
  blocking collectives  30.7 us (23%)
  starting transfers between devices  26.7 us (20%)
  other arithmetic  20.2 us (15%)
  local copies, waits for them, and re-layouts  15.3 us (11%)
  matrix products  2.95 us (2%)
    all_to_all x1, blocking collectives, per_device(): lax.all_to_all(state.reshape(slices, group, row_count, col_count), 'tm',...  30.7 us
    all_to_all x1, waiting for transfers between devices, per_device(): lax.all_to_all(done, 'tm', 0, 0, tiled=True)  24.1 us
    ppermute x9, starting transfers between devices, quad_sum(): lax.ppermute(value, axis, [(i, i ^ k * bit) for i in range(count)])  16.2 us
    mul x5, other arithmetic, advance(): return (middle + step_size * tendency) * inside  11.1 us
    ppermute x9, waiting for transfers between devices, quad_sum(): lax.ppermute(value, axis, [(i, i ^ k * bit) for i in range(count)])  10.2 us
    slice x7, local copies, waits for them, and re-layouts, advance(): west_cell = jnp.pad(middle[:, :, :-1], ((0, 0), (0, 0), (1, 0)))  5.62 us
    ppermute x1, starting transfers between devices, with_halo(): lax.ppermute(tail, axis, [(i, i + 1) for i in range(ends)])  5.32 us
    slice x7, local copies, waits for them, and re-layouts, step(): wide_inside[lo:hi]  3.76 us
  transfers between devices with their start and end apart: 14, of which 10 were waited for; matrix products, arithmetic and copies ran while one was open for 3% of the time, Pallas kernels for 0%

profile of v8, /device:TPU:0, one launch (start us, length us, event | category | flops | bytes accessed | tf_op | source)
XLA Modules:
  0.0 134.8 jit_solution(6578225094745807486)
XLA Ops:
  0.6 30.7 %all_to_all.10 = f32[4,2,64,1024]{3,2,1,0:T(8,128)S(1)} all-to-all(f32[4,2,64,1024]{3,2,1,0:T(8,128)} %bitcast.126), channel_id=1, replica_groups=mesh['tm'=4,'space'=16,'ens'=2] {'tm'}, dimensions={0} | all-to-all | bytes 4194304 | tf_op jit(solution)/shard_map/all_to_all | solution.py:95
  31.6 0.7 copy-done
  32.6 0.9 fusion.47
  33.5 1.3 collective-permute-start.1
  34.8 5.3 %collective-permute-start = (f32[12,7,1024]{2,1,0:T(8,128)}, f32[12,7,1024]{2,1,0:T(8,128)}, u32[]{:S(2)}, u32[]{:S(2)}) collective-permute-start(f32[12,7,1024]{2,1,0:T(8,128)} %get-tuple-element.26), channel_id=1, source_target_pairs={{0,2},{2,4},{4,6},{6,8},{8,10},{10,12},{12,14},{14,16},{16,18},{18... | collective-permute-start | bytes 1032200 | tf_op jit(solution)/shard_map/ppermute | solution.py:21
  40.2 0.6 slice.374
  40.8 0.6 slice.384
  41.4 0.7 slice.394
  42.0 0.6 slice.407
  42.6 0.6 slice.420
  43.2 0.7 slice.429
  44.1 1.3 collective-permute-done.1
  45.4 1.2 collective-permute-done
  46.5 1.7 %pad_maximum_fusion = f32[12,78,1024]{2,1,0:T(8,128)S(1)} fusion(f32[12,7,1024]{2,1,0:T(8,128)} %collective-permute-done.1, f32[12,64,1024]{2,1,0:T(8,128)S(1)} %bitcast_dynamic-update-slice_fusion, f32[12,7,1024]{2,1,0:T(8,128)} %collective-permute-done), kind=kLoop, calls=%fused_computation | loop fusion | flops 1916928 | bytes 7667712 | tf_op jit(solution)/shard_map/concatenate | solution.py:19
  48.4 1.4 %fusion.46 = (f32[8,76,1023]{2,1,0:T(8,128)S(1)}, f32[8,76,1023]{2,1,0:T(8,128)S(1)}) fusion(f32[12,78,1024]{2,1,0:T(8,128)S(1)} %pad_maximum_fusion), kind=kLoop, calls=%fused_computation.118 | loop fusion | bytes 9951744 | tf_op jit(solution)/shard_map/slice | solution.py:58
  50.8 2.6 %fusion.5 = (f32[8,76,1024]{2,1,0:T(8,128)S(1)}, f32[8,76,1024]{2,1,0:T(8,128)S(1)}) fusion(f32[8,78,1024]{2,1,0:T(8,128)S(1)} %bitcast.119, f32[12,78,1024]{2,1,0:T(8,128)S(1)} %pad_maximum_fusion, f32[76]{0:T(128)S(1)} %slice.364, f32[76,1024]{1,0:T(8,128)S(1)} %get-tuple-element.22, f32[76,1024]{1,0:T(8,128)S(1)} %get-tuple-element.23, ...), kind=kLoop, calls=%fused_computation.8 | loop fusion | flops 11206656 | bytes 20852272 | tf_op jit(solution)/shard_map/mul | solution.py:68
  53.4 0.9 add_multiply_fusion
  54.3 1.4 %fusion.50 = (f32[8,74,1023]{2,1,0:T(8,128)S(1)}, f32[8,74,1023]{2,1,0:T(8,128)S(1)}) fusion(f32[8,76,1024]{2,1,0:T(8,128)S(1)} %get-tuple-element.4), kind=kLoop, calls=%fused_computation.122 | loop fusion | bytes 9689856 | tf_op jit(solution)/shard_map/slice | solution.py:58
  55.8 2.6 %fusion.2 = f32[8,74,1024]{2,1,0:T(8,128)S(1)} fusion(f32[8,78,1024]{2,1,0:T(8,128)S(1)} %bitcast.120, f32[8,76,1024]{2,1,0:T(8,128)S(1)} %get-tuple-element.4, f32[8,74,1023]{2,1,0:T(8,128)S(1)} %get-tuple-element.34, f32[8,74,1023]{2,1,0:T(8,128)S(1)} %get-tuple-element.33, f32[74]{0:T(128)S(1)} %copy-done.12, f32[74,1024]{1,0:T(8,128)S(1)} %get-tuple-element.19, ...), kind=kLoop, calls=%fused_computation.4 | loop fusion | flops 10911744 | bytes 17878696 | tf_op jit(solution)/shard_map/mul | solution.py:68
  58.4 1.1 fusion.49
  59.5 2.4 %fusion.11 = f32[8,72,1024]{2,1,0:T(8,128)S(1)} fusion(f32[8,78,1024]{2,1,0:T(8,128)S(1)} %bitcast.121, f32[8,74,1024]{2,1,0:T(8,128)S(1)} %fusion.2, f32[8,72,1023]{2,1,0:T(8,128)S(1)} %get-tuple-element.32, f32[8,72,1023]{2,1,0:T(8,128)S(1)} %get-tuple-element.31, f32[72]{0:T(128)S(1)} %copy-done.8, f32[72,1024]{1,0:T(8,128)S(1)} %get-tuple-element.16, ...), kind=kLoop, calls=%fused_computation.18 | loop fusion | flops 10616832 | bytes 17395488 | tf_op jit(solution)/shard_map/mul | solution.py:68
  61.9 1.1 fusion.53
  63.0 2.5 %fusion.8 = f32[8,70,1024]{2,1,0:T(8,128)S(1)} fusion(f32[8,78,1024]{2,1,0:T(8,128)S(1)} %bitcast.122, f32[8,72,1024]{2,1,0:T(8,128)S(1)} %fusion.11, f32[8,70,1023]{2,1,0:T(8,128)S(1)} %get-tuple-element.41, f32[8,70,1023]{2,1,0:T(8,128)S(1)} %get-tuple-element.40, f32[70]{0:T(128)S(1)} %copy-done.7, f32[70,1024]{1,0:T(8,128)S(1)} %get-tuple-element.13, ...), kind=kLoop, calls=%fused_computation.14 | loop fusion | flops 10321920 | bytes 16912280 | tf_op jit(solution)/shard_map/mul | solution.py:68
  66.4 0.6 fusion.15
  67.6 0.6 fusion.14
  69.2 1.5 %pad_maximum_fusion.1 = f32[4,2,64,1024]{3,2,1,0:T(8,128)} fusion(f32[1,2,64,1024]{3,2,1,0:T(8,128)S(1)} %get-tuple-element.43, f32[1,2,64,1024]{3,2,1,0:T(8,128)S(1)} %get-tuple-element.42, f32[1,2,64,1024]{3,2,1,0:T(8,128)S(1)} %slice_bitcast_fusion, f32[1,2,64,1024]{3,2,1,0:T(8,128)S(1)} %slice_bitcast_fusion.1), kind=kLoop, calls=%fused_computation.19 | loop fusion | flops 1572864 | bytes 4194304 | tf_op jit(solution)/shard_map/stack | solution.py:130
  70.7 3.8 %all-to-all-start.1 = ((f32[4,2,64,1024]{3,2,1,0:T(8,128)}), f32[4,2,64,1024]{3,2,1,0:T(8,128)S(1)}, u32[]{:S(2)}, u32[]{:S(2)}) async-start(f32[4,2,64,1024]{3,2,1,0:T(8,128)} %pad_maximum_fusion.1), calls=%async_computation.1 | async-start | bytes 4194304 | tf_op jit(solution)/shard_map/all_to_all | solution.py:131
  74.5 24.1 %all-to-all-done.1 = f32[4,2,64,1024]{3,2,1,0:T(8,128)S(1)} async-done(((f32[4,2,64,1024]{3,2,1,0:T(8,128)}), f32[4,2,64,1024]{3,2,1,0:T(8,128)S(1)}, u32[]{:S(2)}, u32[]{:S(2)}) %all-to-all-start.1) | async-done | bytes 2097184 | tf_op jit(solution)/shard_map/all_to_all | solution.py:131
  98.6 1.5 %fusion.12 = f32[8,64]{1,0:T(8,128)S(1)} fusion(f32[8,64,1024]{2,1,0:T(8,128)S(1)} %bitcast.123, s32[64]{0:T(128)S(1)} %and_select_fusion.1, s32[64]{0:T(128)S(1)} %get-tuple-element.2), kind=kOutput, calls=%fused_computation.21 | convolution fusion | flops 404229632 | bytes 2099712 | tf_op jit(solution)/shard_map/or,mrc->moc/dot_general | solution.py:140
  100.2 1.1 collective-permute-done.2
  101.7 0.6 collective-permute-start.4
  102.3 2.7 %collective-permute-start.5 = (f32[2,16,16]{2,1,0:T(8,128)S(1)}, f32[2,16,16]{2,1,0:T(8,128)S(1)}, u32[]{:S(2)}, u32[]{:S(2)}) collective-permute-start(f32[2,16,16]{2,1,0:T(8,128)S(1)} %pad_maximum_fusion.2), channel_id=1, source_target_pairs={{0,96},{32,64},{64,32},{96,0},{1,97},{33,65},{65,33},{97,1},{2,98}... | collective-permute-start | bytes 6152 | tf_op jit(solution)/shard_map/ppermute | solution.py:37
  105.2 1.8 %collective-permute-done.4 = f32[2,16,16]{2,1,0:T(8,128)S(1)} collective-permute-done((f32[2,16,16]{2,1,0:T(8,128)S(1)}, f32[2,16,16]{2,1,0:T(8,128)S(1)}, u32[]{:S(2)}, u32[]{:S(2)}) %collective-permute-start.4) | collective-permute-done | bytes 2080 | tf_op jit(solution)/shard_map/ppermute | solution.py:37
  107.3 1.5 %collective-permute-done.3 = f32[2,16,16]{2,1,0:T(8,128)S(1)} collective-permute-done((f32[2,16,16]{2,1,0:T(8,128)S(1)}, f32[2,16,16]{2,1,0:T(8,128)S(1)}, u32[]{:S(2)}, u32[]{:S(2)}) %collective-permute-start.3) | collective-permute-done | bytes 2080 | tf_op jit(solution)/shard_map/ppermute | solution.py:37
  108.7 4.2 %collective-permute-start.7 = (f32[2,16,16]{2,1,0:T(8,128)S(1)}, f32[2,16,16]{2,1,0:T(8,128)S(1)}, u32[]{:S(2)}, u32[]{:S(2)}) collective-permute-start(f32[2,16,16]{2,1,0:T(8,128)S(1)} %add_add_fusion.2), channel_id=1, source_target_pairs={{0,4},{2,6},{4,0},{6,2},{8,12},{10,14},{12,8},{14,10},{16,20},{18,... | collective-permute-start | bytes 6152 | tf_op jit(solution)/shard_map/ppermute | solution.py:37
  112.9 1.1 collective-permute-start.8
  114.0 0.8 collective-permute-start.6
  114.8 3.0 %collective-permute-done.8 = f32[2,16,16]{2,1,0:T(8,128)S(1)} collective-permute-done((f32[2,16,16]{2,1,0:T(8,128)S(1)}, f32[2,16,16]{2,1,0:T(8,128)S(1)}, u32[]{:S(2)}, u32[]{:S(2)}) %collective-permute-start.8) | collective-permute-done | bytes 2080 | tf_op jit(solution)/shard_map/ppermute | solution.py:37
  117.9 5.3 %collective-permute-start.10 = (f32[2,16,16]{2,1,0:T(8,128)S(1)}, f32[2,16,16]{2,1,0:T(8,128)S(1)}, u32[]{:S(2)}, u32[]{:S(2)}) collective-permute-start(f32[2,16,16]{2,1,0:T(8,128)S(1)} %add_add_fusion.1), channel_id=1, source_target_pairs={{0,16},{2,18},{4,20},{6,22},{8,24},{10,26},{12,28},{14,30},{16,0},... | collective-permute-start | bytes 6152 | tf_op jit(solution)/shard_map/ppermute | solution.py:37
  123.2 0.7 collective-permute-start.11
  123.9 0.6 collective-permute-start.9
  124.9 3.2 %collective-permute-done.11 = f32[2,16,16]{2,1,0:T(8,128)S(1)} collective-permute-done((f32[2,16,16]{2,1,0:T(8,128)S(1)}, f32[2,16,16]{2,1,0:T(8,128)S(1)}, u32[]{:S(2)}, u32[]{:S(2)}) %collective-permute-start.11) | collective-permute-done | bytes 2080 | tf_op jit(solution)/shard_map/ppermute | solution.py:37
  128.2 1.5 %cholesky.17 = f32[16,16]{1,0:T(8,128)S(1)} custom-call(f32[16,16]{1,0:T(8,128)S(1)} %fusion.27), custom_call_target="Cholesky" | custom-call | tf_op jit(solution)/shard_map/jit(cholesky)/cholesky | solution.py:158
  129.7 0.6 compare_reduce_fusion
  130.3 0.6 fusion.21
  131.0 1.2 custom-call.10
  132.6 0.9 fusion.13
  133.5 1.3 copy.19
  (87 shorter events, 6.1 us)
Async XLA Ops:
  31.3 1.0 copy-start
  31.3 1.0 copy-start.1
  31.4 1.1 copy-start.3
  31.4 1.2 copy-start.5
  32.3 11.6 %copy-start.6 = (f32[8,128]{1,0:T(8,128)S(1)}, f32[8,128]{1,0:T(8,128)}, u32[]{:S(2)}) copy-start(f32[8,128]{1,0:T(8,128)} %param.15) | copy-start | bytes 12292
  33.5 11.9 %collective-permute-start.1 = (f32[12,7,1024]{2,1,0:T(8,128)}, f32[12,7,1024]{2,1,0:T(8,128)}, u32[]{:S(2)}, u32[]{:S(2)}) collective-permute-start(f32[12,7,1024]{2,1,0:T(8,128)} %get-tuple-element.27), channel_id=1, source_target_pairs={{2,0},{4,2},{6,4},{8,6},{10,8},{12,10},{14,12},{16,14},{18,16},{20... | collective-permute-start | bytes 1032200 | tf_op jit(solution)/shard_map/ppermute | solution.py:23
  34.8 11.8 %collective-permute-start = (f32[12,7,1024]{2,1,0:T(8,128)}, f32[12,7,1024]{2,1,0:T(8,128)}, u32[]{:S(2)}, u32[]{:S(2)}) collective-permute-start(f32[12,7,1024]{2,1,0:T(8,128)} %get-tuple-element.26), channel_id=1, source_target_pairs={{0,2},{2,4},{4,6},{6,8},{8,10},{10,12},{12,14},{14,16},{16,18},{18... | collective-permute-start | bytes 1032200 | tf_op jit(solution)/shard_map/ppermute | solution.py:21
  54.3 1.4 %copy-start.12 = (f32[74]{0:T(128)S(1)}, f32[74]{0:T(128)}, u32[]{:S(2)}) copy-start(f32[74]{0:T(128)} %slice.374) | copy-start | bytes 892
  58.4 1.1 copy-start.8
  61.9 1.1 copy-start.7
  65.8 0.6 copy-start.11
  67.0 0.6 copy-start.10
  67.6 0.9 copy-start.2
  67.6 1.0 copy-start.4
  67.6 1.0 copy-start.9
  70.7 3.8 %copy-start.13 = (s32[1,64]{1,0:T(1,128)S(1)}, s32[1,64]{1,0:T(1,128)}, u32[]{:S(2)}) copy-start(s32[1,64]{1,0:T(1,128)} %param.16) | copy-start | bytes 772
  70.7 29.5 %copy-start.15 = (f32[1,64]{1,0:T(1,128)S(1)}, f32[1,64]{1,0:T(1,128)}, u32[]{:S(2)}) copy-start(f32[1,64]{1,0:T(1,128)} %param.19) | copy-start | bytes 772
  70.7 30.8 %copy-start.14 = (f32[1,64,16]{1,2,0:T(8,128)S(1)}, f32[1,64,16]{1,2,0:T(8,128)}, u32[]{:S(2)}) copy-start(f32[1,64,16]{1,2,0:T(8,128)} %param.18) | copy-start | bytes 12292
  70.7 30.8 %copy-start.16 = (f32[1,64]{1,0:T(1,128)S(1)}, f32[1,64]{1,0:T(1,128)}, u32[]{:S(2)}) copy-start(f32[1,64]{1,0:T(1,128)} %param.17) | copy-start | bytes 772
  70.7 27.9 %all-to-all-start.1 = ((f32[4,2,64,1024]{3,2,1,0:T(8,128)}), f32[4,2,64,1024]{3,2,1,0:T(8,128)S(1)}, u32[]{:S(2)}, u32[]{:S(2)}) async-start(f32[4,2,64,1024]{3,2,1,0:T(8,128)} %pad_maximum_fusion.1), calls=%async_computation.1 | async-start | bytes 4194304 | tf_op jit(solution)/shard_map/all_to_all | solution.py:131
  100.1 1.2 collective-permute-start.2
  101.7 5.3 %collective-permute-start.4 = (f32[2,16,16]{2,1,0:T(8,128)S(1)}, f32[2,16,16]{2,1,0:T(8,128)S(1)}, u32[]{:S(2)}, u32[]{:S(2)}) collective-permute-start(f32[2,16,16]{2,1,0:T(8,128)S(1)} %pad_maximum_fusion.2), channel_id=1, source_target_pairs={{0,64},{32,96},{64,0},{96,32},{1,65},{33,97},{65,1},{97,33},{2,66}... | collective-permute-start | bytes 6152 | tf_op jit(solution)/shard_map/ppermute | solution.py:37
  102.3 4.9 %collective-permute-start.5 = (f32[2,16,16]{2,1,0:T(8,128)S(1)}, f32[2,16,16]{2,1,0:T(8,128)S(1)}, u32[]{:S(2)}, u32[]{:S(2)}) collective-permute-start(f32[2,16,16]{2,1,0:T(8,128)S(1)} %pad_maximum_fusion.2), channel_id=1, source_target_pairs={{0,96},{32,64},{64,32},{96,0},{1,97},{33,65},{65,33},{97,1},{2,98}... | collective-permute-start | bytes 6152 | tf_op jit(solution)/shard_map/ppermute | solution.py:37
  105.0 3.7 %collective-permute-start.3 = (f32[2,16,16]{2,1,0:T(8,128)S(1)}, f32[2,16,16]{2,1,0:T(8,128)S(1)}, u32[]{:S(2)}, u32[]{:S(2)}) collective-permute-start(f32[2,16,16]{2,1,0:T(8,128)S(1)} %pad_maximum_fusion.2), channel_id=1, source_target_pairs={{0,32},{32,0},{64,96},{96,64},{1,33},{33,1},{65,97},{97,65},{2,34}... | collective-permute-start | bytes 6152 | tf_op jit(solution)/shard_map/ppermute | solution.py:37
  105.2 9.6 %collective-permute-start.12 = (f32[8,128]{1,0:T(8,128)S(1)}, f32[8,128]{1,0:T(8,128)S(1)}, u32[]{:S(2)}, u32[]{:S(2)}) collective-permute-start(f32[8,128]{1,0:T(8,128)S(1)} %copy-done.6), channel_id=1, source_target_pairs={{0,1},{1,0},{2,3},{3,2},{4,5},{5,4},{6,7},{7,6},{8,9},{9,8},{10,11... | collective-permute-start | bytes 12296 | tf_op jit(solution)/shard_map/ppermute | solution.py:49
  108.7 6.1 %collective-permute-start.7 = (f32[2,16,16]{2,1,0:T(8,128)S(1)}, f32[2,16,16]{2,1,0:T(8,128)S(1)}, u32[]{:S(2)}, u32[]{:S(2)}) collective-permute-start(f32[2,16,16]{2,1,0:T(8,128)S(1)} %add_add_fusion.2), channel_id=1, source_target_pairs={{0,4},{2,6},{4,0},{6,2},{8,12},{10,14},{12,8},{14,10},{16,20},{18,... | collective-permute-start | bytes 6152 | tf_op jit(solution)/shard_map/ppermute | solution.py:37
  112.9 4.9 %collective-permute-start.8 = (f32[2,16,16]{2,1,0:T(8,128)S(1)}, f32[2,16,16]{2,1,0:T(8,128)S(1)}, u32[]{:S(2)}, u32[]{:S(2)}) collective-permute-start(f32[2,16,16]{2,1,0:T(8,128)S(1)} %add_add_fusion.2), channel_id=1, source_target_pairs={{0,6},{2,4},{4,2},{6,0},{8,14},{10,12},{12,10},{14,8},{16,22},{18,... | collective-permute-start | bytes 6152 | tf_op jit(solution)/shard_map/ppermute | solution.py:37
  114.0 3.8 %collective-permute-start.6 = (f32[2,16,16]{2,1,0:T(8,128)S(1)}, f32[2,16,16]{2,1,0:T(8,128)S(1)}, u32[]{:S(2)}, u32[]{:S(2)}) collective-permute-start(f32[2,16,16]{2,1,0:T(8,128)S(1)} %add_add_fusion.2), channel_id=1, source_target_pairs={{0,2},{2,0},{4,6},{6,4},{8,10},{10,8},{12,14},{14,12},{16,18},{18,... | collective-permute-start | bytes 6152 | tf_op jit(solution)/shard_map/ppermute | solution.py:37
  117.9 7.0 %collective-permute-start.10 = (f32[2,16,16]{2,1,0:T(8,128)S(1)}, f32[2,16,16]{2,1,0:T(8,128)S(1)}, u32[]{:S(2)}, u32[]{:S(2)}) collective-permute-start(f32[2,16,16]{2,1,0:T(8,128)S(1)} %add_add_fusion.1), channel_id=1, source_target_pairs={{0,16},{2,18},{4,20},{6,22},{8,24},{10,26},{12,28},{14,30},{16,0},... | collective-permute-start | bytes 6152 | tf_op jit(solution)/shard_map/ppermute | solution.py:37
  123.2 4.9 %collective-permute-start.11 = (f32[2,16,16]{2,1,0:T(8,128)S(1)}, f32[2,16,16]{2,1,0:T(8,128)S(1)}, u32[]{:S(2)}, u32[]{:S(2)}) collective-permute-start(f32[2,16,16]{2,1,0:T(8,128)S(1)} %add_add_fusion.1), channel_id=1, source_target_pairs={{0,24},{2,26},{4,28},{6,30},{8,16},{10,18},{12,20},{14,22},{16,8},... | collective-permute-start | bytes 6152 | tf_op jit(solution)/shard_map/ppermute | solution.py:37
  123.9 4.2 %collective-permute-start.9 = (f32[2,16,16]{2,1,0:T(8,128)S(1)}, f32[2,16,16]{2,1,0:T(8,128)S(1)}, u32[]{:S(2)}, u32[]{:S(2)}) collective-permute-start(f32[2,16,16]{2,1,0:T(8,128)S(1)} %add_add_fusion.1), channel_id=1, source_target_pairs={{0,8},{2,10},{4,12},{6,14},{8,0},{10,2},{12,4},{14,6},{16,24},{18,... | collective-permute-start | bytes 6152 | tf_op jit(solution)/shard_map/ppermute | solution.py:37

commit v9 on v7

--- a/solution.py
+++ b/solution.py
@@ -26,14 +26,21 @@
     )
 
 
-def butterfly_sum(value, axis):
+def group_sum(value, axis, radix):
     count = lax.axis_size(axis)
     if count & (count - 1):
         return lax.psum(value, axis)
     bit = 1
     while bit < count:
-        value = value + lax.ppermute(value, axis, [(i, i ^ bit) for i in range(count)])
-        bit *= 2
+        width = min(radix, count // bit)
+        parts = [value] + [
+            lax.ppermute(value, axis, [(i, i ^ (k * bit)) for i in range(count)])
+            for k in range(1, width)
+        ]
+        while len(parts) > 1:
+            parts = [parts[j] + parts[j + 1] for j in range(0, len(parts), 2)]
+        value = parts[0]
+        bit *= width
     return value
 
 
@@ -143,8 +150,8 @@
     gram = jnp.dot(anomaly, anomaly.T, precision=lax.Precision.HIGHEST)
     cross = jnp.dot(anomaly, misfit.T, precision=lax.Precision.HIGHEST)
     sums = jnp.stack([gram, cross])
-    sums = butterfly_sum(sums, "tm")
-    sums = butterfly_sum(sums, "space")
+    sums = group_sum(sums, "tm", 4)
+    sums = group_sum(sums, "space", 16)
     gram, cross = sums[0], sums[1]
     system = jnp.eye(total, dtype=jnp.float32) + gram
     factor = jnp.linalg.cholesky(system)

time: 141 us -> 155 us (1.099)
  starting transfers between devices: 28.4 us -> 49 us
  waiting for transfers between devices: 42.4 us -> 35 us
    ppermute x6 -> x18, starting transfers between devices: 17.9 us -> 38.6 us  [group_sum(): lax.ppermute(value, axis, [(i, i ^ k * bit) for i in range(count)])]
    ppermute x6 -> x18, waiting for transfers between devices: 14.6 us -> 7.22 us  [group_sum(): lax.ppermute(value, axis, [(i, i ^ k * bit) for i in range(count)])]
  transfers between devices with their start and end apart: 11 -> 23, of which waited for: 10 -> 10; matrix products, arithmetic and copies ran while one was open for 3% -> 3% of each run, Pallas kernels for 0% -> 0%
where the time goes in v9:
time: 155 us; the launch traced here: 154 us
  starting transfers between devices  49 us (32%)
  waiting for transfers between devices  35 us (23%)
  blocking collectives  30.7 us (20%)
  other arithmetic  20.2 us (13%)
  local copies, waits for them, and re-layouts  15.4 us (10%)
  matrix products  2.96 us (2%)
    ppermute x18, starting transfers between devices, group_sum(): lax.ppermute(value, axis, [(i, i ^ k * bit) for i in range(count)])  38.6 us
    all_to_all x1, blocking collectives, per_device(): lax.all_to_all(state.reshape(slices, group, row_count, col_count), 'tm',...  30.7 us
    all_to_all x1, waiting for transfers between devices, per_device(): lax.all_to_all(done, 'tm', 0, 0, tiled=True)  24.1 us
    mul x5, other arithmetic, advance(): return (middle + step_size * tendency) * inside  11.1 us
    ppermute x18, waiting for transfers between devices, group_sum(): lax.ppermute(value, axis, [(i, i ^ k * bit) for i in range(count)])  7.22 us
    slice x7, local copies, waits for them, and re-layouts, advance(): west_cell = jnp.pad(middle[:, :, :-1], ((0, 0), (0, 0), (1, 0)))  5.62 us
    ppermute x1, starting transfers between devices, with_halo(): lax.ppermute(tail, axis, [(i, i + 1) for i in range(ends)])  5.29 us
    all_to_all x1, starting transfers between devices, per_device(): lax.all_to_all(done, 'tm', 0, 0, tiled=True)  3.75 us
  transfers between devices with their start and end apart: 23, of which 10 were waited for; matrix products, arithmetic and copies ran while one was open for 3% of the time, Pallas kernels for 0%

profile of v9, /device:TPU:0, one launch (start us, length us, event | category | flops | bytes accessed | tf_op | source)
XLA Modules:
  0.0 154.3 jit_solution(5716553074011584643)
XLA Ops:
  0.6 30.7 %all_to_all.10 = f32[4,2,64,1024]{3,2,1,0:T(8,128)S(1)} all-to-all(f32[4,2,64,1024]{3,2,1,0:T(8,128)} %bitcast.126), channel_id=1, replica_groups=mesh['tm'=4,'space'=16,'ens'=2] {'tm'}, dimensions={0} | all-to-all | bytes 4194304 | tf_op jit(solution)/shard_map/all_to_all | solution.py:94
  31.6 0.7 copy-done
  32.6 0.9 fusion.47
  33.5 1.3 collective-permute-start.1
  34.8 5.3 %collective-permute-start = (f32[12,7,1024]{2,1,0:T(8,128)}, f32[12,7,1024]{2,1,0:T(8,128)}, u32[]{:S(2)}, u32[]{:S(2)}) collective-permute-start(f32[12,7,1024]{2,1,0:T(8,128)} %get-tuple-element.26), channel_id=1, source_target_pairs={{0,2},{2,4},{4,6},{6,8},{8,10},{10,12},{12,14},{14,16},{16,18},{18... | collective-permute-start | bytes 1032200 | tf_op jit(solution)/shard_map/ppermute | solution.py:21
  41.3 0.6 slice.394
  42.0 0.6 slice.407
  42.6 0.6 slice.420
  43.2 0.6 slice.429
  44.1 1.3 collective-permute-done.1
  45.4 1.2 collective-permute-done
  46.5 1.7 %pad_maximum_fusion = f32[12,78,1024]{2,1,0:T(8,128)S(1)} fusion(f32[12,7,1024]{2,1,0:T(8,128)} %collective-permute-done.1, f32[12,64,1024]{2,1,0:T(8,128)S(1)} %bitcast_dynamic-update-slice_fusion, f32[12,7,1024]{2,1,0:T(8,128)} %collective-permute-done), kind=kLoop, calls=%fused_computation | loop fusion | flops 1916928 | bytes 7667712 | tf_op jit(solution)/shard_map/concatenate | solution.py:19
  48.4 1.4 fusion.46
  50.8 2.6 %fusion.5 = (f32[8,76,1024]{2,1,0:T(8,128)S(1)}, f32[8,76,1024]{2,1,0:T(8,128)S(1)}) fusion(f32[8,78,1024]{2,1,0:T(8,128)S(1)} %bitcast.119, f32[12,78,1024]{2,1,0:T(8,128)S(1)} %pad_maximum_fusion, f32[76]{0:T(128)S(1)} %slice.364, f32[76,1024]{1,0:T(8,128)S(1)} %get-tuple-element.22, f32[76,1024]{1,0:T(8,128)S(1)} %get-tuple-element.23, ...), kind=kLoop, calls=%fused_computation.8 | loop fusion | flops 11206656 | bytes 20852272 | tf_op jit(solution)/shard_map/mul | solution.py:67
  53.4 0.9 add_multiply_fusion
  54.3 1.4 fusion.50
  55.8 2.6 %fusion.2 = f32[8,74,1024]{2,1,0:T(8,128)S(1)} fusion(f32[8,78,1024]{2,1,0:T(8,128)S(1)} %bitcast.120, f32[8,76,1024]{2,1,0:T(8,128)S(1)} %get-tuple-element.4, f32[8,74,1023]{2,1,0:T(8,128)S(1)} %get-tuple-element.34, f32[8,74,1023]{2,1,0:T(8,128)S(1)} %get-tuple-element.33, f32[74]{0:T(128)S(1)} %copy-done.12, f32[74,1024]{1,0:T(8,128)S(1)} %get-tuple-element.19, ...), kind=kLoop, calls=%fused_computation.4 | loop fusion | flops 10911744 | bytes 17878696 | tf_op jit(solution)/shard_map/mul | solution.py:67
  58.4 1.1 fusion.49
  59.5 2.4 %fusion.11 = f32[8,72,1024]{2,1,0:T(8,128)S(1)} fusion(f32[8,78,1024]{2,1,0:T(8,128)S(1)} %bitcast.121, f32[8,74,1024]{2,1,0:T(8,128)S(1)} %fusion.2, f32[8,72,1023]{2,1,0:T(8,128)S(1)} %get-tuple-element.32, f32[8,72,1023]{2,1,0:T(8,128)S(1)} %get-tuple-element.31, f32[72]{0:T(128)S(1)} %copy-done.8, f32[72,1024]{1,0:T(8,128)S(1)} %get-tuple-element.16, ...), kind=kLoop, calls=%fused_computation.18 | loop fusion | flops 10616832 | bytes 17395488 | tf_op jit(solution)/shard_map/mul | solution.py:67
  61.9 1.1 fusion.53
  63.0 2.5 %fusion.8 = f32[8,70,1024]{2,1,0:T(8,128)S(1)} fusion(f32[8,78,1024]{2,1,0:T(8,128)S(1)} %bitcast.122, f32[8,72,1024]{2,1,0:T(8,128)S(1)} %fusion.11, f32[8,70,1023]{2,1,0:T(8,128)S(1)} %get-tuple-element.41, f32[8,70,1023]{2,1,0:T(8,128)S(1)} %get-tuple-element.40, f32[70]{0:T(128)S(1)} %copy-done.7, f32[70,1024]{1,0:T(8,128)S(1)} %get-tuple-element.13, ...), kind=kLoop, calls=%fused_computation.14 | loop fusion | flops 10321920 | bytes 16912280 | tf_op jit(solution)/shard_map/mul | solution.py:67
  67.7 0.6 fusion.14
  69.2 1.5 pad_maximum_fusion.1
  70.7 3.8 %all-to-all-start.1 = ((f32[4,2,64,1024]{3,2,1,0:T(8,128)}), f32[4,2,64,1024]{3,2,1,0:T(8,128)S(1)}, u32[]{:S(2)}, u32[]{:S(2)}) async-start(f32[4,2,64,1024]{3,2,1,0:T(8,128)} %pad_maximum_fusion.1), calls=%async_computation.1 | async-start | bytes 4194304 | tf_op jit(solution)/shard_map/all_to_all | solution.py:130
  74.5 24.1 %all-to-all-done.1 = f32[4,2,64,1024]{3,2,1,0:T(8,128)S(1)} async-done(((f32[4,2,64,1024]{3,2,1,0:T(8,128)}), f32[4,2,64,1024]{3,2,1,0:T(8,128)S(1)}, u32[]{:S(2)}, u32[]{:S(2)}) %all-to-all-start.1) | async-done | bytes 2097184 | tf_op jit(solution)/shard_map/all_to_all | solution.py:130
  98.7 1.5 fusion.12
  100.3 1.1 collective-permute-done.2
  101.7 0.6 collective-permute-start.4
  102.4 2.7 %collective-permute-start.5 = (f32[2,16,16]{2,1,0:T(8,128)S(1)}, f32[2,16,16]{2,1,0:T(8,128)S(1)}, u32[]{:S(2)}, u32[]{:S(2)}) collective-permute-start(f32[2,16,16]{2,1,0:T(8,128)S(1)} %pad_maximum_fusion.2), channel_id=1, source_target_pairs={{0,96},{32,64},{64,32},{96,0},{1,97},{33,65},{65,33},{97,1},{2,98}... | collective-permute-start | bytes 6152 | tf_op jit(solution)/shard_map/ppermute | solution.py:37
  105.3 1.8 %collective-permute-done.4 = f32[2,16,16]{2,1,0:T(8,128)S(1)} collective-permute-done((f32[2,16,16]{2,1,0:T(8,128)S(1)}, f32[2,16,16]{2,1,0:T(8,128)S(1)}, u32[]{:S(2)}, u32[]{:S(2)}) %collective-permute-start.4) | collective-permute-done | bytes 2080 | tf_op jit(solution)/shard_map/ppermute | solution.py:37
  107.3 1.5 collective-permute-done.3
  108.8 7.7 %collective-permute-start.19 = (f32[2,16,16]{2,1,0:T(8,128)S(1)}, f32[2,16,16]{2,1,0:T(8,128)S(1)}, u32[]{:S(2)}, u32[]{:S(2)}) collective-permute-start(f32[2,16,16]{2,1,0:T(8,128)S(1)} %add_add_fusion.1), channel_id=1, source_target_pairs={{0,28},{2,30},{4,24},{6,26},{8,20},{10,22},{12,16},{14,18},{16,12}... | collective-permute-start | bytes 6152 | tf_op jit(solution)/shard_map/ppermute | solution.py:37
  116.5 0.9 collective-permute-start.20
  117.4 4.2 %collective-permute-start.17 = (f32[2,16,16]{2,1,0:T(8,128)S(1)}, f32[2,16,16]{2,1,0:T(8,128)S(1)}, u32[]{:S(2)}, u32[]{:S(2)}) collective-permute-start(f32[2,16,16]{2,1,0:T(8,128)S(1)} %add_add_fusion.1), channel_id=1, source_target_pairs={{0,24},{2,26},{4,28},{6,30},{8,16},{10,18},{12,20},{14,22},{16,8},... | collective-permute-start | bytes 6152 | tf_op jit(solution)/shard_map/ppermute | solution.py:37
  121.6 1.8 %collective-permute-start.18 = (f32[2,16,16]{2,1,0:T(8,128)S(1)}, f32[2,16,16]{2,1,0:T(8,128)S(1)}, u32[]{:S(2)}, u32[]{:S(2)}) collective-permute-start(f32[2,16,16]{2,1,0:T(8,128)S(1)} %add_add_fusion.1), channel_id=1, source_target_pairs={{0,26},{2,24},{4,30},{6,28},{8,18},{10,16},{12,22},{14,20},{16,10}... | collective-permute-start | bytes 6152 | tf_op jit(solution)/shard_map/ppermute | solution.py:37
  123.4 5.6 %collective-permute-start.16 = (f32[2,16,16]{2,1,0:T(8,128)S(1)}, f32[2,16,16]{2,1,0:T(8,128)S(1)}, u32[]{:S(2)}, u32[]{:S(2)}) collective-permute-start(f32[2,16,16]{2,1,0:T(8,128)S(1)} %add_add_fusion.1), channel_id=1, source_target_pairs={{0,22},{2,20},{4,18},{6,16},{8,30},{10,28},{12,26},{14,24},{16,6},... | collective-permute-start | bytes 6152 | tf_op jit(solution)/shard_map/ppermute | solution.py:37
  129.0 3.2 %collective-permute-start.14 = (f32[2,16,16]{2,1,0:T(8,128)S(1)}, f32[2,16,16]{2,1,0:T(8,128)S(1)}, u32[]{:S(2)}, u32[]{:S(2)}) collective-permute-start(f32[2,16,16]{2,1,0:T(8,128)S(1)} %add_add_fusion.1), channel_id=1, source_target_pairs={{0,18},{2,16},{4,22},{6,20},{8,26},{10,24},{12,30},{14,28},{16,2},... | collective-permute-start | bytes 6152 | tf_op jit(solution)/shard_map/ppermute | solution.py:37
  132.3 1.9 %collective-permute-start.11 = (f32[2,16,16]{2,1,0:T(8,128)S(1)}, f32[2,16,16]{2,1,0:T(8,128)S(1)}, u32[]{:S(2)}, u32[]{:S(2)}) collective-permute-start(f32[2,16,16]{2,1,0:T(8,128)S(1)} %add_add_fusion.1), channel_id=1, source_target_pairs={{0,12},{2,14},{4,8},{6,10},{8,4},{10,6},{12,0},{14,2},{16,28},{18,... | collective-permute-start | bytes 6152 | tf_op jit(solution)/shard_map/ppermute | solution.py:37
  134.1 3.5 %collective-permute-start.12 = (f32[2,16,16]{2,1,0:T(8,128)S(1)}, f32[2,16,16]{2,1,0:T(8,128)S(1)}, u32[]{:S(2)}, u32[]{:S(2)}) collective-permute-start(f32[2,16,16]{2,1,0:T(8,128)S(1)} %add_add_fusion.1), channel_id=1, source_target_pairs={{0,14},{2,12},{4,10},{6,8},{8,6},{10,4},{12,2},{14,0},{16,30},{18,... | collective-permute-start | bytes 6152 | tf_op jit(solution)/shard_map/ppermute | solution.py:37
  138.2 4.3 %collective-permute-start.7 = (f32[2,16,16]{2,1,0:T(8,128)S(1)}, f32[2,16,16]{2,1,0:T(8,128)S(1)}, u32[]{:S(2)}, u32[]{:S(2)}) collective-permute-start(f32[2,16,16]{2,1,0:T(8,128)S(1)} %add_add_fusion.1), channel_id=1, source_target_pairs={{0,4},{2,6},{4,0},{6,2},{8,12},{10,14},{12,8},{14,10},{16,20},{18,... | collective-permute-start | bytes 6152 | tf_op jit(solution)/shard_map/ppermute | solution.py:37
  142.5 1.4 collective-permute-start.8
  144.4 3.1 %collective-permute-done.8 = f32[2,16,16]{2,1,0:T(8,128)S(1)} collective-permute-done((f32[2,16,16]{2,1,0:T(8,128)S(1)}, f32[2,16,16]{2,1,0:T(8,128)S(1)}, u32[]{:S(2)}, u32[]{:S(2)}) %collective-permute-start.8) | collective-permute-done | bytes 2080 | tf_op jit(solution)/shard_map/ppermute | solution.py:37
  147.8 1.5 cholesky.17
  149.2 0.6 compare_reduce_fusion
  149.9 0.6 fusion.21
  150.5 1.2 custom-call.10
  152.1 0.9 fusion.13
  153.0 1.3 copy.19
  (104 shorter events, 8.8 us)
Async XLA Ops:
  31.3 1.0 copy-start
  31.3 1.0 copy-start.1
  31.4 1.1 copy-start.3
  31.4 1.2 copy-start.5
  32.3 11.5 %copy-start.6 = (f32[8,128]{1,0:T(8,128)S(1)}, f32[8,128]{1,0:T(8,128)}, u32[]{:S(2)}) copy-start(f32[8,128]{1,0:T(8,128)} %param.15) | copy-start | bytes 12292
  33.5 11.9 %collective-permute-start.1 = (f32[12,7,1024]{2,1,0:T(8,128)}, f32[12,7,1024]{2,1,0:T(8,128)}, u32[]{:S(2)}, u32[]{:S(2)}) collective-permute-start(f32[12,7,1024]{2,1,0:T(8,128)} %get-tuple-element.27), channel_id=1, source_target_pairs={{2,0},{4,2},{6,4},{8,6},{10,8},{12,10},{14,12},{16,14},{18,16},{20... | collective-permute-start | bytes 1032200 | tf_op jit(solution)/shard_map/ppermute | solution.py:23
  34.8 11.8 %collective-permute-start = (f32[12,7,1024]{2,1,0:T(8,128)}, f32[12,7,1024]{2,1,0:T(8,128)}, u32[]{:S(2)}, u32[]{:S(2)}) collective-permute-start(f32[12,7,1024]{2,1,0:T(8,128)} %get-tuple-element.26), channel_id=1, source_target_pairs={{0,2},{2,4},{4,6},{6,8},{8,10},{10,12},{12,14},{14,16},{16,18},{18... | collective-permute-start | bytes 1032200 | tf_op jit(solution)/shard_map/ppermute | solution.py:21
  54.3 1.4 copy-start.12
  58.4 1.1 copy-start.8
  61.9 1.1 copy-start.7
  65.8 0.6 copy-start.11
  67.0 0.7 copy-start.10
  67.7 0.9 copy-start.2
  67.7 1.0 copy-start.4
  67.7 1.0 copy-start.9
  70.7 3.8 %copy-start.13 = (s32[1,64]{1,0:T(1,128)S(1)}, s32[1,64]{1,0:T(1,128)}, u32[]{:S(2)}) copy-start(s32[1,64]{1,0:T(1,128)} %param.16) | copy-start | bytes 772
  70.7 29.5 %copy-start.15 = (f32[1,64]{1,0:T(1,128)S(1)}, f32[1,64]{1,0:T(1,128)}, u32[]{:S(2)}) copy-start(f32[1,64]{1,0:T(1,128)} %param.19) | copy-start | bytes 772
  70.7 30.8 %copy-start.14 = (f32[1,64,16]{1,2,0:T(8,128)S(1)}, f32[1,64,16]{1,2,0:T(8,128)}, u32[]{:S(2)}) copy-start(f32[1,64,16]{1,2,0:T(8,128)} %param.18) | copy-start | bytes 12292
  70.7 30.8 %copy-start.16 = (f32[1,64]{1,0:T(1,128)S(1)}, f32[1,64]{1,0:T(1,128)}, u32[]{:S(2)}) copy-start(f32[1,64]{1,0:T(1,128)} %param.17) | copy-start | bytes 772
  70.7 27.9 %all-to-all-start.1 = ((f32[4,2,64,1024]{3,2,1,0:T(8,128)}), f32[4,2,64,1024]{3,2,1,0:T(8,128)S(1)}, u32[]{:S(2)}, u32[]{:S(2)}) async-start(f32[4,2,64,1024]{3,2,1,0:T(8,128)} %pad_maximum_fusion.1), calls=%async_computation.1 | async-start | bytes 4194304 | tf_op jit(solution)/shard_map/all_to_all | solution.py:130
  100.2 1.2 collective-permute-start.2
  101.7 5.3 %collective-permute-start.4 = (f32[2,16,16]{2,1,0:T(8,128)S(1)}, f32[2,16,16]{2,1,0:T(8,128)S(1)}, u32[]{:S(2)}, u32[]{:S(2)}) collective-permute-start(f32[2,16,16]{2,1,0:T(8,128)S(1)} %pad_maximum_fusion.2), channel_id=1, source_target_pairs={{0,64},{32,96},{64,0},{96,32},{1,65},{33,97},{65,1},{97,33},{2,66}... | collective-permute-start | bytes 6152 | tf_op jit(solution)/shard_map/ppermute | solution.py:37
  102.4 4.9 %collective-permute-start.5 = (f32[2,16,16]{2,1,0:T(8,128)S(1)}, f32[2,16,16]{2,1,0:T(8,128)S(1)}, u32[]{:S(2)}, u32[]{:S(2)}) collective-permute-start(f32[2,16,16]{2,1,0:T(8,128)S(1)} %pad_maximum_fusion.2), channel_id=1, source_target_pairs={{0,96},{32,64},{64,32},{96,0},{1,97},{33,65},{65,33},{97,1},{2,98}... | collective-permute-start | bytes 6152 | tf_op jit(solution)/shard_map/ppermute | solution.py:37
  105.1 3.7 %collective-permute-start.3 = (f32[2,16,16]{2,1,0:T(8,128)S(1)}, f32[2,16,16]{2,1,0:T(8,128)S(1)}, u32[]{:S(2)}, u32[]{:S(2)}) collective-permute-start(f32[2,16,16]{2,1,0:T(8,128)S(1)} %pad_maximum_fusion.2), channel_id=1, source_target_pairs={{0,32},{32,0},{64,96},{96,64},{1,33},{33,1},{65,97},{97,65},{2,34}... | collective-permute-start | bytes 6152 | tf_op jit(solution)/shard_map/ppermute | solution.py:37
  105.3 18.1 %collective-permute-start.21 = (f32[8,128]{1,0:T(8,128)S(1)}, f32[8,128]{1,0:T(8,128)S(1)}, u32[]{:S(2)}, u32[]{:S(2)}) collective-permute-start(f32[8,128]{1,0:T(8,128)S(1)} %copy-done.6), channel_id=1, source_target_pairs={{0,1},{1,0},{2,3},{3,2},{4,5},{5,4},{6,7},{7,6},{8,9},{9,8},{10,11... | collective-permute-start | bytes 12296 | tf_op jit(solution)/shard_map/ppermute | solution.py:48
  108.8 14.6 %collective-permute-start.19 = (f32[2,16,16]{2,1,0:T(8,128)S(1)}, f32[2,16,16]{2,1,0:T(8,128)S(1)}, u32[]{:S(2)}, u32[]{:S(2)}) collective-permute-start(f32[2,16,16]{2,1,0:T(8,128)S(1)} %add_add_fusion.1), channel_id=1, source_target_pairs={{0,28},{2,30},{4,24},{6,26},{8,20},{10,22},{12,16},{14,18},{16,12}... | collective-permute-start | bytes 6152 | tf_op jit(solution)/shard_map/ppermute | solution.py:37
  116.5 12.6 %collective-permute-start.20 = (f32[2,16,16]{2,1,0:T(8,128)S(1)}, f32[2,16,16]{2,1,0:T(8,128)S(1)}, u32[]{:S(2)}, u32[]{:S(2)}) collective-permute-start(f32[2,16,16]{2,1,0:T(8,128)S(1)} %add_add_fusion.1), channel_id=1, source_target_pairs={{0,30},{2,28},{4,26},{6,24},{8,22},{10,20},{12,18},{14,16},{16,14}... | collective-permute-start | bytes 6152 | tf_op jit(solution)/shard_map/ppermute | solution.py:37
  117.4 11.6 %collective-permute-start.17 = (f32[2,16,16]{2,1,0:T(8,128)S(1)}, f32[2,16,16]{2,1,0:T(8,128)S(1)}, u32[]{:S(2)}, u32[]{:S(2)}) collective-permute-start(f32[2,16,16]{2,1,0:T(8,128)S(1)} %add_add_fusion.1), channel_id=1, source_target_pairs={{0,24},{2,26},{4,28},{6,30},{8,16},{10,18},{12,20},{14,22},{16,8},... | collective-permute-start | bytes 6152 | tf_op jit(solution)/shard_map/ppermute | solution.py:37
  121.6 10.7 %collective-permute-start.18 = (f32[2,16,16]{2,1,0:T(8,128)S(1)}, f32[2,16,16]{2,1,0:T(8,128)S(1)}, u32[]{:S(2)}, u32[]{:S(2)}) collective-permute-start(f32[2,16,16]{2,1,0:T(8,128)S(1)} %add_add_fusion.1), channel_id=1, source_target_pairs={{0,26},{2,24},{4,30},{6,28},{8,18},{10,16},{12,22},{14,20},{16,10}... | collective-permute-start | bytes 6152 | tf_op jit(solution)/shard_map/ppermute | solution.py:37
  123.4 10.7 %collective-permute-start.15 = (f32[2,16,16]{2,1,0:T(8,128)S(1)}, f32[2,16,16]{2,1,0:T(8,128)S(1)}, u32[]{:S(2)}, u32[]{:S(2)}) collective-permute-start(f32[2,16,16]{2,1,0:T(8,128)S(1)} %add_add_fusion.1), channel_id=1, source_target_pairs={{0,20},{2,22},{4,16},{6,18},{8,28},{10,30},{12,24},{14,26},{16,4},... | collective-permute-start | bytes 6152 | tf_op jit(solution)/shard_map/ppermute | solution.py:37
  123.4 14.2 %collective-permute-start.16 = (f32[2,16,16]{2,1,0:T(8,128)S(1)}, f32[2,16,16]{2,1,0:T(8,128)S(1)}, u32[]{:S(2)}, u32[]{:S(2)}) collective-permute-start(f32[2,16,16]{2,1,0:T(8,128)S(1)} %add_add_fusion.1), channel_id=1, source_target_pairs={{0,22},{2,20},{4,18},{6,16},{8,30},{10,28},{12,26},{14,24},{16,6},... | collective-permute-start | bytes 6152 | tf_op jit(solution)/shard_map/ppermute | solution.py:37
  129.0 8.7 %collective-permute-start.13 = (f32[2,16,16]{2,1,0:T(8,128)S(1)}, f32[2,16,16]{2,1,0:T(8,128)S(1)}, u32[]{:S(2)}, u32[]{:S(2)}) collective-permute-start(f32[2,16,16]{2,1,0:T(8,128)S(1)} %add_add_fusion.1), channel_id=1, source_target_pairs={{0,16},{2,18},{4,20},{6,22},{8,24},{10,26},{12,28},{14,30},{16,0},... | collective-permute-start | bytes 6152 | tf_op jit(solution)/shard_map/ppermute | solution.py:37
  129.0 9.2 %collective-permute-start.14 = (f32[2,16,16]{2,1,0:T(8,128)S(1)}, f32[2,16,16]{2,1,0:T(8,128)S(1)}, u32[]{:S(2)}, u32[]{:S(2)}) collective-permute-start(f32[2,16,16]{2,1,0:T(8,128)S(1)} %add_add_fusion.1), channel_id=1, source_target_pairs={{0,18},{2,16},{4,22},{6,20},{8,26},{10,24},{12,30},{14,28},{16,2},... | collective-permute-start | bytes 6152 | tf_op jit(solution)/shard_map/ppermute | solution.py:37
  132.3 10.3 %collective-permute-start.11 = (f32[2,16,16]{2,1,0:T(8,128)S(1)}, f32[2,16,16]{2,1,0:T(8,128)S(1)}, u32[]{:S(2)}, u32[]{:S(2)}) collective-permute-start(f32[2,16,16]{2,1,0:T(8,128)S(1)} %add_add_fusion.1), channel_id=1, source_target_pairs={{0,12},{2,14},{4,8},{6,10},{8,4},{10,6},{12,0},{14,2},{16,28},{18,... | collective-permute-start | bytes 6152 | tf_op jit(solution)/shard_map/ppermute | solution.py:37
  134.1 9.8 %collective-permute-start.12 = (f32[2,16,16]{2,1,0:T(8,128)S(1)}, f32[2,16,16]{2,1,0:T(8,128)S(1)}, u32[]{:S(2)}, u32[]{:S(2)}) collective-permute-start(f32[2,16,16]{2,1,0:T(8,128)S(1)} %add_add_fusion.1), channel_id=1, source_target_pairs={{0,14},{2,12},{4,10},{6,8},{8,6},{10,4},{12,2},{14,0},{16,30},{18,... | collective-permute-start | bytes 6152 | tf_op jit(solution)/shard_map/ppermute | solution.py:37
  137.6 6.3 %collective-permute-start.9 = (f32[2,16,16]{2,1,0:T(8,128)S(1)}, f32[2,16,16]{2,1,0:T(8,128)S(1)}, u32[]{:S(2)}, u32[]{:S(2)}) collective-permute-start(f32[2,16,16]{2,1,0:T(8,128)S(1)} %add_add_fusion.1), channel_id=1, source_target_pairs={{0,8},{2,10},{4,12},{6,14},{8,0},{10,2},{12,4},{14,6},{16,24},{18,... | collective-permute-start | bytes 6152 | tf_op jit(solution)/shard_map/ppermute | solution.py:37
  137.7 6.2 %collective-permute-start.10 = (f32[2,16,16]{2,1,0:T(8,128)S(1)}, f32[2,16,16]{2,1,0:T(8,128)S(1)}, u32[]{:S(2)}, u32[]{:S(2)}) collective-permute-start(f32[2,16,16]{2,1,0:T(8,128)S(1)} %add_add_fusion.1), channel_id=1, source_target_pairs={{0,10},{2,8},{4,14},{6,12},{8,2},{10,0},{12,6},{14,4},{16,26},{18,... | collective-permute-start | bytes 6152 | tf_op jit(solution)/shard_map/ppermute | solution.py:37
  138.2 6.2 %collective-permute-start.7 = (f32[2,16,16]{2,1,0:T(8,128)S(1)}, f32[2,16,16]{2,1,0:T(8,128)S(1)}, u32[]{:S(2)}, u32[]{:S(2)}) collective-permute-start(f32[2,16,16]{2,1,0:T(8,128)S(1)} %add_add_fusion.1), channel_id=1, source_target_pairs={{0,4},{2,6},{4,0},{6,2},{8,12},{10,14},{12,8},{14,10},{16,20},{18,... | collective-permute-start | bytes 6152 | tf_op jit(solution)/shard_map/ppermute | solution.py:37
  142.5 5.0 %collective-permute-start.8 = (f32[2,16,16]{2,1,0:T(8,128)S(1)}, f32[2,16,16]{2,1,0:T(8,128)S(1)}, u32[]{:S(2)}, u32[]{:S(2)}) collective-permute-start(f32[2,16,16]{2,1,0:T(8,128)S(1)} %add_add_fusion.1), channel_id=1, source_target_pairs={{0,6},{2,4},{4,2},{6,0},{8,14},{10,12},{12,10},{14,8},{16,22},{18,... | collective-permute-start | bytes 6152 | tf_op jit(solution)/shard_map/ppermute | solution.py:37
  143.9 3.7 %collective-permute-start.6 = (f32[2,16,16]{2,1,0:T(8,128)S(1)}, f32[2,16,16]{2,1,0:T(8,128)S(1)}, u32[]{:S(2)}, u32[]{:S(2)}) collective-permute-start(f32[2,16,16]{2,1,0:T(8,128)S(1)} %add_add_fusion.1), channel_id=1, source_target_pairs={{0,2},{2,0},{4,6},{6,4},{8,10},{10,8},{12,14},{14,12},{16,18},{18,... | collective-permute-start | bytes 6152 | tf_op jit(solution)/shard_map/ppermute | solution.py:37

commit v10 on v8

--- a/solution.py
+++ b/solution.py
@@ -92,18 +92,11 @@
     group = members_here // slices
     band_width = col_count // params.shape[1]
 
-    mine = lax.all_to_all(
-        state.reshape(slices, group, row_count, col_count), "tm", 0, 0, tiled=True
-    ).reshape(slices * group, row_count, col_count)
     my_params = lax.dynamic_slice_in_dim(params, slice_index * group, group, 0)
     spread_params = jnp.repeat(my_params, band_width, axis=1)
-
     fields = jnp.stack([diffusivity, velocity_x, velocity_y, source_shape])
-    wide = with_halo(jnp.concatenate([mine, fields]), "space", depth)
-    count = slices * group
-    wide_state = wide[:count]
-    wide_coeffs = wide[count : count + 3]
-    wide_forcing = jnp.tile(wide[count + 3][None] * spread_params[:, None, :], (slices, 1, 1))
+    wide_fields = with_halo(fields, "space", depth)
+    wide_coeffs = wide_fields[:3]
     global_rows = first_row - depth + jnp.arange(row_count + 2 * depth, dtype=jnp.int32)
     wide_inside = ((global_rows >= 0) & (global_rows < slabs)).astype(jnp.float32)[:, None]
 
@@ -113,24 +106,27 @@
         q = None if forcing is None else forcing[:, lo:hi]
         return advance(values, wide_coeffs[:, lo:hi], wide_inside[lo:hi], step_size, q)
 
-    current = wide_state
-    coarse_part = step(wide_state, 0, coarse_dt, None)
-    for section in range(FINE):
-        current = step(current, section, FINE_DT, wide_forcing)
-    coarse_part = coarse_part[:, FINE - 1 : FINE - 1 + current.shape[1]]
-    fine = current.reshape(slices, group, -1, col_count)
-    coarse_part = coarse_part.reshape(slices, group, -1, col_count)
-    running = fine[0]
-    results = [running[:, links : links + row_count]]
-    for link in range(1, slices):
-        correction = fine[link] - coarse_part[link]
-        stepped = step(running, FINE + link - 1, coarse_dt, None)
-        running = correction[:, link : correction.shape[1] - link] + stepped
-        results.append(running[:, links - link : links - link + row_count])
-    done = jnp.stack(results)
-    running = lax.all_to_all(done, "tm", 0, 0, tiled=True).reshape(
-        members_here, row_count, col_count
-    )
+    by_group = state.reshape(slices, group, row_count, col_count)
+    finished = []
+    for member in range(group):
+        mine = lax.all_to_all(by_group[:, member], "tm", 0, 0, tiled=True)
+        wide_state = with_halo(mine, "space", depth)
+        wide_forcing = wide_fields[3][None] * spread_params[member][None, None, :]
+        current = wide_state
+        coarse_part = step(wide_state, 0, coarse_dt, None)
+        for section in range(FINE):
+            current = step(current, section, FINE_DT, wide_forcing)
+        coarse_part = coarse_part[:, FINE - 1 : FINE - 1 + current.shape[1]]
+        running = current[0:1]
+        results = [running[:, links : links + row_count]]
+        for link in range(1, slices):
+            correction = current[link : link + 1] - coarse_part[link : link + 1]
+            stepped = step(running, FINE + link - 1, coarse_dt, None)
+            running = correction[:, link : correction.shape[1] - link] + stepped
+            results.append(running[:, links - link : links - link + row_count])
+        done = jnp.concatenate(results)
+        finished.append(lax.all_to_all(done, "tm", 0, 0, tiled=True))
+    running = jnp.stack(finished, axis=1).reshape(members_here, row_count, col_count)
     new_states = running[None]
 
     local_cell = obs_cell[0] - first_row * col_count

time: 136 us -> 144 us (1.059)
  blocking collectives: 30.7 us -> 0 us
  starting transfers between devices: 26.7 us -> 52.3 us
  local copies, waits for them, and re-layouts: 15.3 us -> 26.2 us
    all_to_all x1 -> x0, blocking collectives: 30.7 us -> none  [per_device(): lax.all_to_all(state.reshape(slices, group, row_count, col_count), 'tm',...]
    all_to_all x1 -> x4, starting transfers between devices: 3.75 us -> 16.6 us  [the longest x2 9.32 us: per_device(): mine = lax.all_to_all(by_group[:, member], 'tm', 0, 0, tiled=True)]
    ppermute x1 -> x3, starting transfers between devices: 5.32 us -> 14.3 us  [with_halo(): lax.ppermute(tail, axis, [(i, i + 1) for i in range(ends)])]
    add x0 -> x4, local copies, waits for them, and re-layouts: none -> 3.48 us  [advance(): tendency = tendency + forcing]
    mul x6 -> x4, local copies, waits for them, and re-layouts: 0.69 us -> 3.94 us  [advance(): coeffs[0] * (above_row + below_row + west_cell + east_cell - 4.0 * middle)]
    squeeze x0 -> x1, local copies, waits for them, and re-layouts: none -> 3.11 us  [per_device(): mine = lax.all_to_all(by_group[:, member], 'tm', 0, 0, tiled=True)]
    ppermute x1 -> x3, starting transfers between devices: 1.28 us -> 3.88 us  [with_halo(): lax.ppermute(head, axis, [(i + 1, i) for i in range(ends)])]
    concatenate x0 -> x2, other arithmetic: none -> 2.14 us  [per_device(): done = jnp.concatenate(results)]
  transfers between devices with their start and end apart: 14 -> 21, of which waited for: 10 -> 13; matrix products, arithmetic and copies ran while one was open for 3% -> 11% of each run, Pallas kernels for 0% -> 0%
where the time goes in v10:
time: 144 us; the launch traced here: 143 us
  starting transfers between devices  52.3 us (36%)
  waiting for transfers between devices  38.9 us (27%)
  local copies, waits for them, and re-layouts  26.2 us (18%)
  other arithmetic  21.6 us (15%)
  matrix products  2.89 us (2%)
  between operations  1.44 us (1%)
    all_to_all x2, waiting for transfers between devices, per_device(): finished.append(lax.all_to_all(done, 'tm', 0, 0, tiled=True))  20.4 us
    ppermute x9, starting transfers between devices, quad_sum(): lax.ppermute(value, axis, [(i, i ^ k * bit) for i in range(count)])  17.5 us
    ppermute x3, starting transfers between devices, with_halo(): lax.ppermute(tail, axis, [(i, i + 1) for i in range(ends)])  14.3 us
    ppermute x9, waiting for transfers between devices, quad_sum(): lax.ppermute(value, axis, [(i, i ^ k * bit) for i in range(count)])  10.1 us
    mul x5, other arithmetic, advance(): return (middle + step_size * tendency) * inside  9.79 us
    all_to_all x2, starting transfers between devices, per_device(): mine = lax.all_to_all(by_group[:, member], 'tm', 0, 0, tiled=True)  9.32 us
    all_to_all x2, starting transfers between devices, per_device(): finished.append(lax.all_to_all(done, 'tm', 0, 0, tiled=True))  7.25 us
    all_to_all x2, waiting for transfers between devices, per_device(): mine = lax.all_to_all(by_group[:, member], 'tm', 0, 0, tiled=True)  5.49 us
  transfers between devices with their start and end apart: 21, of which 13 were waited for; matrix products, arithmetic and copies ran while one was open for 11% of the time, Pallas kernels for 0%

profile of v10, /device:TPU:0, one launch (start us, length us, event | category | flops | bytes accessed | tf_op | source)
XLA Modules:
  0.0 143.3 jit_solution(10906761328237418758)
XLA Ops:
  0.6 3.1 %slice_bitcast_fusion.1 = (f32[4,64,1024]{2,1,0:T(8,128)}, f32[4,64,1024]{2,1,0:T(8,128)}) fusion(f32[4,2,64,1024]{3,2,1,0:T(8,128)} %bitcast.135), kind=kLoop, calls=%fused_computation.24 | loop fusion | bytes 4194304 | tf_op jit(solution)/shard_map/squeeze | solution.py:112
  3.8 4.5 %all-to-all-start = ((f32[4,64,1024]{2,1,0:T(8,128)}), f32[4,64,1024]{2,1,0:T(8,128)S(1)}, u32[]{:S(2)}, u32[]{:S(2)}) async-start(f32[4,64,1024]{2,1,0:T(8,128)} %get-tuple-element.8), calls=%async_computation | async-start | bytes 2097152 | tf_op jit(solution)/shard_map/all_to_all | solution.py:112
  8.3 1.3 collective-permute-start.3
  9.6 5.2 %collective-permute-start.2 = (f32[4,7,1024]{2,1,0:T(8,128)S(1)}, f32[4,7,1024]{2,1,0:T(8,128)}, u32[]{:S(2)}, u32[]{:S(2)}) collective-permute-start(f32[4,7,1024]{2,1,0:T(8,128)S(1)} %get-tuple-element.58), channel_id=1, source_target_pairs={{0,2},{2,4},{4,6},{6,8},{8,10},{10,12},{12,14},{14,16},{16,18},{18... | collective-permute-start | bytes 344072 | tf_op jit(solution)/shard_map/ppermute | solution.py:21
  18.9 1.1 pad_maximum_fusion.2
  20.0 0.9 slice_bitcast_fusion.21
  21.0 0.9 slice_bitcast_fusion.13
  21.9 0.9 slice_bitcast_fusion.12
  22.8 1.0 slice_bitcast_fusion.11
  23.8 1.0 slice_bitcast_fusion.7
  24.8 4.8 %all-to-all-start.2 = ((f32[4,64,1024]{2,1,0:T(8,128)}), f32[4,64,1024]{2,1,0:T(8,128)}, u32[]{:S(2)}, u32[]{:S(2)}) async-start(f32[4,64,1024]{2,1,0:T(8,128)} %get-tuple-element.9), calls=%async_computation.2 | async-start | bytes 2097152 | tf_op jit(solution)/shard_map/all_to_all | solution.py:112
  29.6 1.0 slice_bitcast_fusion.17
  30.6 0.9 slice_bitcast_fusion.3
  31.5 0.8 slice_bitcast_fusion.2
  32.3 1.3 collective-permute-start.1
  33.6 4.6 %collective-permute-start = (f32[4,7,1024]{2,1,0:T(8,128)S(1)}, f32[4,7,1024]{2,1,0:T(8,128)S(1)}, u32[]{:S(2)}, u32[]{:S(2)}) collective-permute-start(f32[4,7,1024]{2,1,0:T(8,128)S(1)} %get-tuple-element.56), channel_id=1, source_target_pairs={{0,2},{2,4},{4,6},{6,8},{8,10},{10,12},{12,14},{14,16},{16,18},{18... | collective-permute-start | bytes 344072 | tf_op jit(solution)/shard_map/ppermute | solution.py:21
  38.2 5.5 %all-to-all-done.2 = f32[4,64,1024]{2,1,0:T(8,128)} async-done(((f32[4,64,1024]{2,1,0:T(8,128)}), f32[4,64,1024]{2,1,0:T(8,128)}, u32[]{:S(2)}, u32[]{:S(2)}) %all-to-all-start.2) | async-done | bytes 1048608 | tf_op jit(solution)/shard_map/all_to_all | solution.py:112
  43.7 1.0 fusion.51
  44.7 1.3 collective-permute-start.5
  46.0 4.6 %collective-permute-start.4 = (f32[4,7,1024]{2,1,0:T(8,128)S(1)}, f32[4,7,1024]{2,1,0:T(8,128)S(1)}, u32[]{:S(2)}, u32[]{:S(2)}) collective-permute-start(f32[4,7,1024]{2,1,0:T(8,128)S(1)} %get-tuple-element.60), channel_id=1, source_target_pairs={{0,2},{2,4},{4,6},{6,8},{8,10},{10,12},{12,14},{14,16},{16,18},{18... | collective-permute-start | bytes 344072 | tf_op jit(solution)/shard_map/ppermute | solution.py:21
  51.5 1.5 %collective-permute-done.4 = f32[4,7,1024]{2,1,0:T(8,128)S(1)} collective-permute-done((f32[4,7,1024]{2,1,0:T(8,128)S(1)}, f32[4,7,1024]{2,1,0:T(8,128)S(1)}, u32[]{:S(2)}, u32[]{:S(2)}) %collective-permute-start.4) | collective-permute-done | bytes 114720 | tf_op jit(solution)/shard_map/ppermute | solution.py:21
  53.0 1.4 pad_maximum_fusion.3
  55.8 2.4 %add_multiply_fusion.5 = (f32[4,76,1024]{2,1,0:T(8,128)S(1)}, f32[4,76,1024]{2,1,0:T(8,128)S(1)}, f32[4,76,1024]{2,1,0:T(8,128)S(1)}, f32[4,76,1024]{2,1,0:T(8,128)S(1)}) fusion(f32[4,78,1024]{2,1,0:T(8,128)S(1)} %pad_maximum_fusion.1, f32[76]{0:T(128)S(1)} %slice.610, f32[76,1024]{1,0:T(8,128)S(1)} %copy-done.9, f32[76,1024]{1,0:T(8,128)S(1)} %copy-done.14, ...), kind=kLoop, calls=%fused_computation.13 | loop fusion | flops 11206656 | bytes 18984496 | tf_op jit(solution)/shard_map/mul | solution.py:68
  60.1 2.4 %add_multiply_fusion.4 = (f32[4,74,1024]{2,1,0:T(8,128)S(1)}, f32[4,74,1024]{2,1,0:T(8,128)S(1)}) fusion(f32[4,76,1024]{2,1,0:T(8,128)S(1)} %get-tuple-element.4, f32[4,74,1023]{2,1,0:T(8,128)S(1)} %get-tuple-element.16, f32[4,74,1023]{2,1,0:T(8,128)S(1)} %get-tuple-element.15, f32[74]{0:T(128)S(1)} %copy-done.33, f32[74,1024]{1,0:T(8,128)S(1)} %copy-done.7, ...), kind=kLoop, calls=%fused_computation.12 | loop fusion | flops 10911744 | bytes 16060072 | tf_op jit(solution)/shard_map/mul | solution.py:68
  64.3 2.1 %add_multiply_fusion.9 = (f32[4,72,1024]{2,1,0:T(8,128)S(1)}, f32[4,72,1024]{2,1,0:T(8,128)S(1)}) fusion(f32[4,74,1024]{2,1,0:T(8,128)S(1)} %get-tuple-element.62, f32[4,72,1023]{2,1,0:T(8,128)S(1)} %get-tuple-element.14, f32[4,72,1023]{2,1,0:T(8,128)S(1)} %get-tuple-element.13, f32[72]{0:T(128)S(1)} %copy-done.32, f32[72,1024]{1,0:T(8,128)S(1)} %copy-done.25, ...), kind=kLoop, calls=%fused_computation.18 | loop fusion | flops 10616832 | bytes 15626016 | tf_op jit(solution)/shard_map/mul | solution.py:68
  68.3 2.2 %add_multiply_fusion.8 = (f32[4,70,1024]{2,1,0:T(8,128)S(1)}, f32[4,70,1024]{2,1,0:T(8,128)S(1)}) fusion(f32[4,72,1024]{2,1,0:T(8,128)S(1)} %get-tuple-element.68, f32[4,70,1023]{2,1,0:T(8,128)S(1)} %get-tuple-element.48, f32[4,70,1023]{2,1,0:T(8,128)S(1)} %get-tuple-element.47, f32[70]{0:T(128)S(1)} %copy-done.31, f32[70,1024]{1,0:T(8,128)S(1)} %copy-done.23, ...), kind=kLoop, calls=%fused_computation.17 | loop fusion | flops 10321920 | bytes 15191960 | tf_op jit(solution)/shard_map/mul | solution.py:68
  75.1 1.1 fusion.7
  76.2 1.1 pad_maximum_fusion.5
  77.3 3.5 %all-to-all-start.3 = ((f32[4,64,1024]{2,1,0:T(8,128)}), f32[4,64,1024]{2,1,0:T(8,128)S(1)}, u32[]{:S(2)}, u32[]{:S(2)}) async-start(f32[4,64,1024]{2,1,0:T(8,128)} %pad_maximum_fusion.5), calls=%async_computation.3 | async-start | bytes 2097152 | tf_op jit(solution)/shard_map/all_to_all | solution.py:128
  80.9 0.8 copy-done.27
  81.8 1.1 pad_maximum_fusion.4
  82.9 9.8 %all-to-all-done.3 = f32[4,64,1024]{2,1,0:T(8,128)S(1)} async-done(((f32[4,64,1024]{2,1,0:T(8,128)}), f32[4,64,1024]{2,1,0:T(8,128)S(1)}, u32[]{:S(2)}, u32[]{:S(2)}) %all-to-all-start.3) | async-done | bytes 1048608 | tf_op jit(solution)/shard_map/all_to_all | solution.py:128
  92.7 3.7 %all-to-all-start.1 = ((f32[4,64,1024]{2,1,0:T(8,128)}), f32[4,64,1024]{2,1,0:T(8,128)S(1)}, u32[]{:S(2)}, u32[]{:S(2)}) async-start(f32[4,64,1024]{2,1,0:T(8,128)} %pad_maximum_fusion.4), calls=%async_computation.1 | async-start | bytes 2097152 | tf_op jit(solution)/shard_map/all_to_all | solution.py:128
  96.5 10.6 %all-to-all-done.1 = f32[4,64,1024]{2,1,0:T(8,128)S(1)} async-done(((f32[4,64,1024]{2,1,0:T(8,128)}), f32[4,64,1024]{2,1,0:T(8,128)S(1)}, u32[]{:S(2)}, u32[]{:S(2)}) %all-to-all-start.1) | async-done | bytes 1048608 | tf_op jit(solution)/shard_map/all_to_all | solution.py:128
  107.4 1.5 %fusion = f32[8,64]{1,0:T(8,128)S(1)} fusion(f32[8,64,1024]{2,1,0:T(8,128)S(1)} %bitcast.125, s32[64]{0:T(128)S(1)} %and_select_fusion.1, s32[64]{0:T(128)S(1)} %get-tuple-element.2), kind=kOutput, calls=%fused_computation.2 | convolution fusion | flops 404229632 | bytes 2099712 | tf_op jit(solution)/shard_map/or,mrc->moc/dot_general | solution.py:136
  109.0 1.1 collective-permute-done.6
  111.1 2.7 %collective-permute-start.9 = (f32[2,16,16]{2,1,0:T(8,128)S(1)}, f32[2,16,16]{2,1,0:T(8,128)S(1)}, u32[]{:S(2)}, u32[]{:S(2)}) collective-permute-start(f32[2,16,16]{2,1,0:T(8,128)S(1)} %pad_maximum_fusion.10), channel_id=1, source_target_pairs={{0,96},{32,64},{64,32},{96,0},{1,97},{33,65},{65,33},{97,1},{2,98}... | collective-permute-start | bytes 6152 | tf_op jit(solution)/shard_map/ppermute | solution.py:37
  114.0 1.8 %collective-permute-done.8 = f32[2,16,16]{2,1,0:T(8,128)S(1)} collective-permute-done((f32[2,16,16]{2,1,0:T(8,128)S(1)}, f32[2,16,16]{2,1,0:T(8,128)S(1)}, u32[]{:S(2)}, u32[]{:S(2)}) %collective-permute-start.8) | collective-permute-done | bytes 2080 | tf_op jit(solution)/shard_map/ppermute | solution.py:37
  116.1 1.5 %collective-permute-done.7 = f32[2,16,16]{2,1,0:T(8,128)S(1)} collective-permute-done((f32[2,16,16]{2,1,0:T(8,128)S(1)}, f32[2,16,16]{2,1,0:T(8,128)S(1)}, u32[]{:S(2)}, u32[]{:S(2)}) %collective-permute-start.7) | collective-permute-done | bytes 2080 | tf_op jit(solution)/shard_map/ppermute | solution.py:37
  117.5 4.4 %collective-permute-start.11 = (f32[2,16,16]{2,1,0:T(8,128)S(1)}, f32[2,16,16]{2,1,0:T(8,128)S(1)}, u32[]{:S(2)}, u32[]{:S(2)}) collective-permute-start(f32[2,16,16]{2,1,0:T(8,128)S(1)} %add_add_fusion.2), channel_id=1, source_target_pairs={{0,4},{2,6},{4,0},{6,2},{8,12},{10,14},{12,8},{14,10},{16,20},{18,... | collective-permute-start | bytes 6152 | tf_op jit(solution)/shard_map/ppermute | solution.py:37
  121.9 2.4 %collective-permute-start.12 = (f32[2,16,16]{2,1,0:T(8,128)S(1)}, f32[2,16,16]{2,1,0:T(8,128)S(1)}, u32[]{:S(2)}, u32[]{:S(2)}) collective-permute-start(f32[2,16,16]{2,1,0:T(8,128)S(1)} %add_add_fusion.2), channel_id=1, source_target_pairs={{0,6},{2,4},{4,2},{6,0},{8,14},{10,12},{12,10},{14,8},{16,22},{18,... | collective-permute-start | bytes 6152 | tf_op jit(solution)/shard_map/ppermute | solution.py:37
  124.3 0.8 collective-permute-start.10
  125.1 1.8 %collective-permute-done.12 = f32[2,16,16]{2,1,0:T(8,128)S(1)} collective-permute-done((f32[2,16,16]{2,1,0:T(8,128)S(1)}, f32[2,16,16]{2,1,0:T(8,128)S(1)}, u32[]{:S(2)}, u32[]{:S(2)}) %collective-permute-start.12) | collective-permute-done | bytes 2080 | tf_op jit(solution)/shard_map/ppermute | solution.py:37
  126.9 1.2 collective-permute-done.10
  128.1 5.0 %collective-permute-start.14 = (f32[2,16,16]{2,1,0:T(8,128)S(1)}, f32[2,16,16]{2,1,0:T(8,128)S(1)}, u32[]{:S(2)}, u32[]{:S(2)}) collective-permute-start(f32[2,16,16]{2,1,0:T(8,128)S(1)} %add_add_fusion.1), channel_id=1, source_target_pairs={{0,16},{2,18},{4,20},{6,22},{8,24},{10,26},{12,28},{14,30},{16,0},... | collective-permute-start | bytes 6152 | tf_op jit(solution)/shard_map/ppermute | solution.py:37
  134.8 3.2 %collective-permute-done.15 = f32[2,16,16]{2,1,0:T(8,128)S(1)} collective-permute-done((f32[2,16,16]{2,1,0:T(8,128)S(1)}, f32[2,16,16]{2,1,0:T(8,128)S(1)}, u32[]{:S(2)}, u32[]{:S(2)}) %collective-permute-start.15) | collective-permute-done | bytes 2080 | tf_op jit(solution)/shard_map/ppermute | solution.py:37
  138.2 1.5 %cholesky.17 = f32[16,16]{1,0:T(8,128)S(1)} custom-call(f32[16,16]{1,0:T(8,128)S(1)} %fusion.17), custom_call_target="Cholesky" | custom-call | tf_op jit(solution)/shard_map/jit(cholesky)/cholesky | solution.py:154
  140.9 1.2 custom-call.10
  (164 shorter events, 22.5 us)
Async XLA Ops:
  3.7 4.5 %copy-start.1 = (f32[64,1024]{1,0:T(8,128)S(1)}, f32[64,1024]{1,0:T(8,128)}, u32[]{:S(2)}) copy-start(f32[64,1024]{1,0:T(8,128)} %param.12) | copy-start | bytes 786436
  3.7 4.5 %copy-start.3 = (f32[64,1024]{1,0:T(8,128)S(1)}, f32[64,1024]{1,0:T(8,128)}, u32[]{:S(2)}) copy-start(f32[64,1024]{1,0:T(8,128)} %param.11) | copy-start | bytes 786436
  3.7 4.5 %copy-start.5 = (f32[64,1024]{1,0:T(8,128)S(1)}, f32[64,1024]{1,0:T(8,128)}, u32[]{:S(2)}) copy-start(f32[64,1024]{1,0:T(8,128)} %param.13) | copy-start | bytes 786436
  3.7 4.6 %copy-start.26 = (f32[64,1024]{1,0:T(8,128)S(1)}, f32[64,1024]{1,0:T(8,128)}, u32[]{:S(2)}) copy-start(f32[64,1024]{1,0:T(8,128)} %param.14) | copy-start | bytes 786436
  3.8 14.8 %copy-start.28 = (f32[8,128]{1,0:T(8,128)S(1)}, f32[8,128]{1,0:T(8,128)}, u32[]{:S(2)}) copy-start(f32[8,128]{1,0:T(8,128)} %param.15) | copy-start | bytes 12292
  3.8 21.0 %all-to-all-start = ((f32[4,64,1024]{2,1,0:T(8,128)}), f32[4,64,1024]{2,1,0:T(8,128)S(1)}, u32[]{:S(2)}, u32[]{:S(2)}) async-start(f32[4,64,1024]{2,1,0:T(8,128)} %get-tuple-element.8), calls=%async_computation | async-start | bytes 2097152 | tf_op jit(solution)/shard_map/all_to_all | solution.py:112
  8.3 10.5 %collective-permute-start.3 = (f32[4,7,1024]{2,1,0:T(8,128)S(1)}, f32[4,7,1024]{2,1,0:T(8,128)S(1)}, u32[]{:S(2)}, u32[]{:S(2)}) collective-permute-start(f32[4,7,1024]{2,1,0:T(8,128)S(1)} %get-tuple-element.59), channel_id=1, source_target_pairs={{2,0},{4,2},{6,4},{8,6},{10,8},{12,10},{14,12},{16,14},{18,16},{20... | collective-permute-start | bytes 344072 | tf_op jit(solution)/shard_map/ppermute | solution.py:23
  9.6 9.3 %collective-permute-start.2 = (f32[4,7,1024]{2,1,0:T(8,128)S(1)}, f32[4,7,1024]{2,1,0:T(8,128)}, u32[]{:S(2)}, u32[]{:S(2)}) collective-permute-start(f32[4,7,1024]{2,1,0:T(8,128)S(1)} %get-tuple-element.58), channel_id=1, source_target_pairs={{0,2},{2,4},{4,6},{6,8},{8,10},{10,12},{12,14},{14,16},{16,18},{18... | collective-permute-start | bytes 344072 | tf_op jit(solution)/shard_map/ppermute | solution.py:21
  24.8 18.9 %all-to-all-start.2 = ((f32[4,64,1024]{2,1,0:T(8,128)}), f32[4,64,1024]{2,1,0:T(8,128)}, u32[]{:S(2)}, u32[]{:S(2)}) async-start(f32[4,64,1024]{2,1,0:T(8,128)} %get-tuple-element.9), calls=%async_computation.2 | async-start | bytes 2097152 | tf_op jit(solution)/shard_map/all_to_all | solution.py:112
  32.3 18.2 %collective-permute-start.1 = (f32[4,7,1024]{2,1,0:T(8,128)S(1)}, f32[4,7,1024]{2,1,0:T(8,128)S(1)}, u32[]{:S(2)}, u32[]{:S(2)}) collective-permute-start(f32[4,7,1024]{2,1,0:T(8,128)S(1)} %get-tuple-element.57), channel_id=1, source_target_pairs={{2,0},{4,2},{6,4},{8,6},{10,8},{12,10},{14,12},{16,14},{18,16},{20... | collective-permute-start | bytes 344072 | tf_op jit(solution)/shard_map/ppermute | solution.py:23
  33.6 16.9 %collective-permute-start = (f32[4,7,1024]{2,1,0:T(8,128)S(1)}, f32[4,7,1024]{2,1,0:T(8,128)S(1)}, u32[]{:S(2)}, u32[]{:S(2)}) collective-permute-start(f32[4,7,1024]{2,1,0:T(8,128)S(1)} %get-tuple-element.56), channel_id=1, source_target_pairs={{0,2},{2,4},{4,6},{6,8},{8,10},{10,12},{12,14},{14,16},{16,18},{18... | collective-permute-start | bytes 344072 | tf_op jit(solution)/shard_map/ppermute | solution.py:21
  44.7 6.9 %collective-permute-start.5 = (f32[4,7,1024]{2,1,0:T(8,128)S(1)}, f32[4,7,1024]{2,1,0:T(8,128)S(1)}, u32[]{:S(2)}, u32[]{:S(2)}) collective-permute-start(f32[4,7,1024]{2,1,0:T(8,128)S(1)} %get-tuple-element.61), channel_id=1, source_target_pairs={{2,0},{4,2},{6,4},{8,6},{10,8},{12,10},{14,12},{16,14},{18,16},{20... | collective-permute-start | bytes 344072 | tf_op jit(solution)/shard_map/ppermute | solution.py:23
  46.0 7.1 %collective-permute-start.4 = (f32[4,7,1024]{2,1,0:T(8,128)S(1)}, f32[4,7,1024]{2,1,0:T(8,128)S(1)}, u32[]{:S(2)}, u32[]{:S(2)}) collective-permute-start(f32[4,7,1024]{2,1,0:T(8,128)S(1)} %get-tuple-element.60), channel_id=1, source_target_pairs={{0,2},{2,4},{4,6},{6,8},{8,10},{10,12},{12,14},{14,16},{16,18},{18... | collective-permute-start | bytes 344072 | tf_op jit(solution)/shard_map/ppermute | solution.py:21
  54.4 1.2 copy-start.13
  54.4 1.2 copy-start.14
  54.5 1.3 copy-start.15
  58.8 1.1 copy-start.10
  58.8 1.2 copy-start.11
  58.8 1.3 copy-start.12
  58.8 1.2 copy-start.33
  63.0 1.1 copy-start.18
  63.0 1.2 copy-start.24
  63.0 1.3 copy-start.25
  63.0 1.3 copy-start.32
  67.0 1.1 copy-start.21
  67.0 1.2 copy-start.22
  67.0 1.3 copy-start.23
  67.0 1.3 copy-start.31
  74.0 1.1 copy-start.6
  74.0 1.1 copy-start.35
  77.3 15.4 %all-to-all-start.3 = ((f32[4,64,1024]{2,1,0:T(8,128)}), f32[4,64,1024]{2,1,0:T(8,128)S(1)}, u32[]{:S(2)}, u32[]{:S(2)}) async-start(f32[4,64,1024]{2,1,0:T(8,128)} %pad_maximum_fusion.5), calls=%async_computation.3 | async-start | bytes 2097152 | tf_op jit(solution)/shard_map/all_to_all | solution.py:128
  82.9 13.6 %copy-start.34 = (s32[1,64]{1,0:T(1,128)S(1)}, s32[1,64]{1,0:T(1,128)}, u32[]{:S(2)}) copy-start(s32[1,64]{1,0:T(1,128)} %param.16) | copy-start | bytes 772
  92.7 14.4 %all-to-all-start.1 = ((f32[4,64,1024]{2,1,0:T(8,128)}), f32[4,64,1024]{2,1,0:T(8,128)S(1)}, u32[]{:S(2)}, u32[]{:S(2)}) async-start(f32[4,64,1024]{2,1,0:T(8,128)} %pad_maximum_fusion.4), calls=%async_computation.1 | async-start | bytes 2097152 | tf_op jit(solution)/shard_map/all_to_all | solution.py:128
  107.4 35.2 %copy-start = (f32[4,2,64,1024]{3,2,1,0:T(8,128)}, f32[4,2,64,1024]{3,2,1,0:T(8,128)S(1)}, u32[]{:S(2)}) copy-start(f32[4,2,64,1024]{3,2,1,0:T(8,128)S(1)} %copy.19) | copy-start | bytes 6291460
  107.4 1.6 %copy-start.37 = (f32[1,64]{1,0:T(1,128)S(1)}, f32[1,64]{1,0:T(1,128)}, u32[]{:S(2)}) copy-start(f32[1,64]{1,0:T(1,128)} %param.19) | copy-start | bytes 772
  107.4 2.9 %copy-start.36 = (f32[1,64,16]{1,2,0:T(8,128)S(1)}, f32[1,64,16]{1,2,0:T(8,128)}, u32[]{:S(2)}) copy-start(f32[1,64,16]{1,2,0:T(8,128)} %param.18) | copy-start | bytes 12292
  107.4 2.9 %copy-start.38 = (f32[1,64]{1,0:T(1,128)S(1)}, f32[1,64]{1,0:T(1,128)}, u32[]{:S(2)}) copy-start(f32[1,64]{1,0:T(1,128)} %param.17) | copy-start | bytes 772
  108.9 1.2 collective-permute-start.6
  110.5 5.3 %collective-permute-start.8 = (f32[2,16,16]{2,1,0:T(8,128)S(1)}, f32[2,16,16]{2,1,0:T(8,128)S(1)}, u32[]{:S(2)}, u32[]{:S(2)}) collective-permute-start(f32[2,16,16]{2,1,0:T(8,128)S(1)} %pad_maximum_fusion.10), channel_id=1, source_target_pairs={{0,64},{32,96},{64,0},{96,32},{1,65},{33,97},{65,1},{97,33},{2,66}... | collective-permute-start | bytes 6152 | tf_op jit(solution)/shard_map/ppermute | solution.py:37
  111.1 4.9 %collective-permute-start.9 = (f32[2,16,16]{2,1,0:T(8,128)S(1)}, f32[2,16,16]{2,1,0:T(8,128)S(1)}, u32[]{:S(2)}, u32[]{:S(2)}) collective-permute-start(f32[2,16,16]{2,1,0:T(8,128)S(1)} %pad_maximum_fusion.10), channel_id=1, source_target_pairs={{0,96},{32,64},{64,32},{96,0},{1,97},{33,65},{65,33},{97,1},{2,98}... | collective-permute-start | bytes 6152 | tf_op jit(solution)/shard_map/ppermute | solution.py:37
  113.8 3.7 %collective-permute-start.7 = (f32[2,16,16]{2,1,0:T(8,128)S(1)}, f32[2,16,16]{2,1,0:T(8,128)S(1)}, u32[]{:S(2)}, u32[]{:S(2)}) collective-permute-start(f32[2,16,16]{2,1,0:T(8,128)S(1)} %pad_maximum_fusion.10), channel_id=1, source_target_pairs={{0,32},{32,0},{64,96},{96,64},{1,33},{33,1},{65,97},{97,65},{2,34}... | collective-permute-start | bytes 6152 | tf_op jit(solution)/shard_map/ppermute | solution.py:37
  114.0 11.0 %collective-permute-start.16 = (f32[8,128]{1,0:T(8,128)S(1)}, f32[8,128]{1,0:T(8,128)S(1)}, u32[]{:S(2)}, u32[]{:S(2)}) collective-permute-start(f32[8,128]{1,0:T(8,128)S(1)} %copy-done.28), channel_id=1, source_target_pairs={{0,1},{1,0},{2,3},{3,2},{4,5},{5,4},{6,7},{7,6},{8,9},{9,8},{10,11... | collective-permute-start | bytes 12296 | tf_op jit(solution)/shard_map/ppermute | solution.py:49
  117.5 7.6 %collective-permute-start.11 = (f32[2,16,16]{2,1,0:T(8,128)S(1)}, f32[2,16,16]{2,1,0:T(8,128)S(1)}, u32[]{:S(2)}, u32[]{:S(2)}) collective-permute-start(f32[2,16,16]{2,1,0:T(8,128)S(1)} %add_add_fusion.2), channel_id=1, source_target_pairs={{0,4},{2,6},{4,0},{6,2},{8,12},{10,14},{12,8},{14,10},{16,20},{18,... | collective-permute-start | bytes 6152 | tf_op jit(solution)/shard_map/ppermute | solution.py:37
  121.9 4.9 %collective-permute-start.12 = (f32[2,16,16]{2,1,0:T(8,128)S(1)}, f32[2,16,16]{2,1,0:T(8,128)S(1)}, u32[]{:S(2)}, u32[]{:S(2)}) collective-permute-start(f32[2,16,16]{2,1,0:T(8,128)S(1)} %add_add_fusion.2), channel_id=1, source_target_pairs={{0,6},{2,4},{4,2},{6,0},{8,14},{10,12},{12,10},{14,8},{16,22},{18,... | collective-permute-start | bytes 6152 | tf_op jit(solution)/shard_map/ppermute | solution.py:37
  124.3 3.7 %collective-permute-start.10 = (f32[2,16,16]{2,1,0:T(8,128)S(1)}, f32[2,16,16]{2,1,0:T(8,128)S(1)}, u32[]{:S(2)}, u32[]{:S(2)}) collective-permute-start(f32[2,16,16]{2,1,0:T(8,128)S(1)} %add_add_fusion.2), channel_id=1, source_target_pairs={{0,2},{2,0},{4,6},{6,4},{8,10},{10,8},{12,14},{14,12},{16,18},{18,... | collective-permute-start | bytes 6152 | tf_op jit(solution)/shard_map/ppermute | solution.py:37
  128.1 6.8 %collective-permute-start.14 = (f32[2,16,16]{2,1,0:T(8,128)S(1)}, f32[2,16,16]{2,1,0:T(8,128)S(1)}, u32[]{:S(2)}, u32[]{:S(2)}) collective-permute-start(f32[2,16,16]{2,1,0:T(8,128)S(1)} %add_add_fusion.1), channel_id=1, source_target_pairs={{0,16},{2,18},{4,20},{6,22},{8,24},{10,26},{12,28},{14,30},{16,0},... | collective-permute-start | bytes 6152 | tf_op jit(solution)/shard_map/ppermute | solution.py:37
  133.1 4.9 %collective-permute-start.15 = (f32[2,16,16]{2,1,0:T(8,128)S(1)}, f32[2,16,16]{2,1,0:T(8,128)S(1)}, u32[]{:S(2)}, u32[]{:S(2)}) collective-permute-start(f32[2,16,16]{2,1,0:T(8,128)S(1)} %add_add_fusion.1), channel_id=1, source_target_pairs={{0,24},{2,26},{4,28},{6,30},{8,16},{10,18},{12,20},{14,22},{16,8},... | collective-permute-start | bytes 6152 | tf_op jit(solution)/shard_map/ppermute | solution.py:37
  133.8 4.2 %collective-permute-start.13 = (f32[2,16,16]{2,1,0:T(8,128)S(1)}, f32[2,16,16]{2,1,0:T(8,128)S(1)}, u32[]{:S(2)}, u32[]{:S(2)}) collective-permute-start(f32[2,16,16]{2,1,0:T(8,128)S(1)} %add_add_fusion.1), channel_id=1, source_target_pairs={{0,8},{2,10},{4,12},{6,14},{8,0},{10,2},{12,4},{14,6},{16,24},{18,... | collective-permute-start | bytes 6152 | tf_op jit(solution)/shard_map/ppermute | solution.py:37
  (12 other events, 11.2 us)

commit v11 on v8

--- a/solution.py
+++ b/solution.py
@@ -99,13 +99,40 @@
     spread_params = jnp.repeat(my_params, band_width, axis=1)
 
     fields = jnp.stack([diffusivity, velocity_x, velocity_y, source_shape])
-    wide = with_halo(jnp.concatenate([mine, fields]), "space", depth)
+    own = jnp.concatenate([mine, fields])
+    wide = with_halo(own, "space", depth)
     count = slices * group
-    wide_state = wide[:count]
-    wide_coeffs = wide[count : count + 3]
-    wide_forcing = jnp.tile(wide[count + 3][None] * spread_params[:, None, :], (slices, 1, 1))
     global_rows = first_row - depth + jnp.arange(row_count + 2 * depth, dtype=jnp.int32)
     wide_inside = ((global_rows >= 0) & (global_rows < slabs)).astype(jnp.float32)[:, None]
+
+    def block_steps(block, inside):
+        states = block[:count]
+        coeffs = block[count : count + 3]
+        forcing = jnp.tile(block[count + 3][None] * spread_params[:, None, :], (slices, 1, 1))
+
+        def step(values, off, step_size, q):
+            lo, hi = off + 1, off + values.shape[1] - 1
+            q = None if q is None else q[:, lo:hi]
+            return advance(values, coeffs[:, lo:hi], inside[lo:hi], step_size, q)
+
+        coarse = step(states, 0, coarse_dt, None)
+        current = states
+        for section in range(FINE):
+            current = step(current, section, FINE_DT, forcing)
+        return current, coarse[:, FINE - 1 : FINE - 1 + current.shape[1]]
+
+    inner_fine, inner_coarse = block_steps(own, wide_inside[depth : depth + row_count])
+    strip = depth + 2 * FINE
+    strips = jnp.concatenate([wide[:, :strip], wide[:, -strip:]], axis=1)
+    strips_inside = jnp.concatenate([wide_inside[:strip], wide_inside[-strip:]])
+    edge_fine, edge_coarse = block_steps(strips, strips_inside)
+
+    def stitch(edges, inner):
+        return jnp.concatenate([edges[:, :depth], inner, edges[:, strip : strip + depth]], axis=1)
+
+    current = stitch(edge_fine, inner_fine)
+    coarse_part = stitch(edge_coarse, inner_coarse)
+    wide_coeffs = wide[count : count + 3]
 
     def step(values, low, step_size, forcing):
         n = values.shape[1]
@@ -113,11 +140,6 @@
         q = None if forcing is None else forcing[:, lo:hi]
         return advance(values, wide_coeffs[:, lo:hi], wide_inside[lo:hi], step_size, q)
 
-    current = wide_state
-    coarse_part = step(wide_state, 0, coarse_dt, None)
-    for section in range(FINE):
-        current = step(current, section, FINE_DT, wide_forcing)
-    coarse_part = coarse_part[:, FINE - 1 : FINE - 1 + current.shape[1]]
     fine = current.reshape(slices, group, -1, col_count)
     coarse_part = coarse_part.reshape(slices, group, -1, col_count)
     running = fine[0]

time: 136 us -> 135 us (level)
  blocking collectives: 30.7 us -> 0 us
  waiting for transfers between devices: 37.9 us -> 62.1 us
  starting transfers between devices: 26.7 us -> 29.8 us
  local copies, waits for them, and re-layouts: 15.3 us -> 17 us
  other arithmetic: 20.2 us -> 21.7 us
    all_to_all x1 -> x0, blocking collectives: 30.7 us -> none  [per_device(): lax.all_to_all(state.reshape(slices, group, row_count, col_count), 'tm',...]
    all_to_all x0 -> x1, waiting for transfers between devices: none -> 17.9 us  [per_device(): lax.all_to_all(state.reshape(slices, group, row_count, col_count), 'tm',...]
    all_to_all x0 -> x1, starting transfers between devices: none -> 4.52 us  [per_device(): lax.all_to_all(state.reshape(slices, group, row_count, col_count), 'tm',...]
    mul x2 -> x10, local copies, waits for them, and re-layouts: 0.14 us -> 3.77 us  [the longest x4 3.35 us: advance(): coeffs[2] * (below_row - above_row) * 0.5]
    slice x7 -> x2, local copies, waits for them, and re-layouts: 3.76 us -> 0.14 us  [step(): wide_inside[lo:hi]]
    ppermute x1, waiting for transfers between devices: 1.25 us -> 4.14 us  [with_halo(): lax.ppermute(head, axis, [(i + 1, i) for i in range(ends)])]
    mul x6 -> x8, local copies, waits for them, and re-layouts: 0.69 us -> 2.99 us  [advance(): coeffs[0] * (above_row + below_row + west_cell + east_cell - 4.0 * middle)]
    ppermute x1, waiting for transfers between devices: 1.18 us -> 3.12 us  [with_halo(): lax.ppermute(tail, axis, [(i, i + 1) for i in range(ends)])]
  transfers between devices with their start and end apart: 14 -> 15, of which waited for: 10 -> 11; matrix products, arithmetic and copies ran while one was open for 3% -> 8% of each run, Pallas kernels for 0% -> 0%
where the time goes in v11:
time: 135 us
  waiting for transfers between devices  62.1 us (46%)
  starting transfers between devices  29.8 us (22%)
  other arithmetic  21.7 us (16%)
  local copies, waits for them, and re-layouts  17 us (13%)
  matrix products  2.96 us (2%)
  between operations  1.36 us (1%)
    all_to_all x1, waiting for transfers between devices, per_device(): lax.all_to_all(done, 'tm', 0, 0, tiled=True)  24.1 us
    all_to_all x1, waiting for transfers between devices, per_device(): lax.all_to_all(state.reshape(slices, group, row_count, col_count), 'tm',...  17.9 us
    ppermute x9, starting transfers between devices, quad_sum(): lax.ppermute(value, axis, [(i, i ^ k * bit) for i in range(count)])  16.1 us
    mul x9, other arithmetic, advance(): return (middle + step_size * tendency) * inside  12.4 us
    ppermute x9, waiting for transfers between devices, quad_sum(): lax.ppermute(value, axis, [(i, i ^ k * bit) for i in range(count)])  11.7 us
    slice x11, local copies, waits for them, and re-layouts, advance(): west_cell = jnp.pad(middle[:, :, :-1], ((0, 0), (0, 0), (1, 0)))  6.24 us
    all_to_all x1, starting transfers between devices, per_device(): lax.all_to_all(state.reshape(slices, group, row_count, col_count), 'tm',...  4.52 us
    ppermute x1, waiting for transfers between devices, with_halo(): lax.ppermute(head, axis, [(i + 1, i) for i in range(ends)])  4.14 us
  transfers between devices with their start and end apart: 15, of which 11 were waited for; matrix products, arithmetic and copies ran while one was open for 8% of the time, Pallas kernels for 0%

profile of v11, /device:TPU:0, one launch (start us, length us, event | category | flops | bytes accessed | tf_op | source)
XLA Modules:
  0.0 134.9 jit_solution(11011900978430349611)
XLA Ops:
  0.7 4.5 %all-to-all-start = ((f32[4,2,64,1024]{3,2,1,0:T(8,128)}), f32[4,2,64,1024]{3,2,1,0:T(8,128)S(1)}, u32[]{:S(2)}, u32[]{:S(2)}) async-start(f32[4,2,64,1024]{3,2,1,0:T(8,128)} %bitcast.181), calls=%async_computation | async-start | bytes 4194304 | tf_op jit(solution)/shard_map/all_to_all | solution.py:95
  5.3 0.7 slice_bitcast_fusion.11
  6.0 0.7 slice_bitcast_fusion.8
  6.9 0.7 slice_bitcast_fusion.14
  8.5 0.7 slice_bitcast_fusion.5
  9.2 1.0 broadcast_multiply_fusion
  10.3 0.8 slice_bitcast_fusion.12
  11.1 0.8 slice_bitcast_fusion.9
  11.9 0.8 slice_bitcast_fusion.6
  12.8 0.8 slice_bitcast_fusion.3
  13.6 17.9 %all-to-all-done = f32[4,2,64,1024]{3,2,1,0:T(8,128)S(1)} async-done(((f32[4,2,64,1024]{3,2,1,0:T(8,128)}), f32[4,2,64,1024]{3,2,1,0:T(8,128)S(1)}, u32[]{:S(2)}, u32[]{:S(2)}) %all-to-all-start) | async-done | bytes 2097184 | tf_op jit(solution)/shard_map/all_to_all | solution.py:95
  31.5 0.9 fusion.67
  33.7 2.1 %fusion.8 = (f32[8,62,1024]{2,1,0:T(8,128)S(1)}, f32[8,62,1024]{2,1,0:T(8,128)S(1)}, f32[8,62,1024]{2,1,0:T(8,128)S(1)}) fusion(f32[8,64,1024]{2,1,0:T(8,128)S(1)} %bitcast.159, f32[62]{0:T(128)S(1)} %slice.620, f32[8,64,1024]{2,1,0:T(8,128)S(1)} %bitcast.158, f32[62,1024]{1,0:T(8,128)S(1)} %copy-done.10, f32[62,1024]{1,0:T(8,128)S(1)} %copy-done.11, ...), kind=kLoop, calls=%fused_computation.12 | loop fusion | flops 9142272 | bytes 19042680 | tf_op jit(solution)/shard_map/mul | solution.py:68
  35.8 1.1 fusion.66
  36.9 2.1 %fusion.5 = f32[8,60,1024]{2,1,0:T(8,128)S(1)} fusion(f32[8,64,1024]{2,1,0:T(8,128)S(1)} %bitcast.160, f32[8,62,1024]{2,1,0:T(8,128)S(1)} %get-tuple-element.6, f32[8,60,1023]{2,1,0:T(8,128)S(1)} %get-tuple-element.27, f32[8,60,1023]{2,1,0:T(8,128)S(1)} %get-tuple-element.26, f32[60]{0:T(128)S(1)} %slice.630, f32[60,1024]{1,0:T(8,128)S(1)} %copy-done.8, ...), kind=kLoop, calls=%fused_computation.8 | loop fusion | flops 8847360 | bytes 14496240 | tf_op jit(solution)/shard_map/mul | solution.py:68
  39.1 1.1 fusion.65
  40.2 2.1 %fusion.2 = f32[8,58,1024]{2,1,0:T(8,128)S(1)} fusion(f32[8,64,1024]{2,1,0:T(8,128)S(1)} %bitcast.161, f32[8,60,1024]{2,1,0:T(8,128)S(1)} %fusion.5, f32[8,58,1023]{2,1,0:T(8,128)S(1)} %get-tuple-element.25, f32[8,58,1023]{2,1,0:T(8,128)S(1)} %get-tuple-element.24, f32[58]{0:T(128)S(1)} %slice.640, f32[58,1024]{1,0:T(8,128)S(1)} %copy-done.6, ...), kind=kLoop, calls=%fused_computation.4 | loop fusion | flops 8552448 | bytes 14013032 | tf_op jit(solution)/shard_map/mul | solution.py:68
  42.3 0.9 fusion.64
  43.5 3.6 %collective-permute-start = (f32[12,7,1024]{2,1,0:T(8,128)S(1)}, f32[12,7,1024]{2,1,0:T(8,128)S(1)}, u32[]{:S(2)}, u32[]{:S(2)}) collective-permute-start(f32[12,7,1024]{2,1,0:T(8,128)S(1)} %get-tuple-element.14), channel_id=1, source_target_pairs={{0,2},{2,4},{4,6},{6,8},{8,10},{10,12},{12,14},{14,16},{16,18},{18... | collective-permute-start | bytes 1032200 | tf_op jit(solution)/shard_map/ppermute | solution.py:21
  47.1 1.5 %collective-permute-start.1 = (f32[12,7,1024]{2,1,0:T(8,128)S(1)}, f32[12,7,1024]{2,1,0:T(8,128)S(1)}, u32[]{:S(2)}, u32[]{:S(2)}) collective-permute-start(f32[12,7,1024]{2,1,0:T(8,128)S(1)} %get-tuple-element.15), channel_id=1, source_target_pairs={{2,0},{4,2},{6,4},{8,6},{10,8},{12,10},{14,12},{16,14},{18,16},{20... | collective-permute-start | bytes 1032200 | tf_op jit(solution)/shard_map/ppermute | solution.py:23
  48.6 2.5 %fusion.10 = (f32[8,56,1024]{2,1,0:T(8,128)S(1)}, f32[8,56,1024]{2,1,0:T(8,128)S(1)}) fusion(f32[8,62,1024]{2,1,0:T(8,128)S(1)} %get-tuple-element.7, f32[8,62,1024]{2,1,0:T(8,128)S(1)} %get-tuple-element.21, f32[56]{0:T(128)S(1)} %slice.650, f32[8,64,1024]{2,1,0:T(8,128)S(1)} %bitcast.162, f32[56,1024]{1,0:T(8,128)S(1)} %copy-done.13, ...), kind=kLoop, calls=%fused_computation.19 | loop fusion | flops 9175040 | bytes 19034848 | tf_op jit(solution)/shard_map/mul | solution.py:68
  51.1 3.1 %collective-permute-done = f32[12,7,1024]{2,1,0:T(8,128)S(1)} collective-permute-done((f32[12,7,1024]{2,1,0:T(8,128)S(1)}, f32[12,7,1024]{2,1,0:T(8,128)S(1)}, u32[]{:S(2)}, u32[]{:S(2)}) %collective-permute-start) | collective-permute-done | bytes 344096 | tf_op jit(solution)/shard_map/ppermute | solution.py:21
  54.3 4.1 %collective-permute-done.1 = f32[12,7,1024]{2,1,0:T(8,128)S(1)} collective-permute-done((f32[12,7,1024]{2,1,0:T(8,128)S(1)}, f32[12,7,1024]{2,1,0:T(8,128)S(1)}, u32[]{:S(2)}, u32[]{:S(2)}) %collective-permute-start.1) | collective-permute-done | bytes 344096 | tf_op jit(solution)/shard_map/ppermute | solution.py:23
  59.4 0.8 add_multiply_fusion
  61.2 1.0 fusion.18
  62.5 0.7 fusion.27
  63.6 0.7 fusion.24
  67.7 1.5 %pad_maximum_fusion.1 = f32[4,2,64,1024]{3,2,1,0:T(8,128)} fusion(f32[1,2,64,1024]{3,2,1,0:T(8,128)S(1)} %get-tuple-element.55, f32[1,2,64,1024]{3,2,1,0:T(8,128)S(1)} %get-tuple-element.54, f32[1,2,64,1024]{3,2,1,0:T(8,128)S(1)} %slice_bitcast_fusion, f32[1,2,64,1024]{3,2,1,0:T(8,128)S(1)} %slice_bitcast_fusion.1), kind=kLoop, calls=%fused_computation.13 | loop fusion | flops 1572864 | bytes 4194304 | tf_op jit(solution)/shard_map/stack | solution.py:152
  69.2 3.7 %all-to-all-start.1 = ((f32[4,2,64,1024]{3,2,1,0:T(8,128)}), f32[4,2,64,1024]{3,2,1,0:T(8,128)S(1)}, u32[]{:S(2)}, u32[]{:S(2)}) async-start(f32[4,2,64,1024]{3,2,1,0:T(8,128)} %pad_maximum_fusion.1), calls=%async_computation.1 | async-start | bytes 4194304 | tf_op jit(solution)/shard_map/all_to_all | solution.py:153
  73.0 24.1 %all-to-all-done.1 = f32[4,2,64,1024]{3,2,1,0:T(8,128)S(1)} async-done(((f32[4,2,64,1024]{3,2,1,0:T(8,128)}), f32[4,2,64,1024]{3,2,1,0:T(8,128)S(1)}, u32[]{:S(2)}, u32[]{:S(2)}) %all-to-all-start.1) | async-done | bytes 2097184 | tf_op jit(solution)/shard_map/all_to_all | solution.py:153
  97.1 1.5 %fusion.9 = f32[8,64]{1,0:T(8,128)S(1)} fusion(f32[8,64,1024]{2,1,0:T(8,128)S(1)} %bitcast.167, s32[64]{0:T(128)S(1)} %and_select_fusion.1, s32[64]{0:T(128)S(1)} %get-tuple-element.2), kind=kOutput, calls=%fused_computation.15 | convolution fusion | flops 404229632 | bytes 2099712 | tf_op jit(solution)/shard_map/or,mrc->moc/dot_general | solution.py:162
  98.9 1.1 collective-permute-done.2
  101.0 2.1 %collective-permute-start.4 = (f32[2,16,16]{2,1,0:T(8,128)S(1)}, f32[2,16,16]{2,1,0:T(8,128)S(1)}, u32[]{:S(2)}, u32[]{:S(2)}) collective-permute-start(f32[2,16,16]{2,1,0:T(8,128)S(1)} %pad_maximum_fusion.11), channel_id=1, source_target_pairs={{0,64},{32,96},{64,0},{96,32},{1,65},{33,97},{65,1},{97,33},{2,66}... | collective-permute-start | bytes 6152 | tf_op jit(solution)/shard_map/ppermute | solution.py:37
  103.1 2.1 %collective-permute-start.5 = (f32[2,16,16]{2,1,0:T(8,128)S(1)}, f32[2,16,16]{2,1,0:T(8,128)S(1)}, u32[]{:S(2)}, u32[]{:S(2)}) collective-permute-start(f32[2,16,16]{2,1,0:T(8,128)S(1)} %pad_maximum_fusion.11), channel_id=1, source_target_pairs={{0,96},{32,64},{64,32},{96,0},{1,97},{33,65},{65,33},{97,1},{2,98}... | collective-permute-start | bytes 6152 | tf_op jit(solution)/shard_map/ppermute | solution.py:37
  105.2 1.1 collective-permute-done.4
  106.3 1.8 %collective-permute-done.5 = f32[2,16,16]{2,1,0:T(8,128)S(1)} collective-permute-done((f32[2,16,16]{2,1,0:T(8,128)S(1)}, f32[2,16,16]{2,1,0:T(8,128)S(1)}, u32[]{:S(2)}, u32[]{:S(2)}) %collective-permute-start.5) | collective-permute-done | bytes 2080 | tf_op jit(solution)/shard_map/ppermute | solution.py:37
  108.1 1.6 %collective-permute-start.6 = (f32[2,16,16]{2,1,0:T(8,128)S(1)}, f32[2,16,16]{2,1,0:T(8,128)S(1)}, u32[]{:S(2)}, u32[]{:S(2)}) collective-permute-start(f32[2,16,16]{2,1,0:T(8,128)S(1)} %add_add_fusion.2), channel_id=1, source_target_pairs={{0,2},{2,0},{4,6},{6,4},{8,10},{10,8},{12,14},{14,12},{16,18},{18,... | collective-permute-start | bytes 6152 | tf_op jit(solution)/shard_map/ppermute | solution.py:37
  109.7 5.0 %collective-permute-start.7 = (f32[2,16,16]{2,1,0:T(8,128)S(1)}, f32[2,16,16]{2,1,0:T(8,128)S(1)}, u32[]{:S(2)}, u32[]{:S(2)}) collective-permute-start(f32[2,16,16]{2,1,0:T(8,128)S(1)} %add_add_fusion.2), channel_id=1, source_target_pairs={{0,4},{2,6},{4,0},{6,2},{8,12},{10,14},{12,8},{14,10},{16,20},{18,... | collective-permute-start | bytes 6152 | tf_op jit(solution)/shard_map/ppermute | solution.py:37
  114.7 2.0 %collective-permute-done.7 = f32[2,16,16]{2,1,0:T(8,128)S(1)} collective-permute-done((f32[2,16,16]{2,1,0:T(8,128)S(1)}, f32[2,16,16]{2,1,0:T(8,128)S(1)}, u32[]{:S(2)}, u32[]{:S(2)}) %collective-permute-start.7) | collective-permute-done | bytes 2080 | tf_op jit(solution)/shard_map/ppermute | solution.py:37
  116.7 3.0 %collective-permute-done.8 = f32[2,16,16]{2,1,0:T(8,128)S(1)} collective-permute-done((f32[2,16,16]{2,1,0:T(8,128)S(1)}, f32[2,16,16]{2,1,0:T(8,128)S(1)}, u32[]{:S(2)}, u32[]{:S(2)}) %collective-permute-start.8) | collective-permute-done | bytes 2080 | tf_op jit(solution)/shard_map/ppermute | solution.py:37
  119.7 3.7 %collective-permute-start.10 = (f32[2,16,16]{2,1,0:T(8,128)S(1)}, f32[2,16,16]{2,1,0:T(8,128)S(1)}, u32[]{:S(2)}, u32[]{:S(2)}) collective-permute-start(f32[2,16,16]{2,1,0:T(8,128)S(1)} %add_add_fusion.1), channel_id=1, source_target_pairs={{0,16},{2,18},{4,20},{6,22},{8,24},{10,26},{12,28},{14,30},{16,0},... | collective-permute-start | bytes 6152 | tf_op jit(solution)/shard_map/ppermute | solution.py:37
  123.3 1.0 collective-permute-start.11
  124.3 0.7 collective-permute-done.10
  125.0 3.2 %collective-permute-done.11 = f32[2,16,16]{2,1,0:T(8,128)S(1)} collective-permute-done((f32[2,16,16]{2,1,0:T(8,128)S(1)}, f32[2,16,16]{2,1,0:T(8,128)S(1)}, u32[]{:S(2)}, u32[]{:S(2)}) %collective-permute-start.11) | collective-permute-done | bytes 2080 | tf_op jit(solution)/shard_map/ppermute | solution.py:37
  128.4 1.5 %cholesky.17 = f32[16,16]{1,0:T(8,128)S(1)} custom-call(f32[16,16]{1,0:T(8,128)S(1)} %fusion.42), custom_call_target="Cholesky" | custom-call | tf_op jit(solution)/shard_map/jit(cholesky)/cholesky | solution.py:180
  131.2 1.2 custom-call.10
  132.7 0.9 fusion.15
  133.6 1.3 copy.19
  (123 shorter events, 11.7 us)
Async XLA Ops:
  0.6 4.7 %copy-start = (f32[64,1024]{1,0:T(8,128)S(1)}, f32[64,1024]{1,0:T(8,128)}, u32[]{:S(2)}) copy-start(f32[64,1024]{1,0:T(8,128)} %param.13) | copy-start | bytes 786436
  0.6 7.6 %copy-start.16 = (f32[8,128]{1,0:T(8,128)S(1)}, f32[8,128]{1,0:T(8,128)}, u32[]{:S(2)}) copy-start(f32[8,128]{1,0:T(8,128)} %param.15) | copy-start | bytes 12292
  0.7 30.9 %all-to-all-start = ((f32[4,2,64,1024]{3,2,1,0:T(8,128)}), f32[4,2,64,1024]{3,2,1,0:T(8,128)S(1)}, u32[]{:S(2)}, u32[]{:S(2)}) async-start(f32[4,2,64,1024]{3,2,1,0:T(8,128)} %bitcast.181), calls=%async_computation | async-start | bytes 4194304 | tf_op jit(solution)/shard_map/all_to_all | solution.py:95
  5.2 5.1 %copy-start.1 = (f32[64,1024]{1,0:T(8,128)S(1)}, f32[64,1024]{1,0:T(8,128)}, u32[]{:S(2)}) copy-start(f32[64,1024]{1,0:T(8,128)} %param.11) | copy-start | bytes 786436
  5.2 5.1 %copy-start.2 = (f32[64,1024]{1,0:T(8,128)S(1)}, f32[64,1024]{1,0:T(8,128)}, u32[]{:S(2)}) copy-start(f32[64,1024]{1,0:T(8,128)} %param.12) | copy-start | bytes 786436
  32.6 1.0 copy-start.4
  32.6 1.0 copy-start.10
  32.6 1.1 copy-start.11
  35.8 1.1 copy-start.3
  35.8 1.1 copy-start.8
  35.8 1.1 copy-start.9
  39.0 1.1 copy-start.5
  39.0 1.1 copy-start.6
  39.0 1.1 copy-start.7
  42.3 1.0 copy-start.12
  43.2 5.4 %copy-start.13 = (f32[56,1024]{1,0:T(8,128)S(1)}, f32[56,1024]{1,0:T(8,128)}, u32[]{:S(2)}) copy-start(f32[56,1024]{1,0:T(8,128)} %get-tuple-element.72) | copy-start | bytes 688132
  43.2 5.4 %copy-start.14 = (f32[56,1024]{1,0:T(8,128)S(1)}, f32[56,1024]{1,0:T(8,128)}, u32[]{:S(2)}) copy-start(f32[56,1024]{1,0:T(8,128)} %get-tuple-element.73) | copy-start | bytes 688132
  43.2 5.4 %copy-start.15 = (f32[56,1024]{1,0:T(8,128)S(1)}, f32[56,1024]{1,0:T(8,128)}, u32[]{:S(2)}) copy-start(f32[56,1024]{1,0:T(8,128)} %slice_bitcast_fusion.14) | copy-start | bytes 688132
  43.5 10.8 %collective-permute-start = (f32[12,7,1024]{2,1,0:T(8,128)S(1)}, f32[12,7,1024]{2,1,0:T(8,128)S(1)}, u32[]{:S(2)}, u32[]{:S(2)}) collective-permute-start(f32[12,7,1024]{2,1,0:T(8,128)S(1)} %get-tuple-element.14), channel_id=1, source_target_pairs={{0,2},{2,4},{4,6},{6,8},{8,10},{10,12},{12,14},{14,16},{16,18},{18... | collective-permute-start | bytes 1032200 | tf_op jit(solution)/shard_map/ppermute | solution.py:21
  47.1 11.3 %collective-permute-start.1 = (f32[12,7,1024]{2,1,0:T(8,128)S(1)}, f32[12,7,1024]{2,1,0:T(8,128)S(1)}, u32[]{:S(2)}, u32[]{:S(2)}) collective-permute-start(f32[12,7,1024]{2,1,0:T(8,128)S(1)} %get-tuple-element.15), channel_id=1, source_target_pairs={{2,0},{4,2},{6,4},{8,6},{10,8},{12,10},{14,12},{16,14},{18,16},{20... | collective-permute-start | bytes 1032200 | tf_op jit(solution)/shard_map/ppermute | solution.py:23
  69.2 3.8 %copy-start.17 = (s32[1,64]{1,0:T(1,128)S(1)}, s32[1,64]{1,0:T(1,128)}, u32[]{:S(2)}) copy-start(s32[1,64]{1,0:T(1,128)} %param.16) | copy-start | bytes 772
  69.2 27.9 %all-to-all-start.1 = ((f32[4,2,64,1024]{3,2,1,0:T(8,128)}), f32[4,2,64,1024]{3,2,1,0:T(8,128)S(1)}, u32[]{:S(2)}, u32[]{:S(2)}) async-start(f32[4,2,64,1024]{3,2,1,0:T(8,128)} %pad_maximum_fusion.1), calls=%async_computation.1 | async-start | bytes 4194304 | tf_op jit(solution)/shard_map/all_to_all | solution.py:153
  72.9 26.0 %copy-start.19 = (f32[1,64]{1,0:T(1,128)S(1)}, f32[1,64]{1,0:T(1,128)}, u32[]{:S(2)}) copy-start(f32[1,64]{1,0:T(1,128)} %param.19) | copy-start | bytes 772
  72.9 27.3 %copy-start.18 = (f32[1,64,16]{1,2,0:T(8,128)S(1)}, f32[1,64,16]{1,2,0:T(8,128)}, u32[]{:S(2)}) copy-start(f32[1,64,16]{1,2,0:T(8,128)} %param.18) | copy-start | bytes 12292
  72.9 27.3 %copy-start.20 = (f32[1,64]{1,0:T(1,128)S(1)}, f32[1,64]{1,0:T(1,128)}, u32[]{:S(2)}) copy-start(f32[1,64]{1,0:T(1,128)} %param.17) | copy-start | bytes 772
  98.6 1.5 %collective-permute-start.2 = (f32[8,64]{1,0:T(8,128)S(1)}, f32[8,64]{1,0:T(8,128)S(1)}, u32[]{:S(2)}, u32[]{:S(2)}) collective-permute-start(f32[8,64]{1,0:T(8,128)S(1)} %fusion.9), channel_id=1, source_target_pairs={{0,1},{1,0},{2,3},{3,2},{4,5},{5,4},{6,7},{7,6},{8,9},{9,8},{10,11... | collective-permute-start | bytes 6152 | tf_op jit(solution)/shard_map/ppermute | solution.py:49
  100.4 4.8 %collective-permute-start.3 = (f32[2,16,16]{2,1,0:T(8,128)S(1)}, f32[2,16,16]{2,1,0:T(8,128)S(1)}, u32[]{:S(2)}, u32[]{:S(2)}) collective-permute-start(f32[2,16,16]{2,1,0:T(8,128)S(1)} %pad_maximum_fusion.11), channel_id=1, source_target_pairs={{0,32},{32,0},{64,96},{96,64},{1,33},{33,1},{65,97},{97,65},{2,34}... | collective-permute-start | bytes 6152 | tf_op jit(solution)/shard_map/ppermute | solution.py:37
  101.0 5.2 %collective-permute-start.4 = (f32[2,16,16]{2,1,0:T(8,128)S(1)}, f32[2,16,16]{2,1,0:T(8,128)S(1)}, u32[]{:S(2)}, u32[]{:S(2)}) collective-permute-start(f32[2,16,16]{2,1,0:T(8,128)S(1)} %pad_maximum_fusion.11), channel_id=1, source_target_pairs={{0,64},{32,96},{64,0},{96,32},{1,65},{33,97},{65,1},{97,33},{2,66}... | collective-permute-start | bytes 6152 | tf_op jit(solution)/shard_map/ppermute | solution.py:37
  103.1 4.9 %collective-permute-start.5 = (f32[2,16,16]{2,1,0:T(8,128)S(1)}, f32[2,16,16]{2,1,0:T(8,128)S(1)}, u32[]{:S(2)}, u32[]{:S(2)}) collective-permute-start(f32[2,16,16]{2,1,0:T(8,128)S(1)} %pad_maximum_fusion.11), channel_id=1, source_target_pairs={{0,96},{32,64},{64,32},{96,0},{1,97},{33,65},{65,33},{97,1},{2,98}... | collective-permute-start | bytes 6152 | tf_op jit(solution)/shard_map/ppermute | solution.py:37
  105.2 9.5 %collective-permute-start.12 = (f32[8,128]{1,0:T(8,128)S(1)}, f32[8,128]{1,0:T(8,128)S(1)}, u32[]{:S(2)}, u32[]{:S(2)}) collective-permute-start(f32[8,128]{1,0:T(8,128)S(1)} %copy-done.16), channel_id=1, source_target_pairs={{0,1},{1,0},{2,3},{3,2},{4,5},{5,4},{6,7},{7,6},{8,9},{9,8},{10,11... | collective-permute-start | bytes 12296 | tf_op jit(solution)/shard_map/ppermute | solution.py:49
  108.1 6.7 %collective-permute-start.6 = (f32[2,16,16]{2,1,0:T(8,128)S(1)}, f32[2,16,16]{2,1,0:T(8,128)S(1)}, u32[]{:S(2)}, u32[]{:S(2)}) collective-permute-start(f32[2,16,16]{2,1,0:T(8,128)S(1)} %add_add_fusion.2), channel_id=1, source_target_pairs={{0,2},{2,0},{4,6},{6,4},{8,10},{10,8},{12,14},{14,12},{16,18},{18,... | collective-permute-start | bytes 6152 | tf_op jit(solution)/shard_map/ppermute | solution.py:37
  109.7 7.0 %collective-permute-start.7 = (f32[2,16,16]{2,1,0:T(8,128)S(1)}, f32[2,16,16]{2,1,0:T(8,128)S(1)}, u32[]{:S(2)}, u32[]{:S(2)}) collective-permute-start(f32[2,16,16]{2,1,0:T(8,128)S(1)} %add_add_fusion.2), channel_id=1, source_target_pairs={{0,4},{2,6},{4,0},{6,2},{8,12},{10,14},{12,8},{14,10},{16,20},{18,... | collective-permute-start | bytes 6152 | tf_op jit(solution)/shard_map/ppermute | solution.py:37
  114.7 4.9 %collective-permute-start.8 = (f32[2,16,16]{2,1,0:T(8,128)S(1)}, f32[2,16,16]{2,1,0:T(8,128)S(1)}, u32[]{:S(2)}, u32[]{:S(2)}) collective-permute-start(f32[2,16,16]{2,1,0:T(8,128)S(1)} %add_add_fusion.2), channel_id=1, source_target_pairs={{0,6},{2,4},{4,2},{6,0},{8,14},{10,12},{12,10},{14,8},{16,22},{18,... | collective-permute-start | bytes 6152 | tf_op jit(solution)/shard_map/ppermute | solution.py:37
  119.7 5.4 %collective-permute-start.10 = (f32[2,16,16]{2,1,0:T(8,128)S(1)}, f32[2,16,16]{2,1,0:T(8,128)S(1)}, u32[]{:S(2)}, u32[]{:S(2)}) collective-permute-start(f32[2,16,16]{2,1,0:T(8,128)S(1)} %add_add_fusion.1), channel_id=1, source_target_pairs={{0,16},{2,18},{4,20},{6,22},{8,24},{10,26},{12,28},{14,30},{16,0},... | collective-permute-start | bytes 6152 | tf_op jit(solution)/shard_map/ppermute | solution.py:37
  123.3 4.9 %collective-permute-start.11 = (f32[2,16,16]{2,1,0:T(8,128)S(1)}, f32[2,16,16]{2,1,0:T(8,128)S(1)}, u32[]{:S(2)}, u32[]{:S(2)}) collective-permute-start(f32[2,16,16]{2,1,0:T(8,128)S(1)} %add_add_fusion.1), channel_id=1, source_target_pairs={{0,24},{2,26},{4,28},{6,30},{8,16},{10,18},{12,20},{14,22},{16,8},... | collective-permute-start | bytes 6152 | tf_op jit(solution)/shard_map/ppermute | solution.py:37
  124.3 3.9 %collective-permute-start.9 = (f32[2,16,16]{2,1,0:T(8,128)S(1)}, f32[2,16,16]{2,1,0:T(8,128)S(1)}, u32[]{:S(2)}, u32[]{:S(2)}) collective-permute-start(f32[2,16,16]{2,1,0:T(8,128)S(1)} %add_add_fusion.1), channel_id=1, source_target_pairs={{0,8},{2,10},{4,12},{6,14},{8,0},{10,2},{12,4},{14,6},{16,24},{18,... | collective-permute-start | bytes 6152 | tf_op jit(solution)/shard_map/ppermute | solution.py:37

commit v12 on v11

--- a/solution.py
+++ b/solution.py
@@ -99,9 +99,21 @@
     spread_params = jnp.repeat(my_params, band_width, axis=1)
 
     fields = jnp.stack([diffusivity, velocity_x, velocity_y, source_shape])
+    count = slices * group
+    both = jnp.concatenate([state, fields])
+    spaces = lax.axis_size("space")
+    from_above = lax.ppermute(
+        both[:, row_count - depth :], "space", [(i, i + 1) for i in range(spaces - 1)]
+    )
+    from_below = lax.ppermute(both[:, :depth], "space", [(i + 1, i) for i in range(spaces - 1)])
+    edge_states = jnp.concatenate([from_above[:members_here], from_below[:members_here]], axis=1)
+    edge_states = lax.all_to_all(
+        edge_states.reshape(slices, group, 2 * depth, col_count), "tm", 0, 0, tiled=True
+    ).reshape(count, 2 * depth, col_count)
+    above = jnp.concatenate([edge_states[:, :depth], from_above[members_here:]])
+    below = jnp.concatenate([edge_states[:, depth:], from_below[members_here:]])
     own = jnp.concatenate([mine, fields])
-    wide = with_halo(own, "space", depth)
-    count = slices * group
+    wide_fields = jnp.concatenate([from_above[members_here:], fields, from_below[members_here:]], axis=1)
     global_rows = first_row - depth + jnp.arange(row_count + 2 * depth, dtype=jnp.int32)
     wide_inside = ((global_rows >= 0) & (global_rows < slabs)).astype(jnp.float32)[:, None]
 
@@ -123,7 +135,9 @@
 
     inner_fine, inner_coarse = block_steps(own, wide_inside[depth : depth + row_count])
     strip = depth + 2 * FINE
-    strips = jnp.concatenate([wide[:, :strip], wide[:, -strip:]], axis=1)
+    strips = jnp.concatenate(
+        [above, own[:, : strip - depth], own[:, row_count - (strip - depth) :], below], axis=1
+    )
     strips_inside = jnp.concatenate([wide_inside[:strip], wide_inside[-strip:]])
     edge_fine, edge_coarse = block_steps(strips, strips_inside)
 
@@ -132,7 +146,7 @@
 
     current = stitch(edge_fine, inner_fine)
     coarse_part = stitch(edge_coarse, inner_coarse)
-    wide_coeffs = wide[count : count + 3]
+    wide_coeffs = wide_fields[:3]
 
     def step(values, low, step_size, forcing):
         n = values.shape[1]

time: 135 us -> 170 us (1.26)
  local copies, waits for them, and re-layouts: 17 us -> 49.4 us
  starting transfers between devices: 29.8 us -> 32.1 us
    unnamed x47 -> x118, local copies, waits for them, and re-layouts: 2.43 us -> 19.9 us
    concatenate x0 -> x3, local copies, waits for them, and re-layouts: none -> 7.3 us  [the longest x1 6.89 us: per_device(): both = jnp.concatenate([state, fields])]
    slice x1 -> x27, local copies, waits for them, and re-layouts: 0.08 us -> 6.47 us  [the longest x1 1.29 us: per_device(): both[:, row_count - depth:]]
    all_to_all x0 -> x1, starting transfers between devices: none -> 4.29 us  [per_device(): lax.all_to_all(edge_states.reshape(slices, group, 2 * depth, col_count),...]
    mul x4 -> x0, local copies, waits for them, and re-layouts: 3.35 us -> none  [advance(): coeffs[2] * (below_row - above_row) * 0.5]
    mul x8 -> x4, local copies, waits for them, and re-layouts: 2.99 us -> 0.14 us  [advance(): coeffs[0] * (above_row + below_row + west_cell + east_cell - 4.0 * middle)]
    ppermute x9, starting transfers between devices: 16.1 us -> 13.6 us  [quad_sum(): lax.ppermute(value, axis, [(i, i ^ k * bit) for i in range(count)])]
    slice x4, local copies, waits for them, and re-layouts: 0.29 us -> 2.47 us  [step(): return advance(values, coeffs[:, lo:hi], inside[lo:hi], step_size, q)]
  transfers between devices with their start and end apart: 15 -> 16, of which waited for: 11 -> 11; matrix products, arithmetic and copies ran while one was open for 8% -> 14% of each run, Pallas kernels for 0% -> 0%
where the time goes in v12:
time: 170 us; the launch traced here: 169 us
  waiting for transfers between devices  60.5 us (36%)
  local copies, waits for them, and re-layouts  49.4 us (29%)
  starting transfers between devices  32.1 us (19%)
  other arithmetic  22.7 us (13%)
  matrix products  2.89 us (2%)
  between operations  1.78 us (1%)
    all_to_all x1, waiting for transfers between devices, per_device(): lax.all_to_all(done, 'tm', 0, 0, tiled=True)  23.5 us
    unnamed x118, local copies, waits for them, and re-layouts  19.9 us
    all_to_all x1, waiting for transfers between devices, per_device(): lax.all_to_all(state.reshape(slices, group, row_count, col_count), 'tm',...  18.1 us
    ppermute x9, starting transfers between devices, quad_sum(): lax.ppermute(value, axis, [(i, i ^ k * bit) for i in range(count)])  13.6 us
    mul x9, other arithmetic, advance(): return (middle + step_size * tendency) * inside  12.6 us
    ppermute x9, waiting for transfers between devices, quad_sum(): lax.ppermute(value, axis, [(i, i ^ k * bit) for i in range(count)])  10.4 us
    ppermute x1, waiting for transfers between devices, per_device(): lax.ppermute(both[:, :depth], 'space', [(i + 1, i) for i in range(spaces...  7.32 us
    concatenate x1, local copies, waits for them, and re-layouts, per_device(): both = jnp.concatenate([state, fields])  6.89 us
  transfers between devices with their start and end apart: 16, of which 11 were waited for; matrix products, arithmetic and copies ran while one was open for 14% of the time, Pallas kernels for 0%

profile of v12, /device:TPU:0, one launch (start us, length us, event | category | flops | bytes accessed | tf_op | source)
XLA Modules:
  0.0 169.4 jit_solution(12974121728247014884)
XLA Ops:
  0.7 2.9 %copy.62 = f32[1,8,64,1024]{3,1,2,0:T(8,128)S(1)} copy(f32[1,8,64,1024]{3,2,1,0:T(8,128)} %param.10) | data formatting | bytes 4194304 | tf_op args[0]
  4.4 6.9 %concatenate.46 = f32[12,64,1024]{2,0,1:T(8,128)} concatenate(f32[8,64,1024]{2,0,1:T(8,128)S(1)} %bitcast.182, f32[1,64,1024]{2,0,1:T(1,128)S(1)} %stack.39, f32[1,64,1024]{2,0,1:T(1,128)S(1)} %stack.40, f32[1,64,1024]{2,0,1:T(1,128)S(1)} %stack.41, f32[1,64,1024]{2,0,1:T(1,128)S(1)} %stack.42), dimensions={0} | concatenate | bytes 6291456 | tf_op jit(solution)/shard_map/concatenate | solution.py:103
  11.3 1.3 fusion.59
  12.6 4.3 %collective-permute-start = (f32[12,7,1024]{2,0,1:T(8,128)S(1)}, f32[12,7,1024]{2,0,1:T(8,128)}, u32[]{:S(2)}, u32[]{:S(2)}) collective-permute-start(f32[12,7,1024]{2,0,1:T(8,128)S(1)} %get-tuple-element.8), channel_id=1, source_target_pairs={{0,2},{2,4},{4,6},{6,8},{8,10},{10,12},{12,14},{14,16},{16,18},{18... | collective-permute-start | bytes 1032200 | tf_op jit(solution)/shard_map/ppermute | solution.py:105
  16.9 1.3 collective-permute-start.1
  19.4 0.9 broadcast_multiply_fusion
  20.3 0.9 copy_bitcast_fusion.13
  21.2 0.9 copy_bitcast_fusion.16
  22.7 0.9 copy_bitcast_fusion.10
  23.6 7.3 %collective-permute-done.1 = f32[12,7,1024]{2,0,1:T(8,128)} collective-permute-done((f32[12,7,1024]{2,0,1:T(8,128)S(1)}, f32[12,7,1024]{2,0,1:T(8,128)}, u32[]{:S(2)}, u32[]{:S(2)}) %collective-permute-start.1) | collective-permute-done | bytes 344096 | tf_op jit(solution)/shard_map/ppermute | solution.py:108
  30.9 1.0 slice.719
  31.9 1.0 slice.717
  33.1 0.8 copy.16
  34.0 4.3 %all-to-all-start = ((f32[4,2,14,1024]{3,1,2,0:T(2,128)}), f32[4,2,14,1024]{3,1,2,0:T(2,128)S(1)}, u32[]{:S(2)}, u32[]{:S(2)}) async-start(f32[4,2,14,1024]{3,1,2,0:T(2,128)} %copy.16), calls=%async_computation | async-start | bytes 917504 | tf_op jit(solution)/shard_map/all_to_all | solution.py:110
  46.2 0.9 copy_bitcast_fusion.7
  47.1 1.0 slice.721
  48.1 1.0 slice.725
  49.8 4.8 %all-to-all-start.1 = ((f32[4,2,64,1024]{3,2,1,0:T(8,128)}), f32[4,2,64,1024]{3,2,1,0:T(8,128)S(1)}, u32[]{:S(2)}, u32[]{:S(2)}) async-start(f32[4,2,64,1024]{3,2,1,0:T(8,128)} %bitcast.183), calls=%async_computation.1 | async-start | bytes 4194304 | tf_op jit(solution)/shard_map/all_to_all | solution.py:95
  54.6 1.0 pad_maximum_fusion.3
  59.2 0.9 copy_bitcast_fusion.1
  61.1 18.1 %all-to-all-done.1 = f32[4,2,64,1024]{3,2,1,0:T(8,128)S(1)} async-done(((f32[4,2,64,1024]{3,2,1,0:T(8,128)}), f32[4,2,64,1024]{3,2,1,0:T(8,128)S(1)}, u32[]{:S(2)}, u32[]{:S(2)}) %all-to-all-start.1) | async-done | bytes 2097184 | tf_op jit(solution)/shard_map/all_to_all | solution.py:95
  81.5 0.9 fusion.66
  84.5 0.9 fusion.17
  89.4 2.3 %fusion.8 = (f32[8,62,1024]{2,1,0:T(8,128)S(1)}, f32[8,62,1024]{2,1,0:T(8,128)S(1)}, f32[8,62,1024]{2,1,0:T(8,128)S(1)}) fusion(f32[8,64,1024]{2,1,0:T(8,128)S(1)} %bitcast.172, f32[62]{0:T(128)S(1)} %copy-done.40, f32[8,64,1024]{2,1,0:T(8,128)S(1)} %bitcast.171, f32[62,1024]{1,0:T(8,128)S(1)} %copy-done.26, f32[62,1024]{1,0:T(8,128)S(1)} %copy-done.27, ...), kind=kLoop, calls=%fused_computation.12 | loop fusion | flops 9142272 | bytes 19042680 | tf_op jit(solution)/shard_map/mul | solution.py:68
  91.7 0.9 fusion.65
  92.8 2.1 %fusion.5 = f32[8,60,1024]{2,1,0:T(8,128)S(1)} fusion(f32[8,64,1024]{2,1,0:T(8,128)S(1)} %bitcast.173, f32[8,62,1024]{2,1,0:T(8,128)S(1)} %get-tuple-element.6, f32[8,60,1023]{2,1,0:T(8,128)S(1)} %get-tuple-element.23, f32[8,60,1023]{2,1,0:T(8,128)S(1)} %get-tuple-element.22, f32[60]{0:T(128)S(1)} %copy-done.37, f32[60,1024]{1,0:T(8,128)S(1)} %copy-done.28, ...), kind=kLoop, calls=%fused_computation.8 | loop fusion | flops 8847360 | bytes 14496240 | tf_op jit(solution)/shard_map/mul | solution.py:68
  94.9 1.1 fusion.64
  96.0 2.1 %fusion.2 = f32[8,58,1024]{2,1,0:T(8,128)S(1)} fusion(f32[8,64,1024]{2,1,0:T(8,128)S(1)} %bitcast.174, f32[8,60,1024]{2,1,0:T(8,128)S(1)} %fusion.5, f32[8,58,1023]{2,1,0:T(8,128)S(1)} %get-tuple-element.21, f32[8,58,1023]{2,1,0:T(8,128)S(1)} %get-tuple-element.20, f32[58]{0:T(128)S(1)} %copy-done.36, f32[58,1024]{1,0:T(8,128)S(1)} %copy-done.30, ...), kind=kLoop, calls=%fused_computation.4 | loop fusion | flops 8552448 | bytes 14013032 | tf_op jit(solution)/shard_map/mul | solution.py:68
  98.2 0.9 fusion.63
  99.3 2.5 %fusion.10 = (f32[8,56,1024]{2,1,0:T(8,128)S(1)}, f32[8,56,1024]{2,1,0:T(8,128)S(1)}) fusion(f32[8,62,1024]{2,1,0:T(8,128)S(1)} %get-tuple-element.7, f32[8,62,1024]{2,1,0:T(8,128)S(1)} %get-tuple-element.17, f32[56]{0:T(128)S(1)} %copy-done.38, f32[8,64,1024]{2,1,0:T(8,128)S(1)} %bitcast.175, f32[56,1024]{1,0:T(8,128)S(1)} %copy-done.32, ...), kind=kLoop, calls=%fused_computation.20 | loop fusion | flops 9175040 | bytes 19034848 | tf_op jit(solution)/shard_map/mul | solution.py:68
  106.9 1.5 pad_maximum_fusion.1
  108.4 3.7 %all-to-all-start.2 = ((f32[4,2,64,1024]{3,2,1,0:T(8,128)}), f32[4,2,64,1024]{3,2,1,0:T(8,128)S(1)}, u32[]{:S(2)}, u32[]{:S(2)}) async-start(f32[4,2,64,1024]{3,2,1,0:T(8,128)} %pad_maximum_fusion.1), calls=%async_computation.2 | async-start | bytes 4194304 | tf_op jit(solution)/shard_map/all_to_all | solution.py:167
  112.2 23.5 %all-to-all-done.2 = f32[4,2,64,1024]{3,2,1,0:T(8,128)S(1)} async-done(((f32[4,2,64,1024]{3,2,1,0:T(8,128)}), f32[4,2,64,1024]{3,2,1,0:T(8,128)S(1)}, u32[]{:S(2)}, u32[]{:S(2)}) %all-to-all-start.2) | async-done | bytes 2097184 | tf_op jit(solution)/shard_map/all_to_all | solution.py:167
  135.8 1.5 fusion.9
  137.4 1.1 collective-permute-done.2
  139.5 2.7 %collective-permute-start.5 = (f32[2,16,16]{2,1,0:T(8,128)S(1)}, f32[2,16,16]{2,1,0:T(8,128)S(1)}, u32[]{:S(2)}, u32[]{:S(2)}) collective-permute-start(f32[2,16,16]{2,1,0:T(8,128)S(1)} %pad_maximum_fusion.13), channel_id=1, source_target_pairs={{0,96},{32,64},{64,32},{96,0},{1,97},{33,65},{65,33},{97,1},{2,98}... | collective-permute-start | bytes 6152 | tf_op jit(solution)/shard_map/ppermute | solution.py:37
  142.4 1.7 %collective-permute-done.4 = f32[2,16,16]{2,1,0:T(8,128)S(1)} collective-permute-done((f32[2,16,16]{2,1,0:T(8,128)S(1)}, f32[2,16,16]{2,1,0:T(8,128)S(1)}, u32[]{:S(2)}, u32[]{:S(2)}) %collective-permute-start.4) | collective-permute-done | bytes 2080 | tf_op jit(solution)/shard_map/ppermute | solution.py:37
  144.4 1.5 collective-permute-done.3
  145.9 2.2 %collective-permute-start.7 = (f32[2,16,16]{2,1,0:T(8,128)S(1)}, f32[2,16,16]{2,1,0:T(8,128)S(1)}, u32[]{:S(2)}, u32[]{:S(2)}) collective-permute-start(f32[2,16,16]{2,1,0:T(8,128)S(1)} %add_add_fusion.2), channel_id=1, source_target_pairs={{0,4},{2,6},{4,0},{6,2},{8,12},{10,14},{12,8},{14,10},{16,20},{18,... | collective-permute-start | bytes 6152 | tf_op jit(solution)/shard_map/ppermute | solution.py:37
  148.1 2.3 %collective-permute-start.8 = (f32[2,16,16]{2,1,0:T(8,128)S(1)}, f32[2,16,16]{2,1,0:T(8,128)S(1)}, u32[]{:S(2)}, u32[]{:S(2)}) collective-permute-start(f32[2,16,16]{2,1,0:T(8,128)S(1)} %add_add_fusion.2), channel_id=1, source_target_pairs={{0,6},{2,4},{4,2},{6,0},{8,14},{10,12},{12,10},{14,8},{16,22},{18,... | collective-permute-start | bytes 6152 | tf_op jit(solution)/shard_map/ppermute | solution.py:37
  151.2 1.8 %collective-permute-done.8 = f32[2,16,16]{2,1,0:T(8,128)S(1)} collective-permute-done((f32[2,16,16]{2,1,0:T(8,128)S(1)}, f32[2,16,16]{2,1,0:T(8,128)S(1)}, u32[]{:S(2)}, u32[]{:S(2)}) %collective-permute-start.8) | collective-permute-done | bytes 2080 | tf_op jit(solution)/shard_map/ppermute | solution.py:37
  153.1 1.1 collective-permute-done.6
  154.2 3.7 %collective-permute-start.10 = (f32[2,16,16]{2,1,0:T(8,128)S(1)}, f32[2,16,16]{2,1,0:T(8,128)S(1)}, u32[]{:S(2)}, u32[]{:S(2)}) collective-permute-start(f32[2,16,16]{2,1,0:T(8,128)S(1)} %add_add_fusion.1), channel_id=1, source_target_pairs={{0,16},{2,18},{4,20},{6,22},{8,24},{10,26},{12,28},{14,30},{16,0},... | collective-permute-start | bytes 6152 | tf_op jit(solution)/shard_map/ppermute | solution.py:37
  157.8 1.0 collective-permute-start.11
  159.6 3.2 %collective-permute-done.11 = f32[2,16,16]{2,1,0:T(8,128)S(1)} collective-permute-done((f32[2,16,16]{2,1,0:T(8,128)S(1)}, f32[2,16,16]{2,1,0:T(8,128)S(1)}, u32[]{:S(2)}, u32[]{:S(2)}) %collective-permute-start.11) | collective-permute-done | bytes 2080 | tf_op jit(solution)/shard_map/ppermute | solution.py:37
  162.9 1.5 cholesky.17
  165.7 1.2 custom-call.10
  168.1 1.3 copy.74
  (226 shorter events, 35.0 us)
Async XLA Ops:
  0.6 2.9 %copy-start.9 = (f32[64,1024]{1,0:T(8,128)S(1)}, f32[64,1024]{1,0:T(8,128)}, u32[]{:S(2)}) copy-start(f32[64,1024]{1,0:T(8,128)} %param.13) | copy-start | bytes 786436
  0.6 3.1 %copy-start.11 = (f32[64,1024]{1,0:T(8,128)S(1)}, f32[64,1024]{1,0:T(8,128)}, u32[]{:S(2)}) copy-start(f32[64,1024]{1,0:T(8,128)} %param.11) | copy-start | bytes 786436
  0.7 3.3 %copy-start.13 = (f32[64,1024]{1,0:T(8,128)S(1)}, f32[64,1024]{1,0:T(8,128)}, u32[]{:S(2)}) copy-start(f32[64,1024]{1,0:T(8,128)} %param.12) | copy-start | bytes 786436
  0.7 3.5 %copy-start.6 = (f32[64,1024]{1,0:T(8,128)S(1)}, f32[64,1024]{1,0:T(8,128)}, u32[]{:S(2)}) copy-start(f32[64,1024]{1,0:T(8,128)} %param.14) | copy-start | bytes 786436
  4.0 15.1 %copy-start = (f32[1,64,1024]{2,0,1:T(1,128)}, f32[1,64,1024]{2,0,1:T(1,128)S(1)}, u32[]{:S(2)}) copy-start(f32[1,64,1024]{2,0,1:T(1,128)S(1)} %stack.40) | copy-start | bytes 786436
  4.2 14.9 %copy-start.2 = (f32[1,64,1024]{2,0,1:T(1,128)}, f32[1,64,1024]{2,0,1:T(1,128)S(1)}, u32[]{:S(2)}) copy-start(f32[1,64,1024]{2,0,1:T(1,128)S(1)} %stack.41) | copy-start | bytes 786436
  4.4 6.9 %copy-start.4 = (f32[1,64,1024]{2,0,1:T(1,128)}, f32[1,64,1024]{2,0,1:T(1,128)S(1)}, u32[]{:S(2)}) copy-start(f32[1,64,1024]{2,0,1:T(1,128)S(1)} %stack.42) | copy-start | bytes 786436
  11.3 7.9 %copy-start.35 = (f32[8,128]{1,0:T(8,128)S(1)}, f32[8,128]{1,0:T(8,128)}, u32[]{:S(2)}) copy-start(f32[8,128]{1,0:T(8,128)} %param.15) | copy-start | bytes 12292
  11.3 8.1 %copy-start.7 = (f32[64,1024]{1,0:T(8,128)S(1)}, f32[64,1024]{1,0:T(8,128)}, u32[]{:S(2)}) copy-start(f32[64,1024]{1,0:T(8,128)} %param.14) | copy-start | bytes 786436
  12.6 19.3 %collective-permute-start = (f32[12,7,1024]{2,0,1:T(8,128)S(1)}, f32[12,7,1024]{2,0,1:T(8,128)}, u32[]{:S(2)}, u32[]{:S(2)}) collective-permute-start(f32[12,7,1024]{2,0,1:T(8,128)S(1)} %get-tuple-element.8), channel_id=1, source_target_pairs={{0,2},{2,4},{4,6},{6,8},{8,10},{10,12},{12,14},{14,16},{16,18},{18... | collective-permute-start | bytes 1032200 | tf_op jit(solution)/shard_map/ppermute | solution.py:105
  16.9 14.0 %collective-permute-start.1 = (f32[12,7,1024]{2,0,1:T(8,128)S(1)}, f32[12,7,1024]{2,0,1:T(8,128)}, u32[]{:S(2)}, u32[]{:S(2)}) collective-permute-start(f32[12,7,1024]{2,0,1:T(8,128)S(1)} %get-tuple-element.9), channel_id=1, source_target_pairs={{2,0},{4,2},{6,4},{8,6},{10,8},{12,10},{14,12},{16,14},{18,16},{20... | collective-permute-start | bytes 1032200 | tf_op jit(solution)/shard_map/ppermute | solution.py:108
  19.1 2.1 %slice-start.3 = ((f32[1,64,1024]{2,0,1:T(1,128)}), f32[1,56,1024]{2,0,1:T(1,128)S(1)}, s32[]{:S(2)}) async-start(f32[1,64,1024]{2,0,1:T(1,128)} %copy-done.2), calls=%async_computation.6 | async-start | bytes 458752 | tf_op jit(solution)/shard_map/slice | solution.py:64
  19.1 2.0 %slice-start = ((f32[1,64,1024]{2,0,1:T(1,128)}), f32[1,56,1024]{2,0,1:T(1,128)S(1)}, s32[]{:S(2)}) async-start(f32[1,64,1024]{2,0,1:T(1,128)} %copy-done), calls=%async_computation.3 | async-start | bytes 458752 | tf_op jit(solution)/shard_map/slice | solution.py:63
  19.1 3.6 %slice-start.1 = ((f32[1,64,1024]{2,0,1:T(1,128)}), f32[1,60,1024]{2,0,1:T(1,128)S(1)}, s32[]{:S(2)}) async-start(f32[1,64,1024]{2,0,1:T(1,128)} %copy-done), calls=%async_computation.4 | async-start | bytes 491520 | tf_op jit(solution)/shard_map/slice | solution.py:63
  19.1 3.6 %slice-start.4 = ((f32[1,64,1024]{2,0,1:T(1,128)}), f32[1,60,1024]{2,0,1:T(1,128)S(1)}, s32[]{:S(2)}) async-start(f32[1,64,1024]{2,0,1:T(1,128)} %copy-done.2), calls=%async_computation.7 | async-start | bytes 491520 | tf_op jit(solution)/shard_map/slice | solution.py:64
  34.0 15.1 %all-to-all-start = ((f32[4,2,14,1024]{3,1,2,0:T(2,128)}), f32[4,2,14,1024]{3,1,2,0:T(2,128)S(1)}, u32[]{:S(2)}, u32[]{:S(2)}) async-start(f32[4,2,14,1024]{3,1,2,0:T(2,128)} %copy.16), calls=%async_computation | async-start | bytes 917504 | tf_op jit(solution)/shard_map/all_to_all | solution.py:110
  40.8 5.5 %slice-start.2 = ((f32[1,64,1024]{2,0,1:T(1,128)}), f32[1,58,1024]{2,0,1:T(1,128)S(1)}, s32[]{:S(2)}) async-start(f32[1,64,1024]{2,0,1:T(1,128)} %copy-done), calls=%async_computation.5 | async-start | bytes 475136 | tf_op jit(solution)/shard_map/slice | solution.py:63
  40.8 5.5 %slice-start.5 = ((f32[1,64,1024]{2,0,1:T(1,128)}), f32[1,58,1024]{2,0,1:T(1,128)S(1)}, s32[]{:S(2)}) async-start(f32[1,64,1024]{2,0,1:T(1,128)} %copy-done.2), calls=%async_computation.8 | async-start | bytes 475136 | tf_op jit(solution)/shard_map/slice | solution.py:64
  49.1 5.6 %copy-start.1 = (f32[1,64,1024]{2,0,1:T(1,128)S(1)}, f32[1,64,1024]{2,0,1:T(1,128)}, u32[]{:S(2)}) copy-start(f32[1,64,1024]{2,0,1:T(1,128)} %copy-done) | copy-start | bytes 786436
  49.1 5.5 %copy-start.3 = (f32[1,64,1024]{2,0,1:T(1,128)S(1)}, f32[1,64,1024]{2,0,1:T(1,128)}, u32[]{:S(2)}) copy-start(f32[1,64,1024]{2,0,1:T(1,128)} %copy-done.2) | copy-start | bytes 786436
  49.1 5.5 %copy-start.5 = (f32[1,64,1024]{2,0,1:T(1,128)S(1)}, f32[1,64,1024]{2,0,1:T(1,128)}, u32[]{:S(2)}) copy-start(f32[1,64,1024]{2,0,1:T(1,128)} %copy-done.4) | copy-start | bytes 786436
  49.8 29.4 %all-to-all-start.1 = ((f32[4,2,64,1024]{3,2,1,0:T(8,128)}), f32[4,2,64,1024]{3,2,1,0:T(8,128)S(1)}, u32[]{:S(2)}, u32[]{:S(2)}) async-start(f32[4,2,64,1024]{3,2,1,0:T(8,128)} %bitcast.183), calls=%async_computation.1 | async-start | bytes 4194304 | tf_op jit(solution)/shard_map/all_to_all | solution.py:95
  57.0 3.1 %copy-start.17 = (f32[4,2,14,1024]{3,1,2,0:T(2,128)S(1)}, f32[4,2,14,1024]{3,1,2,0:T(2,128)}, u32[]{:S(2)}) copy-start(f32[4,2,14,1024]{3,1,2,0:T(2,128)} %copy-done.16) | copy-start | bytes 1376260
  79.2 1.2 copy-start.8
  88.2 1.1 copy-start.27
  88.2 1.1 copy-start.40
  94.9 1.1 copy-start.23
  94.9 1.1 copy-start.30
  94.9 1.1 copy-start.31
  98.2 1.1 copy-start.34
  98.2 1.1 copy-start.38
  104.0 1.1 copy-start.22
  108.4 3.8 %copy-start.43 = (s32[1,64]{1,0:T(1,128)S(1)}, s32[1,64]{1,0:T(1,128)}, u32[]{:S(2)}) copy-start(s32[1,64]{1,0:T(1,128)} %param.16) | copy-start | bytes 772
  108.4 27.4 %all-to-all-start.2 = ((f32[4,2,64,1024]{3,2,1,0:T(8,128)}), f32[4,2,64,1024]{3,2,1,0:T(8,128)S(1)}, u32[]{:S(2)}, u32[]{:S(2)}) async-start(f32[4,2,64,1024]{3,2,1,0:T(8,128)} %pad_maximum_fusion.1), calls=%async_computation.2 | async-start | bytes 4194304 | tf_op jit(solution)/shard_map/all_to_all | solution.py:167
  112.1 25.2 %copy-start.48 = (f32[1,64]{1,0:T(1,128)S(1)}, f32[1,64]{1,0:T(1,128)}, u32[]{:S(2)}) copy-start(f32[1,64]{1,0:T(1,128)} %param.19) | copy-start | bytes 772
  112.1 26.5 %copy-start.47 = (f32[1,64,16]{1,2,0:T(8,128)S(1)}, f32[1,64,16]{1,2,0:T(8,128)}, u32[]{:S(2)}) copy-start(f32[1,64,16]{1,2,0:T(8,128)} %param.18) | copy-start | bytes 12292
  112.2 26.5 %copy-start.49 = (f32[1,64]{1,0:T(1,128)S(1)}, f32[1,64]{1,0:T(1,128)}, u32[]{:S(2)}) copy-start(f32[1,64]{1,0:T(1,128)} %param.17) | copy-start | bytes 772
  137.2 1.2 collective-permute-start.2
  138.8 5.3 %collective-permute-start.4 = (f32[2,16,16]{2,1,0:T(8,128)S(1)}, f32[2,16,16]{2,1,0:T(8,128)S(1)}, u32[]{:S(2)}, u32[]{:S(2)}) collective-permute-start(f32[2,16,16]{2,1,0:T(8,128)S(1)} %pad_maximum_fusion.13), channel_id=1, source_target_pairs={{0,64},{32,96},{64,0},{96,32},{1,65},{33,97},{65,1},{97,33},{2,66}... | collective-permute-start | bytes 6152 | tf_op jit(solution)/shard_map/ppermute | solution.py:37
  139.5 4.9 %collective-permute-start.5 = (f32[2,16,16]{2,1,0:T(8,128)S(1)}, f32[2,16,16]{2,1,0:T(8,128)S(1)}, u32[]{:S(2)}, u32[]{:S(2)}) collective-permute-start(f32[2,16,16]{2,1,0:T(8,128)S(1)} %pad_maximum_fusion.13), channel_id=1, source_target_pairs={{0,96},{32,64},{64,32},{96,0},{1,97},{33,65},{65,33},{97,1},{2,98}... | collective-permute-start | bytes 6152 | tf_op jit(solution)/shard_map/ppermute | solution.py:37
  142.1 3.7 %collective-permute-start.3 = (f32[2,16,16]{2,1,0:T(8,128)S(1)}, f32[2,16,16]{2,1,0:T(8,128)S(1)}, u32[]{:S(2)}, u32[]{:S(2)}) collective-permute-start(f32[2,16,16]{2,1,0:T(8,128)S(1)} %pad_maximum_fusion.13), channel_id=1, source_target_pairs={{0,32},{32,0},{64,96},{96,64},{1,33},{33,1},{65,97},{97,65},{2,34}... | collective-permute-start | bytes 6152 | tf_op jit(solution)/shard_map/ppermute | solution.py:37
  142.4 8.8 %collective-permute-start.12 = (f32[8,128]{1,0:T(8,128)S(1)}, f32[8,128]{1,0:T(8,128)S(1)}, u32[]{:S(2)}, u32[]{:S(2)}) collective-permute-start(f32[8,128]{1,0:T(8,128)S(1)} %copy-done.35), channel_id=1, source_target_pairs={{0,1},{1,0},{2,3},{3,2},{4,5},{5,4},{6,7},{7,6},{8,9},{9,8},{10,11... | collective-permute-start | bytes 12296 | tf_op jit(solution)/shard_map/ppermute | solution.py:49
  145.9 5.3 %collective-permute-start.7 = (f32[2,16,16]{2,1,0:T(8,128)S(1)}, f32[2,16,16]{2,1,0:T(8,128)S(1)}, u32[]{:S(2)}, u32[]{:S(2)}) collective-permute-start(f32[2,16,16]{2,1,0:T(8,128)S(1)} %add_add_fusion.2), channel_id=1, source_target_pairs={{0,4},{2,6},{4,0},{6,2},{8,12},{10,14},{12,8},{14,10},{16,20},{18,... | collective-permute-start | bytes 6152 | tf_op jit(solution)/shard_map/ppermute | solution.py:37
  148.1 4.9 %collective-permute-start.8 = (f32[2,16,16]{2,1,0:T(8,128)S(1)}, f32[2,16,16]{2,1,0:T(8,128)S(1)}, u32[]{:S(2)}, u32[]{:S(2)}) collective-permute-start(f32[2,16,16]{2,1,0:T(8,128)S(1)} %add_add_fusion.2), channel_id=1, source_target_pairs={{0,6},{2,4},{4,2},{6,0},{8,14},{10,12},{12,10},{14,8},{16,22},{18,... | collective-permute-start | bytes 6152 | tf_op jit(solution)/shard_map/ppermute | solution.py:37
  150.4 3.7 %collective-permute-start.6 = (f32[2,16,16]{2,1,0:T(8,128)S(1)}, f32[2,16,16]{2,1,0:T(8,128)S(1)}, u32[]{:S(2)}, u32[]{:S(2)}) collective-permute-start(f32[2,16,16]{2,1,0:T(8,128)S(1)} %add_add_fusion.2), channel_id=1, source_target_pairs={{0,2},{2,0},{4,6},{6,4},{8,10},{10,8},{12,14},{14,12},{16,18},{18,... | collective-permute-start | bytes 6152 | tf_op jit(solution)/shard_map/ppermute | solution.py:37
  154.2 5.4 %collective-permute-start.10 = (f32[2,16,16]{2,1,0:T(8,128)S(1)}, f32[2,16,16]{2,1,0:T(8,128)S(1)}, u32[]{:S(2)}, u32[]{:S(2)}) collective-permute-start(f32[2,16,16]{2,1,0:T(8,128)S(1)} %add_add_fusion.1), channel_id=1, source_target_pairs={{0,16},{2,18},{4,20},{6,22},{8,24},{10,26},{12,28},{14,30},{16,0},... | collective-permute-start | bytes 6152 | tf_op jit(solution)/shard_map/ppermute | solution.py:37
  157.8 4.9 %collective-permute-start.11 = (f32[2,16,16]{2,1,0:T(8,128)S(1)}, f32[2,16,16]{2,1,0:T(8,128)S(1)}, u32[]{:S(2)}, u32[]{:S(2)}) collective-permute-start(f32[2,16,16]{2,1,0:T(8,128)S(1)} %add_add_fusion.1), channel_id=1, source_target_pairs={{0,24},{2,26},{4,28},{6,30},{8,16},{10,18},{12,20},{14,22},{16,8},... | collective-permute-start | bytes 6152 | tf_op jit(solution)/shard_map/ppermute | solution.py:37
  158.8 3.9 %collective-permute-start.9 = (f32[2,16,16]{2,1,0:T(8,128)S(1)}, f32[2,16,16]{2,1,0:T(8,128)S(1)}, u32[]{:S(2)}, u32[]{:S(2)}) collective-permute-start(f32[2,16,16]{2,1,0:T(8,128)S(1)} %add_add_fusion.1), channel_id=1, source_target_pairs={{0,8},{2,10},{4,12},{6,14},{8,0},{10,2},{12,4},{14,6},{16,24},{18,... | collective-permute-start | bytes 6152 | tf_op jit(solution)/shard_map/ppermute | solution.py:37
  (24 other events, 23.1 us)

commit v13 on v11

--- a/solution.py
+++ b/solution.py
@@ -100,7 +100,8 @@
 
     fields = jnp.stack([diffusivity, velocity_x, velocity_y, source_shape])
     own = jnp.concatenate([mine, fields])
-    wide = with_halo(own, "space", depth)
+    wide_fields = with_halo(fields, "space", depth)
+    wide = jnp.concatenate([with_halo(mine, "space", depth), wide_fields])
     count = slices * group
     global_rows = first_row - depth + jnp.arange(row_count + 2 * depth, dtype=jnp.int32)
     wide_inside = ((global_rows >= 0) & (global_rows < slabs)).astype(jnp.float32)[:, None]

time: 135 us -> 132 us (0.978)
  waiting for transfers between devices: 62.1 us -> 42.1 us
  local copies, waits for them, and re-layouts: 17 us -> 25.5 us
  starting transfers between devices: 29.8 us -> 35.5 us
  other arithmetic: 21.7 us -> 23.5 us
    all_to_all x1, waiting for transfers between devices: 17.9 us -> 5.78 us  [per_device(): lax.all_to_all(state.reshape(slices, group, row_count, col_count), 'tm',...]
    ppermute x1 -> x2, starting transfers between devices: 3.64 us -> 9.58 us  [with_halo(): lax.ppermute(tail, axis, [(i, i + 1) for i in range(ends)])]
    ppermute x1 -> x2, waiting for transfers between devices: 4.14 us -> 0.01 us  [with_halo(): lax.ppermute(head, axis, [(i + 1, i) for i in range(ends)])]
    ppermute x1 -> x2, waiting for transfers between devices: 3.12 us -> 0.01 us  [with_halo(): lax.ppermute(tail, axis, [(i, i + 1) for i in range(ends)])]
    slice x4, local copies, waits for them, and re-layouts: 0.29 us -> 2.41 us  [step(): return advance(values, coeffs[:, lo:hi], inside[lo:hi], step_size, q)]
    mul x8 -> x10, local copies, waits for them, and re-layouts: 2.99 us -> 4.95 us  [advance(): coeffs[0] * (above_row + below_row + west_cell + east_cell - 4.0 * middle)]
    unnamed x47 -> x83, local copies, waits for them, and re-layouts: 2.43 us -> 4.21 us
    slice x0 -> x1, other arithmetic: none -> 1.62 us  [with_halo(): tail = cells[:, cells.shape[1] - width:]]
  transfers between devices with their start and end apart: 15 -> 17, of which waited for: 11 -> 10; matrix products, arithmetic and copies ran while one was open for 8% -> 21% of each run, Pallas kernels for 0% -> 0%
where the time goes in v13:
time: 132 us; the launch traced here: 131 us
  waiting for transfers between devices  42.1 us (32%)
  starting transfers between devices  35.5 us (27%)
  local copies, waits for them, and re-layouts  25.5 us (19%)
  other arithmetic  23.5 us (18%)
  matrix products  2.96 us (2%)
  between operations  1.52 us (1%)
    all_to_all x1, waiting for transfers between devices, per_device(): lax.all_to_all(done, 'tm', 0, 0, tiled=True)  24.7 us
    ppermute x9, starting transfers between devices, quad_sum(): lax.ppermute(value, axis, [(i, i ^ k * bit) for i in range(count)])  14.9 us
    mul x9, other arithmetic, advance(): return (middle + step_size * tendency) * inside  12.4 us
    ppermute x9, waiting for transfers between devices, quad_sum(): lax.ppermute(value, axis, [(i, i ^ k * bit) for i in range(count)])  10.5 us
    ppermute x2, starting transfers between devices, with_halo(): lax.ppermute(tail, axis, [(i, i + 1) for i in range(ends)])  9.58 us
    slice x11, local copies, waits for them, and re-layouts, advance(): west_cell = jnp.pad(middle[:, :, :-1], ((0, 0), (0, 0), (1, 0)))  6.22 us
    all_to_all x1, waiting for transfers between devices, per_device(): lax.all_to_all(state.reshape(slices, group, row_count, col_count), 'tm',...  5.78 us
    mul x10, local copies, waits for them, and re-layouts, advance(): coeffs[0] * (above_row + below_row + west_cell + east_cell - 4.0 * middle)  4.95 us
  transfers between devices with their start and end apart: 17, of which 10 were waited for; matrix products, arithmetic and copies ran while one was open for 21% of the time, Pallas kernels for 0%

profile of v13, /device:TPU:0, one launch (start us, length us, event | category | flops | bytes accessed | tf_op | source)
XLA Modules:
  0.0 131.1 jit_solution(1500664634959990587)
XLA Ops:
  0.6 1.6 %pad_maximum_fusion.15 = (f32[4,7,1024]{2,1,0:T(8,128)}, f32[4,7,1024]{2,1,0:T(8,128)}) fusion(f32[1,64,1024]{2,1,0:T(8,128)} %bitcast.187, f32[1,64,1024]{2,1,0:T(8,128)} %bitcast.173, f32[1,64,1024]{2,1,0:T(8,128)} %bitcast.180, f32[1,64,1024]{2,1,0:T(8,128)} %bitcast.166), kind=kLoop, calls=%fused_computation.119 | loop fusion | flops 172032 | bytes 1277952 | tf_op jit(solution)/shard_map/slice | solution.py:18
  2.2 1.3 collective-permute-start.3
  3.6 4.5 %all-to-all-start = ((f32[4,2,64,1024]{3,2,1,0:T(8,128)}), f32[4,2,64,1024]{3,2,1,0:T(8,128)S(1)}, u32[]{:S(2)}, u32[]{:S(2)}) async-start(f32[4,2,64,1024]{3,2,1,0:T(8,128)} %bitcast.190), calls=%async_computation | async-start | bytes 4194304 | tf_op jit(solution)/shard_map/all_to_all | solution.py:95
  8.1 4.7 %collective-permute-start.2 = (f32[4,7,1024]{2,1,0:T(8,128)}, f32[4,7,1024]{2,1,0:T(8,128)S(1)}, u32[]{:S(2)}, u32[]{:S(2)}) collective-permute-start(f32[4,7,1024]{2,1,0:T(8,128)} %get-tuple-element.50), channel_id=1, source_target_pairs={{0,2},{2,4},{4,6},{6,8},{8,10},{10,12},{12,14},{14,16},{16,18},{18... | collective-permute-start | bytes 344072 | tf_op jit(solution)/shard_map/ppermute | solution.py:21
  14.2 0.9 slice_bitcast_fusion.15
  15.0 0.7 slice_bitcast_fusion.17
  16.4 0.8 slice_bitcast_fusion.18
  19.1 0.7 slice_bitcast_fusion.11
  19.9 0.7 slice_bitcast_fusion.20
  22.7 0.9 broadcast_multiply_fusion
  24.2 0.9 slice_bitcast_fusion.12
  25.1 0.8 slice_bitcast_fusion.9
  26.7 1.0 slice_bitcast_fusion.8
  27.7 0.9 slice_bitcast_fusion.5
  28.6 5.8 %all-to-all-done = f32[4,2,64,1024]{3,2,1,0:T(8,128)S(1)} async-done(((f32[4,2,64,1024]{3,2,1,0:T(8,128)}), f32[4,2,64,1024]{3,2,1,0:T(8,128)S(1)}, u32[]{:S(2)}, u32[]{:S(2)}) %all-to-all-start) | async-done | bytes 2097184 | tf_op jit(solution)/shard_map/all_to_all | solution.py:95
  34.5 0.9 fusion.81
  35.5 1.4 %collective-permute-start.1 = (f32[8,7,1024]{2,1,0:T(8,128)S(1)}, f32[8,7,1024]{2,1,0:T(8,128)S(1)}, u32[]{:S(2)}, u32[]{:S(2)}) collective-permute-start(f32[8,7,1024]{2,1,0:T(8,128)S(1)} %get-tuple-element.23), channel_id=1, source_target_pairs={{2,0},{4,2},{6,4},{8,6},{10,8},{12,10},{14,12},{16,14},{18,16},{20... | collective-permute-start | bytes 688136 | tf_op jit(solution)/shard_map/ppermute | solution.py:23
  36.9 4.9 %collective-permute-start = (f32[8,7,1024]{2,1,0:T(8,128)S(1)}, f32[8,7,1024]{2,1,0:T(8,128)S(1)}, u32[]{:S(2)}, u32[]{:S(2)}) collective-permute-start(f32[8,7,1024]{2,1,0:T(8,128)S(1)} %get-tuple-element.22), channel_id=1, source_target_pairs={{0,2},{2,4},{4,6},{6,8},{8,10},{10,12},{12,14},{14,16},{16,18},{18... | collective-permute-start | bytes 688136 | tf_op jit(solution)/shard_map/ppermute | solution.py:21
  42.1 2.1 %fusion.8 = (f32[8,62,1024]{2,1,0:T(8,128)S(1)}, f32[8,62,1024]{2,1,0:T(8,128)S(1)}, f32[8,62,1024]{2,1,0:T(8,128)S(1)}) fusion(f32[8,64,1024]{2,1,0:T(8,128)S(1)} %bitcast.156, f32[62]{0:T(128)S(1)} %copy-done.31, f32[8,64,1024]{2,1,0:T(8,128)S(1)} %bitcast.154, f32[62,1024]{1,0:T(8,128)S(1)} %copy-done.13, f32[62,1024]{1,0:T(8,128)S(1)} %copy-done.14, ...), kind=kLoop, calls=%fused_computation.12 | loop fusion | flops 9142272 | bytes 19042680 | tf_op jit(solution)/shard_map/mul | solution.py:68
  44.2 1.1 fusion.80
  45.4 2.1 %fusion.5 = f32[8,60,1024]{2,1,0:T(8,128)S(1)} fusion(f32[8,64,1024]{2,1,0:T(8,128)S(1)} %bitcast.157, f32[8,62,1024]{2,1,0:T(8,128)S(1)} %get-tuple-element.6, f32[8,60,1023]{2,1,0:T(8,128)S(1)} %get-tuple-element.19, f32[8,60,1023]{2,1,0:T(8,128)S(1)} %get-tuple-element.18, f32[60]{0:T(128)S(1)} %copy-done.28, f32[60,1024]{1,0:T(8,128)S(1)} %copy-done.17, ...), kind=kLoop, calls=%fused_computation.8 | loop fusion | flops 8847360 | bytes 14496240 | tf_op jit(solution)/shard_map/mul | solution.py:68
  47.5 1.1 fusion.79
  48.6 2.1 %fusion.2 = f32[8,58,1024]{2,1,0:T(8,128)S(1)} fusion(f32[8,64,1024]{2,1,0:T(8,128)S(1)} %bitcast.158, f32[8,60,1024]{2,1,0:T(8,128)S(1)} %fusion.5, f32[8,58,1023]{2,1,0:T(8,128)S(1)} %get-tuple-element.17, f32[8,58,1023]{2,1,0:T(8,128)S(1)} %get-tuple-element.16, f32[58]{0:T(128)S(1)} %copy-done.27, f32[58,1024]{1,0:T(8,128)S(1)} %copy-done.15, ...), kind=kLoop, calls=%fused_computation.4 | loop fusion | flops 8552448 | bytes 14013032 | tf_op jit(solution)/shard_map/mul | solution.py:68
  50.8 0.9 fusion.78
  51.9 2.5 %fusion.10 = (f32[8,56,1024]{2,1,0:T(8,128)S(1)}, f32[8,56,1024]{2,1,0:T(8,128)S(1)}) fusion(f32[8,62,1024]{2,1,0:T(8,128)S(1)} %get-tuple-element.7, f32[8,62,1024]{2,1,0:T(8,128)S(1)} %get-tuple-element.13, f32[56]{0:T(128)S(1)} %copy-done.30, f32[8,64,1024]{2,1,0:T(8,128)S(1)} %bitcast.159, f32[56,1024]{1,0:T(8,128)S(1)} %copy-done.19, ...), kind=kLoop, calls=%fused_computation.19 | loop fusion | flops 9175040 | bytes 19034848 | tf_op jit(solution)/shard_map/mul | solution.py:68
  55.8 0.8 add_multiply_fusion
  57.8 1.0 fusion.34
  65.9 1.5 %pad_maximum_fusion.1 = f32[4,2,64,1024]{3,2,1,0:T(8,128)} fusion(f32[1,2,64,1024]{3,2,1,0:T(8,128)S(1)} %get-tuple-element.57, f32[1,2,64,1024]{3,2,1,0:T(8,128)S(1)} %get-tuple-element.56, f32[1,2,64,1024]{3,2,1,0:T(8,128)S(1)} %slice_bitcast_fusion, f32[1,2,64,1024]{3,2,1,0:T(8,128)S(1)} %slice_bitcast_fusion.1), kind=kLoop, calls=%fused_computation.13 | loop fusion | flops 1572864 | bytes 4194304 | tf_op jit(solution)/shard_map/stack | solution.py:153
  67.4 3.7 %all-to-all-start.1 = ((f32[4,2,64,1024]{3,2,1,0:T(8,128)}), f32[4,2,64,1024]{3,2,1,0:T(8,128)S(1)}, u32[]{:S(2)}, u32[]{:S(2)}) async-start(f32[4,2,64,1024]{3,2,1,0:T(8,128)} %pad_maximum_fusion.1), calls=%async_computation.1 | async-start | bytes 4194304 | tf_op jit(solution)/shard_map/all_to_all | solution.py:154
  71.2 24.7 %all-to-all-done.1 = f32[4,2,64,1024]{3,2,1,0:T(8,128)S(1)} async-done(((f32[4,2,64,1024]{3,2,1,0:T(8,128)}), f32[4,2,64,1024]{3,2,1,0:T(8,128)S(1)}, u32[]{:S(2)}, u32[]{:S(2)}) %all-to-all-start.1) | async-done | bytes 2097184 | tf_op jit(solution)/shard_map/all_to_all | solution.py:154
  96.0 1.5 %fusion.9 = f32[8,64]{1,0:T(8,128)S(1)} fusion(f32[8,64,1024]{2,1,0:T(8,128)S(1)} %bitcast.164, s32[64]{0:T(128)S(1)} %and_select_fusion.1, s32[64]{0:T(128)S(1)} %get-tuple-element.2), kind=kOutput, calls=%fused_computation.15 | convolution fusion | flops 404229632 | bytes 2099712 | tf_op jit(solution)/shard_map/or,mrc->moc/dot_general | solution.py:163
  97.6 1.1 collective-permute-done.4
  99.7 2.7 %collective-permute-start.7 = (f32[2,16,16]{2,1,0:T(8,128)S(1)}, f32[2,16,16]{2,1,0:T(8,128)S(1)}, u32[]{:S(2)}, u32[]{:S(2)}) collective-permute-start(f32[2,16,16]{2,1,0:T(8,128)S(1)} %pad_maximum_fusion.16), channel_id=1, source_target_pairs={{0,96},{32,64},{64,32},{96,0},{1,97},{33,65},{65,33},{97,1},{2,98}... | collective-permute-start | bytes 6152 | tf_op jit(solution)/shard_map/ppermute | solution.py:37
  102.6 1.8 %collective-permute-done.6 = f32[2,16,16]{2,1,0:T(8,128)S(1)} collective-permute-done((f32[2,16,16]{2,1,0:T(8,128)S(1)}, f32[2,16,16]{2,1,0:T(8,128)S(1)}, u32[]{:S(2)}, u32[]{:S(2)}) %collective-permute-start.6) | collective-permute-done | bytes 2080 | tf_op jit(solution)/shard_map/ppermute | solution.py:37
  104.6 1.5 %collective-permute-done.5 = f32[2,16,16]{2,1,0:T(8,128)S(1)} collective-permute-done((f32[2,16,16]{2,1,0:T(8,128)S(1)}, f32[2,16,16]{2,1,0:T(8,128)S(1)}, u32[]{:S(2)}, u32[]{:S(2)}) %collective-permute-start.5) | collective-permute-done | bytes 2080 | tf_op jit(solution)/shard_map/ppermute | solution.py:37
  106.1 3.4 %collective-permute-start.9 = (f32[2,16,16]{2,1,0:T(8,128)S(1)}, f32[2,16,16]{2,1,0:T(8,128)S(1)}, u32[]{:S(2)}, u32[]{:S(2)}) collective-permute-start(f32[2,16,16]{2,1,0:T(8,128)S(1)} %add_add_fusion.2), channel_id=1, source_target_pairs={{0,4},{2,6},{4,0},{6,2},{8,12},{10,14},{12,8},{14,10},{16,20},{18,... | collective-permute-start | bytes 6152 | tf_op jit(solution)/shard_map/ppermute | solution.py:37
  109.5 2.3 %collective-permute-start.10 = (f32[2,16,16]{2,1,0:T(8,128)S(1)}, f32[2,16,16]{2,1,0:T(8,128)S(1)}, u32[]{:S(2)}, u32[]{:S(2)}) collective-permute-start(f32[2,16,16]{2,1,0:T(8,128)S(1)} %add_add_fusion.2), channel_id=1, source_target_pairs={{0,6},{2,4},{4,2},{6,0},{8,14},{10,12},{12,10},{14,8},{16,22},{18,... | collective-permute-start | bytes 6152 | tf_op jit(solution)/shard_map/ppermute | solution.py:37
  111.8 0.8 collective-permute-start.8
  112.6 1.8 %collective-permute-done.10 = f32[2,16,16]{2,1,0:T(8,128)S(1)} collective-permute-done((f32[2,16,16]{2,1,0:T(8,128)S(1)}, f32[2,16,16]{2,1,0:T(8,128)S(1)}, u32[]{:S(2)}, u32[]{:S(2)}) %collective-permute-start.10) | collective-permute-done | bytes 2080 | tf_op jit(solution)/shard_map/ppermute | solution.py:37
  114.5 1.1 collective-permute-done.8
  115.6 3.9 %collective-permute-start.12 = (f32[2,16,16]{2,1,0:T(8,128)S(1)}, f32[2,16,16]{2,1,0:T(8,128)S(1)}, u32[]{:S(2)}, u32[]{:S(2)}) collective-permute-start(f32[2,16,16]{2,1,0:T(8,128)S(1)} %add_add_fusion.1), channel_id=1, source_target_pairs={{0,16},{2,18},{4,20},{6,22},{8,24},{10,26},{12,28},{14,30},{16,0},... | collective-permute-start | bytes 6152 | tf_op jit(solution)/shard_map/ppermute | solution.py:37
  119.5 0.7 collective-permute-start.13
  120.4 0.8 collective-permute-done.12
  121.2 3.2 %collective-permute-done.13 = f32[2,16,16]{2,1,0:T(8,128)S(1)} collective-permute-done((f32[2,16,16]{2,1,0:T(8,128)S(1)}, f32[2,16,16]{2,1,0:T(8,128)S(1)}, u32[]{:S(2)}, u32[]{:S(2)}) %collective-permute-start.13) | collective-permute-done | bytes 2080 | tf_op jit(solution)/shard_map/ppermute | solution.py:37
  124.6 1.5 %cholesky.17 = f32[16,16]{1,0:T(8,128)S(1)} custom-call(f32[16,16]{1,0:T(8,128)S(1)} %fusion.57), custom_call_target="Cholesky" | custom-call | tf_op jit(solution)/shard_map/jit(cholesky)/cholesky | solution.py:181
  127.4 1.2 custom-call.10
  128.9 0.9 fusion.31
  129.8 1.3 %copy.15 = f32[1,8,64,1024]{3,2,1,0:T(8,128)} copy(f32[1,8,64,1024]{3,2,1,0:T(8,128)S(1)} %bitcast.165) | data formatting | bytes 4194304
  (164 shorter events, 21.1 us)
Async XLA Ops:
  2.2 23.8 %collective-permute-start.3 = (f32[4,7,1024]{2,1,0:T(8,128)}, f32[4,7,1024]{2,1,0:T(8,128)S(1)}, u32[]{:S(2)}, u32[]{:S(2)}) collective-permute-start(f32[4,7,1024]{2,1,0:T(8,128)} %get-tuple-element.51), channel_id=1, source_target_pairs={{2,0},{4,2},{6,4},{8,6},{10,8},{12,10},{14,12},{16,14},{18,16},{20... | collective-permute-start | bytes 344072 | tf_op jit(solution)/shard_map/ppermute | solution.py:23
  3.5 10.7 %copy-start.1 = (f32[64,1024]{1,0:T(8,128)S(1)}, f32[64,1024]{1,0:T(8,128)}, u32[]{:S(2)}) copy-start(f32[64,1024]{1,0:T(8,128)} %param.12) | copy-start | bytes 786436
  3.5 10.6 %copy-start.2 = (f32[64,1024]{1,0:T(8,128)S(1)}, f32[64,1024]{1,0:T(8,128)}, u32[]{:S(2)}) copy-start(f32[64,1024]{1,0:T(8,128)} %param.11) | copy-start | bytes 786436
  3.6 11.5 %copy-start = (f32[64,1024]{1,0:T(8,128)S(1)}, f32[64,1024]{1,0:T(8,128)}, u32[]{:S(2)}) copy-start(f32[64,1024]{1,0:T(8,128)} %param.13) | copy-start | bytes 786436
  3.6 30.9 %all-to-all-start = ((f32[4,2,64,1024]{3,2,1,0:T(8,128)}), f32[4,2,64,1024]{3,2,1,0:T(8,128)S(1)}, u32[]{:S(2)}, u32[]{:S(2)}) async-start(f32[4,2,64,1024]{3,2,1,0:T(8,128)} %bitcast.190), calls=%async_computation | async-start | bytes 4194304 | tf_op jit(solution)/shard_map/all_to_all | solution.py:95
  8.1 14.4 %copy-start.26 = (f32[8,128]{1,0:T(8,128)S(1)}, f32[8,128]{1,0:T(8,128)}, u32[]{:S(2)}) copy-start(f32[8,128]{1,0:T(8,128)} %param.15) | copy-start | bytes 12292
  8.1 17.9 %collective-permute-start.2 = (f32[4,7,1024]{2,1,0:T(8,128)}, f32[4,7,1024]{2,1,0:T(8,128)S(1)}, u32[]{:S(2)}, u32[]{:S(2)}) collective-permute-start(f32[4,7,1024]{2,1,0:T(8,128)} %get-tuple-element.50), channel_id=1, source_target_pairs={{0,2},{2,4},{4,6},{6,8},{8,10},{10,12},{12,14},{14,16},{16,18},{18... | collective-permute-start | bytes 344072 | tf_op jit(solution)/shard_map/ppermute | solution.py:21
  12.9 9.5 %copy-start.39 = (f32[30,1]{0,1:T(1,128)}, f32[30,1]{0,1:T(1,128)S(1)}, u32[]{:S(2)}) copy-start(f32[30,1]{0,1:T(1,128)S(1)} %pad_maximum_fusion.17) | copy-start | bytes 364
  14.2 8.5 %copy-start.3 = (f32[64,1024]{1,0:T(8,128)S(1)}, f32[64,1024]{1,0:T(8,128)}, u32[]{:S(2)}) copy-start(f32[64,1024]{1,0:T(8,128)} %param.14) | copy-start | bytes 786436
  22.7 3.2 %copy-start.40 = (f32[30,1]{0,1:T(1,128)S(1)}, f32[30,1]{0,1:T(1,128)}, u32[]{:S(2)}) copy-start(f32[30,1]{0,1:T(1,128)} %copy-done.39) | copy-start | bytes 364
  34.5 7.3 %copy-start.4 = (f32[2,64,1024]{2,1,0:T(8,128)S(1)}, f32[2,64,1024]{2,1,0:T(8,128)}, u32[]{:S(2)}) copy-start(f32[2,64,1024]{2,1,0:T(8,128)} %broadcast_multiply_fusion) | copy-start | bytes 1572868
  35.4 6.7 %copy-start.12 = (f32[62,1024]{1,0:T(8,128)S(1)}, f32[62,1024]{1,0:T(8,128)}, u32[]{:S(2)}) copy-start(f32[62,1024]{1,0:T(8,128)} %slice_bitcast_fusion.17) | copy-start | bytes 761860
  35.4 6.7 %copy-start.13 = (f32[62,1024]{1,0:T(8,128)S(1)}, f32[62,1024]{1,0:T(8,128)}, u32[]{:S(2)}) copy-start(f32[62,1024]{1,0:T(8,128)} %get-tuple-element.68) | copy-start | bytes 761860
  35.4 6.7 %copy-start.14 = (f32[62,1024]{1,0:T(8,128)S(1)}, f32[62,1024]{1,0:T(8,128)}, u32[]{:S(2)}) copy-start(f32[62,1024]{1,0:T(8,128)} %get-tuple-element.69) | copy-start | bytes 761860
  35.5 6.7 %copy-start.31 = (f32[62]{0:T(128)S(1)}, f32[62]{0:T(128)}, u32[]{:S(2)}) copy-start(f32[62]{0:T(128)} %slice.626) | copy-start | bytes 748
  35.5 18.9 %collective-permute-start.1 = (f32[8,7,1024]{2,1,0:T(8,128)S(1)}, f32[8,7,1024]{2,1,0:T(8,128)S(1)}, u32[]{:S(2)}, u32[]{:S(2)}) collective-permute-start(f32[8,7,1024]{2,1,0:T(8,128)S(1)} %get-tuple-element.23), channel_id=1, source_target_pairs={{2,0},{4,2},{6,4},{8,6},{10,8},{12,10},{14,12},{16,14},{18,16},{20... | collective-permute-start | bytes 688136 | tf_op jit(solution)/shard_map/ppermute | solution.py:23
  36.9 17.5 %collective-permute-start = (f32[8,7,1024]{2,1,0:T(8,128)S(1)}, f32[8,7,1024]{2,1,0:T(8,128)S(1)}, u32[]{:S(2)}, u32[]{:S(2)}) collective-permute-start(f32[8,7,1024]{2,1,0:T(8,128)S(1)} %get-tuple-element.22), channel_id=1, source_target_pairs={{0,2},{2,4},{4,6},{6,8},{8,10},{10,12},{12,14},{14,16},{16,18},{18... | collective-permute-start | bytes 688136 | tf_op jit(solution)/shard_map/ppermute | solution.py:21
  44.2 1.1 copy-start.11
  44.2 1.1 copy-start.17
  44.2 1.1 copy-start.18
  44.2 1.1 copy-start.28
  47.5 1.1 copy-start.10
  47.5 1.1 copy-start.15
  47.5 1.1 copy-start.16
  47.5 1.1 copy-start.27
  50.8 1.1 copy-start.21
  50.8 1.1 copy-start.30
  51.9 2.5 %copy-start.23 = (f32[4,7,1024]{2,1,0:T(8,128)S(1)}, f32[4,7,1024]{2,1,0:T(8,128)}, u32[]{:S(2)}) copy-start(f32[4,7,1024]{2,1,0:T(8,128)} %copy-done.22) | copy-start | bytes 344068
  51.9 2.5 %copy-start.25 = (f32[4,7,1024]{2,1,0:T(8,128)S(1)}, f32[4,7,1024]{2,1,0:T(8,128)}, u32[]{:S(2)}) copy-start(f32[4,7,1024]{2,1,0:T(8,128)} %copy-done.24) | copy-start | bytes 344068
  61.4 1.0 copy-start.8
  61.4 1.1 copy-start.9
  61.4 1.1 copy-start.35
  67.4 3.8 %copy-start.32 = (s32[1,64]{1,0:T(1,128)S(1)}, s32[1,64]{1,0:T(1,128)}, u32[]{:S(2)}) copy-start(s32[1,64]{1,0:T(1,128)} %param.16) | copy-start | bytes 772
  67.4 28.6 %all-to-all-start.1 = ((f32[4,2,64,1024]{3,2,1,0:T(8,128)}), f32[4,2,64,1024]{3,2,1,0:T(8,128)S(1)}, u32[]{:S(2)}, u32[]{:S(2)}) async-start(f32[4,2,64,1024]{3,2,1,0:T(8,128)} %pad_maximum_fusion.1), calls=%async_computation.1 | async-start | bytes 4194304 | tf_op jit(solution)/shard_map/all_to_all | solution.py:154
  71.1 26.4 %copy-start.37 = (f32[1,64]{1,0:T(1,128)S(1)}, f32[1,64]{1,0:T(1,128)}, u32[]{:S(2)}) copy-start(f32[1,64]{1,0:T(1,128)} %param.19) | copy-start | bytes 772
  71.2 27.7 %copy-start.36 = (f32[1,64,16]{1,2,0:T(8,128)S(1)}, f32[1,64,16]{1,2,0:T(8,128)}, u32[]{:S(2)}) copy-start(f32[1,64,16]{1,2,0:T(8,128)} %param.18) | copy-start | bytes 12292
  71.2 27.7 %copy-start.38 = (f32[1,64]{1,0:T(1,128)S(1)}, f32[1,64]{1,0:T(1,128)}, u32[]{:S(2)}) copy-start(f32[1,64]{1,0:T(1,128)} %param.17) | copy-start | bytes 772
  97.4 1.2 collective-permute-start.4
  99.0 5.3 %collective-permute-start.6 = (f32[2,16,16]{2,1,0:T(8,128)S(1)}, f32[2,16,16]{2,1,0:T(8,128)S(1)}, u32[]{:S(2)}, u32[]{:S(2)}) collective-permute-start(f32[2,16,16]{2,1,0:T(8,128)S(1)} %pad_maximum_fusion.16), channel_id=1, source_target_pairs={{0,64},{32,96},{64,0},{96,32},{1,65},{33,97},{65,1},{97,33},{2,66}... | collective-permute-start | bytes 6152 | tf_op jit(solution)/shard_map/ppermute | solution.py:37
  99.7 4.9 %collective-permute-start.7 = (f32[2,16,16]{2,1,0:T(8,128)S(1)}, f32[2,16,16]{2,1,0:T(8,128)S(1)}, u32[]{:S(2)}, u32[]{:S(2)}) collective-permute-start(f32[2,16,16]{2,1,0:T(8,128)S(1)} %pad_maximum_fusion.16), channel_id=1, source_target_pairs={{0,96},{32,64},{64,32},{96,0},{1,97},{33,65},{65,33},{97,1},{2,98}... | collective-permute-start | bytes 6152 | tf_op jit(solution)/shard_map/ppermute | solution.py:37
  102.3 3.7 %collective-permute-start.5 = (f32[2,16,16]{2,1,0:T(8,128)S(1)}, f32[2,16,16]{2,1,0:T(8,128)S(1)}, u32[]{:S(2)}, u32[]{:S(2)}) collective-permute-start(f32[2,16,16]{2,1,0:T(8,128)S(1)} %pad_maximum_fusion.16), channel_id=1, source_target_pairs={{0,32},{32,0},{64,96},{96,64},{1,33},{33,1},{65,97},{97,65},{2,34}... | collective-permute-start | bytes 6152 | tf_op jit(solution)/shard_map/ppermute | solution.py:37
  102.6 10.0 %collective-permute-start.14 = (f32[8,128]{1,0:T(8,128)S(1)}, f32[8,128]{1,0:T(8,128)S(1)}, u32[]{:S(2)}, u32[]{:S(2)}) collective-permute-start(f32[8,128]{1,0:T(8,128)S(1)} %copy-done.26), channel_id=1, source_target_pairs={{0,1},{1,0},{2,3},{3,2},{4,5},{5,4},{6,7},{7,6},{8,9},{9,8},{10,11... | collective-permute-start | bytes 12296 | tf_op jit(solution)/shard_map/ppermute | solution.py:49
  106.1 6.5 %collective-permute-start.9 = (f32[2,16,16]{2,1,0:T(8,128)S(1)}, f32[2,16,16]{2,1,0:T(8,128)S(1)}, u32[]{:S(2)}, u32[]{:S(2)}) collective-permute-start(f32[2,16,16]{2,1,0:T(8,128)S(1)} %add_add_fusion.2), channel_id=1, source_target_pairs={{0,4},{2,6},{4,0},{6,2},{8,12},{10,14},{12,8},{14,10},{16,20},{18,... | collective-permute-start | bytes 6152 | tf_op jit(solution)/shard_map/ppermute | solution.py:37
  109.5 4.9 %collective-permute-start.10 = (f32[2,16,16]{2,1,0:T(8,128)S(1)}, f32[2,16,16]{2,1,0:T(8,128)S(1)}, u32[]{:S(2)}, u32[]{:S(2)}) collective-permute-start(f32[2,16,16]{2,1,0:T(8,128)S(1)} %add_add_fusion.2), channel_id=1, source_target_pairs={{0,6},{2,4},{4,2},{6,0},{8,14},{10,12},{12,10},{14,8},{16,22},{18,... | collective-permute-start | bytes 6152 | tf_op jit(solution)/shard_map/ppermute | solution.py:37
  111.8 3.7 %collective-permute-start.8 = (f32[2,16,16]{2,1,0:T(8,128)S(1)}, f32[2,16,16]{2,1,0:T(8,128)S(1)}, u32[]{:S(2)}, u32[]{:S(2)}) collective-permute-start(f32[2,16,16]{2,1,0:T(8,128)S(1)} %add_add_fusion.2), channel_id=1, source_target_pairs={{0,2},{2,0},{4,6},{6,4},{8,10},{10,8},{12,14},{14,12},{16,18},{18,... | collective-permute-start | bytes 6152 | tf_op jit(solution)/shard_map/ppermute | solution.py:37
  115.6 5.7 %collective-permute-start.12 = (f32[2,16,16]{2,1,0:T(8,128)S(1)}, f32[2,16,16]{2,1,0:T(8,128)S(1)}, u32[]{:S(2)}, u32[]{:S(2)}) collective-permute-start(f32[2,16,16]{2,1,0:T(8,128)S(1)} %add_add_fusion.1), channel_id=1, source_target_pairs={{0,16},{2,18},{4,20},{6,22},{8,24},{10,26},{12,28},{14,30},{16,0},... | collective-permute-start | bytes 6152 | tf_op jit(solution)/shard_map/ppermute | solution.py:37
  119.5 4.9 %collective-permute-start.13 = (f32[2,16,16]{2,1,0:T(8,128)S(1)}, f32[2,16,16]{2,1,0:T(8,128)S(1)}, u32[]{:S(2)}, u32[]{:S(2)}) collective-permute-start(f32[2,16,16]{2,1,0:T(8,128)S(1)} %add_add_fusion.1), channel_id=1, source_target_pairs={{0,24},{2,26},{4,28},{6,30},{8,16},{10,18},{12,20},{14,22},{16,8},... | collective-permute-start | bytes 6152 | tf_op jit(solution)/shard_map/ppermute | solution.py:37
  120.2 4.2 %collective-permute-start.11 = (f32[2,16,16]{2,1,0:T(8,128)S(1)}, f32[2,16,16]{2,1,0:T(8,128)S(1)}, u32[]{:S(2)}, u32[]{:S(2)}) collective-permute-start(f32[2,16,16]{2,1,0:T(8,128)S(1)} %add_add_fusion.1), channel_id=1, source_target_pairs={{0,8},{2,10},{4,12},{6,14},{8,0},{10,2},{12,4},{14,6},{16,24},{18,... | collective-permute-start | bytes 6152 | tf_op jit(solution)/shard_map/ppermute | solution.py:37
  (10 other events, 8.7 us)

commit v14 on v13

--- a/solution.py
+++ b/solution.py
@@ -144,13 +144,13 @@
     fine = current.reshape(slices, group, -1, col_count)
     coarse_part = coarse_part.reshape(slices, group, -1, col_count)
     running = fine[0]
-    results = [running[:, links : links + row_count]]
+    done = jnp.zeros((slices, group, row_count, col_count), jnp.float32)
+    done = done.at[0].set(running[:, links : links + row_count])
     for link in range(1, slices):
         correction = fine[link] - coarse_part[link]
         stepped = step(running, FINE + link - 1, coarse_dt, None)
         running = correction[:, link : correction.shape[1] - link] + stepped
-        results.append(running[:, links - link : links - link + row_count])
-    done = jnp.stack(results)
+        done = done.at[link].set(running[:, links - link : links - link + row_count])
     running = lax.all_to_all(done, "tm", 0, 0, tiled=True).reshape(
         members_here, row_count, col_count
     )

time: 132 us -> 133 us (level)
  local copies, waits for them, and re-layouts: 25.5 us -> 27.6 us
    scatter x0 -> x3, local copies, waits for them, and re-layouts: none -> 3.25 us  [the longest x2 1.68 us: per_device(): done = done.at[link].set(running[:, links - link:links - link + row_count])]
    another operation x2 -> x0, other arithmetic: 1.98 us -> none  [per_device(): done = jnp.stack(results)]
where the time goes in v14:
time: 133 us
  waiting for transfers between devices  42.1 us (32%)
  starting transfers between devices  35.5 us (27%)
  local copies, waits for them, and re-layouts  27.6 us (21%)
  other arithmetic  22.8 us (17%)
  matrix products  2.96 us (2%)
  between operations  1.52 us (1%)
    all_to_all x1, waiting for transfers between devices, per_device(): lax.all_to_all(done, 'tm', 0, 0, tiled=True)  24.7 us
    ppermute x9, starting transfers between devices, quad_sum(): lax.ppermute(value, axis, [(i, i ^ k * bit) for i in range(count)])  14.9 us
    mul x9, other arithmetic, advance(): return (middle + step_size * tendency) * inside  12.4 us
    ppermute x9, waiting for transfers between devices, quad_sum(): lax.ppermute(value, axis, [(i, i ^ k * bit) for i in range(count)])  10.5 us
    ppermute x2, starting transfers between devices, with_halo(): lax.ppermute(tail, axis, [(i, i + 1) for i in range(ends)])  9.58 us
    slice x11, local copies, waits for them, and re-layouts, advance(): west_cell = jnp.pad(middle[:, :, :-1], ((0, 0), (0, 0), (1, 0)))  6.23 us
    all_to_all x1, waiting for transfers between devices, per_device(): lax.all_to_all(state.reshape(slices, group, row_count, col_count), 'tm',...  5.77 us
    mul x10, local copies, waits for them, and re-layouts, advance(): coeffs[0] * (above_row + below_row + west_cell + east_cell - 4.0 * middle)  4.91 us
  transfers between devices with their start and end apart: 17, of which 10 were waited for; matrix products, arithmetic and copies ran while one was open for 21% of the time, Pallas kernels for 0%

profile of v14, /device:TPU:0, one launch (start us, length us, event | category | flops | bytes accessed | tf_op | source)
XLA Modules:
  0.0 132.6 jit_solution(6430921399344240861)
XLA Ops:
  0.6 1.6 %pad_maximum_fusion.14 = (f32[4,7,1024]{2,1,0:T(8,128)}, f32[4,7,1024]{2,1,0:T(8,128)}) fusion(f32[1,64,1024]{2,1,0:T(8,128)} %bitcast.191, f32[1,64,1024]{2,1,0:T(8,128)} %bitcast.177, f32[1,64,1024]{2,1,0:T(8,128)} %bitcast.184, f32[1,64,1024]{2,1,0:T(8,128)} %bitcast.170), kind=kLoop, calls=%fused_computation.120 | loop fusion | flops 172032 | bytes 1277952 | tf_op jit(solution)/shard_map/slice | solution.py:18
  2.2 1.3 collective-permute-start.3
  3.6 4.5 %all-to-all-start = ((f32[4,2,64,1024]{3,2,1,0:T(8,128)}), f32[4,2,64,1024]{3,2,1,0:T(8,128)S(1)}, u32[]{:S(2)}, u32[]{:S(2)}) async-start(f32[4,2,64,1024]{3,2,1,0:T(8,128)} %bitcast.194), calls=%async_computation | async-start | bytes 4194304 | tf_op jit(solution)/shard_map/all_to_all | solution.py:95
  8.1 4.7 %collective-permute-start.2 = (f32[4,7,1024]{2,1,0:T(8,128)}, f32[4,7,1024]{2,1,0:T(8,128)S(1)}, u32[]{:S(2)}, u32[]{:S(2)}) collective-permute-start(f32[4,7,1024]{2,1,0:T(8,128)} %get-tuple-element.98), channel_id=1, source_target_pairs={{0,2},{2,4},{4,6},{6,8},{8,10},{10,12},{12,14},{14,16},{16,18},{18... | collective-permute-start | bytes 344072 | tf_op jit(solution)/shard_map/ppermute | solution.py:21
  14.3 0.9 slice_bitcast_fusion.14
  16.4 0.8 slice_bitcast_fusion.17
  19.8 0.7 slice_bitcast_fusion.19
  22.7 0.9 broadcast_multiply_fusion
  24.3 0.9 slice_bitcast_fusion.11
  25.1 0.8 slice_bitcast_fusion.8
  26.7 1.0 slice_bitcast_fusion.7
  27.7 0.9 slice_bitcast_fusion.4
  28.6 5.8 %all-to-all-done = f32[4,2,64,1024]{3,2,1,0:T(8,128)S(1)} async-done(((f32[4,2,64,1024]{3,2,1,0:T(8,128)}), f32[4,2,64,1024]{3,2,1,0:T(8,128)S(1)}, u32[]{:S(2)}, u32[]{:S(2)}) %all-to-all-start) | async-done | bytes 2097184 | tf_op jit(solution)/shard_map/all_to_all | solution.py:95
  34.5 0.9 fusion.83
  35.5 1.4 %collective-permute-start.1 = (f32[8,7,1024]{2,1,0:T(8,128)S(1)}, f32[8,7,1024]{2,1,0:T(8,128)S(1)}, u32[]{:S(2)}, u32[]{:S(2)}) collective-permute-start(f32[8,7,1024]{2,1,0:T(8,128)S(1)} %get-tuple-element.71), channel_id=1, source_target_pairs={{2,0},{4,2},{6,4},{8,6},{10,8},{12,10},{14,12},{16,14},{18,16},{20... | collective-permute-start | bytes 688136 | tf_op jit(solution)/shard_map/ppermute | solution.py:23
  36.9 4.9 %collective-permute-start = (f32[8,7,1024]{2,1,0:T(8,128)S(1)}, f32[8,7,1024]{2,1,0:T(8,128)S(1)}, u32[]{:S(2)}, u32[]{:S(2)}) collective-permute-start(f32[8,7,1024]{2,1,0:T(8,128)S(1)} %get-tuple-element.70), channel_id=1, source_target_pairs={{0,2},{2,4},{4,6},{6,8},{8,10},{10,12},{12,14},{14,16},{16,18},{18... | collective-permute-start | bytes 688136 | tf_op jit(solution)/shard_map/ppermute | solution.py:21
  42.1 2.1 %fusion.8 = (f32[8,62,1024]{2,1,0:T(8,128)S(1)}, f32[8,62,1024]{2,1,0:T(8,128)S(1)}, f32[8,62,1024]{2,1,0:T(8,128)S(1)}) fusion(f32[8,64,1024]{2,1,0:T(8,128)S(1)} %bitcast.160, f32[62]{0:T(128)S(1)} %copy-done.32, f32[8,64,1024]{2,1,0:T(8,128)S(1)} %bitcast.158, f32[62,1024]{1,0:T(8,128)S(1)} %copy-done.13, f32[62,1024]{1,0:T(8,128)S(1)} %copy-done.14, ...), kind=kLoop, calls=%fused_computation.12 | loop fusion | flops 9142272 | bytes 19042680 | tf_op jit(solution)/shard_map/mul | solution.py:68
  44.2 1.1 fusion.82
  45.3 2.1 %fusion.5 = f32[8,60,1024]{2,1,0:T(8,128)S(1)} fusion(f32[8,64,1024]{2,1,0:T(8,128)S(1)} %bitcast.161, f32[8,62,1024]{2,1,0:T(8,128)S(1)} %get-tuple-element.54, f32[8,60,1023]{2,1,0:T(8,128)S(1)} %get-tuple-element.67, f32[8,60,1023]{2,1,0:T(8,128)S(1)} %get-tuple-element.66, f32[60]{0:T(128)S(1)} %copy-done.28, f32[60,1024]{1,0:T(8,128)S(1)} %copy-done.17, ...), kind=kLoop, calls=%fused_computation.8 | loop fusion | flops 8847360 | bytes 14496240 | tf_op jit(solution)/shard_map/mul | solution.py:68
  47.5 1.1 fusion.81
  48.6 2.1 %fusion.2 = f32[8,58,1024]{2,1,0:T(8,128)S(1)} fusion(f32[8,64,1024]{2,1,0:T(8,128)S(1)} %bitcast.162, f32[8,60,1024]{2,1,0:T(8,128)S(1)} %fusion.5, f32[8,58,1023]{2,1,0:T(8,128)S(1)} %get-tuple-element.65, f32[8,58,1023]{2,1,0:T(8,128)S(1)} %get-tuple-element.64, f32[58]{0:T(128)S(1)} %copy-done.27, f32[58,1024]{1,0:T(8,128)S(1)} %copy-done.15, ...), kind=kLoop, calls=%fused_computation.4 | loop fusion | flops 8552448 | bytes 14013032 | tf_op jit(solution)/shard_map/mul | solution.py:68
  50.8 0.9 fusion.80
  51.9 2.5 %fusion.10 = (f32[8,56,1024]{2,1,0:T(8,128)S(1)}, f32[8,56,1024]{2,1,0:T(8,128)S(1)}) fusion(f32[8,62,1024]{2,1,0:T(8,128)S(1)} %get-tuple-element.55, f32[8,62,1024]{2,1,0:T(8,128)S(1)} %get-tuple-element.61, f32[56]{0:T(128)S(1)} %copy-done.31, f32[8,64,1024]{2,1,0:T(8,128)S(1)} %bitcast.163, f32[56,1024]{1,0:T(8,128)S(1)} %copy-done.19, ...), kind=kLoop, calls=%fused_computation.18 | loop fusion | flops 9175040 | bytes 19034848 | tf_op jit(solution)/shard_map/mul | solution.py:68
  55.8 0.8 add_multiply_fusion
  57.8 1.0 fusion.34
  63.4 1.6 %scatter.14 = f32[4,2,64,1024]{3,2,1,0:T(8,128)} pad(f32[1,2,64,1024]{3,2,1,0:T(8,128)S(1)} %slice_bitcast_fusion.1, f32[]{:T(128)} %constant.232.clone.1), padding=0_3x0_0x0_0x0_0 | pad | bytes 2621444 | tf_op jit(solution)/shard_map/scatter | solution.py:148
  65.0 0.8 fusion.49
  66.7 0.8 bitcast_dynamic-update-slice_fusion
  67.5 1.3 fusion.48
  68.9 3.7 %all-to-all-start.1 = ((f32[4,2,64,1024]{3,2,1,0:T(8,128)}), f32[4,2,64,1024]{3,2,1,0:T(8,128)S(1)}, u32[]{:S(2)}, u32[]{:S(2)}) async-start(f32[4,2,64,1024]{3,2,1,0:T(8,128)} %fusion.48), calls=%async_computation.1 | async-start | bytes 4194304 | tf_op jit(solution)/shard_map/all_to_all | solution.py:154
  72.7 24.7 %all-to-all-done.1 = f32[4,2,64,1024]{3,2,1,0:T(8,128)S(1)} async-done(((f32[4,2,64,1024]{3,2,1,0:T(8,128)}), f32[4,2,64,1024]{3,2,1,0:T(8,128)S(1)}, u32[]{:S(2)}, u32[]{:S(2)}) %all-to-all-start.1) | async-done | bytes 2097184 | tf_op jit(solution)/shard_map/all_to_all | solution.py:154
  97.4 1.5 %fusion.9 = f32[8,64]{1,0:T(8,128)S(1)} fusion(f32[8,64,1024]{2,1,0:T(8,128)S(1)} %bitcast.168, s32[64]{0:T(128)S(1)} %and_select_fusion.1, s32[64]{0:T(128)S(1)} %get-tuple-element.50), kind=kOutput, calls=%fused_computation.14 | convolution fusion | flops 404229632 | bytes 2099712 | tf_op jit(solution)/shard_map/or,mrc->moc/dot_general | solution.py:163
  99.0 1.1 collective-permute-done.4
  101.1 2.7 %collective-permute-start.7 = (f32[2,16,16]{2,1,0:T(8,128)S(1)}, f32[2,16,16]{2,1,0:T(8,128)S(1)}, u32[]{:S(2)}, u32[]{:S(2)}) collective-permute-start(f32[2,16,16]{2,1,0:T(8,128)S(1)} %pad_maximum_fusion.15), channel_id=1, source_target_pairs={{0,96},{32,64},{64,32},{96,0},{1,97},{33,65},{65,33},{97,1},{2,98}... | collective-permute-start | bytes 6152 | tf_op jit(solution)/shard_map/ppermute | solution.py:37
  104.0 1.8 %collective-permute-done.6 = f32[2,16,16]{2,1,0:T(8,128)S(1)} collective-permute-done((f32[2,16,16]{2,1,0:T(8,128)S(1)}, f32[2,16,16]{2,1,0:T(8,128)S(1)}, u32[]{:S(2)}, u32[]{:S(2)}) %collective-permute-start.6) | collective-permute-done | bytes 2080 | tf_op jit(solution)/shard_map/ppermute | solution.py:37
  106.1 1.5 %collective-permute-done.5 = f32[2,16,16]{2,1,0:T(8,128)S(1)} collective-permute-done((f32[2,16,16]{2,1,0:T(8,128)S(1)}, f32[2,16,16]{2,1,0:T(8,128)S(1)}, u32[]{:S(2)}, u32[]{:S(2)}) %collective-permute-start.5) | collective-permute-done | bytes 2080 | tf_op jit(solution)/shard_map/ppermute | solution.py:37
  107.5 3.4 %collective-permute-start.9 = (f32[2,16,16]{2,1,0:T(8,128)S(1)}, f32[2,16,16]{2,1,0:T(8,128)S(1)}, u32[]{:S(2)}, u32[]{:S(2)}) collective-permute-start(f32[2,16,16]{2,1,0:T(8,128)S(1)} %add_add_fusion.2), channel_id=1, source_target_pairs={{0,4},{2,6},{4,0},{6,2},{8,12},{10,14},{12,8},{14,10},{16,20},{18,... | collective-permute-start | bytes 6152 | tf_op jit(solution)/shard_map/ppermute | solution.py:37
  111.0 2.3 %collective-permute-start.10 = (f32[2,16,16]{2,1,0:T(8,128)S(1)}, f32[2,16,16]{2,1,0:T(8,128)S(1)}, u32[]{:S(2)}, u32[]{:S(2)}) collective-permute-start(f32[2,16,16]{2,1,0:T(8,128)S(1)} %add_add_fusion.2), channel_id=1, source_target_pairs={{0,6},{2,4},{4,2},{6,0},{8,14},{10,12},{12,10},{14,8},{16,22},{18,... | collective-permute-start | bytes 6152 | tf_op jit(solution)/shard_map/ppermute | solution.py:37
  113.3 0.8 collective-permute-start.8
  114.1 1.8 %collective-permute-done.10 = f32[2,16,16]{2,1,0:T(8,128)S(1)} collective-permute-done((f32[2,16,16]{2,1,0:T(8,128)S(1)}, f32[2,16,16]{2,1,0:T(8,128)S(1)}, u32[]{:S(2)}, u32[]{:S(2)}) %collective-permute-start.10) | collective-permute-done | bytes 2080 | tf_op jit(solution)/shard_map/ppermute | solution.py:37
  115.9 1.1 collective-permute-done.8
  117.0 3.9 %collective-permute-start.12 = (f32[2,16,16]{2,1,0:T(8,128)S(1)}, f32[2,16,16]{2,1,0:T(8,128)S(1)}, u32[]{:S(2)}, u32[]{:S(2)}) collective-permute-start(f32[2,16,16]{2,1,0:T(8,128)S(1)} %add_add_fusion.1), channel_id=1, source_target_pairs={{0,16},{2,18},{4,20},{6,22},{8,24},{10,26},{12,28},{14,30},{16,0},... | collective-permute-start | bytes 6152 | tf_op jit(solution)/shard_map/ppermute | solution.py:37
  121.9 0.8 collective-permute-done.12
  122.7 3.2 %collective-permute-done.13 = f32[2,16,16]{2,1,0:T(8,128)S(1)} collective-permute-done((f32[2,16,16]{2,1,0:T(8,128)S(1)}, f32[2,16,16]{2,1,0:T(8,128)S(1)}, u32[]{:S(2)}, u32[]{:S(2)}) %collective-permute-start.13) | collective-permute-done | bytes 2080 | tf_op jit(solution)/shard_map/ppermute | solution.py:37
  126.0 1.5 %cholesky.17 = f32[16,16]{1,0:T(8,128)S(1)} custom-call(f32[16,16]{1,0:T(8,128)S(1)} %fusion.59), custom_call_target="Cholesky" | custom-call | tf_op jit(solution)/shard_map/jit(cholesky)/cholesky | solution.py:181
  128.8 1.2 custom-call.10
  130.4 0.9 fusion.31
  131.3 1.3 copy.18
  (165 shorter events, 21.7 us)
Async XLA Ops:
  2.2 23.8 %collective-permute-start.3 = (f32[4,7,1024]{2,1,0:T(8,128)}, f32[4,7,1024]{2,1,0:T(8,128)S(1)}, u32[]{:S(2)}, u32[]{:S(2)}) collective-permute-start(f32[4,7,1024]{2,1,0:T(8,128)} %get-tuple-element.99), channel_id=1, source_target_pairs={{2,0},{4,2},{6,4},{8,6},{10,8},{12,10},{14,12},{16,14},{18,16},{20... | collective-permute-start | bytes 344072 | tf_op jit(solution)/shard_map/ppermute | solution.py:23
  3.5 10.7 %copy-start.1 = (f32[64,1024]{1,0:T(8,128)S(1)}, f32[64,1024]{1,0:T(8,128)}, u32[]{:S(2)}) copy-start(f32[64,1024]{1,0:T(8,128)} %param.20) | copy-start | bytes 786436
  3.5 10.7 %copy-start.2 = (f32[64,1024]{1,0:T(8,128)S(1)}, f32[64,1024]{1,0:T(8,128)}, u32[]{:S(2)}) copy-start(f32[64,1024]{1,0:T(8,128)} %param.19) | copy-start | bytes 786436
  3.5 11.6 %copy-start = (f32[64,1024]{1,0:T(8,128)S(1)}, f32[64,1024]{1,0:T(8,128)}, u32[]{:S(2)}) copy-start(f32[64,1024]{1,0:T(8,128)} %param.21) | copy-start | bytes 786436
  3.6 30.9 %all-to-all-start = ((f32[4,2,64,1024]{3,2,1,0:T(8,128)}), f32[4,2,64,1024]{3,2,1,0:T(8,128)S(1)}, u32[]{:S(2)}, u32[]{:S(2)}) async-start(f32[4,2,64,1024]{3,2,1,0:T(8,128)} %bitcast.194), calls=%async_computation | async-start | bytes 4194304 | tf_op jit(solution)/shard_map/all_to_all | solution.py:95
  8.1 14.3 %copy-start.26 = (f32[8,128]{1,0:T(8,128)S(1)}, f32[8,128]{1,0:T(8,128)}, u32[]{:S(2)}) copy-start(f32[8,128]{1,0:T(8,128)} %param.23) | copy-start | bytes 12292
  8.1 17.9 %collective-permute-start.2 = (f32[4,7,1024]{2,1,0:T(8,128)}, f32[4,7,1024]{2,1,0:T(8,128)S(1)}, u32[]{:S(2)}, u32[]{:S(2)}) collective-permute-start(f32[4,7,1024]{2,1,0:T(8,128)} %get-tuple-element.98), channel_id=1, source_target_pairs={{0,2},{2,4},{4,6},{6,8},{8,10},{10,12},{12,14},{14,16},{16,18},{18... | collective-permute-start | bytes 344072 | tf_op jit(solution)/shard_map/ppermute | solution.py:21
  12.9 9.5 %copy-start.39 = (f32[30,1]{0,1:T(1,128)}, f32[30,1]{0,1:T(1,128)S(1)}, u32[]{:S(2)}) copy-start(f32[30,1]{0,1:T(1,128)S(1)} %pad_maximum_fusion.16) | copy-start | bytes 364
  14.3 8.4 %copy-start.3 = (f32[64,1024]{1,0:T(8,128)S(1)}, f32[64,1024]{1,0:T(8,128)}, u32[]{:S(2)}) copy-start(f32[64,1024]{1,0:T(8,128)} %param.22) | copy-start | bytes 786436
  22.7 3.3 %copy-start.40 = (f32[30,1]{0,1:T(1,128)S(1)}, f32[30,1]{0,1:T(1,128)}, u32[]{:S(2)}) copy-start(f32[30,1]{0,1:T(1,128)} %copy-done.39) | copy-start | bytes 364
  34.5 7.3 %copy-start.4 = (f32[2,64,1024]{2,1,0:T(8,128)S(1)}, f32[2,64,1024]{2,1,0:T(8,128)}, u32[]{:S(2)}) copy-start(f32[2,64,1024]{2,1,0:T(8,128)} %broadcast_multiply_fusion) | copy-start | bytes 1572868
  35.4 6.7 %copy-start.12 = (f32[62,1024]{1,0:T(8,128)S(1)}, f32[62,1024]{1,0:T(8,128)}, u32[]{:S(2)}) copy-start(f32[62,1024]{1,0:T(8,128)} %slice_bitcast_fusion.16) | copy-start | bytes 761860
  35.4 6.7 %copy-start.13 = (f32[62,1024]{1,0:T(8,128)S(1)}, f32[62,1024]{1,0:T(8,128)}, u32[]{:S(2)}) copy-start(f32[62,1024]{1,0:T(8,128)} %get-tuple-element.114) | copy-start | bytes 761860
  35.4 6.7 %copy-start.14 = (f32[62,1024]{1,0:T(8,128)S(1)}, f32[62,1024]{1,0:T(8,128)}, u32[]{:S(2)}) copy-start(f32[62,1024]{1,0:T(8,128)} %get-tuple-element.115) | copy-start | bytes 761860
  35.4 6.7 %copy-start.32 = (f32[62]{0:T(128)S(1)}, f32[62]{0:T(128)}, u32[]{:S(2)}) copy-start(f32[62]{0:T(128)} %slice.725) | copy-start | bytes 748
  35.5 18.9 %collective-permute-start.1 = (f32[8,7,1024]{2,1,0:T(8,128)S(1)}, f32[8,7,1024]{2,1,0:T(8,128)S(1)}, u32[]{:S(2)}, u32[]{:S(2)}) collective-permute-start(f32[8,7,1024]{2,1,0:T(8,128)S(1)} %get-tuple-element.71), channel_id=1, source_target_pairs={{2,0},{4,2},{6,4},{8,6},{10,8},{12,10},{14,12},{16,14},{18,16},{20... | collective-permute-start | bytes 688136 | tf_op jit(solution)/shard_map/ppermute | solution.py:23
  36.9 17.5 %collective-permute-start = (f32[8,7,1024]{2,1,0:T(8,128)S(1)}, f32[8,7,1024]{2,1,0:T(8,128)S(1)}, u32[]{:S(2)}, u32[]{:S(2)}) collective-permute-start(f32[8,7,1024]{2,1,0:T(8,128)S(1)} %get-tuple-element.70), channel_id=1, source_target_pairs={{0,2},{2,4},{4,6},{6,8},{8,10},{10,12},{12,14},{14,16},{16,18},{18... | collective-permute-start | bytes 688136 | tf_op jit(solution)/shard_map/ppermute | solution.py:21
  44.2 1.1 copy-start.11
  44.2 1.1 copy-start.17
  44.2 1.1 copy-start.18
  44.2 1.1 copy-start.28
  47.5 1.1 copy-start.10
  47.5 1.1 copy-start.15
  50.7 1.1 copy-start.21
  50.8 1.1 copy-start.31
  51.9 2.5 %copy-start.23 = (f32[4,7,1024]{2,1,0:T(8,128)S(1)}, f32[4,7,1024]{2,1,0:T(8,128)}, u32[]{:S(2)}) copy-start(f32[4,7,1024]{2,1,0:T(8,128)} %copy-done.22) | copy-start | bytes 344068
  51.9 2.5 %copy-start.25 = (f32[4,7,1024]{2,1,0:T(8,128)S(1)}, f32[4,7,1024]{2,1,0:T(8,128)}, u32[]{:S(2)}) copy-start(f32[4,7,1024]{2,1,0:T(8,128)} %copy-done.24) | copy-start | bytes 344068
  61.4 1.1 copy-start.9
  61.4 1.1 copy-start.35
  63.4 2.4 %copy-start.5 = (f32[66,1024]{1,0:T(8,128)S(1)}, f32[66,1024]{1,0:T(8,128)}, u32[]{:S(2)}) copy-start(f32[66,1024]{1,0:T(8,128)} %get-tuple-element.87) | copy-start | bytes 811012
  63.4 2.4 %copy-start.6 = (f32[66,1024]{1,0:T(8,128)S(1)}, f32[66,1024]{1,0:T(8,128)}, u32[]{:S(2)}) copy-start(f32[66,1024]{1,0:T(8,128)} %get-tuple-element.88) | copy-start | bytes 811012
  63.4 2.4 %copy-start.34 = (f32[66]{0:T(128)S(1)}, f32[66]{0:T(128)}, u32[]{:S(2)}) copy-start(f32[66]{0:T(128)} %slice.785) | copy-start | bytes 796
  68.9 3.8 %copy-start.33 = (s32[1,64]{1,0:T(1,128)S(1)}, s32[1,64]{1,0:T(1,128)}, u32[]{:S(2)}) copy-start(s32[1,64]{1,0:T(1,128)} %param.24) | copy-start | bytes 772
  68.9 28.6 %all-to-all-start.1 = ((f32[4,2,64,1024]{3,2,1,0:T(8,128)}), f32[4,2,64,1024]{3,2,1,0:T(8,128)S(1)}, u32[]{:S(2)}, u32[]{:S(2)}) async-start(f32[4,2,64,1024]{3,2,1,0:T(8,128)} %fusion.48), calls=%async_computation.1 | async-start | bytes 4194304 | tf_op jit(solution)/shard_map/all_to_all | solution.py:154
  72.6 26.4 %copy-start.37 = (f32[1,64]{1,0:T(1,128)S(1)}, f32[1,64]{1,0:T(1,128)}, u32[]{:S(2)}) copy-start(f32[1,64]{1,0:T(1,128)} %param.27) | copy-start | bytes 772
  72.6 27.7 %copy-start.36 = (f32[1,64,16]{1,2,0:T(8,128)S(1)}, f32[1,64,16]{1,2,0:T(8,128)}, u32[]{:S(2)}) copy-start(f32[1,64,16]{1,2,0:T(8,128)} %param.26) | copy-start | bytes 12292
  72.6 27.7 %copy-start.38 = (f32[1,64]{1,0:T(1,128)S(1)}, f32[1,64]{1,0:T(1,128)}, u32[]{:S(2)}) copy-start(f32[1,64]{1,0:T(1,128)} %param.25) | copy-start | bytes 772
  98.9 1.2 collective-permute-start.4
  100.5 5.3 %collective-permute-start.6 = (f32[2,16,16]{2,1,0:T(8,128)S(1)}, f32[2,16,16]{2,1,0:T(8,128)S(1)}, u32[]{:S(2)}, u32[]{:S(2)}) collective-permute-start(f32[2,16,16]{2,1,0:T(8,128)S(1)} %pad_maximum_fusion.15), channel_id=1, source_target_pairs={{0,64},{32,96},{64,0},{96,32},{1,65},{33,97},{65,1},{97,33},{2,66}... | collective-permute-start | bytes 6152 | tf_op jit(solution)/shard_map/ppermute | solution.py:37
  101.1 4.9 %collective-permute-start.7 = (f32[2,16,16]{2,1,0:T(8,128)S(1)}, f32[2,16,16]{2,1,0:T(8,128)S(1)}, u32[]{:S(2)}, u32[]{:S(2)}) collective-permute-start(f32[2,16,16]{2,1,0:T(8,128)S(1)} %pad_maximum_fusion.15), channel_id=1, source_target_pairs={{0,96},{32,64},{64,32},{96,0},{1,97},{33,65},{65,33},{97,1},{2,98}... | collective-permute-start | bytes 6152 | tf_op jit(solution)/shard_map/ppermute | solution.py:37
  103.8 3.7 %collective-permute-start.5 = (f32[2,16,16]{2,1,0:T(8,128)S(1)}, f32[2,16,16]{2,1,0:T(8,128)S(1)}, u32[]{:S(2)}, u32[]{:S(2)}) collective-permute-start(f32[2,16,16]{2,1,0:T(8,128)S(1)} %pad_maximum_fusion.15), channel_id=1, source_target_pairs={{0,32},{32,0},{64,96},{96,64},{1,33},{33,1},{65,97},{97,65},{2,34}... | collective-permute-start | bytes 6152 | tf_op jit(solution)/shard_map/ppermute | solution.py:37
  104.0 10.0 %collective-permute-start.14 = (f32[8,128]{1,0:T(8,128)S(1)}, f32[8,128]{1,0:T(8,128)S(1)}, u32[]{:S(2)}, u32[]{:S(2)}) collective-permute-start(f32[8,128]{1,0:T(8,128)S(1)} %copy-done.26), channel_id=1, source_target_pairs={{0,1},{1,0},{2,3},{3,2},{4,5},{5,4},{6,7},{7,6},{8,9},{9,8},{10,11... | collective-permute-start | bytes 12296 | tf_op jit(solution)/shard_map/ppermute | solution.py:49
  107.5 6.5 %collective-permute-start.9 = (f32[2,16,16]{2,1,0:T(8,128)S(1)}, f32[2,16,16]{2,1,0:T(8,128)S(1)}, u32[]{:S(2)}, u32[]{:S(2)}) collective-permute-start(f32[2,16,16]{2,1,0:T(8,128)S(1)} %add_add_fusion.2), channel_id=1, source_target_pairs={{0,4},{2,6},{4,0},{6,2},{8,12},{10,14},{12,8},{14,10},{16,20},{18,... | collective-permute-start | bytes 6152 | tf_op jit(solution)/shard_map/ppermute | solution.py:37
  111.0 4.9 %collective-permute-start.10 = (f32[2,16,16]{2,1,0:T(8,128)S(1)}, f32[2,16,16]{2,1,0:T(8,128)S(1)}, u32[]{:S(2)}, u32[]{:S(2)}) collective-permute-start(f32[2,16,16]{2,1,0:T(8,128)S(1)} %add_add_fusion.2), channel_id=1, source_target_pairs={{0,6},{2,4},{4,2},{6,0},{8,14},{10,12},{12,10},{14,8},{16,22},{18,... | collective-permute-start | bytes 6152 | tf_op jit(solution)/shard_map/ppermute | solution.py:37
  113.3 3.7 %collective-permute-start.8 = (f32[2,16,16]{2,1,0:T(8,128)S(1)}, f32[2,16,16]{2,1,0:T(8,128)S(1)}, u32[]{:S(2)}, u32[]{:S(2)}) collective-permute-start(f32[2,16,16]{2,1,0:T(8,128)S(1)} %add_add_fusion.2), channel_id=1, source_target_pairs={{0,2},{2,0},{4,6},{6,4},{8,10},{10,8},{12,14},{14,12},{16,18},{18,... | collective-permute-start | bytes 6152 | tf_op jit(solution)/shard_map/ppermute | solution.py:37
  117.0 5.7 %collective-permute-start.12 = (f32[2,16,16]{2,1,0:T(8,128)S(1)}, f32[2,16,16]{2,1,0:T(8,128)S(1)}, u32[]{:S(2)}, u32[]{:S(2)}) collective-permute-start(f32[2,16,16]{2,1,0:T(8,128)S(1)} %add_add_fusion.1), channel_id=1, source_target_pairs={{0,16},{2,18},{4,20},{6,22},{8,24},{10,26},{12,28},{14,30},{16,0},... | collective-permute-start | bytes 6152 | tf_op jit(solution)/shard_map/ppermute | solution.py:37
  121.0 4.9 %collective-permute-start.13 = (f32[2,16,16]{2,1,0:T(8,128)S(1)}, f32[2,16,16]{2,1,0:T(8,128)S(1)}, u32[]{:S(2)}, u32[]{:S(2)}) collective-permute-start(f32[2,16,16]{2,1,0:T(8,128)S(1)} %add_add_fusion.1), channel_id=1, source_target_pairs={{0,24},{2,26},{4,28},{6,30},{8,16},{10,18},{12,20},{14,22},{16,8},... | collective-permute-start | bytes 6152 | tf_op jit(solution)/shard_map/ppermute | solution.py:37
  121.7 4.2 %collective-permute-start.11 = (f32[2,16,16]{2,1,0:T(8,128)S(1)}, f32[2,16,16]{2,1,0:T(8,128)S(1)}, u32[]{:S(2)}, u32[]{:S(2)}) collective-permute-start(f32[2,16,16]{2,1,0:T(8,128)S(1)} %add_add_fusion.1), channel_id=1, source_target_pairs={{0,8},{2,10},{4,12},{6,14},{8,0},{10,2},{12,4},{14,6},{16,24},{18,... | collective-permute-start | bytes 6152 | tf_op jit(solution)/shard_map/ppermute | solution.py:37
  (10 other events, 9.3 us)

commit v15 on v13

--- a/solution.py
+++ b/solution.py
@@ -174,8 +174,8 @@
     gram = jnp.dot(anomaly, anomaly.T, precision=lax.Precision.HIGHEST)
     cross = jnp.dot(anomaly, misfit.T, precision=lax.Precision.HIGHEST)
     sums = jnp.stack([gram, cross])
+    sums = quad_sum(sums, "space")
     sums = quad_sum(sums, "tm")
-    sums = quad_sum(sums, "space")
     gram, cross = sums[0], sums[1]
     system = jnp.eye(total, dtype=jnp.float32) + gram
     factor = jnp.linalg.cholesky(system)

time: 132 us -> 132 us (level)
  no operation moved by 1% of the time
where the time goes in v15:
time: 132 us; the launch traced here: 131 us
  waiting for transfers between devices  42.1 us (32%)
  starting transfers between devices  35.5 us (27%)
  local copies, waits for them, and re-layouts  25.5 us (19%)
  other arithmetic  23.5 us (18%)
  matrix products  2.96 us (2%)
  between operations  1.52 us (1%)
    all_to_all x1, waiting for transfers between devices, per_device(): lax.all_to_all(done, 'tm', 0, 0, tiled=True)  24.7 us
    ppermute x9, starting transfers between devices, quad_sum(): lax.ppermute(value, axis, [(i, i ^ k * bit) for i in range(count)])  14.9 us
    mul x9, other arithmetic, advance(): return (middle + step_size * tendency) * inside  12.4 us
    ppermute x9, waiting for transfers between devices, quad_sum(): lax.ppermute(value, axis, [(i, i ^ k * bit) for i in range(count)])  10.5 us
    ppermute x2, starting transfers between devices, with_halo(): lax.ppermute(tail, axis, [(i, i + 1) for i in range(ends)])  9.58 us
    slice x11, local copies, waits for them, and re-layouts, advance(): west_cell = jnp.pad(middle[:, :, :-1], ((0, 0), (0, 0), (1, 0)))  6.22 us
    all_to_all x1, waiting for transfers between devices, per_device(): lax.all_to_all(state.reshape(slices, group, row_count, col_count), 'tm',...  5.78 us
    mul x10, local copies, waits for them, and re-layouts, advance(): coeffs[0] * (above_row + below_row + west_cell + east_cell - 4.0 * middle)  4.95 us
  transfers between devices with their start and end apart: 17, of which 10 were waited for; matrix products, arithmetic and copies ran while one was open for 21% of the time, Pallas kernels for 0%

profile of v15, /device:TPU:0, one launch (start us, length us, event | category | flops | bytes accessed | tf_op | source)
XLA Modules:
  0.0 131.1 jit_solution(8395868024010009619)
XLA Ops:
  0.6 1.6 %pad_maximum_fusion.15 = (f32[4,7,1024]{2,1,0:T(8,128)}, f32[4,7,1024]{2,1,0:T(8,128)}) fusion(f32[1,64,1024]{2,1,0:T(8,128)} %bitcast.187, f32[1,64,1024]{2,1,0:T(8,128)} %bitcast.173, f32[1,64,1024]{2,1,0:T(8,128)} %bitcast.180, f32[1,64,1024]{2,1,0:T(8,128)} %bitcast.166), kind=kLoop, calls=%fused_computation.119 | loop fusion | flops 172032 | bytes 1277952 | tf_op jit(solution)/shard_map/slice | solution.py:18
  2.2 1.3 collective-permute-start.3
  3.6 4.5 %all-to-all-start = ((f32[4,2,64,1024]{3,2,1,0:T(8,128)}), f32[4,2,64,1024]{3,2,1,0:T(8,128)S(1)}, u32[]{:S(2)}, u32[]{:S(2)}) async-start(f32[4,2,64,1024]{3,2,1,0:T(8,128)} %bitcast.190), calls=%async_computation | async-start | bytes 4194304 | tf_op jit(solution)/shard_map/all_to_all | solution.py:95
  8.1 4.7 %collective-permute-start.2 = (f32[4,7,1024]{2,1,0:T(8,128)}, f32[4,7,1024]{2,1,0:T(8,128)S(1)}, u32[]{:S(2)}, u32[]{:S(2)}) collective-permute-start(f32[4,7,1024]{2,1,0:T(8,128)} %get-tuple-element.50), channel_id=1, source_target_pairs={{0,2},{2,4},{4,6},{6,8},{8,10},{10,12},{12,14},{14,16},{16,18},{18... | collective-permute-start | bytes 344072 | tf_op jit(solution)/shard_map/ppermute | solution.py:21
  14.2 0.9 slice_bitcast_fusion.15
  15.0 0.7 slice_bitcast_fusion.17
  16.4 0.8 slice_bitcast_fusion.18
  19.1 0.7 slice_bitcast_fusion.11
  19.9 0.7 slice_bitcast_fusion.20
  22.7 0.9 broadcast_multiply_fusion
  24.2 0.9 slice_bitcast_fusion.12
  25.1 0.8 slice_bitcast_fusion.9
  26.7 1.0 slice_bitcast_fusion.8
  27.7 0.9 slice_bitcast_fusion.5
  28.6 5.8 %all-to-all-done = f32[4,2,64,1024]{3,2,1,0:T(8,128)S(1)} async-done(((f32[4,2,64,1024]{3,2,1,0:T(8,128)}), f32[4,2,64,1024]{3,2,1,0:T(8,128)S(1)}, u32[]{:S(2)}, u32[]{:S(2)}) %all-to-all-start) | async-done | bytes 2097184 | tf_op jit(solution)/shard_map/all_to_all | solution.py:95
  34.5 0.9 fusion.81
  35.5 1.4 %collective-permute-start.1 = (f32[8,7,1024]{2,1,0:T(8,128)S(1)}, f32[8,7,1024]{2,1,0:T(8,128)S(1)}, u32[]{:S(2)}, u32[]{:S(2)}) collective-permute-start(f32[8,7,1024]{2,1,0:T(8,128)S(1)} %get-tuple-element.23), channel_id=1, source_target_pairs={{2,0},{4,2},{6,4},{8,6},{10,8},{12,10},{14,12},{16,14},{18,16},{20... | collective-permute-start | bytes 688136 | tf_op jit(solution)/shard_map/ppermute | solution.py:23
  36.9 4.9 %collective-permute-start = (f32[8,7,1024]{2,1,0:T(8,128)S(1)}, f32[8,7,1024]{2,1,0:T(8,128)S(1)}, u32[]{:S(2)}, u32[]{:S(2)}) collective-permute-start(f32[8,7,1024]{2,1,0:T(8,128)S(1)} %get-tuple-element.22), channel_id=1, source_target_pairs={{0,2},{2,4},{4,6},{6,8},{8,10},{10,12},{12,14},{14,16},{16,18},{18... | collective-permute-start | bytes 688136 | tf_op jit(solution)/shard_map/ppermute | solution.py:21
  42.1 2.1 %fusion.8 = (f32[8,62,1024]{2,1,0:T(8,128)S(1)}, f32[8,62,1024]{2,1,0:T(8,128)S(1)}, f32[8,62,1024]{2,1,0:T(8,128)S(1)}) fusion(f32[8,64,1024]{2,1,0:T(8,128)S(1)} %bitcast.156, f32[62]{0:T(128)S(1)} %copy-done.31, f32[8,64,1024]{2,1,0:T(8,128)S(1)} %bitcast.154, f32[62,1024]{1,0:T(8,128)S(1)} %copy-done.13, f32[62,1024]{1,0:T(8,128)S(1)} %copy-done.14, ...), kind=kLoop, calls=%fused_computation.12 | loop fusion | flops 9142272 | bytes 19042680 | tf_op jit(solution)/shard_map/mul | solution.py:68
  44.2 1.1 fusion.80
  45.4 2.1 %fusion.5 = f32[8,60,1024]{2,1,0:T(8,128)S(1)} fusion(f32[8,64,1024]{2,1,0:T(8,128)S(1)} %bitcast.157, f32[8,62,1024]{2,1,0:T(8,128)S(1)} %get-tuple-element.6, f32[8,60,1023]{2,1,0:T(8,128)S(1)} %get-tuple-element.19, f32[8,60,1023]{2,1,0:T(8,128)S(1)} %get-tuple-element.18, f32[60]{0:T(128)S(1)} %copy-done.28, f32[60,1024]{1,0:T(8,128)S(1)} %copy-done.17, ...), kind=kLoop, calls=%fused_computation.8 | loop fusion | flops 8847360 | bytes 14496240 | tf_op jit(solution)/shard_map/mul | solution.py:68
  47.5 1.1 fusion.79
  48.6 2.1 %fusion.2 = f32[8,58,1024]{2,1,0:T(8,128)S(1)} fusion(f32[8,64,1024]{2,1,0:T(8,128)S(1)} %bitcast.158, f32[8,60,1024]{2,1,0:T(8,128)S(1)} %fusion.5, f32[8,58,1023]{2,1,0:T(8,128)S(1)} %get-tuple-element.17, f32[8,58,1023]{2,1,0:T(8,128)S(1)} %get-tuple-element.16, f32[58]{0:T(128)S(1)} %copy-done.27, f32[58,1024]{1,0:T(8,128)S(1)} %copy-done.15, ...), kind=kLoop, calls=%fused_computation.4 | loop fusion | flops 8552448 | bytes 14013032 | tf_op jit(solution)/shard_map/mul | solution.py:68
  50.8 0.9 fusion.78
  51.9 2.5 %fusion.10 = (f32[8,56,1024]{2,1,0:T(8,128)S(1)}, f32[8,56,1024]{2,1,0:T(8,128)S(1)}) fusion(f32[8,62,1024]{2,1,0:T(8,128)S(1)} %get-tuple-element.7, f32[8,62,1024]{2,1,0:T(8,128)S(1)} %get-tuple-element.13, f32[56]{0:T(128)S(1)} %copy-done.30, f32[8,64,1024]{2,1,0:T(8,128)S(1)} %bitcast.159, f32[56,1024]{1,0:T(8,128)S(1)} %copy-done.19, ...), kind=kLoop, calls=%fused_computation.19 | loop fusion | flops 9175040 | bytes 19034848 | tf_op jit(solution)/shard_map/mul | solution.py:68
  55.8 0.8 add_multiply_fusion
  57.8 1.0 fusion.34
  60.1 0.7 fusion.40
  65.9 1.5 %pad_maximum_fusion.1 = f32[4,2,64,1024]{3,2,1,0:T(8,128)} fusion(f32[1,2,64,1024]{3,2,1,0:T(8,128)S(1)} %get-tuple-element.57, f32[1,2,64,1024]{3,2,1,0:T(8,128)S(1)} %get-tuple-element.56, f32[1,2,64,1024]{3,2,1,0:T(8,128)S(1)} %slice_bitcast_fusion, f32[1,2,64,1024]{3,2,1,0:T(8,128)S(1)} %slice_bitcast_fusion.1), kind=kLoop, calls=%fused_computation.13 | loop fusion | flops 1572864 | bytes 4194304 | tf_op jit(solution)/shard_map/stack | solution.py:153
  67.4 3.7 %all-to-all-start.1 = ((f32[4,2,64,1024]{3,2,1,0:T(8,128)}), f32[4,2,64,1024]{3,2,1,0:T(8,128)S(1)}, u32[]{:S(2)}, u32[]{:S(2)}) async-start(f32[4,2,64,1024]{3,2,1,0:T(8,128)} %pad_maximum_fusion.1), calls=%async_computation.1 | async-start | bytes 4194304 | tf_op jit(solution)/shard_map/all_to_all | solution.py:154
  71.2 24.7 %all-to-all-done.1 = f32[4,2,64,1024]{3,2,1,0:T(8,128)S(1)} async-done(((f32[4,2,64,1024]{3,2,1,0:T(8,128)}), f32[4,2,64,1024]{3,2,1,0:T(8,128)S(1)}, u32[]{:S(2)}, u32[]{:S(2)}) %all-to-all-start.1) | async-done | bytes 2097184 | tf_op jit(solution)/shard_map/all_to_all | solution.py:154
  96.0 1.5 %fusion.9 = f32[8,64]{1,0:T(8,128)S(1)} fusion(f32[8,64,1024]{2,1,0:T(8,128)S(1)} %bitcast.164, s32[64]{0:T(128)S(1)} %and_select_fusion.1, s32[64]{0:T(128)S(1)} %get-tuple-element.2), kind=kOutput, calls=%fused_computation.15 | convolution fusion | flops 404229632 | bytes 2099712 | tf_op jit(solution)/shard_map/or,mrc->moc/dot_general | solution.py:163
  97.6 1.1 collective-permute-done.4
  99.0 3.4 %collective-permute-start.6 = (f32[2,16,16]{2,1,0:T(8,128)S(1)}, f32[2,16,16]{2,1,0:T(8,128)S(1)}, u32[]{:S(2)}, u32[]{:S(2)}) collective-permute-start(f32[2,16,16]{2,1,0:T(8,128)S(1)} %pad_maximum_fusion.16), channel_id=1, source_target_pairs={{0,4},{2,6},{4,0},{6,2},{8,12},{10,14},{12,8},{14,10},{16,20},{18,... | collective-permute-start | bytes 6152 | tf_op jit(solution)/shard_map/ppermute | solution.py:37
  102.4 2.3 %collective-permute-start.7 = (f32[2,16,16]{2,1,0:T(8,128)S(1)}, f32[2,16,16]{2,1,0:T(8,128)S(1)}, u32[]{:S(2)}, u32[]{:S(2)}) collective-permute-start(f32[2,16,16]{2,1,0:T(8,128)S(1)} %pad_maximum_fusion.16), channel_id=1, source_target_pairs={{0,6},{2,4},{4,2},{6,0},{8,14},{10,12},{12,10},{14,8},{16,22},{18,... | collective-permute-start | bytes 6152 | tf_op jit(solution)/shard_map/ppermute | solution.py:37
  104.7 0.8 collective-permute-start.5
  105.5 1.9 %collective-permute-done.7 = f32[2,16,16]{2,1,0:T(8,128)S(1)} collective-permute-done((f32[2,16,16]{2,1,0:T(8,128)S(1)}, f32[2,16,16]{2,1,0:T(8,128)S(1)}, u32[]{:S(2)}, u32[]{:S(2)}) %collective-permute-start.7) | collective-permute-done | bytes 2080 | tf_op jit(solution)/shard_map/ppermute | solution.py:37
  107.4 1.1 collective-permute-done.5
  108.5 4.0 %collective-permute-start.9 = (f32[2,16,16]{2,1,0:T(8,128)S(1)}, f32[2,16,16]{2,1,0:T(8,128)S(1)}, u32[]{:S(2)}, u32[]{:S(2)}) collective-permute-start(f32[2,16,16]{2,1,0:T(8,128)S(1)} %add_add_fusion.2), channel_id=1, source_target_pairs={{0,16},{2,18},{4,20},{6,22},{8,24},{10,26},{12,28},{14,30},{16,0},... | collective-permute-start | bytes 6152 | tf_op jit(solution)/shard_map/ppermute | solution.py:37
  113.4 0.8 collective-permute-done.9
  114.2 3.2 %collective-permute-done.10 = f32[2,16,16]{2,1,0:T(8,128)S(1)} collective-permute-done((f32[2,16,16]{2,1,0:T(8,128)S(1)}, f32[2,16,16]{2,1,0:T(8,128)S(1)}, u32[]{:S(2)}, u32[]{:S(2)}) %collective-permute-start.10) | collective-permute-done | bytes 2080 | tf_op jit(solution)/shard_map/ppermute | solution.py:37
  118.1 2.7 %collective-permute-start.13 = (f32[2,16,16]{2,1,0:T(8,128)S(1)}, f32[2,16,16]{2,1,0:T(8,128)S(1)}, u32[]{:S(2)}, u32[]{:S(2)}) collective-permute-start(f32[2,16,16]{2,1,0:T(8,128)S(1)} %add_add_fusion.1), channel_id=1, source_target_pairs={{0,96},{32,64},{64,32},{96,0},{1,97},{33,65},{65,33},{97,1},{2,98}... | collective-permute-start | bytes 6152 | tf_op jit(solution)/shard_map/ppermute | solution.py:37
  121.0 1.8 %collective-permute-done.12 = f32[2,16,16]{2,1,0:T(8,128)S(1)} collective-permute-done((f32[2,16,16]{2,1,0:T(8,128)S(1)}, f32[2,16,16]{2,1,0:T(8,128)S(1)}, u32[]{:S(2)}, u32[]{:S(2)}) %collective-permute-start.12) | collective-permute-done | bytes 2080 | tf_op jit(solution)/shard_map/ppermute | solution.py:37
  123.0 1.5 %collective-permute-done.11 = f32[2,16,16]{2,1,0:T(8,128)S(1)} collective-permute-done((f32[2,16,16]{2,1,0:T(8,128)S(1)}, f32[2,16,16]{2,1,0:T(8,128)S(1)}, u32[]{:S(2)}, u32[]{:S(2)}) %collective-permute-start.11) | collective-permute-done | bytes 2080 | tf_op jit(solution)/shard_map/ppermute | solution.py:37
  124.6 1.5 %cholesky.17 = f32[16,16]{1,0:T(8,128)S(1)} custom-call(f32[16,16]{1,0:T(8,128)S(1)} %fusion.57), custom_call_target="Cholesky" | custom-call | tf_op jit(solution)/shard_map/jit(cholesky)/cholesky | solution.py:181
  127.4 1.2 custom-call.10
  128.9 0.9 fusion.31
  129.8 1.3 %copy.15 = f32[1,8,64,1024]{3,2,1,0:T(8,128)} copy(f32[1,8,64,1024]{3,2,1,0:T(8,128)S(1)} %bitcast.165) | data formatting | bytes 4194304
  (164 shorter events, 21.1 us)
Async XLA Ops:
  2.2 23.8 %collective-permute-start.3 = (f32[4,7,1024]{2,1,0:T(8,128)}, f32[4,7,1024]{2,1,0:T(8,128)S(1)}, u32[]{:S(2)}, u32[]{:S(2)}) collective-permute-start(f32[4,7,1024]{2,1,0:T(8,128)} %get-tuple-element.51), channel_id=1, source_target_pairs={{2,0},{4,2},{6,4},{8,6},{10,8},{12,10},{14,12},{16,14},{18,16},{20... | collective-permute-start | bytes 344072 | tf_op jit(solution)/shard_map/ppermute | solution.py:23
  3.5 10.7 %copy-start.1 = (f32[64,1024]{1,0:T(8,128)S(1)}, f32[64,1024]{1,0:T(8,128)}, u32[]{:S(2)}) copy-start(f32[64,1024]{1,0:T(8,128)} %param.12) | copy-start | bytes 786436
  3.5 10.6 %copy-start.2 = (f32[64,1024]{1,0:T(8,128)S(1)}, f32[64,1024]{1,0:T(8,128)}, u32[]{:S(2)}) copy-start(f32[64,1024]{1,0:T(8,128)} %param.11) | copy-start | bytes 786436
  3.6 11.5 %copy-start = (f32[64,1024]{1,0:T(8,128)S(1)}, f32[64,1024]{1,0:T(8,128)}, u32[]{:S(2)}) copy-start(f32[64,1024]{1,0:T(8,128)} %param.13) | copy-start | bytes 786436
  3.6 30.9 %all-to-all-start = ((f32[4,2,64,1024]{3,2,1,0:T(8,128)}), f32[4,2,64,1024]{3,2,1,0:T(8,128)S(1)}, u32[]{:S(2)}, u32[]{:S(2)}) async-start(f32[4,2,64,1024]{3,2,1,0:T(8,128)} %bitcast.190), calls=%async_computation | async-start | bytes 4194304 | tf_op jit(solution)/shard_map/all_to_all | solution.py:95
  8.1 14.4 %copy-start.26 = (f32[8,128]{1,0:T(8,128)S(1)}, f32[8,128]{1,0:T(8,128)}, u32[]{:S(2)}) copy-start(f32[8,128]{1,0:T(8,128)} %param.15) | copy-start | bytes 12292
  8.1 17.9 %collective-permute-start.2 = (f32[4,7,1024]{2,1,0:T(8,128)}, f32[4,7,1024]{2,1,0:T(8,128)S(1)}, u32[]{:S(2)}, u32[]{:S(2)}) collective-permute-start(f32[4,7,1024]{2,1,0:T(8,128)} %get-tuple-element.50), channel_id=1, source_target_pairs={{0,2},{2,4},{4,6},{6,8},{8,10},{10,12},{12,14},{14,16},{16,18},{18... | collective-permute-start | bytes 344072 | tf_op jit(solution)/shard_map/ppermute | solution.py:21
  12.9 9.5 %copy-start.39 = (f32[30,1]{0,1:T(1,128)}, f32[30,1]{0,1:T(1,128)S(1)}, u32[]{:S(2)}) copy-start(f32[30,1]{0,1:T(1,128)S(1)} %pad_maximum_fusion.17) | copy-start | bytes 364
  14.2 8.5 %copy-start.3 = (f32[64,1024]{1,0:T(8,128)S(1)}, f32[64,1024]{1,0:T(8,128)}, u32[]{:S(2)}) copy-start(f32[64,1024]{1,0:T(8,128)} %param.14) | copy-start | bytes 786436
  22.7 3.2 %copy-start.40 = (f32[30,1]{0,1:T(1,128)S(1)}, f32[30,1]{0,1:T(1,128)}, u32[]{:S(2)}) copy-start(f32[30,1]{0,1:T(1,128)} %copy-done.39) | copy-start | bytes 364
  34.5 7.3 %copy-start.4 = (f32[2,64,1024]{2,1,0:T(8,128)S(1)}, f32[2,64,1024]{2,1,0:T(8,128)}, u32[]{:S(2)}) copy-start(f32[2,64,1024]{2,1,0:T(8,128)} %broadcast_multiply_fusion) | copy-start | bytes 1572868
  35.4 6.7 %copy-start.12 = (f32[62,1024]{1,0:T(8,128)S(1)}, f32[62,1024]{1,0:T(8,128)}, u32[]{:S(2)}) copy-start(f32[62,1024]{1,0:T(8,128)} %slice_bitcast_fusion.17) | copy-start | bytes 761860
  35.4 6.7 %copy-start.13 = (f32[62,1024]{1,0:T(8,128)S(1)}, f32[62,1024]{1,0:T(8,128)}, u32[]{:S(2)}) copy-start(f32[62,1024]{1,0:T(8,128)} %get-tuple-element.68) | copy-start | bytes 761860
  35.4 6.7 %copy-start.14 = (f32[62,1024]{1,0:T(8,128)S(1)}, f32[62,1024]{1,0:T(8,128)}, u32[]{:S(2)}) copy-start(f32[62,1024]{1,0:T(8,128)} %get-tuple-element.69) | copy-start | bytes 761860
  35.5 6.7 %copy-start.31 = (f32[62]{0:T(128)S(1)}, f32[62]{0:T(128)}, u32[]{:S(2)}) copy-start(f32[62]{0:T(128)} %slice.626) | copy-start | bytes 748
  35.5 18.9 %collective-permute-start.1 = (f32[8,7,1024]{2,1,0:T(8,128)S(1)}, f32[8,7,1024]{2,1,0:T(8,128)S(1)}, u32[]{:S(2)}, u32[]{:S(2)}) collective-permute-start(f32[8,7,1024]{2,1,0:T(8,128)S(1)} %get-tuple-element.23), channel_id=1, source_target_pairs={{2,0},{4,2},{6,4},{8,6},{10,8},{12,10},{14,12},{16,14},{18,16},{20... | collective-permute-start | bytes 688136 | tf_op jit(solution)/shard_map/ppermute | solution.py:23
  36.9 17.5 %collective-permute-start = (f32[8,7,1024]{2,1,0:T(8,128)S(1)}, f32[8,7,1024]{2,1,0:T(8,128)S(1)}, u32[]{:S(2)}, u32[]{:S(2)}) collective-permute-start(f32[8,7,1024]{2,1,0:T(8,128)S(1)} %get-tuple-element.22), channel_id=1, source_target_pairs={{0,2},{2,4},{4,6},{6,8},{8,10},{10,12},{12,14},{14,16},{16,18},{18... | collective-permute-start | bytes 688136 | tf_op jit(solution)/shard_map/ppermute | solution.py:21
  44.2 1.1 copy-start.11
  44.2 1.1 copy-start.17
  44.2 1.1 copy-start.18
  44.2 1.1 copy-start.28
  47.5 1.1 copy-start.10
  47.5 1.1 copy-start.15
  47.5 1.1 copy-start.16
  47.5 1.1 copy-start.27
  50.8 1.1 copy-start.21
  50.8 1.1 copy-start.30
  51.9 2.5 %copy-start.23 = (f32[4,7,1024]{2,1,0:T(8,128)S(1)}, f32[4,7,1024]{2,1,0:T(8,128)}, u32[]{:S(2)}) copy-start(f32[4,7,1024]{2,1,0:T(8,128)} %copy-done.22) | copy-start | bytes 344068
  51.9 2.5 %copy-start.25 = (f32[4,7,1024]{2,1,0:T(8,128)S(1)}, f32[4,7,1024]{2,1,0:T(8,128)}, u32[]{:S(2)}) copy-start(f32[4,7,1024]{2,1,0:T(8,128)} %copy-done.24) | copy-start | bytes 344068
  61.4 1.1 copy-start.9
  61.4 1.1 copy-start.35
  63.1 1.0 copy-start.6
  67.4 3.8 %copy-start.32 = (s32[1,64]{1,0:T(1,128)S(1)}, s32[1,64]{1,0:T(1,128)}, u32[]{:S(2)}) copy-start(s32[1,64]{1,0:T(1,128)} %param.16) | copy-start | bytes 772
  67.4 28.6 %all-to-all-start.1 = ((f32[4,2,64,1024]{3,2,1,0:T(8,128)}), f32[4,2,64,1024]{3,2,1,0:T(8,128)S(1)}, u32[]{:S(2)}, u32[]{:S(2)}) async-start(f32[4,2,64,1024]{3,2,1,0:T(8,128)} %pad_maximum_fusion.1), calls=%async_computation.1 | async-start | bytes 4194304 | tf_op jit(solution)/shard_map/all_to_all | solution.py:154
  71.1 26.4 %copy-start.37 = (f32[1,64]{1,0:T(1,128)S(1)}, f32[1,64]{1,0:T(1,128)}, u32[]{:S(2)}) copy-start(f32[1,64]{1,0:T(1,128)} %param.19) | copy-start | bytes 772
  71.2 27.7 %copy-start.36 = (f32[1,64,16]{1,2,0:T(8,128)S(1)}, f32[1,64,16]{1,2,0:T(8,128)}, u32[]{:S(2)}) copy-start(f32[1,64,16]{1,2,0:T(8,128)} %param.18) | copy-start | bytes 12292
  71.2 27.7 %copy-start.38 = (f32[1,64]{1,0:T(1,128)S(1)}, f32[1,64]{1,0:T(1,128)}, u32[]{:S(2)}) copy-start(f32[1,64]{1,0:T(1,128)} %param.17) | copy-start | bytes 772
  97.4 1.2 collective-permute-start.4
  99.0 6.5 %collective-permute-start.6 = (f32[2,16,16]{2,1,0:T(8,128)S(1)}, f32[2,16,16]{2,1,0:T(8,128)S(1)}, u32[]{:S(2)}, u32[]{:S(2)}) collective-permute-start(f32[2,16,16]{2,1,0:T(8,128)S(1)} %pad_maximum_fusion.16), channel_id=1, source_target_pairs={{0,4},{2,6},{4,0},{6,2},{8,12},{10,14},{12,8},{14,10},{16,20},{18,... | collective-permute-start | bytes 6152 | tf_op jit(solution)/shard_map/ppermute | solution.py:37
  102.4 4.9 %collective-permute-start.7 = (f32[2,16,16]{2,1,0:T(8,128)S(1)}, f32[2,16,16]{2,1,0:T(8,128)S(1)}, u32[]{:S(2)}, u32[]{:S(2)}) collective-permute-start(f32[2,16,16]{2,1,0:T(8,128)S(1)} %pad_maximum_fusion.16), channel_id=1, source_target_pairs={{0,6},{2,4},{4,2},{6,0},{8,14},{10,12},{12,10},{14,8},{16,22},{18,... | collective-permute-start | bytes 6152 | tf_op jit(solution)/shard_map/ppermute | solution.py:37
  104.7 3.7 %collective-permute-start.5 = (f32[2,16,16]{2,1,0:T(8,128)S(1)}, f32[2,16,16]{2,1,0:T(8,128)S(1)}, u32[]{:S(2)}, u32[]{:S(2)}) collective-permute-start(f32[2,16,16]{2,1,0:T(8,128)S(1)} %pad_maximum_fusion.16), channel_id=1, source_target_pairs={{0,2},{2,0},{4,6},{6,4},{8,10},{10,8},{12,14},{14,12},{16,18},{18,... | collective-permute-start | bytes 6152 | tf_op jit(solution)/shard_map/ppermute | solution.py:37
  105.5 7.8 %collective-permute-start.14 = (f32[8,128]{1,0:T(8,128)S(1)}, f32[8,128]{1,0:T(8,128)S(1)}, u32[]{:S(2)}, u32[]{:S(2)}) collective-permute-start(f32[8,128]{1,0:T(8,128)S(1)} %copy-done.26), channel_id=1, source_target_pairs={{0,1},{1,0},{2,3},{3,2},{4,5},{5,4},{6,7},{7,6},{8,9},{9,8},{10,11... | collective-permute-start | bytes 12296 | tf_op jit(solution)/shard_map/ppermute | solution.py:49
  108.5 5.7 %collective-permute-start.9 = (f32[2,16,16]{2,1,0:T(8,128)S(1)}, f32[2,16,16]{2,1,0:T(8,128)S(1)}, u32[]{:S(2)}, u32[]{:S(2)}) collective-permute-start(f32[2,16,16]{2,1,0:T(8,128)S(1)} %add_add_fusion.2), channel_id=1, source_target_pairs={{0,16},{2,18},{4,20},{6,22},{8,24},{10,26},{12,28},{14,30},{16,0},... | collective-permute-start | bytes 6152 | tf_op jit(solution)/shard_map/ppermute | solution.py:37
  112.5 4.9 %collective-permute-start.10 = (f32[2,16,16]{2,1,0:T(8,128)S(1)}, f32[2,16,16]{2,1,0:T(8,128)S(1)}, u32[]{:S(2)}, u32[]{:S(2)}) collective-permute-start(f32[2,16,16]{2,1,0:T(8,128)S(1)} %add_add_fusion.2), channel_id=1, source_target_pairs={{0,24},{2,26},{4,28},{6,30},{8,16},{10,18},{12,20},{14,22},{16,8},... | collective-permute-start | bytes 6152 | tf_op jit(solution)/shard_map/ppermute | solution.py:37
  113.2 4.2 %collective-permute-start.8 = (f32[2,16,16]{2,1,0:T(8,128)S(1)}, f32[2,16,16]{2,1,0:T(8,128)S(1)}, u32[]{:S(2)}, u32[]{:S(2)}) collective-permute-start(f32[2,16,16]{2,1,0:T(8,128)S(1)} %add_add_fusion.2), channel_id=1, source_target_pairs={{0,8},{2,10},{4,12},{6,14},{8,0},{10,2},{12,4},{14,6},{16,24},{18,... | collective-permute-start | bytes 6152 | tf_op jit(solution)/shard_map/ppermute | solution.py:37
  117.4 5.3 %collective-permute-start.12 = (f32[2,16,16]{2,1,0:T(8,128)S(1)}, f32[2,16,16]{2,1,0:T(8,128)S(1)}, u32[]{:S(2)}, u32[]{:S(2)}) collective-permute-start(f32[2,16,16]{2,1,0:T(8,128)S(1)} %add_add_fusion.1), channel_id=1, source_target_pairs={{0,64},{32,96},{64,0},{96,32},{1,65},{33,97},{65,1},{97,33},{2,66}... | collective-permute-start | bytes 6152 | tf_op jit(solution)/shard_map/ppermute | solution.py:37
  118.1 4.9 %collective-permute-start.13 = (f32[2,16,16]{2,1,0:T(8,128)S(1)}, f32[2,16,16]{2,1,0:T(8,128)S(1)}, u32[]{:S(2)}, u32[]{:S(2)}) collective-permute-start(f32[2,16,16]{2,1,0:T(8,128)S(1)} %add_add_fusion.1), channel_id=1, source_target_pairs={{0,96},{32,64},{64,32},{96,0},{1,97},{33,65},{65,33},{97,1},{2,98}... | collective-permute-start | bytes 6152 | tf_op jit(solution)/shard_map/ppermute | solution.py:37
  120.7 3.7 %collective-permute-start.11 = (f32[2,16,16]{2,1,0:T(8,128)S(1)}, f32[2,16,16]{2,1,0:T(8,128)S(1)}, u32[]{:S(2)}, u32[]{:S(2)}) collective-permute-start(f32[2,16,16]{2,1,0:T(8,128)S(1)} %add_add_fusion.1), channel_id=1, source_target_pairs={{0,32},{32,0},{64,96},{96,64},{1,33},{33,1},{65,97},{97,65},{2,34}... | collective-permute-start | bytes 6152 | tf_op jit(solution)/shard_map/ppermute | solution.py:37
  (10 other events, 8.7 us)

commit v16 on v13

--- a/solution.py
+++ b/solution.py
@@ -120,19 +120,20 @@
         current = states
         for section in range(FINE):
             current = step(current, section, FINE_DT, forcing)
-        return current, coarse[:, FINE - 1 : FINE - 1 + current.shape[1]]
-
-    inner_fine, inner_coarse = block_steps(own, wide_inside[depth : depth + row_count])
+        coarse = coarse[:, FINE - 1 : FINE - 1 + current.shape[1]] * later[:, None, None]
+        return current - coarse
+
+    later = (jnp.arange(count) >= group).astype(jnp.float32)
+    inner = block_steps(own, wide_inside[depth : depth + row_count])
     strip = depth + 2 * FINE
     strips = jnp.concatenate([wide[:, :strip], wide[:, -strip:]], axis=1)
     strips_inside = jnp.concatenate([wide_inside[:strip], wide_inside[-strip:]])
-    edge_fine, edge_coarse = block_steps(strips, strips_inside)
+    edges = block_steps(strips, strips_inside)
 
     def stitch(edges, inner):
         return jnp.concatenate([edges[:, :depth], inner, edges[:, strip : strip + depth]], axis=1)
 
-    current = stitch(edge_fine, inner_fine)
-    coarse_part = stitch(edge_coarse, inner_coarse)
+    current = stitch(edges, inner)
     wide_coeffs = wide[count : count + 3]
 
     def step(values, low, step_size, forcing):
@@ -142,11 +143,10 @@
         return advance(values, wide_coeffs[:, lo:hi], wide_inside[lo:hi], step_size, q)
 
     fine = current.reshape(slices, group, -1, col_count)
-    coarse_part = coarse_part.reshape(slices, group, -1, col_count)
     running = fine[0]
     results = [running[:, links : links + row_count]]
     for link in range(1, slices):
-        correction = fine[link] - coarse_part[link]
+        correction = fine[link]
         stepped = step(running, FINE + link - 1, coarse_dt, None)
         running = correction[:, link : correction.shape[1] - link] + stepped
         results.append(running[:, links - link : links - link + row_count])

time: 132 us -> 131 us (level)
  local copies, waits for them, and re-layouts: 25.5 us -> 22.9 us
  waiting for transfers between devices: 42.1 us -> 44.6 us
    mul x9 -> x6, other arithmetic: 12.4 us -> 8.9 us  [advance(): return (middle + step_size * tendency) * inside]
    sub x0 -> x2, other arithmetic: none -> 3.44 us  [block_steps(): return current - coarse]
    all_to_all x1, waiting for transfers between devices: 5.78 us -> 8.24 us  [per_device(): lax.all_to_all(state.reshape(slices, group, row_count, col_count), 'tm',...]
    slice x4 -> x3, local copies, waits for them, and re-layouts: 2.41 us -> 0.21 us  [step(): return advance(values, coeffs[:, lo:hi], inside[lo:hi], step_size, q)]
    unnamed x83 -> x71, local copies, waits for them, and re-layouts: 4.21 us -> 4.28 us
  transfers between devices with their start and end apart: 17 -> 17, of which waited for: 10 -> 10; matrix products, arithmetic and copies ran while one was open for 21% -> 19% of each run, Pallas kernels for 0% -> 0%
where the time goes in v16:
time: 131 us
  waiting for transfers between devices  44.6 us (34%)
  starting transfers between devices  35.5 us (27%)
  other arithmetic  23.3 us (18%)
  local copies, waits for them, and re-layouts  22.9 us (17%)
  matrix products  2.96 us (2%)
  between operations  1.43 us (1%)
    all_to_all x1, waiting for transfers between devices, per_device(): lax.all_to_all(done, 'tm', 0, 0, tiled=True)  24.7 us
    ppermute x9, starting transfers between devices, quad_sum(): lax.ppermute(value, axis, [(i, i ^ k * bit) for i in range(count)])  14.9 us
    ppermute x9, waiting for transfers between devices, quad_sum(): lax.ppermute(value, axis, [(i, i ^ k * bit) for i in range(count)])  10.5 us
    ppermute x2, starting transfers between devices, with_halo(): lax.ppermute(tail, axis, [(i, i + 1) for i in range(ends)])  9.58 us
    mul x6, other arithmetic, advance(): return (middle + step_size * tendency) * inside  8.9 us
    all_to_all x1, waiting for transfers between devices, per_device(): lax.all_to_all(state.reshape(slices, group, row_count, col_count), 'tm',...  8.24 us
    slice x11, local copies, waits for them, and re-layouts, advance(): west_cell = jnp.pad(middle[:, :, :-1], ((0, 0), (0, 0), (1, 0)))  6.2 us
    mul x10, local copies, waits for them, and re-layouts, advance(): coeffs[0] * (above_row + below_row + west_cell + east_cell - 4.0 * middle)  4.94 us
  transfers between devices with their start and end apart: 17, of which 10 were waited for; matrix products, arithmetic and copies ran while one was open for 19% of the time, Pallas kernels for 0%

profile of v16, /device:TPU:0, one launch (start us, length us, event | category | flops | bytes accessed | tf_op | source)
XLA Modules:
  0.0 130.7 jit_solution(14288409745180112414)
XLA Ops:
  0.6 1.6 %pad_maximum_fusion.9 = (f32[4,7,1024]{2,1,0:T(8,128)}, f32[4,7,1024]{2,1,0:T(8,128)}) fusion(f32[1,64,1024]{2,1,0:T(8,128)} %bitcast.187, f32[1,64,1024]{2,1,0:T(8,128)} %bitcast.173, f32[1,64,1024]{2,1,0:T(8,128)} %bitcast.180, f32[1,64,1024]{2,1,0:T(8,128)} %bitcast.166), kind=kLoop, calls=%fused_computation.115 | loop fusion | flops 172032 | bytes 1277952 | tf_op jit(solution)/shard_map/slice | solution.py:18
  2.2 1.3 collective-permute-start.3
  3.6 4.5 %all-to-all-start = ((f32[4,2,64,1024]{3,2,1,0:T(8,128)}), f32[4,2,64,1024]{3,2,1,0:T(8,128)S(1)}, u32[]{:S(2)}, u32[]{:S(2)}) async-start(f32[4,2,64,1024]{3,2,1,0:T(8,128)} %bitcast.190), calls=%async_computation | async-start | bytes 4194304 | tf_op jit(solution)/shard_map/all_to_all | solution.py:95
  8.1 4.7 %collective-permute-start.2 = (f32[4,7,1024]{2,1,0:T(8,128)}, f32[4,7,1024]{2,1,0:T(8,128)S(1)}, u32[]{:S(2)}, u32[]{:S(2)}) collective-permute-start(f32[4,7,1024]{2,1,0:T(8,128)} %get-tuple-element.48), channel_id=1, source_target_pairs={{0,2},{2,4},{4,6},{6,8},{8,10},{10,12},{12,14},{14,16},{16,18},{18... | collective-permute-start | bytes 344072 | tf_op jit(solution)/shard_map/ppermute | solution.py:21
  14.1 0.9 slice_bitcast_fusion.15
  15.7 0.7 slice_bitcast_fusion.14
  17.1 0.8 slice_bitcast_fusion.18
  18.9 0.9 broadcast_multiply_fusion
  19.8 0.7 slice_bitcast_fusion.38
  20.5 0.8 slice_bitcast_fusion.12
  21.4 0.8 slice_bitcast_fusion.9
  22.8 0.7 slice.711
  24.2 1.0 slice_bitcast_fusion.8
  25.2 0.9 slice_bitcast_fusion.5
  26.2 8.2 %all-to-all-done = f32[4,2,64,1024]{3,2,1,0:T(8,128)S(1)} async-done(((f32[4,2,64,1024]{3,2,1,0:T(8,128)}), f32[4,2,64,1024]{3,2,1,0:T(8,128)S(1)}, u32[]{:S(2)}, u32[]{:S(2)}) %all-to-all-start) | async-done | bytes 2097184 | tf_op jit(solution)/shard_map/all_to_all | solution.py:95
  34.5 0.9 fusion.82
  35.4 1.4 %collective-permute-start.1 = (f32[8,7,1024]{2,1,0:T(8,128)S(1)}, f32[8,7,1024]{2,1,0:T(8,128)S(1)}, u32[]{:S(2)}, u32[]{:S(2)}) collective-permute-start(f32[8,7,1024]{2,1,0:T(8,128)S(1)} %get-tuple-element.22), channel_id=1, source_target_pairs={{2,0},{4,2},{6,4},{8,6},{10,8},{12,10},{14,12},{16,14},{18,16},{20... | collective-permute-start | bytes 688136 | tf_op jit(solution)/shard_map/ppermute | solution.py:23
  36.9 4.9 %collective-permute-start = (f32[8,7,1024]{2,1,0:T(8,128)S(1)}, f32[8,7,1024]{2,1,0:T(8,128)S(1)}, u32[]{:S(2)}, u32[]{:S(2)}) collective-permute-start(f32[8,7,1024]{2,1,0:T(8,128)S(1)} %get-tuple-element.21), channel_id=1, source_target_pairs={{0,2},{2,4},{4,6},{6,8},{8,10},{10,12},{12,14},{14,16},{16,18},{18... | collective-permute-start | bytes 688136 | tf_op jit(solution)/shard_map/ppermute | solution.py:21
  42.1 2.1 %fusion.8 = (f32[8,62,1024]{2,1,0:T(8,128)S(1)}, f32[8,62,1024]{2,1,0:T(8,128)S(1)}, f32[8,62,1024]{2,1,0:T(8,128)S(1)}) fusion(f32[8,64,1024]{2,1,0:T(8,128)S(1)} %bitcast.156, f32[62]{0:T(128)S(1)} %slice.606, f32[8,64,1024]{2,1,0:T(8,128)S(1)} %bitcast.154, f32[62,1024]{1,0:T(8,128)S(1)} %copy-done.13, f32[62,1024]{1,0:T(8,128)S(1)} %copy-done.14, ...), kind=kLoop, calls=%fused_computation.12 | loop fusion | flops 9142272 | bytes 19042680 | tf_op jit(solution)/shard_map/mul | solution.py:68
  44.2 1.1 fusion.81
  45.3 2.1 %fusion.5 = f32[8,60,1024]{2,1,0:T(8,128)S(1)} fusion(f32[8,64,1024]{2,1,0:T(8,128)S(1)} %bitcast.157, f32[8,62,1024]{2,1,0:T(8,128)S(1)} %get-tuple-element.4, f32[8,60,1023]{2,1,0:T(8,128)S(1)} %get-tuple-element.17, f32[8,60,1023]{2,1,0:T(8,128)S(1)} %get-tuple-element.16, f32[60]{0:T(128)S(1)} %slice.616, f32[60,1024]{1,0:T(8,128)S(1)} %copy-done.17, ...), kind=kLoop, calls=%fused_computation.8 | loop fusion | flops 8847360 | bytes 14496240 | tf_op jit(solution)/shard_map/mul | solution.py:68
  47.5 1.0 fusion.80
  48.5 2.1 %fusion.2 = f32[8,58,1024]{2,1,0:T(8,128)S(1)} fusion(f32[8,64,1024]{2,1,0:T(8,128)S(1)} %bitcast.158, f32[8,60,1024]{2,1,0:T(8,128)S(1)} %fusion.5, f32[8,58,1023]{2,1,0:T(8,128)S(1)} %get-tuple-element.15, f32[8,58,1023]{2,1,0:T(8,128)S(1)} %get-tuple-element.14, f32[58]{0:T(128)S(1)} %slice.626, f32[58,1024]{1,0:T(8,128)S(1)} %copy-done.15, ...), kind=kLoop, calls=%fused_computation.4 | loop fusion | flops 8552448 | bytes 14013032 | tf_op jit(solution)/shard_map/mul | solution.py:68
  50.7 0.9 fusion.79
  51.8 2.4 %fusion.12 = f32[8,56,1024]{2,1,0:T(8,128)S(1)} fusion(f32[8,62,1024]{2,1,0:T(8,128)S(1)} %get-tuple-element.5, f32[8,62,1024]{2,1,0:T(8,128)S(1)} %get-tuple-element.18, f32[8,64,1024]{2,1,0:T(8,128)S(1)} %bitcast.159, f32[8,58,1024]{2,1,0:T(8,128)S(1)} %fusion.2, f32[8,56,1023]{2,1,0:T(8,128)S(1)} %get-tuple-element.13, ...), kind=kLoop, calls=%fused_computation.21 | loop fusion | flops 10092544 | bytes 17199872 | tf_op jit(solution)/shard_map/sub | solution.py:124
  56.1 1.0 fusion.39
  57.7 0.9 fusion.36
  60.0 1.0 fusion.42
  65.5 1.5 %pad_maximum_fusion.1 = f32[4,2,64,1024]{3,2,1,0:T(8,128)} fusion(f32[1,2,64,1024]{3,2,1,0:T(8,128)S(1)} %get-tuple-element.9, f32[1,2,64,1024]{3,2,1,0:T(8,128)S(1)} %get-tuple-element.54, f32[1,2,64,1024]{3,2,1,0:T(8,128)S(1)} %slice_bitcast_fusion, f32[1,2,64,1024]{3,2,1,0:T(8,128)S(1)} %get-tuple-element.8), kind=kLoop, calls=%fused_computation.13 | loop fusion | flops 1572864 | bytes 4194304 | tf_op jit(solution)/shard_map/stack | solution.py:153
  66.9 3.7 %all-to-all-start.1 = ((f32[4,2,64,1024]{3,2,1,0:T(8,128)}), f32[4,2,64,1024]{3,2,1,0:T(8,128)S(1)}, u32[]{:S(2)}, u32[]{:S(2)}) async-start(f32[4,2,64,1024]{3,2,1,0:T(8,128)} %pad_maximum_fusion.1), calls=%async_computation.1 | async-start | bytes 4194304 | tf_op jit(solution)/shard_map/all_to_all | solution.py:154
  70.8 24.7 %all-to-all-done.1 = f32[4,2,64,1024]{3,2,1,0:T(8,128)S(1)} async-done(((f32[4,2,64,1024]{3,2,1,0:T(8,128)}), f32[4,2,64,1024]{3,2,1,0:T(8,128)S(1)}, u32[]{:S(2)}, u32[]{:S(2)}) %all-to-all-start.1) | async-done | bytes 2097184 | tf_op jit(solution)/shard_map/all_to_all | solution.py:154
  95.5 1.5 %fusion.9 = f32[8,64]{1,0:T(8,128)S(1)} fusion(f32[8,64,1024]{2,1,0:T(8,128)S(1)} %bitcast.164, s32[64]{0:T(128)S(1)} %and_select_fusion.1, s32[64]{0:T(128)S(1)} %get-tuple-element.2), kind=kOutput, calls=%fused_computation.15 | convolution fusion | flops 404229632 | bytes 2099712 | tf_op jit(solution)/shard_map/or,mrc->moc/dot_general | solution.py:163
  97.1 1.1 collective-permute-done.4
  99.2 2.7 %collective-permute-start.7 = (f32[2,16,16]{2,1,0:T(8,128)S(1)}, f32[2,16,16]{2,1,0:T(8,128)S(1)}, u32[]{:S(2)}, u32[]{:S(2)}) collective-permute-start(f32[2,16,16]{2,1,0:T(8,128)S(1)} %pad_maximum_fusion.10), channel_id=1, source_target_pairs={{0,96},{32,64},{64,32},{96,0},{1,97},{33,65},{65,33},{97,1},{2,98}... | collective-permute-start | bytes 6152 | tf_op jit(solution)/shard_map/ppermute | solution.py:37
  102.1 1.8 %collective-permute-done.6 = f32[2,16,16]{2,1,0:T(8,128)S(1)} collective-permute-done((f32[2,16,16]{2,1,0:T(8,128)S(1)}, f32[2,16,16]{2,1,0:T(8,128)S(1)}, u32[]{:S(2)}, u32[]{:S(2)}) %collective-permute-start.6) | collective-permute-done | bytes 2080 | tf_op jit(solution)/shard_map/ppermute | solution.py:37
  104.1 1.5 %collective-permute-done.5 = f32[2,16,16]{2,1,0:T(8,128)S(1)} collective-permute-done((f32[2,16,16]{2,1,0:T(8,128)S(1)}, f32[2,16,16]{2,1,0:T(8,128)S(1)}, u32[]{:S(2)}, u32[]{:S(2)}) %collective-permute-start.5) | collective-permute-done | bytes 2080 | tf_op jit(solution)/shard_map/ppermute | solution.py:37
  105.6 3.4 %collective-permute-start.9 = (f32[2,16,16]{2,1,0:T(8,128)S(1)}, f32[2,16,16]{2,1,0:T(8,128)S(1)}, u32[]{:S(2)}, u32[]{:S(2)}) collective-permute-start(f32[2,16,16]{2,1,0:T(8,128)S(1)} %add_add_fusion.2), channel_id=1, source_target_pairs={{0,4},{2,6},{4,0},{6,2},{8,12},{10,14},{12,8},{14,10},{16,20},{18,... | collective-permute-start | bytes 6152 | tf_op jit(solution)/shard_map/ppermute | solution.py:37
  109.0 2.3 %collective-permute-start.10 = (f32[2,16,16]{2,1,0:T(8,128)S(1)}, f32[2,16,16]{2,1,0:T(8,128)S(1)}, u32[]{:S(2)}, u32[]{:S(2)}) collective-permute-start(f32[2,16,16]{2,1,0:T(8,128)S(1)} %add_add_fusion.2), channel_id=1, source_target_pairs={{0,6},{2,4},{4,2},{6,0},{8,14},{10,12},{12,10},{14,8},{16,22},{18,... | collective-permute-start | bytes 6152 | tf_op jit(solution)/shard_map/ppermute | solution.py:37
  111.3 0.8 collective-permute-start.8
  112.1 1.8 %collective-permute-done.10 = f32[2,16,16]{2,1,0:T(8,128)S(1)} collective-permute-done((f32[2,16,16]{2,1,0:T(8,128)S(1)}, f32[2,16,16]{2,1,0:T(8,128)S(1)}, u32[]{:S(2)}, u32[]{:S(2)}) %collective-permute-start.10) | collective-permute-done | bytes 2080 | tf_op jit(solution)/shard_map/ppermute | solution.py:37
  114.0 1.1 collective-permute-done.8
  115.1 4.0 %collective-permute-start.12 = (f32[2,16,16]{2,1,0:T(8,128)S(1)}, f32[2,16,16]{2,1,0:T(8,128)S(1)}, u32[]{:S(2)}, u32[]{:S(2)}) collective-permute-start(f32[2,16,16]{2,1,0:T(8,128)S(1)} %add_add_fusion.1), channel_id=1, source_target_pairs={{0,16},{2,18},{4,20},{6,22},{8,24},{10,26},{12,28},{14,30},{16,0},... | collective-permute-start | bytes 6152 | tf_op jit(solution)/shard_map/ppermute | solution.py:37
  119.9 0.8 collective-permute-done.12
  120.8 3.2 %collective-permute-done.13 = f32[2,16,16]{2,1,0:T(8,128)S(1)} collective-permute-done((f32[2,16,16]{2,1,0:T(8,128)S(1)}, f32[2,16,16]{2,1,0:T(8,128)S(1)}, u32[]{:S(2)}, u32[]{:S(2)}) %collective-permute-start.13) | collective-permute-done | bytes 2080 | tf_op jit(solution)/shard_map/ppermute | solution.py:37
  124.1 1.5 %cholesky.17 = f32[16,16]{1,0:T(8,128)S(1)} custom-call(f32[16,16]{1,0:T(8,128)S(1)} %fusion.59), custom_call_target="Cholesky" | custom-call | tf_op jit(solution)/shard_map/jit(cholesky)/cholesky | solution.py:181
  126.9 1.2 custom-call.10
  128.5 0.9 fusion.33
  129.4 1.3 %copy.15 = f32[1,8,64,1024]{3,2,1,0:T(8,128)} copy(f32[1,8,64,1024]{3,2,1,0:T(8,128)S(1)} %bitcast.165) | data formatting | bytes 4194304
  (150 shorter events, 18.0 us)
Async XLA Ops:
  2.2 21.3 %collective-permute-start.3 = (f32[4,7,1024]{2,1,0:T(8,128)}, f32[4,7,1024]{2,1,0:T(8,128)S(1)}, u32[]{:S(2)}, u32[]{:S(2)}) collective-permute-start(f32[4,7,1024]{2,1,0:T(8,128)} %get-tuple-element.49), channel_id=1, source_target_pairs={{2,0},{4,2},{6,4},{8,6},{10,8},{12,10},{14,12},{16,14},{18,16},{20... | collective-permute-start | bytes 344072 | tf_op jit(solution)/shard_map/ppermute | solution.py:23
  3.5 10.6 %copy-start.1 = (f32[64,1024]{1,0:T(8,128)S(1)}, f32[64,1024]{1,0:T(8,128)}, u32[]{:S(2)}) copy-start(f32[64,1024]{1,0:T(8,128)} %param.12) | copy-start | bytes 786436
  3.5 10.6 %copy-start.2 = (f32[64,1024]{1,0:T(8,128)S(1)}, f32[64,1024]{1,0:T(8,128)}, u32[]{:S(2)}) copy-start(f32[64,1024]{1,0:T(8,128)} %param.11) | copy-start | bytes 786436
  3.5 11.4 %copy-start = (f32[64,1024]{1,0:T(8,128)S(1)}, f32[64,1024]{1,0:T(8,128)}, u32[]{:S(2)}) copy-start(f32[64,1024]{1,0:T(8,128)} %param.13) | copy-start | bytes 786436
  3.6 30.9 %all-to-all-start = ((f32[4,2,64,1024]{3,2,1,0:T(8,128)}), f32[4,2,64,1024]{3,2,1,0:T(8,128)S(1)}, u32[]{:S(2)}, u32[]{:S(2)}) async-start(f32[4,2,64,1024]{3,2,1,0:T(8,128)} %bitcast.190), calls=%async_computation | async-start | bytes 4194304 | tf_op jit(solution)/shard_map/all_to_all | solution.py:95
  8.1 10.6 %copy-start.26 = (f32[8,128]{1,0:T(8,128)S(1)}, f32[8,128]{1,0:T(8,128)}, u32[]{:S(2)}) copy-start(f32[8,128]{1,0:T(8,128)} %param.15) | copy-start | bytes 12292
  8.1 15.5 %collective-permute-start.2 = (f32[4,7,1024]{2,1,0:T(8,128)}, f32[4,7,1024]{2,1,0:T(8,128)S(1)}, u32[]{:S(2)}, u32[]{:S(2)}) collective-permute-start(f32[4,7,1024]{2,1,0:T(8,128)} %get-tuple-element.48), channel_id=1, source_target_pairs={{0,2},{2,4},{4,6},{6,8},{8,10},{10,12},{12,14},{14,16},{16,18},{18... | collective-permute-start | bytes 344072 | tf_op jit(solution)/shard_map/ppermute | solution.py:21
  12.9 5.8 %copy-start.33 = (f32[30,1]{0,1:T(1,128)}, f32[30,1]{0,1:T(1,128)S(1)}, u32[]{:S(2)}) copy-start(f32[30,1]{0,1:T(1,128)S(1)} %pad_maximum_fusion.11) | copy-start | bytes 364
  14.1 4.8 %copy-start.3 = (f32[64,1024]{1,0:T(8,128)S(1)}, f32[64,1024]{1,0:T(8,128)}, u32[]{:S(2)}) copy-start(f32[64,1024]{1,0:T(8,128)} %param.14) | copy-start | bytes 786436
  18.9 3.3 %copy-start.34 = (f32[30,1]{0,1:T(1,128)S(1)}, f32[30,1]{0,1:T(1,128)}, u32[]{:S(2)}) copy-start(f32[30,1]{0,1:T(1,128)} %copy-done.33) | copy-start | bytes 364
  34.5 7.3 %copy-start.4 = (f32[2,64,1024]{2,1,0:T(8,128)S(1)}, f32[2,64,1024]{2,1,0:T(8,128)}, u32[]{:S(2)}) copy-start(f32[2,64,1024]{2,1,0:T(8,128)} %broadcast_multiply_fusion) | copy-start | bytes 1572868
  35.4 6.6 %copy-start.12 = (f32[62,1024]{1,0:T(8,128)S(1)}, f32[62,1024]{1,0:T(8,128)}, u32[]{:S(2)}) copy-start(f32[62,1024]{1,0:T(8,128)} %slice_bitcast_fusion.17) | copy-start | bytes 761860
  35.4 6.6 %copy-start.13 = (f32[62,1024]{1,0:T(8,128)S(1)}, f32[62,1024]{1,0:T(8,128)}, u32[]{:S(2)}) copy-start(f32[62,1024]{1,0:T(8,128)} %get-tuple-element.63) | copy-start | bytes 761860
  35.4 6.6 %copy-start.14 = (f32[62,1024]{1,0:T(8,128)S(1)}, f32[62,1024]{1,0:T(8,128)}, u32[]{:S(2)}) copy-start(f32[62,1024]{1,0:T(8,128)} %get-tuple-element.64) | copy-start | bytes 761860
  35.4 18.8 %collective-permute-start.1 = (f32[8,7,1024]{2,1,0:T(8,128)S(1)}, f32[8,7,1024]{2,1,0:T(8,128)S(1)}, u32[]{:S(2)}, u32[]{:S(2)}) collective-permute-start(f32[8,7,1024]{2,1,0:T(8,128)S(1)} %get-tuple-element.22), channel_id=1, source_target_pairs={{2,0},{4,2},{6,4},{8,6},{10,8},{12,10},{14,12},{16,14},{18,16},{20... | collective-permute-start | bytes 688136 | tf_op jit(solution)/shard_map/ppermute | solution.py:23
  36.9 17.4 %collective-permute-start = (f32[8,7,1024]{2,1,0:T(8,128)S(1)}, f32[8,7,1024]{2,1,0:T(8,128)S(1)}, u32[]{:S(2)}, u32[]{:S(2)}) collective-permute-start(f32[8,7,1024]{2,1,0:T(8,128)S(1)} %get-tuple-element.21), channel_id=1, source_target_pairs={{0,2},{2,4},{4,6},{6,8},{8,10},{10,12},{12,14},{14,16},{16,18},{18... | collective-permute-start | bytes 688136 | tf_op jit(solution)/shard_map/ppermute | solution.py:21
  44.2 1.1 copy-start.11
  44.2 1.1 copy-start.17
  44.2 1.1 copy-start.18
  47.4 1.0 copy-start.10
  47.4 1.0 copy-start.15
  47.4 1.1 copy-start.16
  50.6 0.9 copy-start.19
  50.6 1.0 copy-start.20
  50.7 1.1 copy-start.21
  51.8 2.5 %copy-start.23 = (f32[4,7,1024]{2,1,0:T(8,128)S(1)}, f32[4,7,1024]{2,1,0:T(8,128)}, u32[]{:S(2)}) copy-start(f32[4,7,1024]{2,1,0:T(8,128)} %copy-done.22) | copy-start | bytes 344068
  51.8 2.5 %copy-start.25 = (f32[4,7,1024]{2,1,0:T(8,128)S(1)}, f32[4,7,1024]{2,1,0:T(8,128)}, u32[]{:S(2)}) copy-start(f32[4,7,1024]{2,1,0:T(8,128)} %copy-done.24) | copy-start | bytes 344068
  61.4 1.0 copy-start.7
  61.4 1.0 copy-start.8
  61.4 1.1 copy-start.9
  63.1 1.0 copy-start.5
  63.1 1.0 copy-start.6
  66.9 3.8 %copy-start.29 = (s32[1,64]{1,0:T(1,128)S(1)}, s32[1,64]{1,0:T(1,128)}, u32[]{:S(2)}) copy-start(s32[1,64]{1,0:T(1,128)} %param.16) | copy-start | bytes 772
  66.9 28.6 %all-to-all-start.1 = ((f32[4,2,64,1024]{3,2,1,0:T(8,128)}), f32[4,2,64,1024]{3,2,1,0:T(8,128)S(1)}, u32[]{:S(2)}, u32[]{:S(2)}) async-start(f32[4,2,64,1024]{3,2,1,0:T(8,128)} %pad_maximum_fusion.1), calls=%async_computation.1 | async-start | bytes 4194304 | tf_op jit(solution)/shard_map/all_to_all | solution.py:154
  70.7 26.4 %copy-start.31 = (f32[1,64]{1,0:T(1,128)S(1)}, f32[1,64]{1,0:T(1,128)}, u32[]{:S(2)}) copy-start(f32[1,64]{1,0:T(1,128)} %param.19) | copy-start | bytes 772
  70.7 27.7 %copy-start.30 = (f32[1,64,16]{1,2,0:T(8,128)S(1)}, f32[1,64,16]{1,2,0:T(8,128)}, u32[]{:S(2)}) copy-start(f32[1,64,16]{1,2,0:T(8,128)} %param.18) | copy-start | bytes 12292
  70.7 27.7 %copy-start.32 = (f32[1,64]{1,0:T(1,128)S(1)}, f32[1,64]{1,0:T(1,128)}, u32[]{:S(2)}) copy-start(f32[1,64]{1,0:T(1,128)} %param.17) | copy-start | bytes 772
  97.0 1.2 collective-permute-start.4
  98.5 5.3 %collective-permute-start.6 = (f32[2,16,16]{2,1,0:T(8,128)S(1)}, f32[2,16,16]{2,1,0:T(8,128)S(1)}, u32[]{:S(2)}, u32[]{:S(2)}) collective-permute-start(f32[2,16,16]{2,1,0:T(8,128)S(1)} %pad_maximum_fusion.10), channel_id=1, source_target_pairs={{0,64},{32,96},{64,0},{96,32},{1,65},{33,97},{65,1},{97,33},{2,66}... | collective-permute-start | bytes 6152 | tf_op jit(solution)/shard_map/ppermute | solution.py:37
  99.2 4.9 %collective-permute-start.7 = (f32[2,16,16]{2,1,0:T(8,128)S(1)}, f32[2,16,16]{2,1,0:T(8,128)S(1)}, u32[]{:S(2)}, u32[]{:S(2)}) collective-permute-start(f32[2,16,16]{2,1,0:T(8,128)S(1)} %pad_maximum_fusion.10), channel_id=1, source_target_pairs={{0,96},{32,64},{64,32},{96,0},{1,97},{33,65},{65,33},{97,1},{2,98}... | collective-permute-start | bytes 6152 | tf_op jit(solution)/shard_map/ppermute | solution.py:37
  101.9 3.7 %collective-permute-start.5 = (f32[2,16,16]{2,1,0:T(8,128)S(1)}, f32[2,16,16]{2,1,0:T(8,128)S(1)}, u32[]{:S(2)}, u32[]{:S(2)}) collective-permute-start(f32[2,16,16]{2,1,0:T(8,128)S(1)} %pad_maximum_fusion.10), channel_id=1, source_target_pairs={{0,32},{32,0},{64,96},{96,64},{1,33},{33,1},{65,97},{97,65},{2,34}... | collective-permute-start | bytes 6152 | tf_op jit(solution)/shard_map/ppermute | solution.py:37
  102.1 10.0 %collective-permute-start.14 = (f32[8,128]{1,0:T(8,128)S(1)}, f32[8,128]{1,0:T(8,128)S(1)}, u32[]{:S(2)}, u32[]{:S(2)}) collective-permute-start(f32[8,128]{1,0:T(8,128)S(1)} %copy-done.26), channel_id=1, source_target_pairs={{0,1},{1,0},{2,3},{3,2},{4,5},{5,4},{6,7},{7,6},{8,9},{9,8},{10,11... | collective-permute-start | bytes 12296 | tf_op jit(solution)/shard_map/ppermute | solution.py:49
  105.6 6.5 %collective-permute-start.9 = (f32[2,16,16]{2,1,0:T(8,128)S(1)}, f32[2,16,16]{2,1,0:T(8,128)S(1)}, u32[]{:S(2)}, u32[]{:S(2)}) collective-permute-start(f32[2,16,16]{2,1,0:T(8,128)S(1)} %add_add_fusion.2), channel_id=1, source_target_pairs={{0,4},{2,6},{4,0},{6,2},{8,12},{10,14},{12,8},{14,10},{16,20},{18,... | collective-permute-start | bytes 6152 | tf_op jit(solution)/shard_map/ppermute | solution.py:37
  109.0 4.9 %collective-permute-start.10 = (f32[2,16,16]{2,1,0:T(8,128)S(1)}, f32[2,16,16]{2,1,0:T(8,128)S(1)}, u32[]{:S(2)}, u32[]{:S(2)}) collective-permute-start(f32[2,16,16]{2,1,0:T(8,128)S(1)} %add_add_fusion.2), channel_id=1, source_target_pairs={{0,6},{2,4},{4,2},{6,0},{8,14},{10,12},{12,10},{14,8},{16,22},{18,... | collective-permute-start | bytes 6152 | tf_op jit(solution)/shard_map/ppermute | solution.py:37
  111.3 3.7 %collective-permute-start.8 = (f32[2,16,16]{2,1,0:T(8,128)S(1)}, f32[2,16,16]{2,1,0:T(8,128)S(1)}, u32[]{:S(2)}, u32[]{:S(2)}) collective-permute-start(f32[2,16,16]{2,1,0:T(8,128)S(1)} %add_add_fusion.2), channel_id=1, source_target_pairs={{0,2},{2,0},{4,6},{6,4},{8,10},{10,8},{12,14},{14,12},{16,18},{18,... | collective-permute-start | bytes 6152 | tf_op jit(solution)/shard_map/ppermute | solution.py:37
  115.1 5.7 %collective-permute-start.12 = (f32[2,16,16]{2,1,0:T(8,128)S(1)}, f32[2,16,16]{2,1,0:T(8,128)S(1)}, u32[]{:S(2)}, u32[]{:S(2)}) collective-permute-start(f32[2,16,16]{2,1,0:T(8,128)S(1)} %add_add_fusion.1), channel_id=1, source_target_pairs={{0,16},{2,18},{4,20},{6,22},{8,24},{10,26},{12,28},{14,30},{16,0},... | collective-permute-start | bytes 6152 | tf_op jit(solution)/shard_map/ppermute | solution.py:37
  119.0 4.9 %collective-permute-start.13 = (f32[2,16,16]{2,1,0:T(8,128)S(1)}, f32[2,16,16]{2,1,0:T(8,128)S(1)}, u32[]{:S(2)}, u32[]{:S(2)}) collective-permute-start(f32[2,16,16]{2,1,0:T(8,128)S(1)} %add_add_fusion.1), channel_id=1, source_target_pairs={{0,24},{2,26},{4,28},{6,30},{8,16},{10,18},{12,20},{14,22},{16,8},... | collective-permute-start | bytes 6152 | tf_op jit(solution)/shard_map/ppermute | solution.py:37
  119.8 4.2 %collective-permute-start.11 = (f32[2,16,16]{2,1,0:T(8,128)S(1)}, f32[2,16,16]{2,1,0:T(8,128)S(1)}, u32[]{:S(2)}, u32[]{:S(2)}) collective-permute-start(f32[2,16,16]{2,1,0:T(8,128)S(1)} %add_add_fusion.1), channel_id=1, source_target_pairs={{0,8},{2,10},{4,12},{6,14},{8,0},{10,2},{12,4},{14,6},{16,24},{18,... | collective-permute-start | bytes 6152 | tf_op jit(solution)/shard_map/ppermute | solution.py:37
  (4 other events, 2.6 us)

commit v17 on v16

--- a/solution.py
+++ b/solution.py
@@ -159,10 +159,10 @@
     local_cell = obs_cell[0] - first_row * col_count
     rows = local_cell // col_count
     cols = local_cell % col_count
-    row_pick = (rows[:, None] == jnp.arange(row_count, dtype=jnp.int32)[None, :]).astype(jnp.float32)
-    picked_rows = jnp.einsum("or,mrc->moc", row_pick, running, precision=lax.Precision.HIGHEST)
-    at_col = lax.broadcasted_iota(jnp.int32, picked_rows.shape, 2) == cols[None, :, None]
-    predicted = jnp.sum(jnp.where(at_col, picked_rows, 0.0), axis=2)
+    col_pick = (cols[:, None] == jnp.arange(col_count, dtype=jnp.int32)[None, :]).astype(jnp.float32)
+    picked_cols = jnp.einsum("mrc,oc->mro", running, col_pick, precision=lax.Precision.HIGHEST)
+    at_row = lax.broadcasted_iota(jnp.int32, picked_cols.shape, 1) == rows[None, None, :]
+    predicted = jnp.sum(jnp.where(at_row, picked_cols, 0.0), axis=1)
     every_pred = both_halves(predicted, "ens")
     every_param = both_halves(params, "ens")
     total = every_pred.shape[0]

time: 131 us -> 131 us (level)
  no operation moved by 1% of the time
where the time goes in v17:
time: 131 us; the launch traced here: 130 us
  waiting for transfers between devices  44.6 us (34%)
  starting transfers between devices  35.5 us (27%)
  other arithmetic  23.3 us (18%)
  local copies, waits for them, and re-layouts  22.9 us (17%)
  matrix products  2.66 us (2%)
  between operations  1.42 us (1%)
    all_to_all x1, waiting for transfers between devices, per_device(): lax.all_to_all(done, 'tm', 0, 0, tiled=True)  24.7 us
    ppermute x9, starting transfers between devices, quad_sum(): lax.ppermute(value, axis, [(i, i ^ k * bit) for i in range(count)])  14.9 us
    ppermute x9, waiting for transfers between devices, quad_sum(): lax.ppermute(value, axis, [(i, i ^ k * bit) for i in range(count)])  10.5 us
    ppermute x2, starting transfers between devices, with_halo(): lax.ppermute(tail, axis, [(i, i + 1) for i in range(ends)])  9.58 us
    mul x6, other arithmetic, advance(): return (middle + step_size * tendency) * inside  8.9 us
    all_to_all x1, waiting for transfers between devices, per_device(): lax.all_to_all(state.reshape(slices, group, row_count, col_count), 'tm',...  8.24 us
    slice x11, local copies, waits for them, and re-layouts, advance(): west_cell = jnp.pad(middle[:, :, :-1], ((0, 0), (0, 0), (1, 0)))  6.2 us
    mul x10, local copies, waits for them, and re-layouts, advance(): coeffs[0] * (above_row + below_row + west_cell + east_cell - 4.0 * middle)  4.94 us
  transfers between devices with their start and end apart: 17, of which 10 were waited for; matrix products, arithmetic and copies ran while one was open for 19% of the time, Pallas kernels for 0%

profile of v17, /device:TPU:0, one launch (start us, length us, event | category | flops | bytes accessed | tf_op | source)
XLA Modules:
  0.0 130.4 jit_solution(710790336906588935)
XLA Ops:
  0.6 1.6 %pad_maximum_fusion.9 = (f32[4,7,1024]{2,1,0:T(8,128)}, f32[4,7,1024]{2,1,0:T(8,128)}) fusion(f32[1,64,1024]{2,1,0:T(8,128)} %bitcast.183, f32[1,64,1024]{2,1,0:T(8,128)} %bitcast.169, f32[1,64,1024]{2,1,0:T(8,128)} %bitcast.176, f32[1,64,1024]{2,1,0:T(8,128)} %bitcast.162), kind=kLoop, calls=%fused_computation.117 | loop fusion | flops 172032 | bytes 1277952 | tf_op jit(solution)/shard_map/slice | solution.py:18
  2.2 1.3 collective-permute-start.3
  3.6 4.5 %all-to-all-start = ((f32[4,2,64,1024]{3,2,1,0:T(8,128)}), f32[4,2,64,1024]{3,2,1,0:T(8,128)S(1)}, u32[]{:S(2)}, u32[]{:S(2)}) async-start(f32[4,2,64,1024]{3,2,1,0:T(8,128)} %bitcast.186), calls=%async_computation | async-start | bytes 4194304 | tf_op jit(solution)/shard_map/all_to_all | solution.py:95
  8.1 4.7 %collective-permute-start.2 = (f32[4,7,1024]{2,1,0:T(8,128)}, f32[4,7,1024]{2,1,0:T(8,128)S(1)}, u32[]{:S(2)}, u32[]{:S(2)}) collective-permute-start(f32[4,7,1024]{2,1,0:T(8,128)} %get-tuple-element.48), channel_id=1, source_target_pairs={{0,2},{2,4},{4,6},{6,8},{8,10},{10,12},{12,14},{14,16},{16,18},{18... | collective-permute-start | bytes 344072 | tf_op jit(solution)/shard_map/ppermute | solution.py:21
  14.1 0.9 slice_bitcast_fusion.15
  15.7 0.7 slice_bitcast_fusion.14
  17.1 0.8 slice_bitcast_fusion.18
  18.9 0.9 broadcast_multiply_fusion
  19.8 0.7 slice_bitcast_fusion.38
  20.5 0.8 slice_bitcast_fusion.12
  21.4 0.8 slice_bitcast_fusion.9
  22.8 0.7 slice.711
  24.2 1.0 slice_bitcast_fusion.8
  25.2 0.9 slice_bitcast_fusion.5
  26.2 8.2 %all-to-all-done = f32[4,2,64,1024]{3,2,1,0:T(8,128)S(1)} async-done(((f32[4,2,64,1024]{3,2,1,0:T(8,128)}), f32[4,2,64,1024]{3,2,1,0:T(8,128)S(1)}, u32[]{:S(2)}, u32[]{:S(2)}) %all-to-all-start) | async-done | bytes 2097184 | tf_op jit(solution)/shard_map/all_to_all | solution.py:95
  34.5 0.9 fusion.82
  35.4 1.4 %collective-permute-start.1 = (f32[8,7,1024]{2,1,0:T(8,128)S(1)}, f32[8,7,1024]{2,1,0:T(8,128)S(1)}, u32[]{:S(2)}, u32[]{:S(2)}) collective-permute-start(f32[8,7,1024]{2,1,0:T(8,128)S(1)} %get-tuple-element.22), channel_id=1, source_target_pairs={{2,0},{4,2},{6,4},{8,6},{10,8},{12,10},{14,12},{16,14},{18,16},{20... | collective-permute-start | bytes 688136 | tf_op jit(solution)/shard_map/ppermute | solution.py:23
  36.9 4.9 %collective-permute-start = (f32[8,7,1024]{2,1,0:T(8,128)S(1)}, f32[8,7,1024]{2,1,0:T(8,128)S(1)}, u32[]{:S(2)}, u32[]{:S(2)}) collective-permute-start(f32[8,7,1024]{2,1,0:T(8,128)S(1)} %get-tuple-element.21), channel_id=1, source_target_pairs={{0,2},{2,4},{4,6},{6,8},{8,10},{10,12},{12,14},{14,16},{16,18},{18... | collective-permute-start | bytes 688136 | tf_op jit(solution)/shard_map/ppermute | solution.py:21
  42.1 2.1 %fusion.8 = (f32[8,62,1024]{2,1,0:T(8,128)S(1)}, f32[8,62,1024]{2,1,0:T(8,128)S(1)}, f32[8,62,1024]{2,1,0:T(8,128)S(1)}) fusion(f32[8,64,1024]{2,1,0:T(8,128)S(1)} %bitcast.152, f32[62]{0:T(128)S(1)} %slice.606, f32[8,64,1024]{2,1,0:T(8,128)S(1)} %bitcast.150, f32[62,1024]{1,0:T(8,128)S(1)} %copy-done.13, f32[62,1024]{1,0:T(8,128)S(1)} %copy-done.14, ...), kind=kLoop, calls=%fused_computation.12 | loop fusion | flops 9142272 | bytes 19042680 | tf_op jit(solution)/shard_map/mul | solution.py:68
  44.2 1.1 fusion.81
  45.3 2.1 %fusion.5 = f32[8,60,1024]{2,1,0:T(8,128)S(1)} fusion(f32[8,64,1024]{2,1,0:T(8,128)S(1)} %bitcast.153, f32[8,62,1024]{2,1,0:T(8,128)S(1)} %get-tuple-element.4, f32[8,60,1023]{2,1,0:T(8,128)S(1)} %get-tuple-element.17, f32[8,60,1023]{2,1,0:T(8,128)S(1)} %get-tuple-element.16, f32[60]{0:T(128)S(1)} %slice.616, f32[60,1024]{1,0:T(8,128)S(1)} %copy-done.17, ...), kind=kLoop, calls=%fused_computation.8 | loop fusion | flops 8847360 | bytes 14496240 | tf_op jit(solution)/shard_map/mul | solution.py:68
  47.5 1.0 fusion.80
  48.5 2.1 %fusion.2 = f32[8,58,1024]{2,1,0:T(8,128)S(1)} fusion(f32[8,64,1024]{2,1,0:T(8,128)S(1)} %bitcast.154, f32[8,60,1024]{2,1,0:T(8,128)S(1)} %fusion.5, f32[8,58,1023]{2,1,0:T(8,128)S(1)} %get-tuple-element.15, f32[8,58,1023]{2,1,0:T(8,128)S(1)} %get-tuple-element.14, f32[58]{0:T(128)S(1)} %slice.626, f32[58,1024]{1,0:T(8,128)S(1)} %copy-done.15, ...), kind=kLoop, calls=%fused_computation.4 | loop fusion | flops 8552448 | bytes 14013032 | tf_op jit(solution)/shard_map/mul | solution.py:68
  50.7 0.9 fusion.79
  51.8 2.4 %fusion.11 = f32[8,56,1024]{2,1,0:T(8,128)S(1)} fusion(f32[8,62,1024]{2,1,0:T(8,128)S(1)} %get-tuple-element.5, f32[8,62,1024]{2,1,0:T(8,128)S(1)} %get-tuple-element.18, f32[8,64,1024]{2,1,0:T(8,128)S(1)} %bitcast.155, f32[8,58,1024]{2,1,0:T(8,128)S(1)} %fusion.2, f32[8,56,1023]{2,1,0:T(8,128)S(1)} %get-tuple-element.13, ...), kind=kLoop, calls=%fused_computation.18 | loop fusion | flops 10092544 | bytes 17199872 | tf_op jit(solution)/shard_map/sub | solution.py:124
  56.1 1.0 fusion.39
  57.7 0.9 fusion.36
  60.0 1.0 fusion.42
  65.5 1.5 %pad_maximum_fusion.1 = f32[4,2,64,1024]{3,2,1,0:T(8,128)} fusion(f32[1,2,64,1024]{3,2,1,0:T(8,128)S(1)} %get-tuple-element.9, f32[1,2,64,1024]{3,2,1,0:T(8,128)S(1)} %get-tuple-element.54, f32[1,2,64,1024]{3,2,1,0:T(8,128)S(1)} %slice_bitcast_fusion, f32[1,2,64,1024]{3,2,1,0:T(8,128)S(1)} %get-tuple-element.8), kind=kLoop, calls=%fused_computation.13 | loop fusion | flops 1572864 | bytes 4194304 | tf_op jit(solution)/shard_map/stack | solution.py:153
  66.9 3.7 %all-to-all-start.1 = ((f32[4,2,64,1024]{3,2,1,0:T(8,128)}), f32[4,2,64,1024]{3,2,1,0:T(8,128)S(1)}, u32[]{:S(2)}, u32[]{:S(2)}) async-start(f32[4,2,64,1024]{3,2,1,0:T(8,128)} %pad_maximum_fusion.1), calls=%async_computation.1 | async-start | bytes 4194304 | tf_op jit(solution)/shard_map/all_to_all | solution.py:154
  70.8 24.7 %all-to-all-done.1 = f32[4,2,64,1024]{3,2,1,0:T(8,128)S(1)} async-done(((f32[4,2,64,1024]{3,2,1,0:T(8,128)}), f32[4,2,64,1024]{3,2,1,0:T(8,128)S(1)}, u32[]{:S(2)}, u32[]{:S(2)}) %all-to-all-start.1) | async-done | bytes 2097184 | tf_op jit(solution)/shard_map/all_to_all | solution.py:154
  95.5 1.2 fusion.32
  96.8 1.1 collective-permute-done.4
  98.9 2.7 %collective-permute-start.7 = (f32[2,16,16]{2,1,0:T(8,128)S(1)}, f32[2,16,16]{2,1,0:T(8,128)S(1)}, u32[]{:S(2)}, u32[]{:S(2)}) collective-permute-start(f32[2,16,16]{2,1,0:T(8,128)S(1)} %pad_maximum_fusion.10), channel_id=1, source_target_pairs={{0,96},{32,64},{64,32},{96,0},{1,97},{33,65},{65,33},{97,1},{2,98}... | collective-permute-start | bytes 6152 | tf_op jit(solution)/shard_map/ppermute | solution.py:37
  101.8 1.8 %collective-permute-done.6 = f32[2,16,16]{2,1,0:T(8,128)S(1)} collective-permute-done((f32[2,16,16]{2,1,0:T(8,128)S(1)}, f32[2,16,16]{2,1,0:T(8,128)S(1)}, u32[]{:S(2)}, u32[]{:S(2)}) %collective-permute-start.6) | collective-permute-done | bytes 2080 | tf_op jit(solution)/shard_map/ppermute | solution.py:37
  103.8 1.5 %collective-permute-done.5 = f32[2,16,16]{2,1,0:T(8,128)S(1)} collective-permute-done((f32[2,16,16]{2,1,0:T(8,128)S(1)}, f32[2,16,16]{2,1,0:T(8,128)S(1)}, u32[]{:S(2)}, u32[]{:S(2)}) %collective-permute-start.5) | collective-permute-done | bytes 2080 | tf_op jit(solution)/shard_map/ppermute | solution.py:37
  105.3 3.4 %collective-permute-start.9 = (f32[2,16,16]{2,1,0:T(8,128)S(1)}, f32[2,16,16]{2,1,0:T(8,128)S(1)}, u32[]{:S(2)}, u32[]{:S(2)}) collective-permute-start(f32[2,16,16]{2,1,0:T(8,128)S(1)} %add_add_fusion.2), channel_id=1, source_target_pairs={{0,4},{2,6},{4,0},{6,2},{8,12},{10,14},{12,8},{14,10},{16,20},{18,... | collective-permute-start | bytes 6152 | tf_op jit(solution)/shard_map/ppermute | solution.py:37
  108.7 2.3 %collective-permute-start.10 = (f32[2,16,16]{2,1,0:T(8,128)S(1)}, f32[2,16,16]{2,1,0:T(8,128)S(1)}, u32[]{:S(2)}, u32[]{:S(2)}) collective-permute-start(f32[2,16,16]{2,1,0:T(8,128)S(1)} %add_add_fusion.2), channel_id=1, source_target_pairs={{0,6},{2,4},{4,2},{6,0},{8,14},{10,12},{12,10},{14,8},{16,22},{18,... | collective-permute-start | bytes 6152 | tf_op jit(solution)/shard_map/ppermute | solution.py:37
  111.0 0.8 collective-permute-start.8
  111.8 1.8 %collective-permute-done.10 = f32[2,16,16]{2,1,0:T(8,128)S(1)} collective-permute-done((f32[2,16,16]{2,1,0:T(8,128)S(1)}, f32[2,16,16]{2,1,0:T(8,128)S(1)}, u32[]{:S(2)}, u32[]{:S(2)}) %collective-permute-start.10) | collective-permute-done | bytes 2080 | tf_op jit(solution)/shard_map/ppermute | solution.py:37
  113.7 1.1 collective-permute-done.8
  114.8 4.0 %collective-permute-start.12 = (f32[2,16,16]{2,1,0:T(8,128)S(1)}, f32[2,16,16]{2,1,0:T(8,128)S(1)}, u32[]{:S(2)}, u32[]{:S(2)}) collective-permute-start(f32[2,16,16]{2,1,0:T(8,128)S(1)} %add_add_fusion.1), channel_id=1, source_target_pairs={{0,16},{2,18},{4,20},{6,22},{8,24},{10,26},{12,28},{14,30},{16,0},... | collective-permute-start | bytes 6152 | tf_op jit(solution)/shard_map/ppermute | solution.py:37
  119.6 0.8 collective-permute-done.12
  120.5 3.2 %collective-permute-done.13 = f32[2,16,16]{2,1,0:T(8,128)S(1)} collective-permute-done((f32[2,16,16]{2,1,0:T(8,128)S(1)}, f32[2,16,16]{2,1,0:T(8,128)S(1)}, u32[]{:S(2)}, u32[]{:S(2)}) %collective-permute-start.13) | collective-permute-done | bytes 2080 | tf_op jit(solution)/shard_map/ppermute | solution.py:37
  123.8 1.5 %cholesky.17 = f32[16,16]{1,0:T(8,128)S(1)} custom-call(f32[16,16]{1,0:T(8,128)S(1)} %fusion.59), custom_call_target="Cholesky" | custom-call | tf_op jit(solution)/shard_map/jit(cholesky)/cholesky | solution.py:181
  126.6 1.2 custom-call.10
  128.2 0.9 fusion.33
  129.0 1.3 %copy.15 = f32[1,8,64,1024]{3,2,1,0:T(8,128)} copy(f32[1,8,64,1024]{3,2,1,0:T(8,128)S(1)} %bitcast.161) | data formatting | bytes 4194304
  (150 shorter events, 18.0 us)
Async XLA Ops:
  2.2 21.3 %collective-permute-start.3 = (f32[4,7,1024]{2,1,0:T(8,128)}, f32[4,7,1024]{2,1,0:T(8,128)S(1)}, u32[]{:S(2)}, u32[]{:S(2)}) collective-permute-start(f32[4,7,1024]{2,1,0:T(8,128)} %get-tuple-element.49), channel_id=1, source_target_pairs={{2,0},{4,2},{6,4},{8,6},{10,8},{12,10},{14,12},{16,14},{18,16},{20... | collective-permute-start | bytes 344072 | tf_op jit(solution)/shard_map/ppermute | solution.py:23
  3.5 10.6 %copy-start.1 = (f32[64,1024]{1,0:T(8,128)S(1)}, f32[64,1024]{1,0:T(8,128)}, u32[]{:S(2)}) copy-start(f32[64,1024]{1,0:T(8,128)} %param.12) | copy-start | bytes 786436
  3.5 10.6 %copy-start.2 = (f32[64,1024]{1,0:T(8,128)S(1)}, f32[64,1024]{1,0:T(8,128)}, u32[]{:S(2)}) copy-start(f32[64,1024]{1,0:T(8,128)} %param.11) | copy-start | bytes 786436
  3.5 11.4 %copy-start = (f32[64,1024]{1,0:T(8,128)S(1)}, f32[64,1024]{1,0:T(8,128)}, u32[]{:S(2)}) copy-start(f32[64,1024]{1,0:T(8,128)} %param.13) | copy-start | bytes 786436
  3.6 30.9 %all-to-all-start = ((f32[4,2,64,1024]{3,2,1,0:T(8,128)}), f32[4,2,64,1024]{3,2,1,0:T(8,128)S(1)}, u32[]{:S(2)}, u32[]{:S(2)}) async-start(f32[4,2,64,1024]{3,2,1,0:T(8,128)} %bitcast.186), calls=%async_computation | async-start | bytes 4194304 | tf_op jit(solution)/shard_map/all_to_all | solution.py:95
  8.1 10.6 %copy-start.26 = (f32[8,128]{1,0:T(8,128)S(1)}, f32[8,128]{1,0:T(8,128)}, u32[]{:S(2)}) copy-start(f32[8,128]{1,0:T(8,128)} %param.15) | copy-start | bytes 12292
  8.1 15.5 %collective-permute-start.2 = (f32[4,7,1024]{2,1,0:T(8,128)}, f32[4,7,1024]{2,1,0:T(8,128)S(1)}, u32[]{:S(2)}, u32[]{:S(2)}) collective-permute-start(f32[4,7,1024]{2,1,0:T(8,128)} %get-tuple-element.48), channel_id=1, source_target_pairs={{0,2},{2,4},{4,6},{6,8},{8,10},{10,12},{12,14},{14,16},{16,18},{18... | collective-permute-start | bytes 344072 | tf_op jit(solution)/shard_map/ppermute | solution.py:21
  12.9 5.8 %copy-start.33 = (f32[30,1]{0,1:T(1,128)}, f32[30,1]{0,1:T(1,128)S(1)}, u32[]{:S(2)}) copy-start(f32[30,1]{0,1:T(1,128)S(1)} %pad_maximum_fusion.11) | copy-start | bytes 364
  14.1 4.8 %copy-start.3 = (f32[64,1024]{1,0:T(8,128)S(1)}, f32[64,1024]{1,0:T(8,128)}, u32[]{:S(2)}) copy-start(f32[64,1024]{1,0:T(8,128)} %param.14) | copy-start | bytes 786436
  18.9 3.3 %copy-start.34 = (f32[30,1]{0,1:T(1,128)S(1)}, f32[30,1]{0,1:T(1,128)}, u32[]{:S(2)}) copy-start(f32[30,1]{0,1:T(1,128)} %copy-done.33) | copy-start | bytes 364
  34.5 7.3 %copy-start.4 = (f32[2,64,1024]{2,1,0:T(8,128)S(1)}, f32[2,64,1024]{2,1,0:T(8,128)}, u32[]{:S(2)}) copy-start(f32[2,64,1024]{2,1,0:T(8,128)} %broadcast_multiply_fusion) | copy-start | bytes 1572868
  35.4 6.6 %copy-start.12 = (f32[62,1024]{1,0:T(8,128)S(1)}, f32[62,1024]{1,0:T(8,128)}, u32[]{:S(2)}) copy-start(f32[62,1024]{1,0:T(8,128)} %slice_bitcast_fusion.17) | copy-start | bytes 761860
  35.4 6.6 %copy-start.13 = (f32[62,1024]{1,0:T(8,128)S(1)}, f32[62,1024]{1,0:T(8,128)}, u32[]{:S(2)}) copy-start(f32[62,1024]{1,0:T(8,128)} %get-tuple-element.63) | copy-start | bytes 761860
  35.4 6.6 %copy-start.14 = (f32[62,1024]{1,0:T(8,128)S(1)}, f32[62,1024]{1,0:T(8,128)}, u32[]{:S(2)}) copy-start(f32[62,1024]{1,0:T(8,128)} %get-tuple-element.64) | copy-start | bytes 761860
  35.4 18.8 %collective-permute-start.1 = (f32[8,7,1024]{2,1,0:T(8,128)S(1)}, f32[8,7,1024]{2,1,0:T(8,128)S(1)}, u32[]{:S(2)}, u32[]{:S(2)}) collective-permute-start(f32[8,7,1024]{2,1,0:T(8,128)S(1)} %get-tuple-element.22), channel_id=1, source_target_pairs={{2,0},{4,2},{6,4},{8,6},{10,8},{12,10},{14,12},{16,14},{18,16},{20... | collective-permute-start | bytes 688136 | tf_op jit(solution)/shard_map/ppermute | solution.py:23
  36.9 17.4 %collective-permute-start = (f32[8,7,1024]{2,1,0:T(8,128)S(1)}, f32[8,7,1024]{2,1,0:T(8,128)S(1)}, u32[]{:S(2)}, u32[]{:S(2)}) collective-permute-start(f32[8,7,1024]{2,1,0:T(8,128)S(1)} %get-tuple-element.21), channel_id=1, source_target_pairs={{0,2},{2,4},{4,6},{6,8},{8,10},{10,12},{12,14},{14,16},{16,18},{18... | collective-permute-start | bytes 688136 | tf_op jit(solution)/shard_map/ppermute | solution.py:21
  44.2 1.1 copy-start.11
  44.2 1.1 copy-start.17
  44.2 1.1 copy-start.18
  47.4 1.0 copy-start.10
  47.4 1.0 copy-start.15
  47.4 1.1 copy-start.16
  50.6 0.9 copy-start.19
  50.6 1.0 copy-start.20
  50.7 1.1 copy-start.21
  51.8 2.5 %copy-start.23 = (f32[4,7,1024]{2,1,0:T(8,128)S(1)}, f32[4,7,1024]{2,1,0:T(8,128)}, u32[]{:S(2)}) copy-start(f32[4,7,1024]{2,1,0:T(8,128)} %copy-done.22) | copy-start | bytes 344068
  51.8 2.5 %copy-start.25 = (f32[4,7,1024]{2,1,0:T(8,128)S(1)}, f32[4,7,1024]{2,1,0:T(8,128)}, u32[]{:S(2)}) copy-start(f32[4,7,1024]{2,1,0:T(8,128)} %copy-done.24) | copy-start | bytes 344068
  61.4 1.0 copy-start.7
  61.4 1.0 copy-start.8
  61.4 1.1 copy-start.9
  63.1 1.0 copy-start.5
  63.1 1.0 copy-start.6
  66.9 3.8 %copy-start.29 = (s32[1,64]{1,0:T(1,128)S(1)}, s32[1,64]{1,0:T(1,128)}, u32[]{:S(2)}) copy-start(s32[1,64]{1,0:T(1,128)} %param.16) | copy-start | bytes 772
  66.9 28.6 %all-to-all-start.1 = ((f32[4,2,64,1024]{3,2,1,0:T(8,128)}), f32[4,2,64,1024]{3,2,1,0:T(8,128)S(1)}, u32[]{:S(2)}, u32[]{:S(2)}) async-start(f32[4,2,64,1024]{3,2,1,0:T(8,128)} %pad_maximum_fusion.1), calls=%async_computation.1 | async-start | bytes 4194304 | tf_op jit(solution)/shard_map/all_to_all | solution.py:154
  70.7 26.1 %copy-start.31 = (f32[1,64]{1,0:T(1,128)S(1)}, f32[1,64]{1,0:T(1,128)}, u32[]{:S(2)}) copy-start(f32[1,64]{1,0:T(1,128)} %param.19) | copy-start | bytes 772
  70.7 27.4 %copy-start.30 = (f32[1,64,16]{1,2,0:T(8,128)S(1)}, f32[1,64,16]{1,2,0:T(8,128)}, u32[]{:S(2)}) copy-start(f32[1,64,16]{1,2,0:T(8,128)} %param.18) | copy-start | bytes 12292
  70.7 27.4 %copy-start.32 = (f32[1,64]{1,0:T(1,128)S(1)}, f32[1,64]{1,0:T(1,128)}, u32[]{:S(2)}) copy-start(f32[1,64]{1,0:T(1,128)} %param.17) | copy-start | bytes 772
  96.7 1.2 collective-permute-start.4
  98.2 5.3 %collective-permute-start.6 = (f32[2,16,16]{2,1,0:T(8,128)S(1)}, f32[2,16,16]{2,1,0:T(8,128)S(1)}, u32[]{:S(2)}, u32[]{:S(2)}) collective-permute-start(f32[2,16,16]{2,1,0:T(8,128)S(1)} %pad_maximum_fusion.10), channel_id=1, source_target_pairs={{0,64},{32,96},{64,0},{96,32},{1,65},{33,97},{65,1},{97,33},{2,66}... | collective-permute-start | bytes 6152 | tf_op jit(solution)/shard_map/ppermute | solution.py:37
  98.9 4.9 %collective-permute-start.7 = (f32[2,16,16]{2,1,0:T(8,128)S(1)}, f32[2,16,16]{2,1,0:T(8,128)S(1)}, u32[]{:S(2)}, u32[]{:S(2)}) collective-permute-start(f32[2,16,16]{2,1,0:T(8,128)S(1)} %pad_maximum_fusion.10), channel_id=1, source_target_pairs={{0,96},{32,64},{64,32},{96,0},{1,97},{33,65},{65,33},{97,1},{2,98}... | collective-permute-start | bytes 6152 | tf_op jit(solution)/shard_map/ppermute | solution.py:37
  101.6 3.7 %collective-permute-start.5 = (f32[2,16,16]{2,1,0:T(8,128)S(1)}, f32[2,16,16]{2,1,0:T(8,128)S(1)}, u32[]{:S(2)}, u32[]{:S(2)}) collective-permute-start(f32[2,16,16]{2,1,0:T(8,128)S(1)} %pad_maximum_fusion.10), channel_id=1, source_target_pairs={{0,32},{32,0},{64,96},{96,64},{1,33},{33,1},{65,97},{97,65},{2,34}... | collective-permute-start | bytes 6152 | tf_op jit(solution)/shard_map/ppermute | solution.py:37
  101.8 10.0 %collective-permute-start.14 = (f32[8,128]{1,0:T(8,128)S(1)}, f32[8,128]{1,0:T(8,128)S(1)}, u32[]{:S(2)}, u32[]{:S(2)}) collective-permute-start(f32[8,128]{1,0:T(8,128)S(1)} %copy-done.26), channel_id=1, source_target_pairs={{0,1},{1,0},{2,3},{3,2},{4,5},{5,4},{6,7},{7,6},{8,9},{9,8},{10,11... | collective-permute-start | bytes 12296 | tf_op jit(solution)/shard_map/ppermute | solution.py:49
  105.3 6.5 %collective-permute-start.9 = (f32[2,16,16]{2,1,0:T(8,128)S(1)}, f32[2,16,16]{2,1,0:T(8,128)S(1)}, u32[]{:S(2)}, u32[]{:S(2)}) collective-permute-start(f32[2,16,16]{2,1,0:T(8,128)S(1)} %add_add_fusion.2), channel_id=1, source_target_pairs={{0,4},{2,6},{4,0},{6,2},{8,12},{10,14},{12,8},{14,10},{16,20},{18,... | collective-permute-start | bytes 6152 | tf_op jit(solution)/shard_map/ppermute | solution.py:37
  108.7 4.9 %collective-permute-start.10 = (f32[2,16,16]{2,1,0:T(8,128)S(1)}, f32[2,16,16]{2,1,0:T(8,128)S(1)}, u32[]{:S(2)}, u32[]{:S(2)}) collective-permute-start(f32[2,16,16]{2,1,0:T(8,128)S(1)} %add_add_fusion.2), channel_id=1, source_target_pairs={{0,6},{2,4},{4,2},{6,0},{8,14},{10,12},{12,10},{14,8},{16,22},{18,... | collective-permute-start | bytes 6152 | tf_op jit(solution)/shard_map/ppermute | solution.py:37
  111.0 3.7 %collective-permute-start.8 = (f32[2,16,16]{2,1,0:T(8,128)S(1)}, f32[2,16,16]{2,1,0:T(8,128)S(1)}, u32[]{:S(2)}, u32[]{:S(2)}) collective-permute-start(f32[2,16,16]{2,1,0:T(8,128)S(1)} %add_add_fusion.2), channel_id=1, source_target_pairs={{0,2},{2,0},{4,6},{6,4},{8,10},{10,8},{12,14},{14,12},{16,18},{18,... | collective-permute-start | bytes 6152 | tf_op jit(solution)/shard_map/ppermute | solution.py:37
  114.8 5.7 %collective-permute-start.12 = (f32[2,16,16]{2,1,0:T(8,128)S(1)}, f32[2,16,16]{2,1,0:T(8,128)S(1)}, u32[]{:S(2)}, u32[]{:S(2)}) collective-permute-start(f32[2,16,16]{2,1,0:T(8,128)S(1)} %add_add_fusion.1), channel_id=1, source_target_pairs={{0,16},{2,18},{4,20},{6,22},{8,24},{10,26},{12,28},{14,30},{16,0},... | collective-permute-start | bytes 6152 | tf_op jit(solution)/shard_map/ppermute | solution.py:37
  118.7 4.9 %collective-permute-start.13 = (f32[2,16,16]{2,1,0:T(8,128)S(1)}, f32[2,16,16]{2,1,0:T(8,128)S(1)}, u32[]{:S(2)}, u32[]{:S(2)}) collective-permute-start(f32[2,16,16]{2,1,0:T(8,128)S(1)} %add_add_fusion.1), channel_id=1, source_target_pairs={{0,24},{2,26},{4,28},{6,30},{8,16},{10,18},{12,20},{14,22},{16,8},... | collective-permute-start | bytes 6152 | tf_op jit(solution)/shard_map/ppermute | solution.py:37
  119.5 4.2 %collective-permute-start.11 = (f32[2,16,16]{2,1,0:T(8,128)S(1)}, f32[2,16,16]{2,1,0:T(8,128)S(1)}, u32[]{:S(2)}, u32[]{:S(2)}) collective-permute-start(f32[2,16,16]{2,1,0:T(8,128)S(1)} %add_add_fusion.1), channel_id=1, source_target_pairs={{0,8},{2,10},{4,12},{6,14},{8,0},{10,2},{12,4},{14,6},{16,24},{18,... | collective-permute-start | bytes 6152 | tf_op jit(solution)/shard_map/ppermute | solution.py:37
  (4 other events, 2.6 us)

commit v18 on v17

--- a/solution.py
+++ b/solution.py
@@ -99,17 +99,15 @@
     spread_params = jnp.repeat(my_params, band_width, axis=1)
 
     fields = jnp.stack([diffusivity, velocity_x, velocity_y, source_shape])
-    own = jnp.concatenate([mine, fields])
     wide_fields = with_halo(fields, "space", depth)
-    wide = jnp.concatenate([with_halo(mine, "space", depth), wide_fields])
+    wide_states = with_halo(mine, "space", depth)
     count = slices * group
     global_rows = first_row - depth + jnp.arange(row_count + 2 * depth, dtype=jnp.int32)
     wide_inside = ((global_rows >= 0) & (global_rows < slabs)).astype(jnp.float32)[:, None]
 
-    def block_steps(block, inside):
-        states = block[:count]
-        coeffs = block[count : count + 3]
-        forcing = jnp.tile(block[count + 3][None] * spread_params[:, None, :], (slices, 1, 1))
+    def block_steps(states, block, inside):
+        coeffs = block[:3]
+        forcing = jnp.tile(block[3][None] * spread_params[:, None, :], (slices, 1, 1))
 
         def step(values, off, step_size, q):
             lo, hi = off + 1, off + values.shape[1] - 1
@@ -124,17 +122,18 @@
         return current - coarse
 
     later = (jnp.arange(count) >= group).astype(jnp.float32)
-    inner = block_steps(own, wide_inside[depth : depth + row_count])
+    inner = block_steps(mine, fields, wide_inside[depth : depth + row_count])
     strip = depth + 2 * FINE
-    strips = jnp.concatenate([wide[:, :strip], wide[:, -strip:]], axis=1)
+    strip_states = jnp.concatenate([wide_states[:, :strip], wide_states[:, -strip:]], axis=1)
+    strip_fields = jnp.concatenate([wide_fields[:, :strip], wide_fields[:, -strip:]], axis=1)
     strips_inside = jnp.concatenate([wide_inside[:strip], wide_inside[-strip:]])
-    edges = block_steps(strips, strips_inside)
+    edges = block_steps(strip_states, strip_fields, strips_inside)
 
     def stitch(edges, inner):
         return jnp.concatenate([edges[:, :depth], inner, edges[:, strip : strip + depth]], axis=1)
 
     current = stitch(edges, inner)
-    wide_coeffs = wide[count : count + 3]
+    wide_coeffs = wide_fields[:3]
 
     def step(values, low, step_size, forcing):
         n = values.shape[1]

time: 131 us -> 137 us (1.046)
  local copies, waits for them, and re-layouts: 22.9 us -> 27.4 us
    mul x10, local copies, waits for them, and re-layouts: 4.94 us -> 7.69 us  [advance(): coeffs[0] * (above_row + below_row + west_cell + east_cell - 4.0 * middle)]
    ppermute x9, starting transfers between devices: 14.9 us -> 16.4 us  [quad_sum(): lax.ppermute(value, axis, [(i, i ^ k * bit) for i in range(count)])]
    unnamed x71 -> x87, local copies, waits for them, and re-layouts: 4.28 us -> 5.46 us
  transfers between devices with their start and end apart: 17 -> 17, of which waited for: 10 -> 10; matrix products, arithmetic and copies ran while one was open for 19% -> 21% of each run, Pallas kernels for 0% -> 0%
where the time goes in v18:
time: 137 us; the launch traced here: 136 us
  waiting for transfers between devices  44.6 us (33%)
  starting transfers between devices  36.6 us (27%)
  local copies, waits for them, and re-layouts  27.4 us (20%)
  other arithmetic  23.8 us (17%)
  matrix products  2.66 us (2%)
  between operations  1.46 us (1%)
    all_to_all x1, waiting for transfers between devices, per_device(): lax.all_to_all(done, 'tm', 0, 0, tiled=True)  24.2 us
    ppermute x9, starting transfers between devices, quad_sum(): lax.ppermute(value, axis, [(i, i ^ k * bit) for i in range(count)])  16.4 us
    ppermute x9, waiting for transfers between devices, quad_sum(): lax.ppermute(value, axis, [(i, i ^ k * bit) for i in range(count)])  10.7 us
    ppermute x2, starting transfers between devices, with_halo(): lax.ppermute(tail, axis, [(i, i + 1) for i in range(ends)])  9.11 us
    mul x6, other arithmetic, advance(): return (middle + step_size * tendency) * inside  8.89 us
    all_to_all x1, waiting for transfers between devices, per_device(): lax.all_to_all(state.reshape(slices, group, row_count, col_count), 'tm',...  8.58 us
    mul x10, local copies, waits for them, and re-layouts, advance(): coeffs[0] * (above_row + below_row + west_cell + east_cell - 4.0 * middle)  7.69 us
    slice x11, local copies, waits for them, and re-layouts, advance(): west_cell = jnp.pad(middle[:, :, :-1], ((0, 0), (0, 0), (1, 0)))  6.21 us
  transfers between devices with their start and end apart: 17, of which 10 were waited for; matrix products, arithmetic and copies ran while one was open for 21% of the time, Pallas kernels for 0%

profile of v18, /device:TPU:0, one launch (start us, length us, event | category | flops | bytes accessed | tf_op | source)
XLA Modules:
  0.0 136.4 jit_solution(9061251361554624951)
XLA Ops:
  0.6 1.6 %pad_maximum_fusion.9 = (f32[4,7,1024]{2,1,0:T(8,128)}, f32[4,7,1024]{2,1,0:T(8,128)}) fusion(f32[1,64,1024]{2,1,0:T(8,128)} %bitcast.183, f32[1,64,1024]{2,1,0:T(8,128)} %bitcast.169, f32[1,64,1024]{2,1,0:T(8,128)} %bitcast.176, f32[1,64,1024]{2,1,0:T(8,128)} %bitcast.162), kind=kLoop, calls=%fused_computation.106 | loop fusion | flops 172032 | bytes 1277952 | tf_op jit(solution)/shard_map/slice | solution.py:18
  2.2 1.3 collective-permute-start.3
  3.5 4.6 %collective-permute-start.2 = (f32[4,7,1024]{2,1,0:T(8,128)}, f32[4,7,1024]{2,1,0:T(8,128)S(1)}, u32[]{:S(2)}, u32[]{:S(2)}) collective-permute-start(f32[4,7,1024]{2,1,0:T(8,128)} %get-tuple-element.36), channel_id=1, source_target_pairs={{0,2},{2,4},{4,6},{6,8},{8,10},{10,12},{12,14},{14,16},{16,18},{18... | collective-permute-start | bytes 344072 | tf_op jit(solution)/shard_map/ppermute | solution.py:21
  8.1 4.5 %all-to-all-start = ((f32[4,2,64,1024]{3,2,1,0:T(8,128)}), f32[4,2,64,1024]{3,2,1,0:T(8,128)S(1)}, u32[]{:S(2)}, u32[]{:S(2)}) async-start(f32[4,2,64,1024]{3,2,1,0:T(8,128)} %bitcast.186), calls=%async_computation | async-start | bytes 4194304 | tf_op jit(solution)/shard_map/all_to_all | solution.py:95
  14.7 0.8 slice_bitcast_fusion.15
  16.3 0.8 slice_bitcast_fusion.12
  17.8 0.8 slice_bitcast_fusion.9
  18.7 0.7 slice_bitcast_fusion.11
  19.4 0.8 slice_bitcast_fusion.18
  21.2 0.9 broadcast_multiply_fusion
  26.5 0.8 slice_bitcast_fusion.27
  27.3 0.8 slice_bitcast_fusion.23
  28.0 1.0 slice_bitcast_fusion.8
  29.0 0.8 slice_bitcast_fusion.5
  29.8 8.6 %all-to-all-done = f32[4,2,64,1024]{3,2,1,0:T(8,128)S(1)} async-done(((f32[4,2,64,1024]{3,2,1,0:T(8,128)}), f32[4,2,64,1024]{3,2,1,0:T(8,128)S(1)}, u32[]{:S(2)}, u32[]{:S(2)}) %all-to-all-start) | async-done | bytes 2097184 | tf_op jit(solution)/shard_map/all_to_all | solution.py:95
  38.5 0.9 fusion.67
  39.4 1.4 %collective-permute-start.1 = (f32[8,7,1024]{2,1,0:T(8,128)S(1)}, f32[8,7,1024]{2,1,0:T(8,128)S(1)}, u32[]{:S(2)}, u32[]{:S(2)}) collective-permute-start(f32[8,7,1024]{2,1,0:T(8,128)S(1)} %get-tuple-element.22), channel_id=1, source_target_pairs={{2,0},{4,2},{6,4},{8,6},{10,8},{12,10},{14,12},{16,14},{18,16},{20... | collective-permute-start | bytes 688136 | tf_op jit(solution)/shard_map/ppermute | solution.py:23
  40.9 4.6 %collective-permute-start = (f32[8,7,1024]{2,1,0:T(8,128)S(1)}, f32[8,7,1024]{2,1,0:T(8,128)S(1)}, u32[]{:S(2)}, u32[]{:S(2)}) collective-permute-start(f32[8,7,1024]{2,1,0:T(8,128)S(1)} %get-tuple-element.21), channel_id=1, source_target_pairs={{0,2},{2,4},{4,6},{6,8},{8,10},{10,12},{12,14},{14,16},{16,18},{18... | collective-permute-start | bytes 688136 | tf_op jit(solution)/shard_map/ppermute | solution.py:21
  45.7 2.1 %fusion.8 = (f32[8,62,1024]{2,1,0:T(8,128)S(1)}, f32[8,62,1024]{2,1,0:T(8,128)S(1)}, f32[8,62,1024]{2,1,0:T(8,128)S(1)}) fusion(f32[8,64,1024]{2,1,0:T(8,128)S(1)} %bitcast.152, f32[62]{0:T(128)S(1)} %slice.614, f32[8,64,1024]{2,1,0:T(8,128)S(1)} %bitcast.150, f32[62,1024]{1,0:T(8,128)S(1)} %copy-done.16, f32[62,1024]{1,0:T(8,128)S(1)} %copy-done.17, ...), kind=kLoop, calls=%fused_computation.12 | loop fusion | flops 9142272 | bytes 19042680 | tf_op jit(solution)/shard_map/mul | solution.py:68
  47.9 1.1 fusion.66
  49.0 2.1 %fusion.5 = f32[8,60,1024]{2,1,0:T(8,128)S(1)} fusion(f32[8,64,1024]{2,1,0:T(8,128)S(1)} %bitcast.153, f32[8,62,1024]{2,1,0:T(8,128)S(1)} %get-tuple-element.4, f32[8,60,1023]{2,1,0:T(8,128)S(1)} %get-tuple-element.17, f32[8,60,1023]{2,1,0:T(8,128)S(1)} %get-tuple-element.16, f32[60]{0:T(128)S(1)} %slice.624, f32[60,1024]{1,0:T(8,128)S(1)} %copy-done.14, ...), kind=kLoop, calls=%fused_computation.8 | loop fusion | flops 8847360 | bytes 14496240 | tf_op jit(solution)/shard_map/mul | solution.py:68
  51.1 1.0 fusion.65
  52.2 2.1 %fusion.2 = f32[8,58,1024]{2,1,0:T(8,128)S(1)} fusion(f32[8,64,1024]{2,1,0:T(8,128)S(1)} %bitcast.154, f32[8,60,1024]{2,1,0:T(8,128)S(1)} %fusion.5, f32[8,58,1023]{2,1,0:T(8,128)S(1)} %get-tuple-element.15, f32[8,58,1023]{2,1,0:T(8,128)S(1)} %get-tuple-element.14, f32[58]{0:T(128)S(1)} %slice.634, f32[58,1024]{1,0:T(8,128)S(1)} %copy-done.12, ...), kind=kLoop, calls=%fused_computation.4 | loop fusion | flops 8552448 | bytes 14013032 | tf_op jit(solution)/shard_map/mul | solution.py:68
  54.3 0.9 fusion.64
  55.5 2.6 %fusion.11 = f32[8,56,1024]{2,1,0:T(8,128)S(1)} fusion(f32[8,62,1024]{2,1,0:T(8,128)S(1)} %get-tuple-element.5, f32[8,62,1024]{2,1,0:T(8,128)S(1)} %get-tuple-element.18, f32[8,64,1024]{2,1,0:T(8,128)S(1)} %bitcast.155, f32[8,58,1024]{2,1,0:T(8,128)S(1)} %fusion.2, f32[8,56,1023]{2,1,0:T(8,128)S(1)} %get-tuple-element.13, ...), kind=kLoop, calls=%fused_computation.18 | loop fusion | flops 10092544 | bytes 17199872 | tf_op jit(solution)/shard_map/sub | solution.py:122
  59.4 1.0 fusion.22
  61.4 0.9 fusion.19
  65.1 1.0 fusion.26
  70.5 1.5 %pad_maximum_fusion.1 = f32[4,2,64,1024]{3,2,1,0:T(8,128)} fusion(f32[1,2,64,1024]{3,2,1,0:T(8,128)S(1)} %get-tuple-element.9, f32[1,2,64,1024]{3,2,1,0:T(8,128)S(1)} %get-tuple-element.42, f32[1,2,64,1024]{3,2,1,0:T(8,128)S(1)} %slice_bitcast_fusion, f32[1,2,64,1024]{3,2,1,0:T(8,128)S(1)} %get-tuple-element.8), kind=kLoop, calls=%fused_computation.13 | loop fusion | flops 1572864 | bytes 4194304 | tf_op jit(solution)/shard_map/stack | solution.py:152
  71.9 3.7 %all-to-all-start.1 = ((f32[4,2,64,1024]{3,2,1,0:T(8,128)}), f32[4,2,64,1024]{3,2,1,0:T(8,128)S(1)}, u32[]{:S(2)}, u32[]{:S(2)}) async-start(f32[4,2,64,1024]{3,2,1,0:T(8,128)} %pad_maximum_fusion.1), calls=%async_computation.1 | async-start | bytes 4194304 | tf_op jit(solution)/shard_map/all_to_all | solution.py:153
  75.7 24.2 %all-to-all-done.1 = f32[4,2,64,1024]{3,2,1,0:T(8,128)S(1)} async-done(((f32[4,2,64,1024]{3,2,1,0:T(8,128)}), f32[4,2,64,1024]{3,2,1,0:T(8,128)S(1)}, u32[]{:S(2)}, u32[]{:S(2)}) %all-to-all-start.1) | async-done | bytes 2097184 | tf_op jit(solution)/shard_map/all_to_all | solution.py:153
  99.9 1.2 fusion.15
  101.2 1.1 collective-permute-done.4
  103.3 2.7 %collective-permute-start.7 = (f32[2,16,16]{2,1,0:T(8,128)S(1)}, f32[2,16,16]{2,1,0:T(8,128)S(1)}, u32[]{:S(2)}, u32[]{:S(2)}) collective-permute-start(f32[2,16,16]{2,1,0:T(8,128)S(1)} %pad_maximum_fusion.10), channel_id=1, source_target_pairs={{0,96},{32,64},{64,32},{96,0},{1,97},{33,65},{65,33},{97,1},{2,98}... | collective-permute-start | bytes 6152 | tf_op jit(solution)/shard_map/ppermute | solution.py:37
  106.2 1.8 %collective-permute-done.6 = f32[2,16,16]{2,1,0:T(8,128)S(1)} collective-permute-done((f32[2,16,16]{2,1,0:T(8,128)S(1)}, f32[2,16,16]{2,1,0:T(8,128)S(1)}, u32[]{:S(2)}, u32[]{:S(2)}) %collective-permute-start.6) | collective-permute-done | bytes 2080 | tf_op jit(solution)/shard_map/ppermute | solution.py:37
  108.2 1.5 %collective-permute-done.5 = f32[2,16,16]{2,1,0:T(8,128)S(1)} collective-permute-done((f32[2,16,16]{2,1,0:T(8,128)S(1)}, f32[2,16,16]{2,1,0:T(8,128)S(1)}, u32[]{:S(2)}, u32[]{:S(2)}) %collective-permute-start.5) | collective-permute-done | bytes 2080 | tf_op jit(solution)/shard_map/ppermute | solution.py:37
  109.7 4.9 %collective-permute-start.9 = (f32[2,16,16]{2,1,0:T(8,128)S(1)}, f32[2,16,16]{2,1,0:T(8,128)S(1)}, u32[]{:S(2)}, u32[]{:S(2)}) collective-permute-start(f32[2,16,16]{2,1,0:T(8,128)S(1)} %add_add_fusion.2), channel_id=1, source_target_pairs={{0,4},{2,6},{4,0},{6,2},{8,12},{10,14},{12,8},{14,10},{16,20},{18,... | collective-permute-start | bytes 6152 | tf_op jit(solution)/shard_map/ppermute | solution.py:37
  114.6 2.5 %collective-permute-start.10 = (f32[2,16,16]{2,1,0:T(8,128)S(1)}, f32[2,16,16]{2,1,0:T(8,128)S(1)}, u32[]{:S(2)}, u32[]{:S(2)}) collective-permute-start(f32[2,16,16]{2,1,0:T(8,128)S(1)} %add_add_fusion.2), channel_id=1, source_target_pairs={{0,6},{2,4},{4,2},{6,0},{8,14},{10,12},{12,10},{14,8},{16,22},{18,... | collective-permute-start | bytes 6152 | tf_op jit(solution)/shard_map/ppermute | solution.py:37
  117.1 0.8 collective-permute-start.8
  117.9 1.7 %collective-permute-done.10 = f32[2,16,16]{2,1,0:T(8,128)S(1)} collective-permute-done((f32[2,16,16]{2,1,0:T(8,128)S(1)}, f32[2,16,16]{2,1,0:T(8,128)S(1)}, u32[]{:S(2)}, u32[]{:S(2)}) %collective-permute-start.10) | collective-permute-done | bytes 2080 | tf_op jit(solution)/shard_map/ppermute | solution.py:37
  119.6 1.3 collective-permute-done.8
  120.9 4.0 %collective-permute-start.12 = (f32[2,16,16]{2,1,0:T(8,128)S(1)}, f32[2,16,16]{2,1,0:T(8,128)S(1)}, u32[]{:S(2)}, u32[]{:S(2)}) collective-permute-start(f32[2,16,16]{2,1,0:T(8,128)S(1)} %add_add_fusion.1), channel_id=1, source_target_pairs={{0,16},{2,18},{4,20},{6,22},{8,24},{10,26},{12,28},{14,30},{16,0},... | collective-permute-start | bytes 6152 | tf_op jit(solution)/shard_map/ppermute | solution.py:37
  125.5 1.0 collective-permute-done.12
  126.5 3.2 %collective-permute-done.13 = f32[2,16,16]{2,1,0:T(8,128)S(1)} collective-permute-done((f32[2,16,16]{2,1,0:T(8,128)S(1)}, f32[2,16,16]{2,1,0:T(8,128)S(1)}, u32[]{:S(2)}, u32[]{:S(2)}) %collective-permute-start.13) | collective-permute-done | bytes 2080 | tf_op jit(solution)/shard_map/ppermute | solution.py:37
  129.9 1.5 %cholesky.17 = f32[16,16]{1,0:T(8,128)S(1)} custom-call(f32[16,16]{1,0:T(8,128)S(1)} %fusion.44), custom_call_target="Cholesky" | custom-call | tf_op jit(solution)/shard_map/jit(cholesky)/cholesky | solution.py:180
  132.7 1.2 custom-call.10
  134.2 0.9 fusion.16
  135.1 1.3 copy.15
  (167 shorter events, 22.7 us)
Async XLA Ops:
  2.2 21.7 %collective-permute-start.3 = (f32[4,7,1024]{2,1,0:T(8,128)}, f32[4,7,1024]{2,1,0:T(8,128)S(1)}, u32[]{:S(2)}, u32[]{:S(2)}) collective-permute-start(f32[4,7,1024]{2,1,0:T(8,128)} %get-tuple-element.37), channel_id=1, source_target_pairs={{2,0},{4,2},{6,4},{8,6},{10,8},{12,10},{14,12},{16,14},{18,16},{20... | collective-permute-start | bytes 344072 | tf_op jit(solution)/shard_map/ppermute | solution.py:23
  3.5 20.5 %collective-permute-start.2 = (f32[4,7,1024]{2,1,0:T(8,128)}, f32[4,7,1024]{2,1,0:T(8,128)S(1)}, u32[]{:S(2)}, u32[]{:S(2)}) collective-permute-start(f32[4,7,1024]{2,1,0:T(8,128)} %get-tuple-element.36), channel_id=1, source_target_pairs={{0,2},{2,4},{4,6},{6,8},{8,10},{10,12},{12,14},{14,16},{16,18},{18... | collective-permute-start | bytes 344072 | tf_op jit(solution)/shard_map/ppermute | solution.py:21
  8.1 6.6 %copy-start.1 = (f32[64,1024]{1,0:T(8,128)S(1)}, f32[64,1024]{1,0:T(8,128)}, u32[]{:S(2)}) copy-start(f32[64,1024]{1,0:T(8,128)} %param.12) | copy-start | bytes 786436
  8.1 6.6 %copy-start.2 = (f32[64,1024]{1,0:T(8,128)S(1)}, f32[64,1024]{1,0:T(8,128)}, u32[]{:S(2)}) copy-start(f32[64,1024]{1,0:T(8,128)} %param.11) | copy-start | bytes 786436
  8.1 7.4 %copy-start = (f32[64,1024]{1,0:T(8,128)S(1)}, f32[64,1024]{1,0:T(8,128)}, u32[]{:S(2)}) copy-start(f32[64,1024]{1,0:T(8,128)} %param.13) | copy-start | bytes 786436
  8.1 30.3 %all-to-all-start = ((f32[4,2,64,1024]{3,2,1,0:T(8,128)}), f32[4,2,64,1024]{3,2,1,0:T(8,128)S(1)}, u32[]{:S(2)}, u32[]{:S(2)}) async-start(f32[4,2,64,1024]{3,2,1,0:T(8,128)} %bitcast.186), calls=%async_computation | async-start | bytes 4194304 | tf_op jit(solution)/shard_map/all_to_all | solution.py:95
  12.8 8.2 %copy-start.42 = (f32[30,1]{0,1:T(1,128)}, f32[30,1]{0,1:T(1,128)S(1)}, u32[]{:S(2)}) copy-start(f32[30,1]{0,1:T(1,128)S(1)} %pad_maximum_fusion.11) | copy-start | bytes 364
  16.3 4.7 %copy-start.34 = (f32[8,128]{1,0:T(8,128)S(1)}, f32[8,128]{1,0:T(8,128)}, u32[]{:S(2)}) copy-start(f32[8,128]{1,0:T(8,128)} %param.15) | copy-start | bytes 12292
  17.1 4.1 %copy-start.3 = (f32[64,1024]{1,0:T(8,128)S(1)}, f32[64,1024]{1,0:T(8,128)}, u32[]{:S(2)}) copy-start(f32[64,1024]{1,0:T(8,128)} %param.14) | copy-start | bytes 786436
  38.5 7.0 %copy-start.4 = (f32[2,64,1024]{2,1,0:T(8,128)S(1)}, f32[2,64,1024]{2,1,0:T(8,128)}, u32[]{:S(2)}) copy-start(f32[2,64,1024]{2,1,0:T(8,128)} %broadcast_multiply_fusion) | copy-start | bytes 1572868
  39.4 6.3 %copy-start.11 = (f32[62,1024]{1,0:T(8,128)S(1)}, f32[62,1024]{1,0:T(8,128)}, u32[]{:S(2)}) copy-start(f32[62,1024]{1,0:T(8,128)} %slice_bitcast_fusion.17) | copy-start | bytes 761860
  39.4 6.3 %copy-start.16 = (f32[62,1024]{1,0:T(8,128)S(1)}, f32[62,1024]{1,0:T(8,128)}, u32[]{:S(2)}) copy-start(f32[62,1024]{1,0:T(8,128)} %get-tuple-element.63) | copy-start | bytes 761860
  39.4 6.3 %copy-start.17 = (f32[62,1024]{1,0:T(8,128)S(1)}, f32[62,1024]{1,0:T(8,128)}, u32[]{:S(2)}) copy-start(f32[62,1024]{1,0:T(8,128)} %get-tuple-element.64) | copy-start | bytes 761860
  39.4 18.6 %collective-permute-start.1 = (f32[8,7,1024]{2,1,0:T(8,128)S(1)}, f32[8,7,1024]{2,1,0:T(8,128)S(1)}, u32[]{:S(2)}, u32[]{:S(2)}) collective-permute-start(f32[8,7,1024]{2,1,0:T(8,128)S(1)} %get-tuple-element.22), channel_id=1, source_target_pairs={{2,0},{4,2},{6,4},{8,6},{10,8},{12,10},{14,12},{16,14},{18,16},{20... | collective-permute-start | bytes 688136 | tf_op jit(solution)/shard_map/ppermute | solution.py:23
  40.9 17.2 %collective-permute-start = (f32[8,7,1024]{2,1,0:T(8,128)S(1)}, f32[8,7,1024]{2,1,0:T(8,128)S(1)}, u32[]{:S(2)}, u32[]{:S(2)}) collective-permute-start(f32[8,7,1024]{2,1,0:T(8,128)S(1)} %get-tuple-element.21), channel_id=1, source_target_pairs={{0,2},{2,4},{4,6},{6,8},{8,10},{10,12},{12,14},{14,16},{16,18},{18... | collective-permute-start | bytes 688136 | tf_op jit(solution)/shard_map/ppermute | solution.py:21
  47.8 1.1 copy-start.10
  47.8 1.1 copy-start.14
  47.8 1.1 copy-start.15
  51.1 1.0 copy-start.9
  51.1 1.0 copy-start.12
  51.1 1.1 copy-start.13
  54.3 1.0 copy-start.20
  54.3 1.1 copy-start.21
  58.3 1.1 copy-start.25
  58.3 1.1 copy-start.26
  58.4 1.1 copy-start.27
  58.4 1.1 copy-start.37
  60.4 1.0 copy-start.24
  60.4 1.0 copy-start.36
  62.4 1.0 copy-start.33
  66.5 1.0 copy-start.7
  66.5 1.1 copy-start.8
  71.9 3.8 %copy-start.38 = (s32[1,64]{1,0:T(1,128)S(1)}, s32[1,64]{1,0:T(1,128)}, u32[]{:S(2)}) copy-start(s32[1,64]{1,0:T(1,128)} %param.16) | copy-start | bytes 772
  71.9 28.0 %all-to-all-start.1 = ((f32[4,2,64,1024]{3,2,1,0:T(8,128)}), f32[4,2,64,1024]{3,2,1,0:T(8,128)S(1)}, u32[]{:S(2)}, u32[]{:S(2)}) async-start(f32[4,2,64,1024]{3,2,1,0:T(8,128)} %pad_maximum_fusion.1), calls=%async_computation.1 | async-start | bytes 4194304 | tf_op jit(solution)/shard_map/all_to_all | solution.py:153
  75.7 25.5 %copy-start.40 = (f32[1,64]{1,0:T(1,128)S(1)}, f32[1,64]{1,0:T(1,128)}, u32[]{:S(2)}) copy-start(f32[1,64]{1,0:T(1,128)} %param.19) | copy-start | bytes 772
  75.7 26.8 %copy-start.39 = (f32[1,64,16]{1,2,0:T(8,128)S(1)}, f32[1,64,16]{1,2,0:T(8,128)}, u32[]{:S(2)}) copy-start(f32[1,64,16]{1,2,0:T(8,128)} %param.18) | copy-start | bytes 12292
  75.7 26.8 %copy-start.41 = (f32[1,64]{1,0:T(1,128)S(1)}, f32[1,64]{1,0:T(1,128)}, u32[]{:S(2)}) copy-start(f32[1,64]{1,0:T(1,128)} %param.17) | copy-start | bytes 772
  101.1 1.2 collective-permute-start.4
  102.7 5.3 %collective-permute-start.6 = (f32[2,16,16]{2,1,0:T(8,128)S(1)}, f32[2,16,16]{2,1,0:T(8,128)S(1)}, u32[]{:S(2)}, u32[]{:S(2)}) collective-permute-start(f32[2,16,16]{2,1,0:T(8,128)S(1)} %pad_maximum_fusion.10), channel_id=1, source_target_pairs={{0,64},{32,96},{64,0},{96,32},{1,65},{33,97},{65,1},{97,33},{2,66}... | collective-permute-start | bytes 6152 | tf_op jit(solution)/shard_map/ppermute | solution.py:37
  103.3 4.9 %collective-permute-start.7 = (f32[2,16,16]{2,1,0:T(8,128)S(1)}, f32[2,16,16]{2,1,0:T(8,128)S(1)}, u32[]{:S(2)}, u32[]{:S(2)}) collective-permute-start(f32[2,16,16]{2,1,0:T(8,128)S(1)} %pad_maximum_fusion.10), channel_id=1, source_target_pairs={{0,96},{32,64},{64,32},{96,0},{1,97},{33,65},{65,33},{97,1},{2,98}... | collective-permute-start | bytes 6152 | tf_op jit(solution)/shard_map/ppermute | solution.py:37
  106.0 3.7 %collective-permute-start.5 = (f32[2,16,16]{2,1,0:T(8,128)S(1)}, f32[2,16,16]{2,1,0:T(8,128)S(1)}, u32[]{:S(2)}, u32[]{:S(2)}) collective-permute-start(f32[2,16,16]{2,1,0:T(8,128)S(1)} %pad_maximum_fusion.10), channel_id=1, source_target_pairs={{0,32},{32,0},{64,96},{96,64},{1,33},{33,1},{65,97},{97,65},{2,34}... | collective-permute-start | bytes 6152 | tf_op jit(solution)/shard_map/ppermute | solution.py:37
  106.2 11.7 %collective-permute-start.14 = (f32[8,128]{1,0:T(8,128)S(1)}, f32[8,128]{1,0:T(8,128)S(1)}, u32[]{:S(2)}, u32[]{:S(2)}) collective-permute-start(f32[8,128]{1,0:T(8,128)S(1)} %copy-done.34), channel_id=1, source_target_pairs={{0,1},{1,0},{2,3},{3,2},{4,5},{5,4},{6,7},{7,6},{8,9},{9,8},{10,11... | collective-permute-start | bytes 12296 | tf_op jit(solution)/shard_map/ppermute | solution.py:49
  109.7 8.2 %collective-permute-start.9 = (f32[2,16,16]{2,1,0:T(8,128)S(1)}, f32[2,16,16]{2,1,0:T(8,128)S(1)}, u32[]{:S(2)}, u32[]{:S(2)}) collective-permute-start(f32[2,16,16]{2,1,0:T(8,128)S(1)} %add_add_fusion.2), channel_id=1, source_target_pairs={{0,4},{2,6},{4,0},{6,2},{8,12},{10,14},{12,8},{14,10},{16,20},{18,... | collective-permute-start | bytes 6152 | tf_op jit(solution)/shard_map/ppermute | solution.py:37
  114.6 4.9 %collective-permute-start.10 = (f32[2,16,16]{2,1,0:T(8,128)S(1)}, f32[2,16,16]{2,1,0:T(8,128)S(1)}, u32[]{:S(2)}, u32[]{:S(2)}) collective-permute-start(f32[2,16,16]{2,1,0:T(8,128)S(1)} %add_add_fusion.2), channel_id=1, source_target_pairs={{0,6},{2,4},{4,2},{6,0},{8,14},{10,12},{12,10},{14,8},{16,22},{18,... | collective-permute-start | bytes 6152 | tf_op jit(solution)/shard_map/ppermute | solution.py:37
  117.1 3.7 %collective-permute-start.8 = (f32[2,16,16]{2,1,0:T(8,128)S(1)}, f32[2,16,16]{2,1,0:T(8,128)S(1)}, u32[]{:S(2)}, u32[]{:S(2)}) collective-permute-start(f32[2,16,16]{2,1,0:T(8,128)S(1)} %add_add_fusion.2), channel_id=1, source_target_pairs={{0,2},{2,0},{4,6},{6,4},{8,10},{10,8},{12,14},{14,12},{16,18},{18,... | collective-permute-start | bytes 6152 | tf_op jit(solution)/shard_map/ppermute | solution.py:37
  120.9 5.7 %collective-permute-start.12 = (f32[2,16,16]{2,1,0:T(8,128)S(1)}, f32[2,16,16]{2,1,0:T(8,128)S(1)}, u32[]{:S(2)}, u32[]{:S(2)}) collective-permute-start(f32[2,16,16]{2,1,0:T(8,128)S(1)} %add_add_fusion.1), channel_id=1, source_target_pairs={{0,16},{2,18},{4,20},{6,22},{8,24},{10,26},{12,28},{14,30},{16,0},... | collective-permute-start | bytes 6152 | tf_op jit(solution)/shard_map/ppermute | solution.py:37
  124.8 4.9 %collective-permute-start.13 = (f32[2,16,16]{2,1,0:T(8,128)S(1)}, f32[2,16,16]{2,1,0:T(8,128)S(1)}, u32[]{:S(2)}, u32[]{:S(2)}) collective-permute-start(f32[2,16,16]{2,1,0:T(8,128)S(1)} %add_add_fusion.1), channel_id=1, source_target_pairs={{0,24},{2,26},{4,28},{6,30},{8,16},{10,18},{12,20},{14,22},{16,8},... | collective-permute-start | bytes 6152 | tf_op jit(solution)/shard_map/ppermute | solution.py:37
  125.5 4.2 %collective-permute-start.11 = (f32[2,16,16]{2,1,0:T(8,128)S(1)}, f32[2,16,16]{2,1,0:T(8,128)S(1)}, u32[]{:S(2)}, u32[]{:S(2)}) collective-permute-start(f32[2,16,16]{2,1,0:T(8,128)S(1)} %add_add_fusion.1), channel_id=1, source_target_pairs={{0,8},{2,10},{4,12},{6,14},{8,0},{10,2},{12,4},{14,6},{16,24},{18,... | collective-permute-start | bytes 6152 | tf_op jit(solution)/shard_map/ppermute | solution.py:37
  (12 other events, 11.3 us)

commit v19 on v17

--- a/solution.py
+++ b/solution.py
@@ -179,11 +179,11 @@
     gram, cross = sums[0], sums[1]
     system = jnp.eye(total, dtype=jnp.float32) + gram
     factor = jnp.linalg.cholesky(system)
-    weights = jax.scipy.linalg.cho_solve((factor, True), cross)
+    own_cross = lax.dynamic_slice_in_dim(
+        cross, lax.axis_index("ens") * members_here, members_here, 1
+    )
+    own_weights = jax.scipy.linalg.cho_solve((factor, True), own_cross)
     param_anom = every_param - jnp.mean(every_param, axis=0)
-    own_weights = lax.dynamic_slice_in_dim(
-        weights, lax.axis_index("ens") * members_here, members_here, 1
-    )
     new_params = (
         params + jnp.dot(own_weights.T, param_anom, precision=lax.Precision.HIGHEST) * norm_factor
     )

time: 131 us -> 131 us (level)
  no operation moved by 1% of the time
where the time goes in v19:
time: 131 us; the launch traced here: 130 us
  waiting for transfers between devices  44.6 us (34%)
  starting transfers between devices  35.5 us (27%)
  other arithmetic  23.3 us (18%)
  local copies, waits for them, and re-layouts  22.9 us (17%)
  matrix products  2.61 us (2%)
  between operations  1.43 us (1%)
    all_to_all x1, waiting for transfers between devices, per_device(): lax.all_to_all(done, 'tm', 0, 0, tiled=True)  24.7 us
    ppermute x9, starting transfers between devices, quad_sum(): lax.ppermute(value, axis, [(i, i ^ k * bit) for i in range(count)])  14.9 us
    ppermute x9, waiting for transfers between devices, quad_sum(): lax.ppermute(value, axis, [(i, i ^ k * bit) for i in range(count)])  10.5 us
    ppermute x2, starting transfers between devices, with_halo(): lax.ppermute(tail, axis, [(i, i + 1) for i in range(ends)])  9.58 us
    mul x6, other arithmetic, advance(): return (middle + step_size * tendency) * inside  8.9 us
    all_to_all x1, waiting for transfers between devices, per_device(): lax.all_to_all(state.reshape(slices, group, row_count, col_count), 'tm',...  8.24 us
    slice x11, local copies, waits for them, and re-layouts, advance(): west_cell = jnp.pad(middle[:, :, :-1], ((0, 0), (0, 0), (1, 0)))  6.2 us
    mul x10, local copies, waits for them, and re-layouts, advance(): coeffs[0] * (above_row + below_row + west_cell + east_cell - 4.0 * middle)  4.94 us
  transfers between devices with their start and end apart: 17, of which 10 were waited for; matrix products, arithmetic and copies ran while one was open for 19% of the time, Pallas kernels for 0%

profile of v19, /device:TPU:0, one launch (start us, length us, event | category | flops | bytes accessed | tf_op | source)
XLA Modules:
  0.0 130.3 jit_solution(5953892185072295850)
XLA Ops:
  0.6 1.6 %pad_maximum_fusion.9 = (f32[4,7,1024]{2,1,0:T(8,128)}, f32[4,7,1024]{2,1,0:T(8,128)}) fusion(f32[1,64,1024]{2,1,0:T(8,128)} %bitcast.185, f32[1,64,1024]{2,1,0:T(8,128)} %bitcast.171, f32[1,64,1024]{2,1,0:T(8,128)} %bitcast.178, f32[1,64,1024]{2,1,0:T(8,128)} %bitcast.164), kind=kLoop, calls=%fused_computation.117 | loop fusion | flops 172032 | bytes 1277952 | tf_op jit(solution)/shard_map/slice | solution.py:18
  2.2 1.3 collective-permute-start.3
  3.6 4.5 %all-to-all-start = ((f32[4,2,64,1024]{3,2,1,0:T(8,128)}), f32[4,2,64,1024]{3,2,1,0:T(8,128)S(1)}, u32[]{:S(2)}, u32[]{:S(2)}) async-start(f32[4,2,64,1024]{3,2,1,0:T(8,128)} %bitcast.188), calls=%async_computation | async-start | bytes 4194304 | tf_op jit(solution)/shard_map/all_to_all | solution.py:95
  8.1 4.7 %collective-permute-start.2 = (f32[4,7,1024]{2,1,0:T(8,128)}, f32[4,7,1024]{2,1,0:T(8,128)S(1)}, u32[]{:S(2)}, u32[]{:S(2)}) collective-permute-start(f32[4,7,1024]{2,1,0:T(8,128)} %get-tuple-element.48), channel_id=1, source_target_pairs={{0,2},{2,4},{4,6},{6,8},{8,10},{10,12},{12,14},{14,16},{16,18},{18... | collective-permute-start | bytes 344072 | tf_op jit(solution)/shard_map/ppermute | solution.py:21
  14.1 0.9 slice_bitcast_fusion.15
  15.7 0.7 slice_bitcast_fusion.14
  17.1 0.8 slice_bitcast_fusion.18
  18.9 0.9 broadcast_multiply_fusion
  19.8 0.7 slice_bitcast_fusion.36
  20.5 0.8 slice_bitcast_fusion.12
  21.4 0.8 slice_bitcast_fusion.9
  22.8 0.7 slice.711
  24.2 1.0 slice_bitcast_fusion.8
  25.2 0.9 slice_bitcast_fusion.5
  26.2 8.2 %all-to-all-done = f32[4,2,64,1024]{3,2,1,0:T(8,128)S(1)} async-done(((f32[4,2,64,1024]{3,2,1,0:T(8,128)}), f32[4,2,64,1024]{3,2,1,0:T(8,128)S(1)}, u32[]{:S(2)}, u32[]{:S(2)}) %all-to-all-start) | async-done | bytes 2097184 | tf_op jit(solution)/shard_map/all_to_all | solution.py:95
  34.5 0.9 fusion.83
  35.4 1.4 %collective-permute-start.1 = (f32[8,7,1024]{2,1,0:T(8,128)S(1)}, f32[8,7,1024]{2,1,0:T(8,128)S(1)}, u32[]{:S(2)}, u32[]{:S(2)}) collective-permute-start(f32[8,7,1024]{2,1,0:T(8,128)S(1)} %get-tuple-element.22), channel_id=1, source_target_pairs={{2,0},{4,2},{6,4},{8,6},{10,8},{12,10},{14,12},{16,14},{18,16},{20... | collective-permute-start | bytes 688136 | tf_op jit(solution)/shard_map/ppermute | solution.py:23
  36.9 4.9 %collective-permute-start = (f32[8,7,1024]{2,1,0:T(8,128)S(1)}, f32[8,7,1024]{2,1,0:T(8,128)S(1)}, u32[]{:S(2)}, u32[]{:S(2)}) collective-permute-start(f32[8,7,1024]{2,1,0:T(8,128)S(1)} %get-tuple-element.21), channel_id=1, source_target_pairs={{0,2},{2,4},{4,6},{6,8},{8,10},{10,12},{12,14},{14,16},{16,18},{18... | collective-permute-start | bytes 688136 | tf_op jit(solution)/shard_map/ppermute | solution.py:21
  42.1 2.1 %fusion.8 = (f32[8,62,1024]{2,1,0:T(8,128)S(1)}, f32[8,62,1024]{2,1,0:T(8,128)S(1)}, f32[8,62,1024]{2,1,0:T(8,128)S(1)}) fusion(f32[8,64,1024]{2,1,0:T(8,128)S(1)} %bitcast.154, f32[62]{0:T(128)S(1)} %slice.606, f32[8,64,1024]{2,1,0:T(8,128)S(1)} %bitcast.152, f32[62,1024]{1,0:T(8,128)S(1)} %copy-done.13, f32[62,1024]{1,0:T(8,128)S(1)} %copy-done.14, ...), kind=kLoop, calls=%fused_computation.12 | loop fusion | flops 9142272 | bytes 19042680 | tf_op jit(solution)/shard_map/mul | solution.py:68
  44.2 1.1 fusion.82
  45.3 2.1 %fusion.5 = f32[8,60,1024]{2,1,0:T(8,128)S(1)} fusion(f32[8,64,1024]{2,1,0:T(8,128)S(1)} %bitcast.155, f32[8,62,1024]{2,1,0:T(8,128)S(1)} %get-tuple-element.4, f32[8,60,1023]{2,1,0:T(8,128)S(1)} %get-tuple-element.17, f32[8,60,1023]{2,1,0:T(8,128)S(1)} %get-tuple-element.16, f32[60]{0:T(128)S(1)} %slice.616, f32[60,1024]{1,0:T(8,128)S(1)} %copy-done.17, ...), kind=kLoop, calls=%fused_computation.8 | loop fusion | flops 8847360 | bytes 14496240 | tf_op jit(solution)/shard_map/mul | solution.py:68
  47.5 1.0 fusion.81
  48.5 2.1 %fusion.2 = f32[8,58,1024]{2,1,0:T(8,128)S(1)} fusion(f32[8,64,1024]{2,1,0:T(8,128)S(1)} %bitcast.156, f32[8,60,1024]{2,1,0:T(8,128)S(1)} %fusion.5, f32[8,58,1023]{2,1,0:T(8,128)S(1)} %get-tuple-element.15, f32[8,58,1023]{2,1,0:T(8,128)S(1)} %get-tuple-element.14, f32[58]{0:T(128)S(1)} %slice.626, f32[58,1024]{1,0:T(8,128)S(1)} %copy-done.15, ...), kind=kLoop, calls=%fused_computation.4 | loop fusion | flops 8552448 | bytes 14013032 | tf_op jit(solution)/shard_map/mul | solution.py:68
  50.7 0.9 fusion.80
  51.8 2.4 %fusion.11 = f32[8,56,1024]{2,1,0:T(8,128)S(1)} fusion(f32[8,62,1024]{2,1,0:T(8,128)S(1)} %get-tuple-element.5, f32[8,62,1024]{2,1,0:T(8,128)S(1)} %get-tuple-element.18, f32[8,64,1024]{2,1,0:T(8,128)S(1)} %bitcast.157, f32[8,58,1024]{2,1,0:T(8,128)S(1)} %fusion.2, f32[8,56,1023]{2,1,0:T(8,128)S(1)} %get-tuple-element.13, ...), kind=kLoop, calls=%fused_computation.18 | loop fusion | flops 10092544 | bytes 17199872 | tf_op jit(solution)/shard_map/sub | solution.py:124
  56.1 1.0 fusion.39
  57.7 0.9 fusion.36
  60.0 1.0 fusion.42
  65.5 1.5 %pad_maximum_fusion.1 = f32[4,2,64,1024]{3,2,1,0:T(8,128)} fusion(f32[1,2,64,1024]{3,2,1,0:T(8,128)S(1)} %get-tuple-element.9, f32[1,2,64,1024]{3,2,1,0:T(8,128)S(1)} %get-tuple-element.54, f32[1,2,64,1024]{3,2,1,0:T(8,128)S(1)} %slice_bitcast_fusion, f32[1,2,64,1024]{3,2,1,0:T(8,128)S(1)} %get-tuple-element.8), kind=kLoop, calls=%fused_computation.13 | loop fusion | flops 1572864 | bytes 4194304 | tf_op jit(solution)/shard_map/stack | solution.py:153
  66.9 3.7 %all-to-all-start.1 = ((f32[4,2,64,1024]{3,2,1,0:T(8,128)}), f32[4,2,64,1024]{3,2,1,0:T(8,128)S(1)}, u32[]{:S(2)}, u32[]{:S(2)}) async-start(f32[4,2,64,1024]{3,2,1,0:T(8,128)} %pad_maximum_fusion.1), calls=%async_computation.1 | async-start | bytes 4194304 | tf_op jit(solution)/shard_map/all_to_all | solution.py:154
  70.8 24.7 %all-to-all-done.1 = f32[4,2,64,1024]{3,2,1,0:T(8,128)S(1)} async-done(((f32[4,2,64,1024]{3,2,1,0:T(8,128)}), f32[4,2,64,1024]{3,2,1,0:T(8,128)S(1)}, u32[]{:S(2)}, u32[]{:S(2)}) %all-to-all-start.1) | async-done | bytes 2097184 | tf_op jit(solution)/shard_map/all_to_all | solution.py:154
  95.5 1.2 fusion.32
  96.8 1.1 collective-permute-done.4
  98.9 2.7 %collective-permute-start.7 = (f32[2,16,16]{2,1,0:T(8,128)S(1)}, f32[2,16,16]{2,1,0:T(8,128)S(1)}, u32[]{:S(2)}, u32[]{:S(2)}) collective-permute-start(f32[2,16,16]{2,1,0:T(8,128)S(1)} %pad_maximum_fusion.10), channel_id=1, source_target_pairs={{0,96},{32,64},{64,32},{96,0},{1,97},{33,65},{65,33},{97,1},{2,98}... | collective-permute-start | bytes 6152 | tf_op jit(solution)/shard_map/ppermute | solution.py:37
  101.8 1.8 %collective-permute-done.6 = f32[2,16,16]{2,1,0:T(8,128)S(1)} collective-permute-done((f32[2,16,16]{2,1,0:T(8,128)S(1)}, f32[2,16,16]{2,1,0:T(8,128)S(1)}, u32[]{:S(2)}, u32[]{:S(2)}) %collective-permute-start.6) | collective-permute-done | bytes 2080 | tf_op jit(solution)/shard_map/ppermute | solution.py:37
  103.8 1.5 %collective-permute-done.5 = f32[2,16,16]{2,1,0:T(8,128)S(1)} collective-permute-done((f32[2,16,16]{2,1,0:T(8,128)S(1)}, f32[2,16,16]{2,1,0:T(8,128)S(1)}, u32[]{:S(2)}, u32[]{:S(2)}) %collective-permute-start.5) | collective-permute-done | bytes 2080 | tf_op jit(solution)/shard_map/ppermute | solution.py:37
  105.3 3.4 %collective-permute-start.9 = (f32[2,16,16]{2,1,0:T(8,128)S(1)}, f32[2,16,16]{2,1,0:T(8,128)S(1)}, u32[]{:S(2)}, u32[]{:S(2)}) collective-permute-start(f32[2,16,16]{2,1,0:T(8,128)S(1)} %add_add_fusion.2), channel_id=1, source_target_pairs={{0,4},{2,6},{4,0},{6,2},{8,12},{10,14},{12,8},{14,10},{16,20},{18,... | collective-permute-start | bytes 6152 | tf_op jit(solution)/shard_map/ppermute | solution.py:37
  108.7 2.3 %collective-permute-start.10 = (f32[2,16,16]{2,1,0:T(8,128)S(1)}, f32[2,16,16]{2,1,0:T(8,128)S(1)}, u32[]{:S(2)}, u32[]{:S(2)}) collective-permute-start(f32[2,16,16]{2,1,0:T(8,128)S(1)} %add_add_fusion.2), channel_id=1, source_target_pairs={{0,6},{2,4},{4,2},{6,0},{8,14},{10,12},{12,10},{14,8},{16,22},{18,... | collective-permute-start | bytes 6152 | tf_op jit(solution)/shard_map/ppermute | solution.py:37
  111.0 0.8 collective-permute-start.8
  111.8 1.8 %collective-permute-done.10 = f32[2,16,16]{2,1,0:T(8,128)S(1)} collective-permute-done((f32[2,16,16]{2,1,0:T(8,128)S(1)}, f32[2,16,16]{2,1,0:T(8,128)S(1)}, u32[]{:S(2)}, u32[]{:S(2)}) %collective-permute-start.10) | collective-permute-done | bytes 2080 | tf_op jit(solution)/shard_map/ppermute | solution.py:37
  113.7 1.1 collective-permute-done.8
  114.8 4.0 %collective-permute-start.12 = (f32[2,16,16]{2,1,0:T(8,128)S(1)}, f32[2,16,16]{2,1,0:T(8,128)S(1)}, u32[]{:S(2)}, u32[]{:S(2)}) collective-permute-start(f32[2,16,16]{2,1,0:T(8,128)S(1)} %add_add_fusion.1), channel_id=1, source_target_pairs={{0,16},{2,18},{4,20},{6,22},{8,24},{10,26},{12,28},{14,30},{16,0},... | collective-permute-start | bytes 6152 | tf_op jit(solution)/shard_map/ppermute | solution.py:37
  119.6 0.8 collective-permute-done.12
  120.5 3.2 %collective-permute-done.13 = f32[2,16,16]{2,1,0:T(8,128)S(1)} collective-permute-done((f32[2,16,16]{2,1,0:T(8,128)S(1)}, f32[2,16,16]{2,1,0:T(8,128)S(1)}, u32[]{:S(2)}, u32[]{:S(2)}) %collective-permute-start.13) | collective-permute-done | bytes 2080 | tf_op jit(solution)/shard_map/ppermute | solution.py:37
  123.8 1.5 %cholesky.17 = f32[16,16]{1,0:T(8,128)S(1)} custom-call(f32[16,16]{1,0:T(8,128)S(1)} %fusion.60), custom_call_target="Cholesky" | custom-call | tf_op jit(solution)/shard_map/jit(cholesky)/cholesky | solution.py:181
  126.6 1.2 custom-call.10
  128.2 0.8 fusion.33
  129.0 1.3 %copy.23 = f32[1,8,64,1024]{3,2,1,0:T(8,128)} copy(f32[1,8,64,1024]{3,2,1,0:T(8,128)S(1)} %bitcast.163) | data formatting | bytes 4194304
  (151 shorter events, 18.0 us)
Async XLA Ops:
  2.2 21.3 %collective-permute-start.3 = (f32[4,7,1024]{2,1,0:T(8,128)}, f32[4,7,1024]{2,1,0:T(8,128)S(1)}, u32[]{:S(2)}, u32[]{:S(2)}) collective-permute-start(f32[4,7,1024]{2,1,0:T(8,128)} %get-tuple-element.49), channel_id=1, source_target_pairs={{2,0},{4,2},{6,4},{8,6},{10,8},{12,10},{14,12},{16,14},{18,16},{20... | collective-permute-start | bytes 344072 | tf_op jit(solution)/shard_map/ppermute | solution.py:23
  3.5 10.6 %copy-start.1 = (f32[64,1024]{1,0:T(8,128)S(1)}, f32[64,1024]{1,0:T(8,128)}, u32[]{:S(2)}) copy-start(f32[64,1024]{1,0:T(8,128)} %param.12) | copy-start | bytes 786436
  3.5 10.6 %copy-start.2 = (f32[64,1024]{1,0:T(8,128)S(1)}, f32[64,1024]{1,0:T(8,128)}, u32[]{:S(2)}) copy-start(f32[64,1024]{1,0:T(8,128)} %param.11) | copy-start | bytes 786436
  3.5 11.4 %copy-start = (f32[64,1024]{1,0:T(8,128)S(1)}, f32[64,1024]{1,0:T(8,128)}, u32[]{:S(2)}) copy-start(f32[64,1024]{1,0:T(8,128)} %param.13) | copy-start | bytes 786436
  3.6 30.9 %all-to-all-start = ((f32[4,2,64,1024]{3,2,1,0:T(8,128)}), f32[4,2,64,1024]{3,2,1,0:T(8,128)S(1)}, u32[]{:S(2)}, u32[]{:S(2)}) async-start(f32[4,2,64,1024]{3,2,1,0:T(8,128)} %bitcast.188), calls=%async_computation | async-start | bytes 4194304 | tf_op jit(solution)/shard_map/all_to_all | solution.py:95
  8.1 10.6 %copy-start.26 = (f32[8,128]{1,0:T(8,128)S(1)}, f32[8,128]{1,0:T(8,128)}, u32[]{:S(2)}) copy-start(f32[8,128]{1,0:T(8,128)} %param.15) | copy-start | bytes 12292
  8.1 15.5 %collective-permute-start.2 = (f32[4,7,1024]{2,1,0:T(8,128)}, f32[4,7,1024]{2,1,0:T(8,128)S(1)}, u32[]{:S(2)}, u32[]{:S(2)}) collective-permute-start(f32[4,7,1024]{2,1,0:T(8,128)} %get-tuple-element.48), channel_id=1, source_target_pairs={{0,2},{2,4},{4,6},{6,8},{8,10},{10,12},{12,14},{14,16},{16,18},{18... | collective-permute-start | bytes 344072 | tf_op jit(solution)/shard_map/ppermute | solution.py:21
  12.9 5.8 %copy-start.33 = (f32[30,1]{0,1:T(1,128)}, f32[30,1]{0,1:T(1,128)S(1)}, u32[]{:S(2)}) copy-start(f32[30,1]{0,1:T(1,128)S(1)} %pad_maximum_fusion.11) | copy-start | bytes 364
  14.1 4.8 %copy-start.3 = (f32[64,1024]{1,0:T(8,128)S(1)}, f32[64,1024]{1,0:T(8,128)}, u32[]{:S(2)}) copy-start(f32[64,1024]{1,0:T(8,128)} %param.14) | copy-start | bytes 786436
  18.9 3.3 %copy-start.34 = (f32[30,1]{0,1:T(1,128)S(1)}, f32[30,1]{0,1:T(1,128)}, u32[]{:S(2)}) copy-start(f32[30,1]{0,1:T(1,128)} %copy-done.33) | copy-start | bytes 364
  34.5 7.3 %copy-start.4 = (f32[2,64,1024]{2,1,0:T(8,128)S(1)}, f32[2,64,1024]{2,1,0:T(8,128)}, u32[]{:S(2)}) copy-start(f32[2,64,1024]{2,1,0:T(8,128)} %broadcast_multiply_fusion) | copy-start | bytes 1572868
  35.4 6.6 %copy-start.12 = (f32[62,1024]{1,0:T(8,128)S(1)}, f32[62,1024]{1,0:T(8,128)}, u32[]{:S(2)}) copy-start(f32[62,1024]{1,0:T(8,128)} %slice_bitcast_fusion.17) | copy-start | bytes 761860
  35.4 6.6 %copy-start.13 = (f32[62,1024]{1,0:T(8,128)S(1)}, f32[62,1024]{1,0:T(8,128)}, u32[]{:S(2)}) copy-start(f32[62,1024]{1,0:T(8,128)} %get-tuple-element.63) | copy-start | bytes 761860
  35.4 6.6 %copy-start.14 = (f32[62,1024]{1,0:T(8,128)S(1)}, f32[62,1024]{1,0:T(8,128)}, u32[]{:S(2)}) copy-start(f32[62,1024]{1,0:T(8,128)} %get-tuple-element.64) | copy-start | bytes 761860
  35.4 18.8 %collective-permute-start.1 = (f32[8,7,1024]{2,1,0:T(8,128)S(1)}, f32[8,7,1024]{2,1,0:T(8,128)S(1)}, u32[]{:S(2)}, u32[]{:S(2)}) collective-permute-start(f32[8,7,1024]{2,1,0:T(8,128)S(1)} %get-tuple-element.22), channel_id=1, source_target_pairs={{2,0},{4,2},{6,4},{8,6},{10,8},{12,10},{14,12},{16,14},{18,16},{20... | collective-permute-start | bytes 688136 | tf_op jit(solution)/shard_map/ppermute | solution.py:23
  36.9 17.4 %collective-permute-start = (f32[8,7,1024]{2,1,0:T(8,128)S(1)}, f32[8,7,1024]{2,1,0:T(8,128)S(1)}, u32[]{:S(2)}, u32[]{:S(2)}) collective-permute-start(f32[8,7,1024]{2,1,0:T(8,128)S(1)} %get-tuple-element.21), channel_id=1, source_target_pairs={{0,2},{2,4},{4,6},{6,8},{8,10},{10,12},{12,14},{14,16},{16,18},{18... | collective-permute-start | bytes 688136 | tf_op jit(solution)/shard_map/ppermute | solution.py:21
  44.2 1.1 copy-start.11
  44.2 1.1 copy-start.17
  44.2 1.1 copy-start.18
  47.4 1.0 copy-start.10
  47.4 1.0 copy-start.15
  47.4 1.1 copy-start.16
  50.6 0.9 copy-start.19
  50.6 1.0 copy-start.20
  50.7 1.1 copy-start.21
  51.8 2.5 %copy-start.23 = (f32[4,7,1024]{2,1,0:T(8,128)S(1)}, f32[4,7,1024]{2,1,0:T(8,128)}, u32[]{:S(2)}) copy-start(f32[4,7,1024]{2,1,0:T(8,128)} %copy-done.22) | copy-start | bytes 344068
  51.8 2.5 %copy-start.25 = (f32[4,7,1024]{2,1,0:T(8,128)S(1)}, f32[4,7,1024]{2,1,0:T(8,128)}, u32[]{:S(2)}) copy-start(f32[4,7,1024]{2,1,0:T(8,128)} %copy-done.24) | copy-start | bytes 344068
  61.4 1.0 copy-start.7
  61.4 1.0 copy-start.8
  61.4 1.1 copy-start.9
  63.1 1.0 copy-start.5
  63.1 1.0 copy-start.6
  66.9 3.8 %copy-start.29 = (s32[1,64]{1,0:T(1,128)S(1)}, s32[1,64]{1,0:T(1,128)}, u32[]{:S(2)}) copy-start(s32[1,64]{1,0:T(1,128)} %param.16) | copy-start | bytes 772
  66.9 28.6 %all-to-all-start.1 = ((f32[4,2,64,1024]{3,2,1,0:T(8,128)}), f32[4,2,64,1024]{3,2,1,0:T(8,128)S(1)}, u32[]{:S(2)}, u32[]{:S(2)}) async-start(f32[4,2,64,1024]{3,2,1,0:T(8,128)} %pad_maximum_fusion.1), calls=%async_computation.1 | async-start | bytes 4194304 | tf_op jit(solution)/shard_map/all_to_all | solution.py:154
  70.7 26.1 %copy-start.31 = (f32[1,64]{1,0:T(1,128)S(1)}, f32[1,64]{1,0:T(1,128)}, u32[]{:S(2)}) copy-start(f32[1,64]{1,0:T(1,128)} %param.19) | copy-start | bytes 772
  70.7 27.4 %copy-start.30 = (f32[1,64,16]{1,2,0:T(8,128)S(1)}, f32[1,64,16]{1,2,0:T(8,128)}, u32[]{:S(2)}) copy-start(f32[1,64,16]{1,2,0:T(8,128)} %param.18) | copy-start | bytes 12292
  70.7 27.4 %copy-start.32 = (f32[1,64]{1,0:T(1,128)S(1)}, f32[1,64]{1,0:T(1,128)}, u32[]{:S(2)}) copy-start(f32[1,64]{1,0:T(1,128)} %param.17) | copy-start | bytes 772
  96.7 1.2 collective-permute-start.4
  98.2 5.3 %collective-permute-start.6 = (f32[2,16,16]{2,1,0:T(8,128)S(1)}, f32[2,16,16]{2,1,0:T(8,128)S(1)}, u32[]{:S(2)}, u32[]{:S(2)}) collective-permute-start(f32[2,16,16]{2,1,0:T(8,128)S(1)} %pad_maximum_fusion.10), channel_id=1, source_target_pairs={{0,64},{32,96},{64,0},{96,32},{1,65},{33,97},{65,1},{97,33},{2,66}... | collective-permute-start | bytes 6152 | tf_op jit(solution)/shard_map/ppermute | solution.py:37
  98.9 4.9 %collective-permute-start.7 = (f32[2,16,16]{2,1,0:T(8,128)S(1)}, f32[2,16,16]{2,1,0:T(8,128)S(1)}, u32[]{:S(2)}, u32[]{:S(2)}) collective-permute-start(f32[2,16,16]{2,1,0:T(8,128)S(1)} %pad_maximum_fusion.10), channel_id=1, source_target_pairs={{0,96},{32,64},{64,32},{96,0},{1,97},{33,65},{65,33},{97,1},{2,98}... | collective-permute-start | bytes 6152 | tf_op jit(solution)/shard_map/ppermute | solution.py:37
  101.6 3.7 %collective-permute-start.5 = (f32[2,16,16]{2,1,0:T(8,128)S(1)}, f32[2,16,16]{2,1,0:T(8,128)S(1)}, u32[]{:S(2)}, u32[]{:S(2)}) collective-permute-start(f32[2,16,16]{2,1,0:T(8,128)S(1)} %pad_maximum_fusion.10), channel_id=1, source_target_pairs={{0,32},{32,0},{64,96},{96,64},{1,33},{33,1},{65,97},{97,65},{2,34}... | collective-permute-start | bytes 6152 | tf_op jit(solution)/shard_map/ppermute | solution.py:37
  101.8 10.0 %collective-permute-start.14 = (f32[8,128]{1,0:T(8,128)S(1)}, f32[8,128]{1,0:T(8,128)S(1)}, u32[]{:S(2)}, u32[]{:S(2)}) collective-permute-start(f32[8,128]{1,0:T(8,128)S(1)} %copy-done.26), channel_id=1, source_target_pairs={{0,1},{1,0},{2,3},{3,2},{4,5},{5,4},{6,7},{7,6},{8,9},{9,8},{10,11... | collective-permute-start | bytes 12296 | tf_op jit(solution)/shard_map/ppermute | solution.py:49
  105.3 6.5 %collective-permute-start.9 = (f32[2,16,16]{2,1,0:T(8,128)S(1)}, f32[2,16,16]{2,1,0:T(8,128)S(1)}, u32[]{:S(2)}, u32[]{:S(2)}) collective-permute-start(f32[2,16,16]{2,1,0:T(8,128)S(1)} %add_add_fusion.2), channel_id=1, source_target_pairs={{0,4},{2,6},{4,0},{6,2},{8,12},{10,14},{12,8},{14,10},{16,20},{18,... | collective-permute-start | bytes 6152 | tf_op jit(solution)/shard_map/ppermute | solution.py:37
  108.7 4.9 %collective-permute-start.10 = (f32[2,16,16]{2,1,0:T(8,128)S(1)}, f32[2,16,16]{2,1,0:T(8,128)S(1)}, u32[]{:S(2)}, u32[]{:S(2)}) collective-permute-start(f32[2,16,16]{2,1,0:T(8,128)S(1)} %add_add_fusion.2), channel_id=1, source_target_pairs={{0,6},{2,4},{4,2},{6,0},{8,14},{10,12},{12,10},{14,8},{16,22},{18,... | collective-permute-start | bytes 6152 | tf_op jit(solution)/shard_map/ppermute | solution.py:37
  111.0 3.7 %collective-permute-start.8 = (f32[2,16,16]{2,1,0:T(8,128)S(1)}, f32[2,16,16]{2,1,0:T(8,128)S(1)}, u32[]{:S(2)}, u32[]{:S(2)}) collective-permute-start(f32[2,16,16]{2,1,0:T(8,128)S(1)} %add_add_fusion.2), channel_id=1, source_target_pairs={{0,2},{2,0},{4,6},{6,4},{8,10},{10,8},{12,14},{14,12},{16,18},{18,... | collective-permute-start | bytes 6152 | tf_op jit(solution)/shard_map/ppermute | solution.py:37
  114.8 5.7 %collective-permute-start.12 = (f32[2,16,16]{2,1,0:T(8,128)S(1)}, f32[2,16,16]{2,1,0:T(8,128)S(1)}, u32[]{:S(2)}, u32[]{:S(2)}) collective-permute-start(f32[2,16,16]{2,1,0:T(8,128)S(1)} %add_add_fusion.1), channel_id=1, source_target_pairs={{0,16},{2,18},{4,20},{6,22},{8,24},{10,26},{12,28},{14,30},{16,0},... | collective-permute-start | bytes 6152 | tf_op jit(solution)/shard_map/ppermute | solution.py:37
  118.7 4.9 %collective-permute-start.13 = (f32[2,16,16]{2,1,0:T(8,128)S(1)}, f32[2,16,16]{2,1,0:T(8,128)S(1)}, u32[]{:S(2)}, u32[]{:S(2)}) collective-permute-start(f32[2,16,16]{2,1,0:T(8,128)S(1)} %add_add_fusion.1), channel_id=1, source_target_pairs={{0,24},{2,26},{4,28},{6,30},{8,16},{10,18},{12,20},{14,22},{16,8},... | collective-permute-start | bytes 6152 | tf_op jit(solution)/shard_map/ppermute | solution.py:37
  119.5 4.2 %collective-permute-start.11 = (f32[2,16,16]{2,1,0:T(8,128)S(1)}, f32[2,16,16]{2,1,0:T(8,128)S(1)}, u32[]{:S(2)}, u32[]{:S(2)}) collective-permute-start(f32[2,16,16]{2,1,0:T(8,128)S(1)} %add_add_fusion.1), channel_id=1, source_target_pairs={{0,8},{2,10},{4,12},{6,14},{8,0},{10,2},{12,4},{14,6},{16,24},{18,... | collective-permute-start | bytes 6152 | tf_op jit(solution)/shard_map/ppermute | solution.py:37
  (4 other events, 2.6 us)
